TPU v7x, 32 devices: a whole 2x2x4 slice. The times are simulated.
32 devices in a mesh: rows: 4 (over x, core), aux: 8 (over z, y).
Axes of the slice: x: 2, y: 2, z: 4, core: 2. Of those that a mesh axis runs over, the one named last changes fastest.
Arguments:
- b_rows: bfloat16 [6144, 8192], P(('rows', 'aux')), may hold values from -0.079589844 to 0.079589844
- pair_index: int32 [6144], P(('rows', 'aux')), may hold values from 0 to 6143, each once
- e_occ: float32 [512], replicated, may hold values from -3 to -0.5
- e_vir: float32 [1536], replicated, may hold values from 0.2 to 3
- occ_batch: int32 [1], replicated, may hold values from 0 to 127
- freq: float32 [1], replicated, may hold values from 0.3 to 3
Outputs:
- q_matrix: float32 [8192, 8192], P('aux', 'rows')
All inputs are finite; a program needn't handle non-finite values.
Results may differ from a plain program's by a relative error of at most 0.0022.
Values may be sent and summed in bfloat16 or wider, within the bound.
No kernel may reach another device: no remote copies, remote signals or barrier semaphores. Data moves between devices by JAX's collectives and lax.ppermute only.
A program may use at most 192 MiB of HBM per device.

v0:
```python
import jax
import jax.numpy as jnp
from jax import lax
from jax.sharding import Mesh, PartitionSpec as P

NVIR = 1536
NOCC_B = 4


def row_weights(pairs, e_occ, e_vir, occ_batch, freq):
    batch_start = occ_batch[0] * NOCC_B
    e_batch = lax.dynamic_slice_in_dim(e_occ, batch_start, NOCC_B, 0)
    occ = pairs // NVIR
    vir = pairs % NVIR
    occ_hit = occ[:, None] == jnp.arange(NOCC_B, dtype=jnp.int32)[None, :]
    vir_hit = vir[:, None] == jnp.arange(e_vir.shape[0], dtype=jnp.int32)[None, :]
    e_low = jnp.sum(jnp.where(occ_hit, e_batch[None, :], 0.0), axis=1)
    e_high = jnp.sum(jnp.where(vir_hit, e_vir[None, :], 0.0), axis=1)
    delta = e_high - e_low
    return 2.0 * delta / (delta * delta + freq[0] * freq[0])


def contract(left, right):
    return lax.dot_general(
        left, right, (((0,), (0,)), ((), ())), preferred_element_type=jnp.float32
    )


def swap(x, axis):
    return lax.ppermute(x, axis, [(0, 1), (1, 0)])


def scale(weight, cols):
    return (weight[:, None] * cols.astype(jnp.float32)).astype(jnp.bfloat16)


def make_body(n_rx, n_rc, n_az, n_ay):
    def body(b_rows, pair_index, e_occ, e_vir, occ_batch, freq):
        nloc, naux = b_rows.shape
        width = naux // (n_az * n_ay)
        rw = naux // (n_rx * n_rc)
        z = lax.axis_index("az")
        x = lax.axis_index("rx")
        c = lax.axis_index("rc")
        a = z * n_ay + lax.axis_index("ay")
        order = [(1 - x) * 2 + (1 - c), x * 2 + (1 - c), (1 - x) * 2 + c, x * 2 + c]
        home = (a * width) // rw
        off = (a * width) % rw

        def others(v):
            doubled = jnp.concatenate([v, v], axis=0)
            return lax.dynamic_slice_in_dim(doubled, (z + 1) * nloc, (n_az - 1) * nloc, axis=0)

        def pick(blocks):
            out = lax.dynamic_slice_in_dim(blocks[0], off, width, axis=1)
            for k in range(1, len(blocks)):
                out = jnp.where(order[k] == home, lax.dynamic_slice_in_dim(blocks[k], off, width, axis=1), out)
            return out

        w_own = row_weights(pair_index, e_occ, e_vir, occ_batch, freq)
        w_z = lax.all_gather(w_own, "az", axis=0, tiled=True)
        first = lax.dynamic_slice_in_dim(b_rows, order[0] * rw, rw, axis=1)
        mine = [lax.all_gather(first, "az", axis=0, tiled=True)]
        w_a = swap(w_own, "ay")
        w_b = swap(others(w_z), "ay")
        theirs_own = swap(b_rows, "ay")
        theirs_own, w_a, w_b, rest = lax.optimization_barrier((theirs_own, w_a, w_b, b_rows))
        theirs = [swap(others(mine[0]), "ay")]
        pieces = []
        for k, m in enumerate(order[1:], start=1):
            parts = 2 if (k == len(order) - 1 and rw % 256 == 0) else 1
            pieces += [(k, m * rw + p * (rw // parts), rw // parts) for p in range(parts)]
        got_mine, got_theirs = [mine[0]], [theirs[0]]
        by_block = {}
        for k, start, pw in pieces:
            _, _, rest = lax.optimization_barrier((got_mine[-1], got_theirs[-2] if len(got_theirs) > 1 else w_a, rest))
            piece = lax.all_gather(lax.dynamic_slice_in_dim(rest, start, pw, axis=1), "az", axis=0, tiled=True)
            got_mine.append(piece)
            got_theirs.append(swap(others(piece), "ay"))
            by_block.setdefault(k, []).append(len(got_mine) - 1)
        for k in range(1, len(order)):
            idx = by_block[k]
            mine.append(jnp.concatenate([got_mine[i] for i in idx], axis=1) if len(idx) > 1 else got_mine[idx[0]])
            theirs.append(jnp.concatenate([got_theirs[i] for i in idx], axis=1) if len(idx) > 1 else got_theirs[idx[0]])
        s_mine = scale(w_z, pick(mine))
        s_a = scale(w_a, lax.dynamic_slice_in_dim(theirs_own, a * width, width, axis=1))
        early = []
        for k, m in enumerate(order):
            cols_a = lax.dynamic_slice_in_dim(theirs_own, m * rw, rw, axis=1)
            early.append(contract(s_a, cols_a) + contract(s_mine, mine[k]))
        s_b = scale(w_b, pick(theirs))
        halves = 2 if width % 16 == 0 else 1
        hw = width // halves
        outs = []
        for h in range(halves):
            rows = slice(h * hw, (h + 1) * hw)
            s_h = s_b[:, rows]
            blocks = [early[k][rows] + contract(s_h, theirs[k]) for k in range(len(order))]
            got_other = swap(blocks[0], "rc")
            other_x = blocks[2] + got_other
            got_x = swap(other_x.astype(jnp.bfloat16), "rx")
            got_own = swap(blocks[1], "rc")
            own_x = lax.optimization_barrier(blocks[3] + got_own)
            outs.append(own_x + got_x.astype(jnp.float32))
        return jnp.concatenate(outs, axis=0) if halves > 1 else outs[0]

    return body


def make_plain_body(n_rows, n_aux):
    def body(b_rows, pair_index, e_occ, e_vir, occ_batch, freq):
        width = b_rows.shape[1] // n_aux
        group_pairs = lax.all_gather(pair_index, "aux", axis=0, tiled=True)
        group = lax.all_gather(b_rows, "aux", axis=0, tiled=True)
        own = lax.dynamic_slice_in_dim(group, lax.axis_index("aux") * width, width, axis=1)
        scaled = scale(row_weights(group_pairs, e_occ, e_vir, occ_batch, freq), own)
        return lax.psum_scatter(contract(scaled, group), "rows", scatter_dimension=1, tiled=True)

    return body


def solution(mesh):
    n_rows = mesh.shape["rows"]
    n_aux = mesh.shape["aux"]
    naux = 8192
    fits = n_rows == 4 and n_aux % 2 == 0 and (naux // n_rows) % (naux // n_aux) == 0
    if not fits:
        placed = (P(("rows", "aux"), None), P(("rows", "aux")), P(), P(), P(), P())
        return jax.shard_map(
            make_plain_body(n_rows, n_aux), mesh=mesh, in_specs=placed,
            out_specs=P("aux", "rows"), check_vma=False,
        )
    n_rx, n_rc, n_ay = 2, 2, 2
    n_az = n_aux // n_ay
    split = Mesh(mesh.devices.reshape(n_rx, n_rc, n_az, n_ay), ("rx", "rc", "az", "ay"))
    rows_all = ("rx", "rc", "az", "ay")
    placed = (P(rows_all, None), P(rows_all), P(), P(), P(), P())
    return jax.shard_map(
        make_body(n_rx, n_rc, n_az, n_ay),
        mesh=split,
        in_specs=placed,
        out_specs=P(("az", "ay"), ("rx", "rc")),
        check_vma=False,
    )
```

profile of v0, /device:TPU:0, one launch (start us, length us, event | category | flops | bytes accessed | tf_op | source)
XLA Modules:
  0.0 493.3 jit_solution(15361000499497166426)
XLA Ops:
  6.5 2.1 constant_dynamic-slice_fusion.4
  8.7 3.0 collective-permute-start
  17.6 12.3 %all-reduce = f32[768]{0:T(1024)S(1)} all-reduce(f32[768]{0:T(1024)S(1)} %get-tuple-element.21), channel_id=1, replica_groups=mesh['rx'=2,'rc'=2,'az'=4,'ay'=2] {'az'}, use_global_device_ids=true, to_apply=%add | all-reduce | flops 768 | bytes 6144
  32.0 48.2 %collective-permute-done.1 = f32[192]{0:T(256)S(1)} collective-permute-done((f32[192]{0:T(256)S(1)}, f32[192]{0:T(256)S(1)}, u32[]{:S(2)}, u32[]{:S(2)}) %collective-permute-start.1) | collective-permute-done | bytes 800 | tf_op jit(solution)/shard_map/ppermute | solution.py:30
  80.2 2.1 constant_dynamic-slice_fusion.3
  82.4 5.0 %fusion.8 = bf16[576,2048]{1,0:T(8,128)(2,1)} fusion(s32[]{:T(128)S(6)} %select_n.118, bf16[768,2048]{1,0:T(8,128)(2,1)} %all-gather.6.cloned.1.call-done), kind=kLoop, calls=%fused_computation.34 | loop fusion | flops 4718592 | bytes 5505028 | tf_op jit(solution)/shard_map/concatenate | solution.py:51
  89.2 51.0 %collective-permute-done.3 = bf16[576,2048]{1,0:T(8,128)(2,1)S(1)} collective-permute-done((bf16[576,2048]{1,0:T(8,128)(2,1)}, bf16[576,2048]{1,0:T(8,128)(2,1)S(1)}, u32[]{:S(2)}, u32[]{:S(2)}) %collective-permute-start.3) | collective-permute-done | bytes 2359328 | tf_op jit(solution)/shard_map/ppermute | solution.py:30
  140.1 7.4 %all-gather.8.cloned.1.call-done = bf16[768,2048]{1,0:T(8,128)(2,1)} async-done(((bf16[192,2048]{1,0:T(8,128)(2,1)}), bf16[768,2048]{1,0:T(8,128)(2,1)}) %all-gather.8.cloned.1.call-update) | async-done | bytes 3145744 | tf_op jit(solution)/shard_map/all_gather | solution.py:77
  147.5 2.1 constant_dynamic-slice_fusion.2
  149.7 5.0 %fusion.7 = bf16[576,2048]{1,0:T(8,128)(2,1)} fusion(s32[]{:T(128)S(6)} %select_n.118, bf16[768,2048]{1,0:T(8,128)(2,1)} %all-gather.8.cloned.1.call-done), kind=kLoop, calls=%fused_computation.33 | loop fusion | flops 4718592 | bytes 5505028 | tf_op jit(solution)/shard_map/concatenate | solution.py:51
  156.2 51.8 %collective-permute-done.4 = bf16[576,2048]{1,0:T(8,128)(2,1)} collective-permute-done((bf16[576,2048]{1,0:T(8,128)(2,1)}, bf16[576,2048]{1,0:T(8,128)(2,1)}, u32[]{:S(2)}, u32[]{:S(2)}) %collective-permute-start.4) | collective-permute-done | bytes 2359328 | tf_op jit(solution)/shard_map/ppermute | solution.py:30
  208.0 4.0 all-gather.10.cloned.1.call-done
  214.0 5.0 %fusion.6 = bf16[576,2048]{1,0:T(8,128)(2,1)} fusion(s32[]{:T(128)S(6)} %select_n.118, bf16[768,2048]{1,0:T(8,128)(2,1)} %all-gather.10.cloned.1.call-done), kind=kLoop, calls=%fused_computation.32 | loop fusion | flops 4718592 | bytes 5505028 | tf_op jit(solution)/shard_map/concatenate | solution.py:51
  220.5 29.2 %all-gather.12.cloned.1.call-done = bf16[768,1024]{1,0:T(8,128)(2,1)} async-done(((bf16[192,1024]{1,0:T(8,128)(2,1)}), bf16[768,1024]{1,0:T(8,128)(2,1)}) %all-gather.12.cloned.1.call-update) | async-done | bytes 1572880 | tf_op jit(solution)/shard_map/all_gather | solution.py:77
  249.6 22.5 %collective-permute-done.5 = bf16[576,2048]{1,0:T(8,128)(2,1)S(1)} collective-permute-done((bf16[576,2048]{1,0:T(8,128)(2,1)}, bf16[576,2048]{1,0:T(8,128)(2,1)S(1)}, u32[]{:S(2)}, u32[]{:S(2)}) %collective-permute-start.5) | collective-permute-done | bytes 2359328 | tf_op jit(solution)/shard_map/ppermute | solution.py:30
  272.1 2.0 constant_dynamic-slice_fusion
  274.2 3.2 fusion.10
  278.9 2.7 constant_dynamic-update-slice_fusion.1
  281.7 22.8 %collective-permute-done.6 = bf16[576,1024]{1,0:T(8,128)(2,1)S(1)} collective-permute-done((bf16[576,1024]{1,0:T(8,128)(2,1)}, bf16[576,1024]{1,0:T(8,128)(2,1)S(1)}, u32[]{:S(2)}, u32[]{:S(2)}) %collective-permute-start.6) | collective-permute-done | bytes 1179680 | tf_op jit(solution)/shard_map/ppermute | solution.py:30
  304.6 5.7 %all-gather.14.cloned.1.call-done = bf16[768,1024]{1,0:T(8,128)(2,1)} async-done(((bf16[192,1024]{1,0:T(8,128)(2,1)}), bf16[768,1024]{1,0:T(8,128)(2,1)}) %all-gather.14.cloned.1.call-update) | async-done | bytes 1572880 | tf_op jit(solution)/shard_map/all_gather | solution.py:77
  310.3 2.4 fusion.9
  314.2 2.7 constant_dynamic-update-slice_fusion
  316.8 3.2 multiply_convert_fusion
  320.1 3.5 fusion.36
  323.6 2.8 convolution_add_fusion
  326.4 3.9 fusion.34
  330.4 9.9 %collective-permute-done.7 = bf16[576,1024]{1,0:T(8,128)(2,1)S(1)} collective-permute-done((bf16[576,1024]{1,0:T(8,128)(2,1)S(1)}, bf16[576,1024]{1,0:T(8,128)(2,1)S(1)}, u32[]{:S(2)}, u32[]{:S(2)}) %collective-permute-start.7) | collective-permute-done | bytes 1179680 | tf_op jit(solution)/shard_map/ppermute | solution.py:30
  340.4 2.0 multiply_convert_fusion.1
  342.4 4.0 slice_add_fusion
  346.4 3.9 slice_add_fusion.4
  350.8 2.9 convolution_add_fusion.2
  353.7 3.5 fusion.35
  357.3 5.7 %slice_add_fusion.2 = f32[512,2048]{1,0:T(8,128)} fusion(f32[1024,2048]{1,0:T(8,128)S(1)} %convolution_add_fusion.2, bf16[576,2048]{1,0:T(8,128)(2,1)} %collective-permute-done.4, bf16[576,1024]{1,0:T(8,128)(2,1)S(1)} %multiply_convert_fusion.1), kind=kOutput, calls=%fused_computation.15 | convolution fusion | flops 1209008128 | bytes 11337728 | tf_op jit(solution)/shard_map/dot_general | solution.py:24
  362.9 5.6 %slice_add_fusion.6 = f32[512,2048]{1,0:T(8,128)} fusion(f32[1024,2048]{1,0:T(8,128)S(1)} %convolution_add_fusion.2, bf16[576,2048]{1,0:T(8,128)(2,1)} %collective-permute-done.4, bf16[576,1024]{1,0:T(8,128)(2,1)S(1)} %multiply_convert_fusion.1), kind=kOutput, calls=%fused_computation.22 | convolution fusion | flops 1209008128 | bytes 11337728 | tf_op jit(solution)/shard_map/dot_general | solution.py:24
  369.1 2.9 convolution_add_fusion.1
  372.0 5.9 %fusion.33 = f32[1024,2048]{1,0:T(8,128)} fusion(bf16[768,1024]{1,0:T(8,128)(2,1)S(1)} %copy-done.9, bf16[768,2048]{1,0:T(8,128)(2,1)S(1)} %copy-done.7), kind=kOutput, calls=%fused_computation.80 | convolution fusion | flops 3221225472 | bytes 13107200 | tf_op jit(solution)/shard_map/dot_general | solution.py:24
  377.9 1.8 fusion.16
  379.8 1.8 fusion.22
  381.6 6.0 %fusion.4 = (bf16[512,2048]{1,0:T(8,128)(2,1)}, bf16[512,2048]{1,0:T(8,128)(2,1)}) fusion(f32[512,2048]{1,0:T(8,128)} %collective-permute-done.9, f32[512,2048]{1,0:T(8,128)S(1)} %fusion.22, f32[1024,2048]{1,0:T(8,128)S(1)} %convolution_add_fusion.1, f32[512,2048]{1,0:T(8,128)} %collective-permute-done.12, f32[512,2048]{1,0:T(8,128)S(1)} %fusion.16), kind=kLoop, calls=%fused_computation.21 | loop fusion | flops 6291456 | bytes 29360128 | tf_op jit(solution)/shard_map/convert_element_type | solution.py:101
  389.1 5.1 %convolution_add_fusion.3 = f32[1024,2048]{1,0:T(8,128)S(1)} fusion(f32[1024,2048]{1,0:T(8,128)} %fusion.33, bf16[192,8192]{1,0:T(8,128)(2,1)} %collective-permute-done, s32[]{:T(128)S(6)} %select_n.120, s32[]{:T(128)S(6)} %select_n.119, f32[192]{0:T(256)S(1)} %collective-permute-done.1), kind=kOutput, calls=%fused_computation.10 | convolution fusion | flops 807993344 | bytes 17957640 | tf_op jit(solution)/shard_map/dot_general | solution.py:24
  394.3 1.9 fusion.19
  396.8 1.8 fusion.25
  398.6 6.4 %fusion.5 = (f32[512,2048]{1,0:T(8,128)}, f32[512,2048]{1,0:T(8,128)S(1)}) fusion(f32[512,2048]{1,0:T(8,128)} %collective-permute-done.8, f32[512,2048]{1,0:T(8,128)S(1)} %fusion.25, f32[1024,2048]{1,0:T(8,128)S(1)} %convolution_add_fusion.3, f32[512,2048]{1,0:T(8,128)} %collective-permute-done.11, f32[512,2048]{1,0:T(8,128)S(1)} %fusion.19), kind=kLoop, calls=%fused_computation.24 | loop fusion | flops 4194304 | bytes 33554432 | tf_op jit(solution)/shard_map/add | solution.py:103
  405.0 31.4 %collective-permute-done.10 = bf16[512,2048]{1,0:T(8,128)(2,1)} collective-permute-done((bf16[512,2048]{1,0:T(8,128)(2,1)}, bf16[512,2048]{1,0:T(8,128)(2,1)}, u32[]{:S(2)}, u32[]{:S(2)}) %collective-permute-start.10) | collective-permute-done | bytes 2097184 | tf_op jit(solution)/shard_map/ppermute | solution.py:30
  436.5 3.4 convert_add_fusion.1
  439.9 40.5 %collective-permute-done.13 = bf16[512,2048]{1,0:T(8,128)(2,1)} collective-permute-done((bf16[512,2048]{1,0:T(8,128)(2,1)}, bf16[512,2048]{1,0:T(8,128)(2,1)}, u32[]{:S(2)}, u32[]{:S(2)}) %collective-permute-start.13) | collective-permute-done | bytes 2097184 | tf_op jit(solution)/shard_map/ppermute | solution.py:30
  480.3 2.3 convert_add_fusion
  482.6 4.0 pad_maximum_fusion
  (61 shorter events, 19.3 us)
Async XLA Ops:
  6.5 73.7 %all-gather.6.cloned.1.call-start = ((), (), s32[]{:S(2)}) async-start(), calls=%async_computation | async-start | bytes 3932160 | tf_op jit(solution)/shard_map/all_gather | solution.py:63
  8.6 138.8 %all-gather.8.cloned.1.call-start = ((), (), s32[]{:S(2)}) async-start(), calls=%async_computation.1 | async-start | bytes 3932160 | tf_op jit(solution)/shard_map/all_gather | solution.py:77
  8.7 71.5 %collective-permute-start = (bf16[192,8192]{1,0:T(8,128)(2,1)}, bf16[192,8192]{1,0:T(8,128)(2,1)}, u32[]{:S(2)}, u32[]{:S(2)}) collective-permute-start(bf16[192,8192]{1,0:T(8,128)(2,1)} %param.6), channel_id=1, source_target_pairs={{0,1},{1,0},{2,3},{3,2},{4,5},{5,4},{6,7},{7,6},{8,9},{9,8},{10,11... | collective-permute-start | bytes 9437192 | tf_op jit(solution)/shard_map/ppermute | solution.py:30
  30.0 50.2 %collective-permute-start.2 = (f32[576]{0:T(1024)S(1)}, f32[576]{0:T(1024)S(1)}, u32[]{:S(2)}, u32[]{:S(2)}) collective-permute-start(f32[576]{0:T(1024)S(1)} %fusion.31), channel_id=1, source_target_pairs={{0,1},{1,0},{2,3},{3,2},{4,5},{5,4},{6,7},{7,6},{8,9},{9,8},{10,11... | collective-permute-start | bytes 6920 | tf_op jit(solution)/shard_map/ppermute | solution.py:30
  30.4 49.8 %collective-permute-start.1 = (f32[192]{0:T(256)S(1)}, f32[192]{0:T(256)S(1)}, u32[]{:S(2)}, u32[]{:S(2)}) collective-permute-start(f32[192]{0:T(256)S(1)} %get-tuple-element.22), channel_id=1, source_target_pairs={{0,1},{1,0},{2,3},{3,2},{4,5},{5,4},{6,7},{7,6},{8,9},{9,8},{10,11... | collective-permute-start | bytes 2312 | tf_op jit(solution)/shard_map/ppermute | solution.py:30
  82.4 129.6 %all-gather.10.cloned.1.call-start = ((), (), s32[]{:S(2)}) async-start(), calls=%async_computation.2 | async-start | bytes 3932160 | tf_op jit(solution)/shard_map/all_gather | solution.py:77
  87.4 52.7 %collective-permute-start.3 = (bf16[576,2048]{1,0:T(8,128)(2,1)}, bf16[576,2048]{1,0:T(8,128)(2,1)S(1)}, u32[]{:S(2)}, u32[]{:S(2)}) collective-permute-start(bf16[576,2048]{1,0:T(8,128)(2,1)} %fusion.8), channel_id=1, source_target_pairs={{0,1},{1,0},{2,3},{3,2},{4,5},{5,4},{6,7},{7,6},{8,9},{9,8},{10,11... | collective-permute-start | bytes 7077896 | tf_op jit(solution)/shard_map/ppermute | solution.py:30
  140.1 14.6 %copy-start.2 = (bf16[576,2048]{1,0:T(8,128)(2,1)}, bf16[576,2048]{1,0:T(8,128)(2,1)S(1)}, u32[]{:S(2)}) copy-start(bf16[576,2048]{1,0:T(8,128)(2,1)S(1)} %collective-permute-done.3) | copy-start | bytes 7077892
  149.6 100.0 %all-gather.12.cloned.1.call-start = ((), (), s32[]{:S(2)}) async-start(), calls=%async_computation.3 | async-start | bytes 1966080 | tf_op jit(solution)/shard_map/all_gather | solution.py:77
  154.7 53.3 %collective-permute-start.4 = (bf16[576,2048]{1,0:T(8,128)(2,1)}, bf16[576,2048]{1,0:T(8,128)(2,1)}, u32[]{:S(2)}, u32[]{:S(2)}) collective-permute-start(bf16[576,2048]{1,0:T(8,128)(2,1)} %fusion.7), channel_id=1, source_target_pairs={{0,1},{1,0},{2,3},{3,2},{4,5},{5,4},{6,7},{7,6},{8,9},{9,8},{10,11... | collective-permute-start | bytes 7077896 | tf_op jit(solution)/shard_map/ppermute | solution.py:30
  213.7 96.5 %all-gather.14.cloned.1.call-start = ((), (), s32[]{:S(2)}) async-start(), calls=%async_computation.4 | async-start | bytes 1966080 | tf_op jit(solution)/shard_map/all_gather | solution.py:77
  219.0 53.2 %collective-permute-start.5 = (bf16[576,2048]{1,0:T(8,128)(2,1)}, bf16[576,2048]{1,0:T(8,128)(2,1)S(1)}, u32[]{:S(2)}, u32[]{:S(2)}) collective-permute-start(bf16[576,2048]{1,0:T(8,128)(2,1)} %fusion.6), channel_id=1, source_target_pairs={{0,1},{1,0},{2,3},{3,2},{4,5},{5,4},{6,7},{7,6},{8,9},{9,8},{10,11... | collective-permute-start | bytes 7077896 | tf_op jit(solution)/shard_map/ppermute | solution.py:30
  272.1 9.5 %copy-start = (bf16[576,2048]{1,0:T(8,128)(2,1)}, bf16[576,2048]{1,0:T(8,128)(2,1)S(1)}, u32[]{:S(2)}) copy-start(bf16[576,2048]{1,0:T(8,128)(2,1)S(1)} %collective-permute-done.5) | copy-start | bytes 7077892
  277.4 27.0 %collective-permute-start.6 = (bf16[576,1024]{1,0:T(8,128)(2,1)}, bf16[576,1024]{1,0:T(8,128)(2,1)S(1)}, u32[]{:S(2)}, u32[]{:S(2)}) collective-permute-start(bf16[576,1024]{1,0:T(8,128)(2,1)} %fusion.10), channel_id=1, source_target_pairs={{0,1},{1,0},{2,3},{3,2},{4,5},{5,4},{6,7},{7,6},{8,9},{9,8},{10,11... | collective-permute-start | bytes 3538952 | tf_op jit(solution)/shard_map/ppermute | solution.py:30
  310.3 6.6 %copy-start.4 = (bf16[768,2048]{1,0:T(8,128)(2,1)S(1)}, bf16[768,2048]{1,0:T(8,128)(2,1)}, u32[]{:S(2)}) copy-start(bf16[768,2048]{1,0:T(8,128)(2,1)} %all-gather.6.cloned.1.call-done) | copy-start | bytes 9437188
  312.6 27.7 %collective-permute-start.7 = (bf16[576,1024]{1,0:T(8,128)(2,1)S(1)}, bf16[576,1024]{1,0:T(8,128)(2,1)S(1)}, u32[]{:S(2)}, u32[]{:S(2)}) collective-permute-start(bf16[576,1024]{1,0:T(8,128)(2,1)S(1)} %fusion.9), channel_id=1, source_target_pairs={{0,1},{1,0},{2,3},{3,2},{4,5},{5,4},{6,7},{7,6},{8,9},{9,8},{10,11... | collective-permute-start | bytes 3538952 | tf_op jit(solution)/shard_map/ppermute | solution.py:30
  320.1 33.7 %copy-start.8 = (bf16[768,1024]{1,0:T(8,128)(2,1)}, bf16[768,1024]{1,0:T(8,128)(2,1)S(1)}, u32[]{:S(2)}) copy-start(bf16[768,1024]{1,0:T(8,128)(2,1)S(1)} %multiply_convert_fusion) | copy-start | bytes 4718596
  323.6 2.8 copy-start.5
  326.4 14.0 %copy-start.3 = (bf16[576,2048]{1,0:T(8,128)(2,1)S(1)}, bf16[576,2048]{1,0:T(8,128)(2,1)}, u32[]{:S(2)}) copy-start(bf16[576,2048]{1,0:T(8,128)(2,1)} %copy-done.2) | copy-start | bytes 7077892
  330.4 10.0 %copy-start.1 = (bf16[576,2048]{1,0:T(8,128)(2,1)S(1)}, bf16[576,2048]{1,0:T(8,128)(2,1)}, u32[]{:S(2)}) copy-start(bf16[576,2048]{1,0:T(8,128)(2,1)} %copy-done) | copy-start | bytes 7077892
  346.4 35.2 %collective-permute-start.12 = (f32[512,2048]{1,0:T(8,128)}, f32[512,2048]{1,0:T(8,128)}, u32[]{:S(2)}, u32[]{:S(2)}) collective-permute-start(f32[512,2048]{1,0:T(8,128)} %slice_add_fusion), channel_id=1, source_target_pairs={{0,8},{8,0},{1,9},{9,1},{2,10},{10,2},{3,11},{11,3},{4,12},{12,4},... | collective-permute-start | bytes 12582920 | tf_op jit(solution)/shard_map/ppermute | solution.py:30
  350.3 3.4 copy-start.6
  350.3 31.3 %collective-permute-start.9 = (f32[512,2048]{1,0:T(8,128)}, f32[512,2048]{1,0:T(8,128)}, u32[]{:S(2)}, u32[]{:S(2)}) collective-permute-start(f32[512,2048]{1,0:T(8,128)} %slice_add_fusion.4), channel_id=1, source_target_pairs={{0,8},{8,0},{1,9},{9,1},{2,10},{10,2},{3,11},{11,3},{4,12},{12,4},... | collective-permute-start | bytes 12582920 | tf_op jit(solution)/shard_map/ppermute | solution.py:30
  362.9 35.7 %collective-permute-start.11 = (f32[512,2048]{1,0:T(8,128)}, f32[512,2048]{1,0:T(8,128)}, u32[]{:S(2)}, u32[]{:S(2)}) collective-permute-start(f32[512,2048]{1,0:T(8,128)} %slice_add_fusion.2), channel_id=1, source_target_pairs={{0,8},{8,0},{1,9},{9,1},{2,10},{10,2},{3,11},{11,3},{4,12},{12,4},... | collective-permute-start | bytes 12582920 | tf_op jit(solution)/shard_map/ppermute | solution.py:30
  368.6 3.4 copy-start.7
  368.6 3.4 copy-start.9
  368.6 30.1 %collective-permute-start.8 = (f32[512,2048]{1,0:T(8,128)}, f32[512,2048]{1,0:T(8,128)}, u32[]{:S(2)}, u32[]{:S(2)}) collective-permute-start(f32[512,2048]{1,0:T(8,128)} %slice_add_fusion.6), channel_id=1, source_target_pairs={{0,8},{8,0},{1,9},{9,1},{2,10},{10,2},{3,11},{11,3},{4,12},{12,4},... | collective-permute-start | bytes 12582920 | tf_op jit(solution)/shard_map/ppermute | solution.py:30
  387.6 48.8 %collective-permute-start.10 = (bf16[512,2048]{1,0:T(8,128)(2,1)}, bf16[512,2048]{1,0:T(8,128)(2,1)}, u32[]{:S(2)}, u32[]{:S(2)}) collective-permute-start(bf16[512,2048]{1,0:T(8,128)(2,1)} %get-tuple-element.23), channel_id=1, source_target_pairs={{0,16},{16,0},{1,17},{17,1},{2,18},{18,2},{3,19},{19,3},{4,20},{20... | collective-permute-start | bytes 6291464 | tf_op jit(solution)/shard_map/ppermute | solution.py:30
  396.1 84.2 %collective-permute-start.13 = (bf16[512,2048]{1,0:T(8,128)(2,1)}, bf16[512,2048]{1,0:T(8,128)(2,1)}, u32[]{:S(2)}, u32[]{:S(2)}) collective-permute-start(bf16[512,2048]{1,0:T(8,128)(2,1)} %get-tuple-element.24), channel_id=1, source_target_pairs={{0,16},{16,0},{1,17},{17,1},{2,18},{18,2},{3,19},{19,3},{4,20},{20... | collective-permute-start | bytes 6291464 | tf_op jit(solution)/shard_map/ppermute | solution.py:30
Sparse Core Ops, SparseCore 0:
  8.9 66.3 all-gather.5
  82.5 64.9 all-gather.7
  149.7 62.1 all-gather.9
  213.9 35.7 all-gather.11
  274.3 35.8 all-gather.13
where the time goes:
time: 499 us; the launch traced here: 493 us
  waiting for transfers between devices  324 us (65%)
  matrix products  57.2 us (11%)
  other arithmetic  49.9 us (10%)
  local copies, waits for them, and re-layouts  17.8 us (4%)
  starting transfers between devices  16.2 us (3%)
  between operations  15.5 us (3%)
  blocking collectives  12.3 us (2%)
    ppermute x14, waiting for transfers between devices, swap(): return lax.ppermute(x, axis, [(0, 1), (1, 0)])  278 us
    dot_general x16, matrix products, contract(): lax.dot_general(left, right, (((0,), (0,)), ((), ())), preferred_element_...  57.2 us
    all_gather x4, waiting for transfers between devices, body(): lax.all_gather(lax.dynamic_slice_in_dim(rest, start, pw, axis=1), 'az', a...  46.2 us
    concatenate x6, other arithmetic, others(): doubled = jnp.concatenate([v, v], axis=0)  20.7 us
    ppermute x14, starting transfers between devices, swap(): return lax.ppermute(x, axis, [(0, 1), (1, 0)])  15.9 us
    unnamed x1, blocking collectives  12.3 us
  transfers between devices with their start and end apart: 19, of which 12 were waited for; matrix products, arithmetic and copies ran while one was open for 20% of the time, Pallas kernels for 0%

commit v1 on v0

--- a/solution.py
+++ b/solution.py
@@ -73,7 +73,7 @@
         got_mine, got_theirs = [mine[0]], [theirs[0]]
         by_block = {}
         for k, start, pw in pieces:
-            _, _, rest = lax.optimization_barrier((got_mine[-1], got_theirs[-2] if len(got_theirs) > 1 else w_a, rest))
+            _, _, rest = lax.optimization_barrier((got_mine[-1], got_theirs[-3] if len(got_theirs) > 2 else w_a, rest))
             piece = lax.all_gather(lax.dynamic_slice_in_dim(rest, start, pw, axis=1), "az", axis=0, tiled=True)
             got_mine.append(piece)
             got_theirs.append(swap(others(piece), "ay"))
@@ -91,17 +91,23 @@
         s_b = scale(w_b, pick(theirs))
         halves = 2 if width % 16 == 0 else 1
         hw = width // halves
+        cuts = [slice(h * hw, (h + 1) * hw) for h in range(halves)]
+        sent, got_x = [], []
+        for rows in cuts:
+            s_h = s_b[:, rows]
+            give = early[0][rows] + contract(s_h, theirs[0])
+            other_x = early[2][rows] + contract(s_h, theirs[2]) + swap(give, "rc")
+            sent.append(other_x.astype(jnp.bfloat16))
+            got_x.append(swap(sent[-1], "rx"))
+        _, late_give, late_keep, t_give, t_keep = lax.optimization_barrier(
+            (tuple(sent), early[1], early[3], theirs[1], theirs[3])
+        )
         outs = []
-        for h in range(halves):
-            rows = slice(h * hw, (h + 1) * hw)
+        for h, rows in enumerate(cuts):
             s_h = s_b[:, rows]
-            blocks = [early[k][rows] + contract(s_h, theirs[k]) for k in range(len(order))]
-            got_other = swap(blocks[0], "rc")
-            other_x = blocks[2] + got_other
-            got_x = swap(other_x.astype(jnp.bfloat16), "rx")
-            got_own = swap(blocks[1], "rc")
-            own_x = lax.optimization_barrier(blocks[3] + got_own)
-            outs.append(own_x + got_x.astype(jnp.float32))
+            give = late_give[rows] + contract(s_h, t_give)
+            own_x = late_keep[rows] + contract(s_h, t_keep) + swap(give, "rc")
+            outs.append(own_x + got_x[h].astype(jnp.float32))
         return jnp.concatenate(outs, axis=0) if halves > 1 else outs[0]
 
     return body

time: 499 us -> 541 us (1.084)
  waiting for transfers between devices: 324 us -> 369 us
    all_gather x4, waiting for transfers between devices: 46.2 us -> 71.4 us  [body(): lax.all_gather(lax.dynamic_slice_in_dim(rest, start, pw, axis=1), 'az', a...]
    ppermute x14, waiting for transfers between devices: 278 us -> 297 us  [swap(): return lax.ppermute(x, axis, [(0, 1), (1, 0)])]
    add x3 -> x2, other arithmetic: 12.1 us -> 11.5 us  [body(): outs.append(own_x + got_x[h].astype(jnp.float32))]
  transfers between devices with their start and end apart: 19 -> 19, of which waited for: 12 -> 10; matrix products, arithmetic and copies ran while one was open for 20% -> 15% of each run, Pallas kernels for 0% -> 0%
where the time goes in v1:
time: 541 us; the launch traced here: 536 us
  waiting for transfers between devices  369 us (68%)
  matrix products  60.7 us (11%)
  other arithmetic  47.2 us (9%)
  local copies, waits for them, and re-layouts  17.1 us (3%)
  between operations  15.5 us (3%)
  starting transfers between devices  14 us (3%)
  blocking collectives  12.3 us (2%)
    ppermute x14, waiting for transfers between devices, swap(): return lax.ppermute(x, axis, [(0, 1), (1, 0)])  297 us
    all_gather x4, waiting for transfers between devices, body(): lax.all_gather(lax.dynamic_slice_in_dim(rest, start, pw, axis=1), 'az', a...  71.4 us
    dot_general x16, matrix products, contract(): lax.dot_general(left, right, (((0,), (0,)), ((), ())), preferred_element_...  60.7 us
    concatenate x6, other arithmetic, others(): doubled = jnp.concatenate([v, v], axis=0)  21.1 us
    ppermute x14, starting transfers between devices, swap(): return lax.ppermute(x, axis, [(0, 1), (1, 0)])  13.7 us
    unnamed x1, blocking collectives  12.3 us
    add x2, other arithmetic, body(): outs.append(own_x + got_x[h].astype(jnp.float32))  11.5 us
  transfers between devices with their start and end apart: 19, of which 10 were waited for; matrix products, arithmetic and copies ran while one was open for 15% of the time, Pallas kernels for 0%

profile of v1, /device:TPU:0, one launch (start us, length us, event | category | flops | bytes accessed | tf_op | source)
XLA Modules:
  0.0 535.5 jit_solution(1923860320234198677)
XLA Ops:
  6.5 2.1 constant_dynamic-slice_fusion.4
  8.7 3.0 collective-permute-start
  17.6 12.3 %all-reduce = f32[768]{0:T(1024)S(1)} all-reduce(f32[768]{0:T(1024)S(1)} %get-tuple-element.29), channel_id=1, replica_groups=mesh['rx'=2,'rc'=2,'az'=4,'ay'=2] {'az'}, use_global_device_ids=true, to_apply=%add | all-reduce | flops 768 | bytes 6144
  30.4 1.6 collective-permute-start.1
  32.0 48.2 %collective-permute-done.1 = f32[192]{0:T(256)S(1)} collective-permute-done((f32[192]{0:T(256)S(1)}, f32[192]{0:T(256)S(1)}, u32[]{:S(2)}, u32[]{:S(2)}) %collective-permute-start.1) | collective-permute-done | bytes 800 | tf_op jit(solution)/shard_map/ppermute | solution.py:30
  80.2 2.7 constant_dynamic-slice_fusion.3
  83.0 65.1 %all-gather.8.cloned.1.call-done = bf16[768,2048]{1,0:T(8,128)(2,1)} async-done(((bf16[192,2048]{1,0:T(8,128)(2,1)}), bf16[768,2048]{1,0:T(8,128)(2,1)}) %all-gather.8.cloned.1.call-update) | async-done | bytes 3145744 | tf_op jit(solution)/shard_map/all_gather | solution.py:77
  148.1 2.1 constant_dynamic-slice_fusion.2
  150.3 5.0 fusion.6
  155.3 1.5 collective-permute-start.3
  156.8 5.1 fusion.5
  162.6 47.2 %collective-permute-done.3 = bf16[576,2048]{1,0:T(8,128)(2,1)} collective-permute-done((bf16[576,2048]{1,0:T(8,128)(2,1)}, bf16[576,2048]{1,0:T(8,128)(2,1)}, u32[]{:S(2)}, u32[]{:S(2)}) %collective-permute-start.3) | collective-permute-done | bytes 2359328 | tf_op jit(solution)/shard_map/ppermute | solution.py:30
  209.8 2.8 all-gather.10.cloned.1.call-done
  212.6 1.8 constant_dynamic-slice_fusion.1
  214.6 44.5 %collective-permute-done.4 = bf16[576,2048]{1,0:T(8,128)(2,1)S(1)} collective-permute-done((bf16[576,2048]{1,0:T(8,128)(2,1)}, bf16[576,2048]{1,0:T(8,128)(2,1)S(1)}, u32[]{:S(2)}, u32[]{:S(2)}) %collective-permute-start.4) | collective-permute-done | bytes 2359328 | tf_op jit(solution)/shard_map/ppermute | solution.py:30
  259.1 2.0 constant_dynamic-slice_fusion
  261.1 3.3 fusion.8
  264.4 1.5 collective-permute-start.5
  265.9 5.2 fusion.4
  271.5 1.4 constant_dynamic-update-slice_fusion.1
  272.9 20.6 %collective-permute-done.5 = bf16[576,1024]{1,0:T(8,128)(2,1)S(1)} collective-permute-done((bf16[576,1024]{1,0:T(8,128)(2,1)}, bf16[576,1024]{1,0:T(8,128)(2,1)S(1)}, u32[]{:S(2)}, u32[]{:S(2)}) %collective-permute-start.5) | collective-permute-done | bytes 1179680 | tf_op jit(solution)/shard_map/ppermute | solution.py:30
  293.6 3.6 all-gather.14.cloned.1.call-done
  297.2 2.4 fusion.7
  299.5 1.5 collective-permute-start.6
  301.1 2.7 constant_dynamic-update-slice_fusion
  303.8 3.2 multiply_convert_fusion
  307.0 3.5 fusion.38
  310.6 1.4 convolution_add_fusion.2
  312.0 5.6 %fusion.37 = f32[1024,2048]{1,0:T(8,128)S(1)} fusion(bf16[768,1024]{1,0:T(8,128)(2,1)S(1)} %multiply_convert_fusion, bf16[768,2048]{1,0:T(8,128)(2,1)} %all-gather.10.cloned.1.call-done), kind=kOutput, calls=%fused_computation.78 | convolution fusion | flops 3221225472 | bytes 13107200 | tf_op jit(solution)/shard_map/dot_general | solution.py:24
  317.6 49.6 %collective-permute-done.6 = bf16[576,1024]{1,0:T(8,128)(2,1)S(1)} collective-permute-done((bf16[576,1024]{1,0:T(8,128)(2,1)S(1)}, bf16[576,1024]{1,0:T(8,128)(2,1)S(1)}, u32[]{:S(2)}, u32[]{:S(2)}) %collective-permute-start.6) | collective-permute-done | bytes 1179680 | tf_op jit(solution)/shard_map/ppermute | solution.py:30
  367.4 2.3 multiply_convert_fusion.1
  369.7 5.6 %slice_add_fusion = f32[512,2048]{1,0:T(8,128)} fusion(f32[1024,2048]{1,0:T(8,128)S(1)} %convolution_add_fusion.2, bf16[576,2048]{1,0:T(8,128)(2,1)} %collective-permute-done.3, bf16[576,1024]{1,0:T(8,128)(2,1)S(1)} %multiply_convert_fusion.1), kind=kOutput, calls=%fused_computation.11 | convolution fusion | flops 1209008128 | bytes 11337728 | tf_op jit(solution)/shard_map/dot_general | solution.py:24
  375.2 5.6 %slice_add_fusion.2 = f32[512,2048]{1,0:T(8,128)} fusion(f32[1024,2048]{1,0:T(8,128)S(1)} %convolution_add_fusion.2, bf16[576,2048]{1,0:T(8,128)(2,1)} %collective-permute-done.3, bf16[576,1024]{1,0:T(8,128)(2,1)S(1)} %multiply_convert_fusion.1), kind=kOutput, calls=%fused_computation.15 | convolution fusion | flops 1209008128 | bytes 11337728 | tf_op jit(solution)/shard_map/dot_general | solution.py:24
  382.8 5.4 %fusion.40 = f32[1024,2048]{1,0:T(8,128)S(1)} fusion(bf16[768,1024]{1,0:T(8,128)(2,1)S(1)} %multiply_convert_fusion, bf16[768,2048]{1,0:T(8,128)(2,1)} %constant_dynamic-update-slice_fusion), kind=kOutput, calls=%fused_computation.81 | convolution fusion | flops 3221225472 | bytes 13107200 | tf_op jit(solution)/shard_map/dot_general | solution.py:24
  388.2 4.7 convolution_add_fusion
  392.9 3.9 fusion.39
  396.9 1.4 convolution_add_fusion.1
  398.3 3.5 fusion.18
  401.8 5.5 %fusion.27 = f32[512,2048]{1,0:T(8,128)} fusion(bf16[576,2048]{1,0:T(8,128)(2,1)} %collective-permute-done.7, bf16[576,1024]{1,0:T(8,128)(2,1)S(1)} %multiply_convert_fusion.1), kind=kOutput, calls=%fused_computation.53 | convolution fusion | flops 1207959552 | bytes 7143424 | tf_op jit(solution)/shard_map/dot_general | solution.py:24
  407.3 7.2 %fusion.3 = (bf16[512,2048]{1,0:T(8,128)(2,1)}, bf16[512,2048]{1,0:T(8,128)(2,1)}) fusion(f32[512,2048]{1,0:T(8,128)} %collective-permute-done.8, f32[512,2048]{1,0:T(8,128)} %fusion.27, f32[1024,2048]{1,0:T(8,128)S(1)} %convolution_add_fusion.3, f32[512,2048]{1,0:T(8,128)} %collective-permute-done.9, f32[512,2048]{1,0:T(8,128)S(1)} %fusion.18), kind=kLoop, calls=%fused_computation.18 | loop fusion | flops 6291456 | bytes 29360128 | tf_op jit(solution)/shard_map/convert_element_type | solution.py:100
  414.5 5.6 %slice_add_fusion.4 = f32[512,2048]{1,0:T(8,128)} fusion(f32[1024,2048]{1,0:T(8,128)S(1)} %convolution_add_fusion.1, bf16[576,2048]{1,0:T(8,128)(2,1)} %copy-done, bf16[576,1024]{1,0:T(8,128)(2,1)S(1)} %multiply_convert_fusion.1), kind=kOutput, calls=%fused_computation.20 | convolution fusion | flops 1209008128 | bytes 11337728 | tf_op jit(solution)/shard_map/dot_general | solution.py:24
  420.1 3.8 slice_add_fusion.5
  424.5 1.5 collective-permute-start.11
  426.5 1.8 fusion.15
  428.3 1.8 fusion.24
  430.2 43.1 %collective-permute-done.11 = bf16[512,2048]{1,0:T(8,128)(2,1)} collective-permute-done((bf16[512,2048]{1,0:T(8,128)(2,1)}, bf16[512,2048]{1,0:T(8,128)(2,1)}, u32[]{:S(2)}, u32[]{:S(2)}) %collective-permute-start.11) | collective-permute-done | bytes 2097184 | tf_op jit(solution)/shard_map/ppermute | solution.py:30
  473.3 44.0 %collective-permute-done.13 = bf16[512,2048]{1,0:T(8,128)(2,1)} collective-permute-done((bf16[512,2048]{1,0:T(8,128)(2,1)}, bf16[512,2048]{1,0:T(8,128)(2,1)}, u32[]{:S(2)}, u32[]{:S(2)}) %collective-permute-start.13) | collective-permute-done | bytes 2097184 | tf_op jit(solution)/shard_map/ppermute | solution.py:30
  517.3 11.5 %convert_add_fusion.1 = (f32[1024,2048]{1,0:T(8,128)}, f32[1024,2048]{1,0:T(8,128)}) fusion(bf16[512,2048]{1,0:T(8,128)(2,1)} %collective-permute-done.11, f32[512,2048]{1,0:T(8,128)} %collective-permute-done.10, f32[512,2048]{1,0:T(8,128)S(1)} %fusion.24, f32[1024,2048]{1,0:T(8,128)} %convolution_add_fusion, ...), kind=kLoop, output_to_operand_aliasing={{0}: (7, {}), {1}: (7, {})}, calls=%fused_computation.21 | loop fusion | flops 8388608 | bytes 37748736 | tf_op jit(solution)/shard_map/add | solution.py:110
  (55 shorter events, 9.1 us)
Async XLA Ops:
  6.5 73.7 %all-gather.6.cloned.1.call-start = ((), (), s32[]{:S(2)}) async-start(), calls=%async_computation | async-start | bytes 3932160 | tf_op jit(solution)/shard_map/all_gather | solution.py:63
  8.7 139.4 %all-gather.8.cloned.1.call-start = ((), (), s32[]{:S(2)}) async-start(), calls=%async_computation.1 | async-start | bytes 3932160 | tf_op jit(solution)/shard_map/all_gather | solution.py:77
  8.7 71.5 %collective-permute-start = (bf16[192,8192]{1,0:T(8,128)(2,1)}, bf16[192,8192]{1,0:T(8,128)(2,1)S(1)}, u32[]{:S(2)}, u32[]{:S(2)}) collective-permute-start(bf16[192,8192]{1,0:T(8,128)(2,1)} %param.6), channel_id=1, source_target_pairs={{0,1},{1,0},{2,3},{3,2},{4,5},{5,4},{6,7},{7,6},{8,9},{9,8},{10,11... | collective-permute-start | bytes 9437192 | tf_op jit(solution)/shard_map/ppermute | solution.py:30
  30.0 50.2 %collective-permute-start.2 = (f32[576]{0:T(1024)S(1)}, f32[576]{0:T(1024)S(1)}, u32[]{:S(2)}, u32[]{:S(2)}) collective-permute-start(f32[576]{0:T(1024)S(1)} %fusion.35), channel_id=1, source_target_pairs={{0,1},{1,0},{2,3},{3,2},{4,5},{5,4},{6,7},{7,6},{8,9},{9,8},{10,11... | collective-permute-start | bytes 6920 | tf_op jit(solution)/shard_map/ppermute | solution.py:30
  30.4 49.8 %collective-permute-start.1 = (f32[192]{0:T(256)S(1)}, f32[192]{0:T(256)S(1)}, u32[]{:S(2)}, u32[]{:S(2)}) collective-permute-start(f32[192]{0:T(256)S(1)} %get-tuple-element.30), channel_id=1, source_target_pairs={{0,1},{1,0},{2,3},{3,2},{4,5},{5,4},{6,7},{7,6},{8,9},{9,8},{10,11... | collective-permute-start | bytes 2312 | tf_op jit(solution)/shard_map/ppermute | solution.py:30
  80.2 75.1 %copy-start.3 = (bf16[192,8192]{1,0:T(8,128)(2,1)}, bf16[192,8192]{1,0:T(8,128)(2,1)S(1)}, u32[]{:S(2)}) copy-start(bf16[192,8192]{1,0:T(8,128)(2,1)S(1)} %collective-permute-done) | copy-start | bytes 9437188
  83.0 129.6 %all-gather.10.cloned.1.call-start = ((), (), s32[]{:S(2)}) async-start(), calls=%async_computation.2 | async-start | bytes 3932160 | tf_op jit(solution)/shard_map/all_gather | solution.py:77
  150.2 108.8 %all-gather.12.cloned.1.call-start = ((), (), s32[]{:S(2)}) async-start(), calls=%async_computation.3 | async-start | bytes 1966080 | tf_op jit(solution)/shard_map/all_gather | solution.py:77
  155.3 54.5 %collective-permute-start.3 = (bf16[576,2048]{1,0:T(8,128)(2,1)}, bf16[576,2048]{1,0:T(8,128)(2,1)}, u32[]{:S(2)}, u32[]{:S(2)}) collective-permute-start(bf16[576,2048]{1,0:T(8,128)(2,1)} %fusion.6), channel_id=1, source_target_pairs={{0,1},{1,0},{2,3},{3,2},{4,5},{5,4},{6,7},{7,6},{8,9},{9,8},{10,11... | collective-permute-start | bytes 7077896 | tf_op jit(solution)/shard_map/ppermute | solution.py:30
  161.9 97.1 %collective-permute-start.4 = (bf16[576,2048]{1,0:T(8,128)(2,1)}, bf16[576,2048]{1,0:T(8,128)(2,1)S(1)}, u32[]{:S(2)}, u32[]{:S(2)}) collective-permute-start(bf16[576,2048]{1,0:T(8,128)(2,1)} %fusion.5), channel_id=1, source_target_pairs={{0,1},{1,0},{2,3},{3,2},{4,5},{5,4},{6,7},{7,6},{8,9},{9,8},{10,11... | collective-permute-start | bytes 7077896 | tf_op jit(solution)/shard_map/ppermute | solution.py:30
  214.3 82.8 %all-gather.14.cloned.1.call-start = ((), (), s32[]{:S(2)}) async-start(), calls=%async_computation.4 | async-start | bytes 1966080 | tf_op jit(solution)/shard_map/all_gather | solution.py:77
  259.1 12.0 %copy-start = (bf16[576,2048]{1,0:T(8,128)(2,1)}, bf16[576,2048]{1,0:T(8,128)(2,1)S(1)}, u32[]{:S(2)}) copy-start(bf16[576,2048]{1,0:T(8,128)(2,1)S(1)} %collective-permute-done.4) | copy-start | bytes 7077892
  264.4 29.1 %collective-permute-start.5 = (bf16[576,1024]{1,0:T(8,128)(2,1)}, bf16[576,1024]{1,0:T(8,128)(2,1)S(1)}, u32[]{:S(2)}, u32[]{:S(2)}) collective-permute-start(bf16[576,1024]{1,0:T(8,128)(2,1)} %fusion.8), channel_id=1, source_target_pairs={{0,1},{1,0},{2,3},{3,2},{4,5},{5,4},{6,7},{7,6},{8,9},{9,8},{10,11... | collective-permute-start | bytes 3538952 | tf_op jit(solution)/shard_map/ppermute | solution.py:30
  265.9 5.7 %copy-start.7 = (bf16[768,1024]{1,0:T(8,128)(2,1)S(1)}, bf16[768,1024]{1,0:T(8,128)(2,1)}, u32[]{:S(2)}) copy-start(bf16[768,1024]{1,0:T(8,128)(2,1)} %all-gather.12.cloned.1.call-done) | copy-start | bytes 4718596
  271.1 96.2 %collective-permute-start.7 = (bf16[576,2048]{1,0:T(8,128)(2,1)}, bf16[576,2048]{1,0:T(8,128)(2,1)}, u32[]{:S(2)}, u32[]{:S(2)}) collective-permute-start(bf16[576,2048]{1,0:T(8,128)(2,1)} %fusion.4), channel_id=1, source_target_pairs={{0,1},{1,0},{2,3},{3,2},{4,5},{5,4},{6,7},{7,6},{8,9},{9,8},{10,11... | collective-permute-start | bytes 7077896 | tf_op jit(solution)/shard_map/ppermute | solution.py:30
  297.2 6.6 %copy-start.5 = (bf16[768,2048]{1,0:T(8,128)(2,1)S(1)}, bf16[768,2048]{1,0:T(8,128)(2,1)}, u32[]{:S(2)}) copy-start(bf16[768,2048]{1,0:T(8,128)(2,1)} %all-gather.6.cloned.1.call-done) | copy-start | bytes 9437188
  299.5 67.7 %collective-permute-start.6 = (bf16[576,1024]{1,0:T(8,128)(2,1)S(1)}, bf16[576,1024]{1,0:T(8,128)(2,1)S(1)}, u32[]{:S(2)}, u32[]{:S(2)}) collective-permute-start(bf16[576,1024]{1,0:T(8,128)(2,1)S(1)} %fusion.7), channel_id=1, source_target_pairs={{0,1},{1,0},{2,3},{3,2},{4,5},{5,4},{6,7},{7,6},{8,9},{9,8},{10,11... | collective-permute-start | bytes 3538952 | tf_op jit(solution)/shard_map/ppermute | solution.py:30
  307.0 3.6 copy-start.4
  317.6 49.8 %copy-start.1 = (bf16[576,2048]{1,0:T(8,128)(2,1)S(1)}, bf16[576,2048]{1,0:T(8,128)(2,1)}, u32[]{:S(2)}) copy-start(bf16[576,2048]{1,0:T(8,128)(2,1)} %copy-done) | copy-start | bytes 7077892
  375.2 32.1 %collective-permute-start.9 = (f32[512,2048]{1,0:T(8,128)}, f32[512,2048]{1,0:T(8,128)}, u32[]{:S(2)}, u32[]{:S(2)}) collective-permute-start(f32[512,2048]{1,0:T(8,128)} %slice_add_fusion), channel_id=1, source_target_pairs={{0,8},{8,0},{1,9},{9,1},{2,10},{10,2},{3,11},{11,3},{4,12},{12,4},... | collective-permute-start | bytes 12582920 | tf_op jit(solution)/shard_map/ppermute | solution.py:30
  380.9 26.4 %collective-permute-start.8 = (f32[512,2048]{1,0:T(8,128)}, f32[512,2048]{1,0:T(8,128)}, u32[]{:S(2)}, u32[]{:S(2)}) collective-permute-start(f32[512,2048]{1,0:T(8,128)} %slice_add_fusion.2), channel_id=1, source_target_pairs={{0,8},{8,0},{1,9},{9,1},{2,10},{10,2},{3,11},{11,3},{4,12},{12,4},... | collective-permute-start | bytes 12582920 | tf_op jit(solution)/shard_map/ppermute | solution.py:30
  388.2 4.7 copy-start.6
  414.5 5.6 %copy-start.2 = (bf16[576,2048]{1,0:T(8,128)(2,1)S(1)}, bf16[576,2048]{1,0:T(8,128)(2,1)}, u32[]{:S(2)}) copy-start(bf16[576,2048]{1,0:T(8,128)(2,1)} %copy-done) | copy-start | bytes 7077892
  423.9 93.3 %collective-permute-start.12 = (f32[512,2048]{1,0:T(8,128)}, f32[512,2048]{1,0:T(8,128)}, u32[]{:S(2)}, u32[]{:S(2)}) collective-permute-start(f32[512,2048]{1,0:T(8,128)} %slice_add_fusion.4), channel_id=1, source_target_pairs={{0,8},{8,0},{1,9},{9,1},{2,10},{10,2},{3,11},{11,3},{4,12},{12,4},... | collective-permute-start | bytes 12582920 | tf_op jit(solution)/shard_map/ppermute | solution.py:30
  423.9 93.3 %collective-permute-start.10 = (f32[512,2048]{1,0:T(8,128)}, f32[512,2048]{1,0:T(8,128)}, u32[]{:S(2)}, u32[]{:S(2)}) collective-permute-start(f32[512,2048]{1,0:T(8,128)} %slice_add_fusion.5), channel_id=1, source_target_pairs={{0,8},{8,0},{1,9},{9,1},{2,10},{10,2},{3,11},{11,3},{4,12},{12,4},... | collective-permute-start | bytes 12582920 | tf_op jit(solution)/shard_map/ppermute | solution.py:30
  424.5 48.8 %collective-permute-start.11 = (bf16[512,2048]{1,0:T(8,128)(2,1)}, bf16[512,2048]{1,0:T(8,128)(2,1)}, u32[]{:S(2)}, u32[]{:S(2)}) collective-permute-start(bf16[512,2048]{1,0:T(8,128)(2,1)} %get-tuple-element.33), channel_id=1, source_target_pairs={{0,16},{16,0},{1,17},{17,1},{2,18},{18,2},{3,19},{19,3},{4,20},{20... | collective-permute-start | bytes 6291464 | tf_op jit(solution)/shard_map/ppermute | solution.py:30
  425.9 91.3 %collective-permute-start.13 = (bf16[512,2048]{1,0:T(8,128)(2,1)}, bf16[512,2048]{1,0:T(8,128)(2,1)}, u32[]{:S(2)}, u32[]{:S(2)}) collective-permute-start(bf16[512,2048]{1,0:T(8,128)(2,1)} %get-tuple-element.34), channel_id=1, source_target_pairs={{0,16},{16,0},{1,17},{17,1},{2,18},{18,2},{3,19},{19,3},{4,20},{20... | collective-permute-start | bytes 6291464 | tf_op jit(solution)/shard_map/ppermute | solution.py:30
Sparse Core Ops, SparseCore 0:
  8.9 66.3 all-gather.5
  83.1 64.9 all-gather.7
  150.4 62.1 all-gather.9
  214.5 35.7 all-gather.11
  261.2 35.8 all-gather.13

commit v2 on v1

--- a/solution.py
+++ b/solution.py
@@ -68,12 +68,12 @@
         theirs = [swap(others(mine[0]), "ay")]
         pieces = []
         for k, m in enumerate(order[1:], start=1):
-            parts = 2 if (k == len(order) - 1 and rw % 256 == 0) else 1
+            parts = 1
             pieces += [(k, m * rw + p * (rw // parts), rw // parts) for p in range(parts)]
         got_mine, got_theirs = [mine[0]], [theirs[0]]
         by_block = {}
         for k, start, pw in pieces:
-            _, _, rest = lax.optimization_barrier((got_mine[-1], got_theirs[-3] if len(got_theirs) > 2 else w_a, rest))
+            _, _, rest = lax.optimization_barrier((got_mine[-1], got_theirs[-2] if len(got_theirs) > 1 else w_a, rest))
             piece = lax.all_gather(lax.dynamic_slice_in_dim(rest, start, pw, axis=1), "az", axis=0, tiled=True)
             got_mine.append(piece)
             got_theirs.append(swap(others(piece), "ay"))

time: 541 us -> 502 us (0.928)
  waiting for transfers between devices: 369 us -> 342 us
  local copies, waits for them, and re-layouts: 17.1 us -> 11.1 us
    ppermute x14 -> x13, waiting for transfers between devices: 297 us -> 275 us  [swap(): return lax.ppermute(x, axis, [(0, 1), (1, 0)])]
    all_gather x4 -> x3, waiting for transfers between devices: 71.4 us -> 67 us  [body(): lax.all_gather(lax.dynamic_slice_in_dim(rest, start, pw, axis=1), 'az', a...]
    concatenate x6 -> x5, other arithmetic: 21.1 us -> 19 us  [others(): doubled = jnp.concatenate([v, v], axis=0)]
    ppermute x14 -> x13, starting transfers between devices: 13.7 us -> 14.3 us  [swap(): return lax.ppermute(x, axis, [(0, 1), (1, 0)])]
  transfers between devices with their start and end apart: 19 -> 17, of which waited for: 10 -> 9; matrix products, arithmetic and copies ran while one was open for 15% -> 14% of each run, Pallas kernels for 0% -> 0%
where the time goes in v2:
time: 502 us; the launch traced here: 498 us
  waiting for transfers between devices  342 us (68%)
  matrix products  57.6 us (11%)
  other arithmetic  44.8 us (9%)
  between operations  15.5 us (3%)
  starting transfers between devices  14.6 us (3%)
  blocking collectives  12.3 us (2%)
  local copies, waits for them, and re-layouts  11.1 us (2%)
    ppermute x13, waiting for transfers between devices, swap(): return lax.ppermute(x, axis, [(0, 1), (1, 0)])  275 us
    all_gather x3, waiting for transfers between devices, body(): lax.all_gather(lax.dynamic_slice_in_dim(rest, start, pw, axis=1), 'az', a...  67 us
    dot_general x16, matrix products, contract(): lax.dot_general(left, right, (((0,), (0,)), ((), ())), preferred_element_...  57.6 us
    concatenate x5, other arithmetic, others(): doubled = jnp.concatenate([v, v], axis=0)  19 us
    ppermute x13, starting transfers between devices, swap(): return lax.ppermute(x, axis, [(0, 1), (1, 0)])  14.3 us
    unnamed x1, blocking collectives  12.3 us
    add x2, other arithmetic, body(): outs.append(own_x + got_x[h].astype(jnp.float32))  11.5 us
  transfers between devices with their start and end apart: 17, of which 9 were waited for; matrix products, arithmetic and copies ran while one was open for 14% of the time, Pallas kernels for 0%

profile of v2, /device:TPU:0, one launch (start us, length us, event | category | flops | bytes accessed | tf_op | source)
XLA Modules:
  0.0 498.3 jit_solution(1770291726445939313)
XLA Ops:
  6.5 2.1 constant_dynamic-slice_fusion.3
  8.7 3.0 collective-permute-start
  13.0 0.8 dynamic_slice.69
  13.8 1.2 dynamic-slice
  16.5 1.0 select_reduce_fusion
  17.6 12.3 %all-reduce = f32[768]{0:T(1024)S(1)} all-reduce(f32[768]{0:T(1024)S(1)} %get-tuple-element.27), channel_id=1, replica_groups=mesh['rx'=2,'rc'=2,'az'=4,'ay'=2] {'az'}, use_global_device_ids=true, to_apply=%add | all-reduce | flops 768 | bytes 6144
  30.4 1.6 collective-permute-start.1
  32.0 48.2 %collective-permute-done.1 = f32[192]{0:T(256)S(1)} collective-permute-done((f32[192]{0:T(256)S(1)}, f32[192]{0:T(256)S(1)}, u32[]{:S(2)}, u32[]{:S(2)}) %collective-permute-start.1) | collective-permute-done | bytes 800 | tf_op jit(solution)/shard_map/ppermute | solution.py:30
  80.2 2.7 constant_dynamic-slice_fusion.2
  83.0 5.0 %fusion.7 = bf16[576,2048]{1,0:T(8,128)(2,1)} fusion(s32[]{:T(128)S(6)} %select_n.114, bf16[768,2048]{1,0:T(8,128)(2,1)} %all-gather.5.cloned.1.call-done), kind=kLoop, calls=%fused_computation.29 | loop fusion | flops 4718592 | bytes 5505028 | tf_op jit(solution)/shard_map/concatenate | solution.py:51
  88.1 1.7 collective-permute-start.3
  89.8 50.9 %collective-permute-done.3 = bf16[576,2048]{1,0:T(8,128)(2,1)S(1)} collective-permute-done((bf16[576,2048]{1,0:T(8,128)(2,1)}, bf16[576,2048]{1,0:T(8,128)(2,1)S(1)}, u32[]{:S(2)}, u32[]{:S(2)}) %collective-permute-start.3) | collective-permute-done | bytes 2359328 | tf_op jit(solution)/shard_map/ppermute | solution.py:30
  140.7 7.4 %all-gather.7.cloned.1.call-done = bf16[768,2048]{1,0:T(8,128)(2,1)} async-done(((bf16[192,2048]{1,0:T(8,128)(2,1)}), bf16[768,2048]{1,0:T(8,128)(2,1)}) %all-gather.7.cloned.1.call-update) | async-done | bytes 3145744 | tf_op jit(solution)/shard_map/all_gather | solution.py:77
  148.1 2.1 constant_dynamic-slice_fusion.1
  150.5 5.0 %fusion.6 = bf16[576,2048]{1,0:T(8,128)(2,1)} fusion(s32[]{:T(128)S(6)} %select_n.114, bf16[768,2048]{1,0:T(8,128)(2,1)} %all-gather.7.cloned.1.call-done), kind=kLoop, calls=%fused_computation.28 | loop fusion | flops 4718592 | bytes 5505028 | tf_op jit(solution)/shard_map/concatenate | solution.py:51
  155.5 1.5 collective-permute-start.4
  157.0 51.7 %collective-permute-done.4 = bf16[576,2048]{1,0:T(8,128)(2,1)S(1)} collective-permute-done((bf16[576,2048]{1,0:T(8,128)(2,1)}, bf16[576,2048]{1,0:T(8,128)(2,1)S(1)}, u32[]{:S(2)}, u32[]{:S(2)}) %collective-permute-start.4) | collective-permute-done | bytes 2359328 | tf_op jit(solution)/shard_map/ppermute | solution.py:30
  208.7 3.9 all-gather.9.cloned.1.call-done
  212.6 2.1 constant_dynamic-slice_fusion
  214.7 5.0 %fusion.4 = bf16[576,2048]{1,0:T(8,128)(2,1)} fusion(s32[]{:T(128)S(6)} %select_n.114, bf16[768,2048]{1,0:T(8,128)(2,1)} %all-gather.9.cloned.1.call-done), kind=kLoop, calls=%fused_computation.26 | loop fusion | flops 4718592 | bytes 5505028 | tf_op jit(solution)/shard_map/concatenate | solution.py:51
  219.8 1.5 collective-permute-start.6
  221.3 55.7 %all-gather.11.cloned.1.call-done = bf16[768,2048]{1,0:T(8,128)(2,1)} async-done(((bf16[192,2048]{1,0:T(8,128)(2,1)}), bf16[768,2048]{1,0:T(8,128)(2,1)}) %all-gather.11.cloned.1.call-update) | async-done | bytes 3145744 | tf_op jit(solution)/shard_map/all_gather | solution.py:77
  277.0 3.7 fusion.5
  280.7 1.5 collective-permute-start.5
  282.3 3.3 multiply_convert_fusion
  285.6 3.5 fusion.37
  289.1 1.4 convolution_add_fusion.2
  290.6 5.7 %fusion.36 = f32[1024,2048]{1,0:T(8,128)S(1)} fusion(bf16[768,1024]{1,0:T(8,128)(2,1)S(1)} %multiply_convert_fusion, bf16[768,2048]{1,0:T(8,128)(2,1)} %all-gather.9.cloned.1.call-done), kind=kOutput, calls=%fused_computation.70 | convolution fusion | flops 3221225472 | bytes 13107200 | tf_op jit(solution)/shard_map/dot_general | solution.py:24
  296.3 37.5 %collective-permute-done.5 = bf16[576,2048]{1,0:T(8,128)(2,1)S(1)} collective-permute-done((bf16[576,2048]{1,0:T(8,128)(2,1)S(1)}, bf16[576,2048]{1,0:T(8,128)(2,1)S(1)}, u32[]{:S(2)}, u32[]{:S(2)}) %collective-permute-start.5) | collective-permute-done | bytes 2359328 | tf_op jit(solution)/shard_map/ppermute | solution.py:30
  333.8 2.0 multiply_convert_fusion.1
  335.7 3.9 slice_add_fusion
  339.7 3.9 slice_add_fusion.2
  344.1 1.4 convolution_add_fusion.3
  345.5 5.4 %fusion.39 = f32[1024,2048]{1,0:T(8,128)S(1)} fusion(bf16[768,1024]{1,0:T(8,128)(2,1)S(1)} %multiply_convert_fusion, bf16[768,2048]{1,0:T(8,128)(2,1)} %all-gather.11.cloned.1.call-done), kind=kOutput, calls=%fused_computation.73 | convolution fusion | flops 3221225472 | bytes 13107200 | tf_op jit(solution)/shard_map/dot_general | solution.py:24
  351.0 5.1 %convolution_add_fusion = f32[1024,2048]{1,0:T(8,128)} fusion(f32[1024,2048]{1,0:T(8,128)S(1)} %fusion.39, bf16[192,8192]{1,0:T(8,128)(2,1)S(1)} %copy-done.6, s32[]{:T(128)S(6)} %select_n.121, s32[]{:T(128)S(6)} %select_n.115, f32[192]{0:T(256)S(1)} %collective-permute-done.1), kind=kOutput, calls=%fused_computation.9 | convolution fusion | flops 807993344 | bytes 17957896 | tf_op jit(solution)/shard_map/dot_general | solution.py:24
  356.1 3.5 fusion.38
  359.6 1.4 convolution_add_fusion.1
  361.0 3.5 fusion.17
  364.5 5.5 %fusion.26 = f32[512,2048]{1,0:T(8,128)} fusion(bf16[576,2048]{1,0:T(8,128)(2,1)} %collective-permute-done.6, bf16[576,1024]{1,0:T(8,128)(2,1)S(1)} %multiply_convert_fusion.1), kind=kOutput, calls=%fused_computation.50 | convolution fusion | flops 1207959552 | bytes 7143424 | tf_op jit(solution)/shard_map/dot_general | solution.py:24
  370.1 7.2 %fusion.3 = (bf16[512,2048]{1,0:T(8,128)(2,1)}, bf16[512,2048]{1,0:T(8,128)(2,1)}) fusion(f32[512,2048]{1,0:T(8,128)} %collective-permute-done.7, f32[512,2048]{1,0:T(8,128)} %fusion.26, f32[1024,2048]{1,0:T(8,128)S(1)} %convolution_add_fusion.3, f32[512,2048]{1,0:T(8,128)} %collective-permute-done.8, f32[512,2048]{1,0:T(8,128)S(1)} %fusion.17), kind=kLoop, calls=%fused_computation.20 | loop fusion | flops 6291456 | bytes 29360128 | tf_op jit(solution)/shard_map/convert_element_type | solution.py:100
  377.2 5.6 %slice_add_fusion.4 = f32[512,2048]{1,0:T(8,128)} fusion(f32[1024,2048]{1,0:T(8,128)S(1)} %convolution_add_fusion.1, bf16[576,2048]{1,0:T(8,128)(2,1)} %copy-done, bf16[576,1024]{1,0:T(8,128)(2,1)S(1)} %multiply_convert_fusion.1), kind=kOutput, calls=%fused_computation.22 | convolution fusion | flops 1209008128 | bytes 11337728 | tf_op jit(solution)/shard_map/dot_general | solution.py:24
  382.8 3.9 slice_add_fusion.5
  387.2 1.5 collective-permute-start.10
  389.2 1.8 fusion.14
  391.1 1.8 fusion.23
  392.9 43.1 %collective-permute-done.10 = bf16[512,2048]{1,0:T(8,128)(2,1)} collective-permute-done((bf16[512,2048]{1,0:T(8,128)(2,1)}, bf16[512,2048]{1,0:T(8,128)(2,1)}, u32[]{:S(2)}, u32[]{:S(2)}) %collective-permute-start.10) | collective-permute-done | bytes 2097184 | tf_op jit(solution)/shard_map/ppermute | solution.py:30
  436.0 44.0 %collective-permute-done.12 = bf16[512,2048]{1,0:T(8,128)(2,1)} collective-permute-done((bf16[512,2048]{1,0:T(8,128)(2,1)}, bf16[512,2048]{1,0:T(8,128)(2,1)}, u32[]{:S(2)}, u32[]{:S(2)}) %collective-permute-start.12) | collective-permute-done | bytes 2097184 | tf_op jit(solution)/shard_map/ppermute | solution.py:30
  480.0 11.5 %convert_add_fusion.1 = (f32[1024,2048]{1,0:T(8,128)}, f32[1024,2048]{1,0:T(8,128)}) fusion(bf16[512,2048]{1,0:T(8,128)(2,1)} %collective-permute-done.10, f32[512,2048]{1,0:T(8,128)} %collective-permute-done.9, f32[512,2048]{1,0:T(8,128)S(1)} %fusion.23, f32[1024,2048]{1,0:T(8,128)} %convolution_add_fusion, ...), kind=kLoop, output_to_operand_aliasing={{0}: (7, {}), {1}: (7, {})}, calls=%fused_computation.23 | loop fusion | flops 8388608 | bytes 37748736 | tf_op jit(solution)/shard_map/add | solution.py:110
  (48 shorter events, 3.4 us)
Async XLA Ops:
  6.5 73.7 %all-gather.5.cloned.1.call-start = ((), (), s32[]{:S(2)}) async-start(), calls=%async_computation | async-start | bytes 3932160 | tf_op jit(solution)/shard_map/all_gather | solution.py:63
  8.7 139.4 %all-gather.7.cloned.1.call-start = ((), (), s32[]{:S(2)}) async-start(), calls=%async_computation.1 | async-start | bytes 3932160 | tf_op jit(solution)/shard_map/all_gather | solution.py:77
  8.7 71.5 %collective-permute-start = (bf16[192,8192]{1,0:T(8,128)(2,1)}, bf16[192,8192]{1,0:T(8,128)(2,1)S(1)}, u32[]{:S(2)}, u32[]{:S(2)}) collective-permute-start(bf16[192,8192]{1,0:T(8,128)(2,1)} %param.6), channel_id=1, source_target_pairs={{0,1},{1,0},{2,3},{3,2},{4,5},{5,4},{6,7},{7,6},{8,9},{9,8},{10,11... | collective-permute-start | bytes 9437192 | tf_op jit(solution)/shard_map/ppermute | solution.py:30
  30.0 50.2 %collective-permute-start.2 = (f32[576]{0:T(1024)S(1)}, f32[576]{0:T(1024)S(1)}, u32[]{:S(2)}, u32[]{:S(2)}) collective-permute-start(f32[576]{0:T(1024)S(1)} %fusion.34), channel_id=1, source_target_pairs={{0,1},{1,0},{2,3},{3,2},{4,5},{5,4},{6,7},{7,6},{8,9},{9,8},{10,11... | collective-permute-start | bytes 6920 | tf_op jit(solution)/shard_map/ppermute | solution.py:30
  30.4 49.8 %collective-permute-start.1 = (f32[192]{0:T(256)S(1)}, f32[192]{0:T(256)S(1)}, u32[]{:S(2)}, u32[]{:S(2)}) collective-permute-start(f32[192]{0:T(256)S(1)} %get-tuple-element.28), channel_id=1, source_target_pairs={{0,1},{1,0},{2,3},{3,2},{4,5},{5,4},{6,7},{7,6},{8,9},{9,8},{10,11... | collective-permute-start | bytes 2312 | tf_op jit(solution)/shard_map/ppermute | solution.py:30
  80.2 2.8 copy-start.5
  83.0 129.6 %all-gather.9.cloned.1.call-start = ((), (), s32[]{:S(2)}) async-start(), calls=%async_computation.2 | async-start | bytes 3932160 | tf_op jit(solution)/shard_map/all_gather | solution.py:77
  88.1 52.6 %collective-permute-start.3 = (bf16[576,2048]{1,0:T(8,128)(2,1)}, bf16[576,2048]{1,0:T(8,128)(2,1)S(1)}, u32[]{:S(2)}, u32[]{:S(2)}) collective-permute-start(bf16[576,2048]{1,0:T(8,128)(2,1)} %fusion.7), channel_id=1, source_target_pairs={{0,1},{1,0},{2,3},{3,2},{4,5},{5,4},{6,7},{7,6},{8,9},{9,8},{10,11... | collective-permute-start | bytes 7077896 | tf_op jit(solution)/shard_map/ppermute | solution.py:30
  140.7 9.8 %copy-start.3 = (bf16[576,2048]{1,0:T(8,128)(2,1)}, bf16[576,2048]{1,0:T(8,128)(2,1)S(1)}, u32[]{:S(2)}) copy-start(bf16[576,2048]{1,0:T(8,128)(2,1)S(1)} %collective-permute-done.3) | copy-start | bytes 7077892
  150.3 126.7 %all-gather.11.cloned.1.call-start = ((), (), s32[]{:S(2)}) async-start(), calls=%async_computation.3 | async-start | bytes 3932160 | tf_op jit(solution)/shard_map/all_gather | solution.py:77
  155.5 53.2 %collective-permute-start.4 = (bf16[576,2048]{1,0:T(8,128)(2,1)}, bf16[576,2048]{1,0:T(8,128)(2,1)S(1)}, u32[]{:S(2)}, u32[]{:S(2)}) collective-permute-start(bf16[576,2048]{1,0:T(8,128)(2,1)} %fusion.6), channel_id=1, source_target_pairs={{0,1},{1,0},{2,3},{3,2},{4,5},{5,4},{6,7},{7,6},{8,9},{9,8},{10,11... | collective-permute-start | bytes 7077896 | tf_op jit(solution)/shard_map/ppermute | solution.py:30
  208.7 11.1 %copy-start = (bf16[576,2048]{1,0:T(8,128)(2,1)}, bf16[576,2048]{1,0:T(8,128)(2,1)S(1)}, u32[]{:S(2)}) copy-start(bf16[576,2048]{1,0:T(8,128)(2,1)S(1)} %collective-permute-done.4) | copy-start | bytes 7077892
  219.8 76.5 %collective-permute-start.6 = (bf16[576,2048]{1,0:T(8,128)(2,1)}, bf16[576,2048]{1,0:T(8,128)(2,1)}, u32[]{:S(2)}, u32[]{:S(2)}) collective-permute-start(bf16[576,2048]{1,0:T(8,128)(2,1)} %fusion.4), channel_id=1, source_target_pairs={{0,1},{1,0},{2,3},{3,2},{4,5},{5,4},{6,7},{7,6},{8,9},{9,8},{10,11... | collective-permute-start | bytes 7077896 | tf_op jit(solution)/shard_map/ppermute | solution.py:30
  277.0 5.3 %copy-start.9 = (bf16[768,2048]{1,0:T(8,128)(2,1)S(1)}, bf16[768,2048]{1,0:T(8,128)(2,1)}, u32[]{:S(2)}) copy-start(bf16[768,2048]{1,0:T(8,128)(2,1)} %all-gather.11.cloned.1.call-done) | copy-start | bytes 9437188
  280.7 4.8 copy-start.7
  280.7 53.0 %collective-permute-start.5 = (bf16[576,2048]{1,0:T(8,128)(2,1)S(1)}, bf16[576,2048]{1,0:T(8,128)(2,1)S(1)}, u32[]{:S(2)}, u32[]{:S(2)}) collective-permute-start(bf16[576,2048]{1,0:T(8,128)(2,1)S(1)} %fusion.5), channel_id=1, source_target_pairs={{0,1},{1,0},{2,3},{3,2},{4,5},{5,4},{6,7},{7,6},{8,9},{9,8},{10,11... | collective-permute-start | bytes 7077896 | tf_op jit(solution)/shard_map/ppermute | solution.py:30
  285.6 3.5 copy-start.6
  290.5 43.2 %copy-start.1 = (bf16[576,2048]{1,0:T(8,128)(2,1)S(1)}, bf16[576,2048]{1,0:T(8,128)(2,1)}, u32[]{:S(2)}) copy-start(bf16[576,2048]{1,0:T(8,128)(2,1)} %copy-done) | copy-start | bytes 7077892
  290.5 43.2 %copy-start.4 = (bf16[576,2048]{1,0:T(8,128)(2,1)S(1)}, bf16[576,2048]{1,0:T(8,128)(2,1)}, u32[]{:S(2)}) copy-start(bf16[576,2048]{1,0:T(8,128)(2,1)} %copy-done.3) | copy-start | bytes 7077892
  339.7 30.4 %collective-permute-start.8 = (f32[512,2048]{1,0:T(8,128)}, f32[512,2048]{1,0:T(8,128)}, u32[]{:S(2)}, u32[]{:S(2)}) collective-permute-start(f32[512,2048]{1,0:T(8,128)} %slice_add_fusion), channel_id=1, source_target_pairs={{0,8},{8,0},{1,9},{9,1},{2,10},{10,2},{3,11},{11,3},{4,12},{12,4},... | collective-permute-start | bytes 12582920 | tf_op jit(solution)/shard_map/ppermute | solution.py:30
  343.6 26.4 %collective-permute-start.7 = (f32[512,2048]{1,0:T(8,128)}, f32[512,2048]{1,0:T(8,128)}, u32[]{:S(2)}, u32[]{:S(2)}) collective-permute-start(f32[512,2048]{1,0:T(8,128)} %slice_add_fusion.2), channel_id=1, source_target_pairs={{0,8},{8,0},{1,9},{9,1},{2,10},{10,2},{3,11},{11,3},{4,12},{12,4},... | collective-permute-start | bytes 12582920 | tf_op jit(solution)/shard_map/ppermute | solution.py:30
  351.0 5.1 %copy-start.8 = (bf16[768,2048]{1,0:T(8,128)(2,1)S(1)}, bf16[768,2048]{1,0:T(8,128)(2,1)}, u32[]{:S(2)}) copy-start(bf16[768,2048]{1,0:T(8,128)(2,1)} %all-gather.7.cloned.1.call-done) | copy-start | bytes 9437188
  377.2 5.6 %copy-start.2 = (bf16[576,2048]{1,0:T(8,128)(2,1)S(1)}, bf16[576,2048]{1,0:T(8,128)(2,1)}, u32[]{:S(2)}) copy-start(bf16[576,2048]{1,0:T(8,128)(2,1)} %copy-done) | copy-start | bytes 7077892
  386.7 93.3 %collective-permute-start.11 = (f32[512,2048]{1,0:T(8,128)}, f32[512,2048]{1,0:T(8,128)}, u32[]{:S(2)}, u32[]{:S(2)}) collective-permute-start(f32[512,2048]{1,0:T(8,128)} %slice_add_fusion.4), channel_id=1, source_target_pairs={{0,8},{8,0},{1,9},{9,1},{2,10},{10,2},{3,11},{11,3},{4,12},{12,4},... | collective-permute-start | bytes 12582920 | tf_op jit(solution)/shard_map/ppermute | solution.py:30
  386.7 93.3 %collective-permute-start.9 = (f32[512,2048]{1,0:T(8,128)}, f32[512,2048]{1,0:T(8,128)}, u32[]{:S(2)}, u32[]{:S(2)}) collective-permute-start(f32[512,2048]{1,0:T(8,128)} %slice_add_fusion.5), channel_id=1, source_target_pairs={{0,8},{8,0},{1,9},{9,1},{2,10},{10,2},{3,11},{11,3},{4,12},{12,4},... | collective-permute-start | bytes 12582920 | tf_op jit(solution)/shard_map/ppermute | solution.py:30
  387.2 48.8 %collective-permute-start.10 = (bf16[512,2048]{1,0:T(8,128)(2,1)}, bf16[512,2048]{1,0:T(8,128)(2,1)}, u32[]{:S(2)}, u32[]{:S(2)}) collective-permute-start(bf16[512,2048]{1,0:T(8,128)(2,1)} %get-tuple-element.31), channel_id=1, source_target_pairs={{0,16},{16,0},{1,17},{17,1},{2,18},{18,2},{3,19},{19,3},{4,20},{20... | collective-permute-start | bytes 6291464 | tf_op jit(solution)/shard_map/ppermute | solution.py:30
  388.7 91.3 %collective-permute-start.12 = (bf16[512,2048]{1,0:T(8,128)(2,1)}, bf16[512,2048]{1,0:T(8,128)(2,1)}, u32[]{:S(2)}, u32[]{:S(2)}) collective-permute-start(bf16[512,2048]{1,0:T(8,128)(2,1)} %get-tuple-element.32), channel_id=1, source_target_pairs={{0,16},{16,0},{1,17},{17,1},{2,18},{18,2},{3,19},{19,3},{4,20},{20... | collective-permute-start | bytes 6291464 | tf_op jit(solution)/shard_map/ppermute | solution.py:30
Sparse Core Ops, SparseCore 0:
  8.9 66.3 all-gather.4
  83.1 64.9 all-gather.6
  150.4 62.1 all-gather.8
  214.8 62.1 all-gather.10

commit v3 on v2

--- a/solution.py
+++ b/solution.py
@@ -96,19 +96,20 @@
         for rows in cuts:
             s_h = s_b[:, rows]
             give = early[0][rows] + contract(s_h, theirs[0])
-            other_x = early[2][rows] + contract(s_h, theirs[2]) + swap(give, "rc")
+            got = swap(give.astype(jnp.bfloat16), "rc").astype(jnp.float32)
+            other_x = early[2][rows] + contract(s_h, theirs[2]) + got
             sent.append(other_x.astype(jnp.bfloat16))
             got_x.append(swap(sent[-1], "rx"))
         _, late_give, late_keep, t_give, t_keep = lax.optimization_barrier(
             (tuple(sent), early[1], early[3], theirs[1], theirs[3])
         )
-        outs = []
+        out = jnp.zeros((width, rw), jnp.float32)
         for h, rows in enumerate(cuts):
             s_h = s_b[:, rows]
             give = late_give[rows] + contract(s_h, t_give)
             own_x = late_keep[rows] + contract(s_h, t_keep) + swap(give, "rc")
-            outs.append(own_x + got_x[h].astype(jnp.float32))
-        return jnp.concatenate(outs, axis=0) if halves > 1 else outs[0]
+            out = lax.dynamic_update_slice_in_dim(out, own_x + got_x[h].astype(jnp.float32), h * hw, axis=0)
+        return out
 
     return body
 

time: 502 us -> 490 us (0.976)
  other arithmetic: 44.8 us -> 38 us
  waiting for transfers between devices: 342 us -> 336 us
    convert_element_type x1 -> x0, other arithmetic: 7.17 us -> none  [body(): sent.append(other_x.astype(jnp.bfloat16))]
    ppermute x13, waiting for transfers between devices: 275 us -> 269 us  [swap(): return lax.ppermute(x, axis, [(0, 1), (1, 0)])]
where the time goes in v3:
time: 490 us; the launch traced here: 486 us
  waiting for transfers between devices  336 us (69%)
  matrix products  58 us (12%)
  other arithmetic  38 us (8%)
  between operations  15.7 us (3%)
  starting transfers between devices  14.8 us (3%)
  blocking collectives  12.3 us (3%)
  local copies, waits for them, and re-layouts  11.5 us (2%)
    ppermute x13, waiting for transfers between devices, swap(): return lax.ppermute(x, axis, [(0, 1), (1, 0)])  269 us
    all_gather x3, waiting for transfers between devices, body(): lax.all_gather(lax.dynamic_slice_in_dim(rest, start, pw, axis=1), 'az', a...  66.8 us
    dot_general x16, matrix products, contract(): lax.dot_general(left, right, (((0,), (0,)), ((), ())), preferred_element_...  58 us
    concatenate x5, other arithmetic, others(): doubled = jnp.concatenate([v, v], axis=0)  19.1 us
    ppermute x13, starting transfers between devices, swap(): return lax.ppermute(x, axis, [(0, 1), (1, 0)])  14.5 us
    unnamed x1, blocking collectives  12.3 us
    add x2, other arithmetic, body(): own_x + got_x[h].astype(jnp.float32)  11.5 us
  transfers between devices with their start and end apart: 17, of which 9 were waited for; matrix products, arithmetic and copies ran while one was open for 14% of the time, Pallas kernels for 0%

profile of v3, /device:TPU:0, one launch (start us, length us, event | category | flops | bytes accessed | tf_op | source)
XLA Modules:
  0.0 486.2 jit_solution(15308028534752588834)
XLA Ops:
  6.5 2.1 constant_dynamic-slice_fusion.3
  8.7 3.0 collective-permute-start
  13.0 1.2 dynamic-slice
  14.9 0.8 dynamic_slice.69
  15.7 0.7 and_select_fusion
  16.5 1.0 select_reduce_fusion
  17.6 12.3 %all-reduce = f32[768]{0:T(1024)S(1)} all-reduce(f32[768]{0:T(1024)S(1)} %get-tuple-element.27), channel_id=1, replica_groups=mesh['rx'=2,'rc'=2,'az'=4,'ay'=2] {'az'}, use_global_device_ids=true, to_apply=%add | all-reduce | flops 768 | bytes 6144
  30.4 1.6 collective-permute-start.1
  32.0 48.2 %collective-permute-done.1 = f32[192]{0:T(256)S(1)} collective-permute-done((f32[192]{0:T(256)S(1)}, f32[192]{0:T(256)S(1)}, u32[]{:S(2)}, u32[]{:S(2)}) %collective-permute-start.1) | collective-permute-done | bytes 800 | tf_op jit(solution)/shard_map/ppermute | solution.py:30
  80.2 2.7 constant_dynamic-slice_fusion.2
  83.0 5.1 %fusion.9 = bf16[576,2048]{1,0:T(8,128)(2,1)} fusion(s32[]{:T(128)S(6)} %select_n.114, bf16[768,2048]{1,0:T(8,128)(2,1)} %all-gather.5.cloned.1.call-done), kind=kLoop, calls=%fused_computation.31 | loop fusion | flops 4718592 | bytes 5505028 | tf_op jit(solution)/shard_map/concatenate | solution.py:51
  88.1 1.7 collective-permute-start.3
  89.9 51.0 %collective-permute-done.3 = bf16[576,2048]{1,0:T(8,128)(2,1)} collective-permute-done((bf16[576,2048]{1,0:T(8,128)(2,1)}, bf16[576,2048]{1,0:T(8,128)(2,1)}, u32[]{:S(2)}, u32[]{:S(2)}) %collective-permute-start.3) | collective-permute-done | bytes 2359328 | tf_op jit(solution)/shard_map/ppermute | solution.py:30
  140.8 7.3 %all-gather.7.cloned.1.call-done = bf16[768,2048]{1,0:T(8,128)(2,1)} async-done(((bf16[192,2048]{1,0:T(8,128)(2,1)}), bf16[768,2048]{1,0:T(8,128)(2,1)}) %all-gather.7.cloned.1.call-update) | async-done | bytes 3145744 | tf_op jit(solution)/shard_map/all_gather | solution.py:77
  148.1 2.1 constant_dynamic-slice_fusion.1
  150.4 5.1 %fusion.8 = bf16[576,2048]{1,0:T(8,128)(2,1)} fusion(s32[]{:T(128)S(6)} %select_n.114, bf16[768,2048]{1,0:T(8,128)(2,1)} %all-gather.7.cloned.1.call-done), kind=kLoop, calls=%fused_computation.30 | loop fusion | flops 4718592 | bytes 5505028 | tf_op jit(solution)/shard_map/concatenate | solution.py:51
  155.5 1.5 collective-permute-start.4
  157.0 51.7 %collective-permute-done.4 = bf16[576,2048]{1,0:T(8,128)(2,1)S(1)} collective-permute-done((bf16[576,2048]{1,0:T(8,128)(2,1)}, bf16[576,2048]{1,0:T(8,128)(2,1)S(1)}, u32[]{:S(2)}, u32[]{:S(2)}) %collective-permute-start.4) | collective-permute-done | bytes 2359328 | tf_op jit(solution)/shard_map/ppermute | solution.py:30
  208.7 3.9 all-gather.9.cloned.1.call-done
  212.5 2.1 constant_dynamic-slice_fusion
  214.7 5.1 %fusion.6 = bf16[576,2048]{1,0:T(8,128)(2,1)} fusion(s32[]{:T(128)S(6)} %select_n.114, bf16[768,2048]{1,0:T(8,128)(2,1)} %all-gather.9.cloned.1.call-done), kind=kLoop, calls=%fused_computation.28 | loop fusion | flops 4718592 | bytes 5505028 | tf_op jit(solution)/shard_map/concatenate | solution.py:51
  219.8 1.5 collective-permute-start.6
  221.3 55.7 %all-gather.11.cloned.1.call-done = bf16[768,2048]{1,0:T(8,128)(2,1)} async-done(((bf16[192,2048]{1,0:T(8,128)(2,1)}), bf16[768,2048]{1,0:T(8,128)(2,1)}) %all-gather.11.cloned.1.call-update) | async-done | bytes 3145744 | tf_op jit(solution)/shard_map/all_gather | solution.py:77
  276.9 3.7 fusion.7
  280.7 1.5 collective-permute-start.5
  282.2 3.3 multiply_convert_fusion
  285.5 3.5 fusion.39
  289.0 4.7 convolution_add_fusion
  293.9 3.5 fusion.37
  297.4 1.4 convolution_add_fusion.2
  299.3 3.5 fusion.38
  302.8 30.9 %collective-permute-done.5 = bf16[576,2048]{1,0:T(8,128)(2,1)S(1)} collective-permute-done((bf16[576,2048]{1,0:T(8,128)(2,1)S(1)}, bf16[576,2048]{1,0:T(8,128)(2,1)S(1)}, u32[]{:S(2)}, u32[]{:S(2)}) %collective-permute-start.5) | collective-permute-done | bytes 2359328 | tf_op jit(solution)/shard_map/ppermute | solution.py:30
  333.7 2.3 multiply_convert_fusion.1
  336.0 4.9 %fusion = bf16[512,2048]{1,0:T(8,128)(2,1)} fusion(f32[1024,2048]{1,0:T(8,128)S(1)} %convolution_add_fusion.2, bf16[576,2048]{1,0:T(8,128)(2,1)} %collective-permute-done.3, bf16[576,1024]{1,0:T(8,128)(2,1)S(1)} %multiply_convert_fusion.1), kind=kOutput, calls=%fused_computation.14 | convolution fusion | flops 1210056704 | bytes 9240576 | tf_op jit(solution)/shard_map/dot_general | solution.py:24
  340.9 4.9 %fusion.3 = bf16[512,2048]{1,0:T(8,128)(2,1)} fusion(f32[1024,2048]{1,0:T(8,128)S(1)} %convolution_add_fusion.2, bf16[576,2048]{1,0:T(8,128)(2,1)} %collective-permute-done.3, bf16[576,1024]{1,0:T(8,128)(2,1)S(1)} %multiply_convert_fusion.1), kind=kOutput, calls=%fused_computation.19 | convolution fusion | flops 1210056704 | bytes 9240576 | tf_op jit(solution)/shard_map/dot_general | solution.py:24
  346.3 1.8 convolution_add_fusion.1
  348.2 5.5 %fusion.36 = f32[1024,2048]{1,0:T(8,128)S(1)} fusion(bf16[768,1024]{1,0:T(8,128)(2,1)S(1)} %multiply_convert_fusion, bf16[768,2048]{1,0:T(8,128)(2,1)} %all-gather.9.cloned.1.call-done), kind=kOutput, calls=%fused_computation.70 | convolution fusion | flops 3221225472 | bytes 13107200 | tf_op jit(solution)/shard_map/dot_general | solution.py:24
  353.6 1.4 convolution_add_fusion.3
  355.0 5.8 %fusion.2 = bf16[512,2048]{1,0:T(8,128)(2,1)} fusion(f32[1024,2048]{1,0:T(8,128)S(1)} %convolution_add_fusion.3, bf16[512,2048]{1,0:T(8,128)(2,1)} %collective-permute-done.8, bf16[576,2048]{1,0:T(8,128)(2,1)} %collective-permute-done.6, bf16[576,1024]{1,0:T(8,128)(2,1)S(1)} %multiply_convert_fusion.1), kind=kOutput, calls=%fused_computation.17 | convolution fusion | flops 1212153856 | bytes 11337728 | tf_op jit(solution)/shard_map/dot_general | solution.py:24
  360.8 5.7 %fusion.5 = bf16[512,2048]{1,0:T(8,128)(2,1)} fusion(f32[1024,2048]{1,0:T(8,128)S(1)} %convolution_add_fusion.3, bf16[512,2048]{1,0:T(8,128)(2,1)} %collective-permute-done.7, bf16[576,2048]{1,0:T(8,128)(2,1)} %collective-permute-done.6, bf16[576,1024]{1,0:T(8,128)(2,1)S(1)} %multiply_convert_fusion.1), kind=kOutput, calls=%fused_computation.22 | convolution fusion | flops 1212153856 | bytes 11337728 | tf_op jit(solution)/shard_map/dot_general | solution.py:24
  366.5 3.9 slice_add_fusion.4
  370.4 4.0 slice_add_fusion.5
  375.1 1.5 collective-permute-start.10
  377.1 1.8 fusion.16
  378.9 1.8 fusion.24
  380.8 43.1 %collective-permute-done.10 = bf16[512,2048]{1,0:T(8,128)(2,1)} collective-permute-done((bf16[512,2048]{1,0:T(8,128)(2,1)}, bf16[512,2048]{1,0:T(8,128)(2,1)}, u32[]{:S(2)}, u32[]{:S(2)}) %collective-permute-start.10) | collective-permute-done | bytes 2097184 | tf_op jit(solution)/shard_map/ppermute | solution.py:30
  423.9 44.1 %collective-permute-done.12 = bf16[512,2048]{1,0:T(8,128)(2,1)} collective-permute-done((bf16[512,2048]{1,0:T(8,128)(2,1)}, bf16[512,2048]{1,0:T(8,128)(2,1)}, u32[]{:S(2)}, u32[]{:S(2)}) %collective-permute-start.12) | collective-permute-done | bytes 2097184 | tf_op jit(solution)/shard_map/ppermute | solution.py:30
  468.0 11.5 %convert_add_fusion.1 = (f32[1024,2048]{1,0:T(8,128)}, f32[1024,2048]{1,0:T(8,128)}) fusion(bf16[512,2048]{1,0:T(8,128)(2,1)} %collective-permute-done.10, f32[512,2048]{1,0:T(8,128)} %collective-permute-done.9, f32[512,2048]{1,0:T(8,128)S(1)} %fusion.24, f32[1024,2048]{1,0:T(8,128)} %convolution_add_fusion, ...), kind=kLoop, output_to_operand_aliasing={{0}: (7, {}), {1}: (7, {})}, calls=%fused_computation.25 | loop fusion | flops 8388608 | bytes 37748736 | tf_op jit(solution)/shard_map/add | solution.py:111
  (41 shorter events, 3.4 us)
Async XLA Ops:
  6.5 73.7 %all-gather.5.cloned.1.call-start = ((), (), s32[]{:S(2)}) async-start(), calls=%async_computation | async-start | bytes 3932160 | tf_op jit(solution)/shard_map/all_gather | solution.py:63
  8.7 139.4 %all-gather.7.cloned.1.call-start = ((), (), s32[]{:S(2)}) async-start(), calls=%async_computation.1 | async-start | bytes 3932160 | tf_op jit(solution)/shard_map/all_gather | solution.py:77
  8.7 71.5 %collective-permute-start = (bf16[192,8192]{1,0:T(8,128)(2,1)}, bf16[192,8192]{1,0:T(8,128)(2,1)S(1)}, u32[]{:S(2)}, u32[]{:S(2)}) collective-permute-start(bf16[192,8192]{1,0:T(8,128)(2,1)} %param.6), channel_id=1, source_target_pairs={{0,1},{1,0},{2,3},{3,2},{4,5},{5,4},{6,7},{7,6},{8,9},{9,8},{10,11... | collective-permute-start | bytes 9437192 | tf_op jit(solution)/shard_map/ppermute | solution.py:30
  30.0 50.2 %collective-permute-start.2 = (f32[576]{0:T(1024)S(1)}, f32[576]{0:T(1024)S(1)}, u32[]{:S(2)}, u32[]{:S(2)}) collective-permute-start(f32[576]{0:T(1024)S(1)} %fusion.34), channel_id=1, source_target_pairs={{0,1},{1,0},{2,3},{3,2},{4,5},{5,4},{6,7},{7,6},{8,9},{9,8},{10,11... | collective-permute-start | bytes 6920 | tf_op jit(solution)/shard_map/ppermute | solution.py:30
  30.4 49.8 %collective-permute-start.1 = (f32[192]{0:T(256)S(1)}, f32[192]{0:T(256)S(1)}, u32[]{:S(2)}, u32[]{:S(2)}) collective-permute-start(f32[192]{0:T(256)S(1)} %get-tuple-element.28), channel_id=1, source_target_pairs={{0,1},{1,0},{2,3},{3,2},{4,5},{5,4},{6,7},{7,6},{8,9},{9,8},{10,11... | collective-permute-start | bytes 2312 | tf_op jit(solution)/shard_map/ppermute | solution.py:30
  80.2 7.9 %copy-start.2 = (bf16[192,8192]{1,0:T(8,128)(2,1)}, bf16[192,8192]{1,0:T(8,128)(2,1)S(1)}, u32[]{:S(2)}) copy-start(bf16[192,8192]{1,0:T(8,128)(2,1)S(1)} %collective-permute-done) | copy-start | bytes 9437188
  83.0 129.5 %all-gather.9.cloned.1.call-start = ((), (), s32[]{:S(2)}) async-start(), calls=%async_computation.2 | async-start | bytes 3932160 | tf_op jit(solution)/shard_map/all_gather | solution.py:77
  88.1 52.7 %collective-permute-start.3 = (bf16[576,2048]{1,0:T(8,128)(2,1)}, bf16[576,2048]{1,0:T(8,128)(2,1)}, u32[]{:S(2)}, u32[]{:S(2)}) collective-permute-start(bf16[576,2048]{1,0:T(8,128)(2,1)} %fusion.9), channel_id=1, source_target_pairs={{0,1},{1,0},{2,3},{3,2},{4,5},{5,4},{6,7},{7,6},{8,9},{9,8},{10,11... | collective-permute-start | bytes 7077896 | tf_op jit(solution)/shard_map/ppermute | solution.py:30
  150.2 126.7 %all-gather.11.cloned.1.call-start = ((), (), s32[]{:S(2)}) async-start(), calls=%async_computation.3 | async-start | bytes 3932160 | tf_op jit(solution)/shard_map/all_gather | solution.py:77
  155.5 53.2 %collective-permute-start.4 = (bf16[576,2048]{1,0:T(8,128)(2,1)}, bf16[576,2048]{1,0:T(8,128)(2,1)S(1)}, u32[]{:S(2)}, u32[]{:S(2)}) collective-permute-start(bf16[576,2048]{1,0:T(8,128)(2,1)} %fusion.8), channel_id=1, source_target_pairs={{0,1},{1,0},{2,3},{3,2},{4,5},{5,4},{6,7},{7,6},{8,9},{9,8},{10,11... | collective-permute-start | bytes 7077896 | tf_op jit(solution)/shard_map/ppermute | solution.py:30
  208.7 11.1 %copy-start = (bf16[576,2048]{1,0:T(8,128)(2,1)}, bf16[576,2048]{1,0:T(8,128)(2,1)S(1)}, u32[]{:S(2)}) copy-start(bf16[576,2048]{1,0:T(8,128)(2,1)S(1)} %collective-permute-done.4) | copy-start | bytes 7077892
  219.8 83.0 %collective-permute-start.6 = (bf16[576,2048]{1,0:T(8,128)(2,1)}, bf16[576,2048]{1,0:T(8,128)(2,1)}, u32[]{:S(2)}, u32[]{:S(2)}) collective-permute-start(bf16[576,2048]{1,0:T(8,128)(2,1)} %fusion.6), channel_id=1, source_target_pairs={{0,1},{1,0},{2,3},{3,2},{4,5},{5,4},{6,7},{7,6},{8,9},{9,8},{10,11... | collective-permute-start | bytes 7077896 | tf_op jit(solution)/shard_map/ppermute | solution.py:30
  276.9 5.3 %copy-start.6 = (bf16[768,2048]{1,0:T(8,128)(2,1)S(1)}, bf16[768,2048]{1,0:T(8,128)(2,1)}, u32[]{:S(2)}) copy-start(bf16[768,2048]{1,0:T(8,128)(2,1)} %all-gather.11.cloned.1.call-done) | copy-start | bytes 9437188
  280.7 53.0 %collective-permute-start.5 = (bf16[576,2048]{1,0:T(8,128)(2,1)S(1)}, bf16[576,2048]{1,0:T(8,128)(2,1)S(1)}, u32[]{:S(2)}, u32[]{:S(2)}) collective-permute-start(bf16[576,2048]{1,0:T(8,128)(2,1)S(1)} %fusion.7), channel_id=1, source_target_pairs={{0,1},{1,0},{2,3},{3,2},{4,5},{5,4},{6,7},{7,6},{8,9},{9,8},{10,11... | collective-permute-start | bytes 7077896 | tf_op jit(solution)/shard_map/ppermute | solution.py:30
  285.5 3.5 copy-start.3
  289.0 4.7 copy-start.4
  297.4 1.9 copy-start.5
  299.3 34.4 %copy-start.1 = (bf16[576,2048]{1,0:T(8,128)(2,1)S(1)}, bf16[576,2048]{1,0:T(8,128)(2,1)}, u32[]{:S(2)}) copy-start(bf16[576,2048]{1,0:T(8,128)(2,1)} %copy-done) | copy-start | bytes 7077892
  340.9 14.1 %collective-permute-start.8 = (bf16[512,2048]{1,0:T(8,128)(2,1)}, bf16[512,2048]{1,0:T(8,128)(2,1)}, u32[]{:S(2)}, u32[]{:S(2)}) collective-permute-start(bf16[512,2048]{1,0:T(8,128)(2,1)} %fusion), channel_id=1, source_target_pairs={{0,8},{8,0},{1,9},{9,1},{2,10},{10,2},{3,11},{11,3},{4,12},{12,4},... | collective-permute-start | bytes 6291464 | tf_op jit(solution)/shard_map/ppermute | solution.py:30
  345.8 15.0 %collective-permute-start.7 = (bf16[512,2048]{1,0:T(8,128)(2,1)}, bf16[512,2048]{1,0:T(8,128)(2,1)}, u32[]{:S(2)}, u32[]{:S(2)}) collective-permute-start(bf16[512,2048]{1,0:T(8,128)(2,1)} %fusion.3), channel_id=1, source_target_pairs={{0,8},{8,0},{1,9},{9,1},{2,10},{10,2},{3,11},{11,3},{4,12},{12,4},... | collective-permute-start | bytes 6291464 | tf_op jit(solution)/shard_map/ppermute | solution.py:30
  374.4 93.6 %collective-permute-start.9 = (f32[512,2048]{1,0:T(8,128)}, f32[512,2048]{1,0:T(8,128)}, u32[]{:S(2)}, u32[]{:S(2)}) collective-permute-start(f32[512,2048]{1,0:T(8,128)} %slice_add_fusion.5), channel_id=1, source_target_pairs={{0,8},{8,0},{1,9},{9,1},{2,10},{10,2},{3,11},{11,3},{4,12},{12,4},... | collective-permute-start | bytes 12582920 | tf_op jit(solution)/shard_map/ppermute | solution.py:30
  374.6 93.4 %collective-permute-start.11 = (f32[512,2048]{1,0:T(8,128)}, f32[512,2048]{1,0:T(8,128)}, u32[]{:S(2)}, u32[]{:S(2)}) collective-permute-start(f32[512,2048]{1,0:T(8,128)} %slice_add_fusion.4), channel_id=1, source_target_pairs={{0,8},{8,0},{1,9},{9,1},{2,10},{10,2},{3,11},{11,3},{4,12},{12,4},... | collective-permute-start | bytes 12582920 | tf_op jit(solution)/shard_map/ppermute | solution.py:30
  375.1 48.8 %collective-permute-start.10 = (bf16[512,2048]{1,0:T(8,128)(2,1)}, bf16[512,2048]{1,0:T(8,128)(2,1)}, u32[]{:S(2)}, u32[]{:S(2)}) collective-permute-start(bf16[512,2048]{1,0:T(8,128)(2,1)} %fusion.5), channel_id=1, source_target_pairs={{0,16},{16,0},{1,17},{17,1},{2,18},{18,2},{3,19},{19,3},{4,20},{20... | collective-permute-start | bytes 6291464 | tf_op jit(solution)/shard_map/ppermute | solution.py:30
  376.5 91.4 %collective-permute-start.12 = (bf16[512,2048]{1,0:T(8,128)(2,1)}, bf16[512,2048]{1,0:T(8,128)(2,1)}, u32[]{:S(2)}, u32[]{:S(2)}) collective-permute-start(bf16[512,2048]{1,0:T(8,128)(2,1)} %fusion.2), channel_id=1, source_target_pairs={{0,16},{16,0},{1,17},{17,1},{2,18},{18,2},{3,19},{19,3},{4,20},{20... | collective-permute-start | bytes 6291464 | tf_op jit(solution)/shard_map/ppermute | solution.py:30
Sparse Core Ops, SparseCore 0:
  8.9 66.3 all-gather.4
  83.1 64.9 all-gather.6
  150.3 62.1 all-gather.8
  214.8 62.1 all-gather.10

commit v4 on v3

--- a/solution.py
+++ b/solution.py
@@ -109,6 +109,8 @@
             give = late_give[rows] + contract(s_h, t_give)
             own_x = late_keep[rows] + contract(s_h, t_keep) + swap(give, "rc")
             out = lax.dynamic_update_slice_in_dim(out, own_x + got_x[h].astype(jnp.float32), h * hw, axis=0)
+            if h < halves - 1:
+                out = lax.optimization_barrier(out)
         return out
 
     return body

time: 490 us -> 488 us (level)
  waiting for transfers between devices: 336 us -> 319 us
  matrix products: 58 us -> 64.9 us
  local copies, waits for them, and re-layouts: 11.5 us -> 18.3 us
    ppermute x13, waiting for transfers between devices: 269 us -> 252 us  [swap(): return lax.ppermute(x, axis, [(0, 1), (1, 0)])]
    dot_general x16, matrix products: 58 us -> 64.9 us  [contract(): lax.dot_general(left, right, (((0,), (0,)), ((), ())), preferred_element_...]
    dynamic_update_slice x0 -> x1, local copies, waits for them, and re-layouts: none -> 6.82 us  [body(): lax.dynamic_update_slice_in_dim(out, own_x + got_x[h].astype(jnp.float32)...]
    dynamic_update_slice x0 -> x1, other arithmetic: none -> 6.51 us  [body(): lax.dynamic_update_slice_in_dim(out, own_x + got_x[h].astype(jnp.float32)...]
    add x2 -> x1, other arithmetic: 11.5 us -> 6.64 us  [body(): own_x + got_x[h].astype(jnp.float32)]
  transfers between devices with their start and end apart: 17 -> 17, of which waited for: 9 -> 9; matrix products, arithmetic and copies ran while one was open for 14% -> 19% of each run, Pallas kernels for 0% -> 0%
where the time goes in v4:
time: 488 us; the launch traced here: 485 us
  waiting for transfers between devices  319 us (65%)
  matrix products  64.9 us (13%)
  other arithmetic  39.6 us (8%)
  local copies, waits for them, and re-layouts  18.3 us (4%)
  between operations  15.6 us (3%)
  starting transfers between devices  14.8 us (3%)
  blocking collectives  12.3 us (3%)
    ppermute x13, waiting for transfers between devices, swap(): return lax.ppermute(x, axis, [(0, 1), (1, 0)])  252 us
    all_gather x3, waiting for transfers between devices, body(): lax.all_gather(lax.dynamic_slice_in_dim(rest, start, pw, axis=1), 'az', a...  66.8 us
    dot_general x16, matrix products, contract(): lax.dot_general(left, right, (((0,), (0,)), ((), ())), preferred_element_...  64.9 us
    concatenate x5, other arithmetic, others(): doubled = jnp.concatenate([v, v], axis=0)  19 us
    ppermute x13, starting transfers between devices, swap(): return lax.ppermute(x, axis, [(0, 1), (1, 0)])  14.5 us
    unnamed x1, blocking collectives  12.3 us
  transfers between devices with their start and end apart: 17, of which 9 were waited for; matrix products, arithmetic and copies ran while one was open for 19% of the time, Pallas kernels for 0%

profile of v4, /device:TPU:0, one launch (start us, length us, event | category | flops | bytes accessed | tf_op | source)
XLA Modules:
  0.0 484.7 jit_solution(12132483039516105365)
XLA Ops:
  6.5 2.1 constant_dynamic-slice_fusion.3
  8.7 3.0 collective-permute-start
  13.8 1.2 dynamic-slice
  16.5 1.0 select_reduce_fusion
  17.6 12.3 %all-reduce.1 = f32[768]{0:T(1024)S(1)} all-reduce(f32[768]{0:T(1024)S(1)} %get-tuple-element.27), channel_id=1, replica_groups=mesh['rx'=2,'rc'=2,'az'=4,'ay'=2] {'az'}, use_global_device_ids=true, to_apply=%add.1 | all-reduce | flops 768 | bytes 6144
  30.4 1.6 collective-permute-start.1
  32.0 48.2 %collective-permute-done.1 = f32[192]{0:T(256)S(1)} collective-permute-done((f32[192]{0:T(256)S(1)}, f32[192]{0:T(256)S(1)}, u32[]{:S(2)}, u32[]{:S(2)}) %collective-permute-start.1) | collective-permute-done | bytes 800 | tf_op jit(solution)/shard_map/ppermute | solution.py:30
  80.2 2.7 constant_dynamic-slice_fusion.2
  83.0 5.1 %fusion.9 = bf16[576,2048]{1,0:T(8,128)(2,1)} fusion(s32[]{:T(128)S(6)} %select_n.114, bf16[768,2048]{1,0:T(8,128)(2,1)} %all-gather.5.cloned.1.call-done), kind=kLoop, calls=%fused_computation.30 | loop fusion | flops 4718592 | bytes 5505028 | tf_op jit(solution)/shard_map/concatenate | solution.py:51
  88.1 1.7 collective-permute-start.3
  89.9 51.0 %collective-permute-done.3 = bf16[576,2048]{1,0:T(8,128)(2,1)} collective-permute-done((bf16[576,2048]{1,0:T(8,128)(2,1)}, bf16[576,2048]{1,0:T(8,128)(2,1)}, u32[]{:S(2)}, u32[]{:S(2)}) %collective-permute-start.3) | collective-permute-done | bytes 2359328 | tf_op jit(solution)/shard_map/ppermute | solution.py:30
  140.8 7.3 %all-gather.7.cloned.1.call-done = bf16[768,2048]{1,0:T(8,128)(2,1)} async-done(((bf16[192,2048]{1,0:T(8,128)(2,1)}), bf16[768,2048]{1,0:T(8,128)(2,1)}) %all-gather.7.cloned.1.call-update) | async-done | bytes 3145744 | tf_op jit(solution)/shard_map/all_gather | solution.py:77
  148.1 2.1 constant_dynamic-slice_fusion.1
  150.5 5.1 %fusion.8 = bf16[576,2048]{1,0:T(8,128)(2,1)} fusion(s32[]{:T(128)S(6)} %select_n.114, bf16[768,2048]{1,0:T(8,128)(2,1)} %all-gather.7.cloned.1.call-done), kind=kLoop, calls=%fused_computation.29 | loop fusion | flops 4718592 | bytes 5505028 | tf_op jit(solution)/shard_map/concatenate | solution.py:51
  155.6 1.5 collective-permute-start.4
  157.0 51.7 %collective-permute-done.4 = bf16[576,2048]{1,0:T(8,128)(2,1)S(1)} collective-permute-done((bf16[576,2048]{1,0:T(8,128)(2,1)}, bf16[576,2048]{1,0:T(8,128)(2,1)S(1)}, u32[]{:S(2)}, u32[]{:S(2)}) %collective-permute-start.4) | collective-permute-done | bytes 2359328 | tf_op jit(solution)/shard_map/ppermute | solution.py:30
  208.7 3.8 all-gather.9.cloned.1.call-done
  212.5 2.1 constant_dynamic-slice_fusion
  214.7 5.1 %fusion.6 = bf16[576,2048]{1,0:T(8,128)(2,1)} fusion(s32[]{:T(128)S(6)} %select_n.114, bf16[768,2048]{1,0:T(8,128)(2,1)} %all-gather.9.cloned.1.call-done), kind=kLoop, calls=%fused_computation.27 | loop fusion | flops 4718592 | bytes 5505028 | tf_op jit(solution)/shard_map/concatenate | solution.py:51
  219.8 1.5 collective-permute-start.6
  221.2 55.7 %all-gather.11.cloned.1.call-done = bf16[768,2048]{1,0:T(8,128)(2,1)} async-done(((bf16[192,2048]{1,0:T(8,128)(2,1)}), bf16[768,2048]{1,0:T(8,128)(2,1)}) %all-gather.11.cloned.1.call-update) | async-done | bytes 3145744 | tf_op jit(solution)/shard_map/all_gather | solution.py:77
  277.0 3.7 fusion.7
  280.7 1.5 collective-permute-start.5
  282.3 3.2 multiply_convert_fusion
  285.5 3.6 fusion.37
  289.1 1.4 convolution_add_fusion.2
  291.0 4.0 fusion.36
  295.0 4.8 convolution_add_fusion.3
  299.8 5.9 %fusion.39 = f32[1024,2048]{1,0:T(8,128)} fusion(bf16[768,1024]{1,0:T(8,128)(2,1)S(1)} %multiply_convert_fusion, bf16[768,2048]{1,0:T(8,128)(2,1)S(1)} %copy-done.5), kind=kOutput, calls=%fused_computation.72 | convolution fusion | flops 3221225472 | bytes 13107200 | tf_op jit(solution)/shard_map/dot_general | solution.py:24
  305.7 28.0 %collective-permute-done.5 = bf16[576,2048]{1,0:T(8,128)(2,1)S(1)} collective-permute-done((bf16[576,2048]{1,0:T(8,128)(2,1)S(1)}, bf16[576,2048]{1,0:T(8,128)(2,1)S(1)}, u32[]{:S(2)}, u32[]{:S(2)}) %collective-permute-start.5) | collective-permute-done | bytes 2359328 | tf_op jit(solution)/shard_map/ppermute | solution.py:30
  333.7 2.3 multiply_convert_fusion.1
  336.1 5.0 %fusion = bf16[512,2048]{1,0:T(8,128)(2,1)} fusion(f32[1024,2048]{1,0:T(8,128)S(1)} %convolution_add_fusion.2, bf16[576,2048]{1,0:T(8,128)(2,1)} %collective-permute-done.3, bf16[576,1024]{1,0:T(8,128)(2,1)S(1)} %multiply_convert_fusion.1), kind=kOutput, calls=%fused_computation.13 | convolution fusion | flops 1210056704 | bytes 9240576 | tf_op jit(solution)/shard_map/dot_general | solution.py:24
  341.1 3.6 fusion.3
  345.3 5.0 %convolution_add_fusion = f32[1024,2048]{1,0:T(8,128)S(1)} fusion(f32[1024,2048]{1,0:T(8,128)} %fusion.39, bf16[192,8192]{1,0:T(8,128)(2,1)S(1)} %copy-done.1, s32[]{:T(128)S(6)} %select_n.121, s32[]{:T(128)S(6)} %select_n.115, f32[192]{0:T(256)S(1)} %collective-permute-done.1), kind=kOutput, calls=%fused_computation.8 | convolution fusion | flops 807993344 | bytes 17957896 | tf_op jit(solution)/shard_map/dot_general | solution.py:24
  350.4 6.1 %fusion.38 = f32[1024,2048]{1,0:T(8,128)} fusion(bf16[768,1024]{1,0:T(8,128)(2,1)S(1)} %copy-done.7, bf16[768,2048]{1,0:T(8,128)(2,1)S(1)} %copy-done.3), kind=kOutput, calls=%fused_computation.71 | convolution fusion | flops 3221225472 | bytes 13107200 | tf_op jit(solution)/shard_map/dot_general | solution.py:24
  356.5 4.8 convolution_add_fusion.1
  361.3 6.3 %fusion.2 = bf16[512,2048]{1,0:T(8,128)(2,1)} fusion(f32[1024,2048]{1,0:T(8,128)} %convolution_add_fusion.3, bf16[512,2048]{1,0:T(8,128)(2,1)S(1)} %collective-permute-done.8, bf16[576,2048]{1,0:T(8,128)(2,1)} %collective-permute-done.6, bf16[576,1024]{1,0:T(8,128)(2,1)S(1)} %multiply_convert_fusion.1), kind=kOutput, calls=%fused_computation.16 | convolution fusion | flops 1212153856 | bytes 11337728 | tf_op jit(solution)/shard_map/dot_general | solution.py:24
  367.6 4.9 %fusion.5 = bf16[512,2048]{1,0:T(8,128)(2,1)S(1)} fusion(f32[1024,2048]{1,0:T(8,128)} %convolution_add_fusion.3, bf16[512,2048]{1,0:T(8,128)(2,1)S(1)} %collective-permute-done.7, bf16[576,2048]{1,0:T(8,128)(2,1)} %collective-permute-done.6, bf16[576,1024]{1,0:T(8,128)(2,1)S(1)} %multiply_convert_fusion.1), kind=kOutput, calls=%fused_computation.21 | convolution fusion | flops 1212153856 | bytes 11337728 | tf_op jit(solution)/shard_map/dot_general | solution.py:24
  372.5 1.9 slice_add_fusion.5
  374.4 3.9 slice_add_fusion.4
  378.8 1.5 collective-permute-start.10
  380.8 1.9 fusion.16
  382.7 1.9 fusion.24
  384.6 42.8 %collective-permute-done.10 = bf16[512,2048]{1,0:T(8,128)(2,1)} collective-permute-done((bf16[512,2048]{1,0:T(8,128)(2,1)S(1)}, bf16[512,2048]{1,0:T(8,128)(2,1)}, u32[]{:S(2)}, u32[]{:S(2)}) %collective-permute-start.10) | collective-permute-done | bytes 2097184 | tf_op jit(solution)/shard_map/ppermute | solution.py:30
  427.4 6.6 %convert_add_fusion = f32[512,2048]{1,0:T(8,128)} fusion(bf16[512,2048]{1,0:T(8,128)(2,1)} %collective-permute-done.10, f32[512,2048]{1,0:T(8,128)} %collective-permute-done.9, f32[512,2048]{1,0:T(8,128)S(1)} %fusion.24, f32[1024,2048]{1,0:T(8,128)S(1)} %convolution_add_fusion), kind=kLoop, calls=%fused_computation.24 | loop fusion | flops 4194304 | bytes 18874368 | tf_op jit(solution)/shard_map/add | solution.py:111
  434.0 6.8 %dynamic_update_slice.6 = f32[1024,2048]{1,0:T(8,128)} pad(f32[512,2048]{1,0:T(8,128)} %convert_add_fusion, f32[]{:T(128)} %constant.62.clone.1), padding=0_512x0_0 | pad | bytes 12582916 | tf_op jit(solution)/shard_map/dynamic_update_slice | solution.py:111
  440.8 30.5 %collective-permute-done.12 = bf16[512,2048]{1,0:T(8,128)(2,1)} collective-permute-done((bf16[512,2048]{1,0:T(8,128)(2,1)}, bf16[512,2048]{1,0:T(8,128)(2,1)}, u32[]{:S(2)}, u32[]{:S(2)}) %collective-permute-start.12) | collective-permute-done | bytes 2097184 | tf_op jit(solution)/shard_map/ppermute | solution.py:30
  471.4 6.5 %add_dynamic-update-slice_fusion = f32[1024,2048]{1,0:T(8,128)} fusion(f32[1024,2048]{1,0:T(8,128)} %dynamic_update_slice.6, bf16[512,2048]{1,0:T(8,128)(2,1)} %collective-permute-done.12, f32[512,2048]{1,0:T(8,128)} %collective-permute-done.11, f32[512,2048]{1,0:T(8,128)S(1)} %fusion.16, f32[1024,2048]{1,0:T(8,128)S(1)} %convolution_add_fusion), kind=kLoop, calls=%fused_computation.22 | loop fusion | flops 4194304 | bytes 18874368 | tf_op jit(solution)/shard_map/dynamic_update_slice | solution.py:111
  (44 shorter events, 4.8 us)
Async XLA Ops:
  6.5 73.7 %all-gather.5.cloned.1.call-start = ((), (), s32[]{:S(2)}) async-start(), calls=%async_computation | async-start | bytes 3932160 | tf_op jit(solution)/shard_map/all_gather | solution.py:63
  8.7 139.4 %all-gather.7.cloned.1.call-start = ((), (), s32[]{:S(2)}) async-start(), calls=%async_computation.1 | async-start | bytes 3932160 | tf_op jit(solution)/shard_map/all_gather | solution.py:77
  8.7 71.5 %collective-permute-start = (bf16[192,8192]{1,0:T(8,128)(2,1)}, bf16[192,8192]{1,0:T(8,128)(2,1)S(1)}, u32[]{:S(2)}, u32[]{:S(2)}) collective-permute-start(bf16[192,8192]{1,0:T(8,128)(2,1)} %param.6), channel_id=1, source_target_pairs={{0,1},{1,0},{2,3},{3,2},{4,5},{5,4},{6,7},{7,6},{8,9},{9,8},{10,11... | collective-permute-start | bytes 9437192 | tf_op jit(solution)/shard_map/ppermute | solution.py:30
  30.0 50.2 %collective-permute-start.2 = (f32[576]{0:T(1024)S(1)}, f32[576]{0:T(1024)S(1)}, u32[]{:S(2)}, u32[]{:S(2)}) collective-permute-start(f32[576]{0:T(1024)S(1)} %fusion.34), channel_id=1, source_target_pairs={{0,1},{1,0},{2,3},{3,2},{4,5},{5,4},{6,7},{7,6},{8,9},{9,8},{10,11... | collective-permute-start | bytes 6920 | tf_op jit(solution)/shard_map/ppermute | solution.py:30
  30.4 49.8 %collective-permute-start.1 = (f32[192]{0:T(256)S(1)}, f32[192]{0:T(256)S(1)}, u32[]{:S(2)}, u32[]{:S(2)}) collective-permute-start(f32[192]{0:T(256)S(1)} %get-tuple-element.28), channel_id=1, source_target_pairs={{0,1},{1,0},{2,3},{3,2},{4,5},{5,4},{6,7},{7,6},{8,9},{9,8},{10,11... | collective-permute-start | bytes 2312 | tf_op jit(solution)/shard_map/ppermute | solution.py:30
  80.2 7.9 %copy-start = (bf16[192,8192]{1,0:T(8,128)(2,1)}, bf16[192,8192]{1,0:T(8,128)(2,1)S(1)}, u32[]{:S(2)}) copy-start(bf16[192,8192]{1,0:T(8,128)(2,1)S(1)} %collective-permute-done) | copy-start | bytes 9437188
  83.0 129.6 %all-gather.9.cloned.1.call-start = ((), (), s32[]{:S(2)}) async-start(), calls=%async_computation.2 | async-start | bytes 3932160 | tf_op jit(solution)/shard_map/all_gather | solution.py:77
  88.1 52.7 %collective-permute-start.3 = (bf16[576,2048]{1,0:T(8,128)(2,1)}, bf16[576,2048]{1,0:T(8,128)(2,1)}, u32[]{:S(2)}, u32[]{:S(2)}) collective-permute-start(bf16[576,2048]{1,0:T(8,128)(2,1)} %fusion.9), channel_id=1, source_target_pairs={{0,1},{1,0},{2,3},{3,2},{4,5},{5,4},{6,7},{7,6},{8,9},{9,8},{10,11... | collective-permute-start | bytes 7077896 | tf_op jit(solution)/shard_map/ppermute | solution.py:30
  150.2 126.7 %all-gather.11.cloned.1.call-start = ((), (), s32[]{:S(2)}) async-start(), calls=%async_computation.3 | async-start | bytes 3932160 | tf_op jit(solution)/shard_map/all_gather | solution.py:77
  155.6 53.2 %collective-permute-start.4 = (bf16[576,2048]{1,0:T(8,128)(2,1)}, bf16[576,2048]{1,0:T(8,128)(2,1)S(1)}, u32[]{:S(2)}, u32[]{:S(2)}) collective-permute-start(bf16[576,2048]{1,0:T(8,128)(2,1)} %fusion.8), channel_id=1, source_target_pairs={{0,1},{1,0},{2,3},{3,2},{4,5},{5,4},{6,7},{7,6},{8,9},{9,8},{10,11... | collective-permute-start | bytes 7077896 | tf_op jit(solution)/shard_map/ppermute | solution.py:30
  219.8 86.0 %collective-permute-start.6 = (bf16[576,2048]{1,0:T(8,128)(2,1)}, bf16[576,2048]{1,0:T(8,128)(2,1)}, u32[]{:S(2)}, u32[]{:S(2)}) collective-permute-start(bf16[576,2048]{1,0:T(8,128)(2,1)} %fusion.6), channel_id=1, source_target_pairs={{0,1},{1,0},{2,3},{3,2},{4,5},{5,4},{6,7},{7,6},{8,9},{9,8},{10,11... | collective-permute-start | bytes 7077896 | tf_op jit(solution)/shard_map/ppermute | solution.py:30
  277.0 5.3 %copy-start.2 = (bf16[768,2048]{1,0:T(8,128)(2,1)S(1)}, bf16[768,2048]{1,0:T(8,128)(2,1)}, u32[]{:S(2)}) copy-start(bf16[768,2048]{1,0:T(8,128)(2,1)} %all-gather.5.cloned.1.call-done) | copy-start | bytes 9437188
  280.7 53.0 %collective-permute-start.5 = (bf16[576,2048]{1,0:T(8,128)(2,1)S(1)}, bf16[576,2048]{1,0:T(8,128)(2,1)S(1)}, u32[]{:S(2)}, u32[]{:S(2)}) collective-permute-start(bf16[576,2048]{1,0:T(8,128)(2,1)S(1)} %fusion.7), channel_id=1, source_target_pairs={{0,1},{1,0},{2,3},{3,2},{4,5},{5,4},{6,7},{7,6},{8,9},{9,8},{10,11... | collective-permute-start | bytes 7077896 | tf_op jit(solution)/shard_map/ppermute | solution.py:30
  285.5 14.3 %copy-start.6 = (bf16[768,1024]{1,0:T(8,128)(2,1)}, bf16[768,1024]{1,0:T(8,128)(2,1)S(1)}, u32[]{:S(2)}) copy-start(bf16[768,1024]{1,0:T(8,128)(2,1)S(1)} %multiply_convert_fusion) | copy-start | bytes 4718596
  285.5 3.6 copy-start.1
  289.1 1.9 copy-start.4
  295.0 4.8 copy-start.5
  341.1 20.1 %collective-permute-start.8 = (bf16[512,2048]{1,0:T(8,128)(2,1)}, bf16[512,2048]{1,0:T(8,128)(2,1)S(1)}, u32[]{:S(2)}, u32[]{:S(2)}) collective-permute-start(bf16[512,2048]{1,0:T(8,128)(2,1)} %fusion), channel_id=1, source_target_pairs={{0,8},{8,0},{1,9},{9,1},{2,10},{10,2},{3,11},{11,3},{4,12},{12,4},... | collective-permute-start | bytes 6291464 | tf_op jit(solution)/shard_map/ppermute | solution.py:30
  344.7 5.7 %copy-start.3 = (bf16[768,2048]{1,0:T(8,128)(2,1)S(1)}, bf16[768,2048]{1,0:T(8,128)(2,1)}, u32[]{:S(2)}) copy-start(bf16[768,2048]{1,0:T(8,128)(2,1)} %all-gather.7.cloned.1.call-done) | copy-start | bytes 9437188
  344.7 5.7 %copy-start.7 = (bf16[768,1024]{1,0:T(8,128)(2,1)S(1)}, bf16[768,1024]{1,0:T(8,128)(2,1)}, u32[]{:S(2)}) copy-start(bf16[768,1024]{1,0:T(8,128)(2,1)} %copy-done.6) | copy-start | bytes 4718596
  344.7 22.8 %collective-permute-start.7 = (bf16[512,2048]{1,0:T(8,128)(2,1)S(1)}, bf16[512,2048]{1,0:T(8,128)(2,1)S(1)}, u32[]{:S(2)}, u32[]{:S(2)}) collective-permute-start(bf16[512,2048]{1,0:T(8,128)(2,1)S(1)} %fusion.3), channel_id=1, source_target_pairs={{0,8},{8,0},{1,9},{9,1},{2,10},{10,2},{3,11},{11,3},{4,12},{12,4},... | collective-permute-start | bytes 6291464 | tf_op jit(solution)/shard_map/ppermute | solution.py:30
  374.3 53.0 %collective-permute-start.9 = (f32[512,2048]{1,0:T(8,128)S(1)}, f32[512,2048]{1,0:T(8,128)}, u32[]{:S(2)}, u32[]{:S(2)}) collective-permute-start(f32[512,2048]{1,0:T(8,128)S(1)} %slice_add_fusion.5), channel_id=1, source_target_pairs={{0,8},{8,0},{1,9},{9,1},{2,10},{10,2},{3,11},{11,3},{4,12},{12,4},... | collective-permute-start | bytes 12582920 | tf_op jit(solution)/shard_map/ppermute | solution.py:30
  378.3 93.1 %collective-permute-start.11 = (f32[512,2048]{1,0:T(8,128)}, f32[512,2048]{1,0:T(8,128)}, u32[]{:S(2)}, u32[]{:S(2)}) collective-permute-start(f32[512,2048]{1,0:T(8,128)} %slice_add_fusion.4), channel_id=1, source_target_pairs={{0,8},{8,0},{1,9},{9,1},{2,10},{10,2},{3,11},{11,3},{4,12},{12,4},... | collective-permute-start | bytes 12582920 | tf_op jit(solution)/shard_map/ppermute | solution.py:30
  378.8 48.6 %collective-permute-start.10 = (bf16[512,2048]{1,0:T(8,128)(2,1)S(1)}, bf16[512,2048]{1,0:T(8,128)(2,1)}, u32[]{:S(2)}, u32[]{:S(2)}) collective-permute-start(bf16[512,2048]{1,0:T(8,128)(2,1)S(1)} %fusion.5), channel_id=1, source_target_pairs={{0,16},{16,0},{1,17},{17,1},{2,18},{18,2},{3,19},{19,3},{4,20},{20... | collective-permute-start | bytes 6291464 | tf_op jit(solution)/shard_map/ppermute | solution.py:30
  380.3 91.1 %collective-permute-start.12 = (bf16[512,2048]{1,0:T(8,128)(2,1)}, bf16[512,2048]{1,0:T(8,128)(2,1)}, u32[]{:S(2)}, u32[]{:S(2)}) collective-permute-start(bf16[512,2048]{1,0:T(8,128)(2,1)} %fusion.2), channel_id=1, source_target_pairs={{0,16},{16,0},{1,17},{17,1},{2,18},{18,2},{3,19},{19,3},{4,20},{20... | collective-permute-start | bytes 6291464 | tf_op jit(solution)/shard_map/ppermute | solution.py:30
Sparse Core Ops, SparseCore 0:
  8.9 66.3 all-gather.4
  83.1 64.9 all-gather.6
  150.4 62.1 all-gather.8
  214.8 62.1 all-gather.10

commit v5 on v4

--- a/solution.py
+++ b/solution.py
@@ -43,52 +43,34 @@
         x = lax.axis_index("rx")
         c = lax.axis_index("rc")
         a = z * n_ay + lax.axis_index("ay")
-        order = [(1 - x) * 2 + (1 - c), x * 2 + (1 - c), (1 - x) * 2 + c, x * 2 + c]
-        home = (a * width) // rw
-        off = (a * width) % rw
+        order = [(1 - x) * 2 + (1 - c), (1 - x) * 2 + c, x * 2 + (1 - c), x * 2 + c]
+        y = lax.axis_index("ay")
 
         def others(v):
             doubled = jnp.concatenate([v, v], axis=0)
             return lax.dynamic_slice_in_dim(doubled, (z + 1) * nloc, (n_az - 1) * nloc, axis=0)
 
-        def pick(blocks):
-            out = lax.dynamic_slice_in_dim(blocks[0], off, width, axis=1)
-            for k in range(1, len(blocks)):
-                out = jnp.where(order[k] == home, lax.dynamic_slice_in_dim(blocks[k], off, width, axis=1), out)
-            return out
-
-        w_own = row_weights(pair_index, e_occ, e_vir, occ_batch, freq)
-        w_z = lax.all_gather(w_own, "az", axis=0, tiled=True)
         first = lax.dynamic_slice_in_dim(b_rows, order[0] * rw, rw, axis=1)
         mine = [lax.all_gather(first, "az", axis=0, tiled=True)]
-        w_a = swap(w_own, "ay")
-        w_b = swap(others(w_z), "ay")
         theirs_own = swap(b_rows, "ay")
-        theirs_own, w_a, w_b, rest = lax.optimization_barrier((theirs_own, w_a, w_b, b_rows))
+        w_own = row_weights(pair_index, e_occ, e_vir, occ_batch, freq)
+        scaled_rows = lax.all_to_all(scale(w_own, b_rows), ("az", "ay"), 1, 0, tiled=True)
+        theirs_own, scaled_rows, rest = lax.optimization_barrier((theirs_own, scaled_rows, b_rows))
         theirs = [swap(others(mine[0]), "ay")]
-        pieces = []
-        for k, m in enumerate(order[1:], start=1):
-            parts = 1
-            pieces += [(k, m * rw + p * (rw // parts), rw // parts) for p in range(parts)]
-        got_mine, got_theirs = [mine[0]], [theirs[0]]
-        by_block = {}
-        for k, start, pw in pieces:
-            _, _, rest = lax.optimization_barrier((got_mine[-1], got_theirs[-2] if len(got_theirs) > 1 else w_a, rest))
-            piece = lax.all_gather(lax.dynamic_slice_in_dim(rest, start, pw, axis=1), "az", axis=0, tiled=True)
-            got_mine.append(piece)
-            got_theirs.append(swap(others(piece), "ay"))
-            by_block.setdefault(k, []).append(len(got_mine) - 1)
-        for k in range(1, len(order)):
-            idx = by_block[k]
-            mine.append(jnp.concatenate([got_mine[i] for i in idx], axis=1) if len(idx) > 1 else got_mine[idx[0]])
-            theirs.append(jnp.concatenate([got_theirs[i] for i in idx], axis=1) if len(idx) > 1 else got_theirs[idx[0]])
-        s_mine = scale(w_z, pick(mine))
-        s_a = scale(w_a, lax.dynamic_slice_in_dim(theirs_own, a * width, width, axis=1))
+        for m in order[1:]:
+            _, _, rest = lax.optimization_barrier((mine[-1], theirs[-2] if len(theirs) > 1 else theirs_own, rest))
+            piece = lax.all_gather(lax.dynamic_slice_in_dim(rest, m * rw, rw, axis=1), "az", axis=0, tiled=True)
+            mine.append(piece)
+            theirs.append(swap(others(piece), "ay"))
+        by_source = scaled_rows.reshape(n_az, n_ay, nloc, width)
+        s_mine = lax.dynamic_index_in_dim(by_source, y, axis=1, keepdims=False).reshape(n_az * nloc, width)
+        s_other = lax.dynamic_index_in_dim(by_source, 1 - y, axis=1, keepdims=False).reshape(n_az * nloc, width)
+        s_a = lax.dynamic_slice_in_dim(s_other, z * nloc, nloc, axis=0)
+        s_b = others(s_other)
         early = []
         for k, m in enumerate(order):
             cols_a = lax.dynamic_slice_in_dim(theirs_own, m * rw, rw, axis=1)
             early.append(contract(s_a, cols_a) + contract(s_mine, mine[k]))
-        s_b = scale(w_b, pick(theirs))
         halves = 2 if width % 16 == 0 else 1
         hw = width // halves
         cuts = [slice(h * hw, (h + 1) * hw) for h in range(halves)]
@@ -97,11 +79,11 @@
             s_h = s_b[:, rows]
             give = early[0][rows] + contract(s_h, theirs[0])
             got = swap(give.astype(jnp.bfloat16), "rc").astype(jnp.float32)
-            other_x = early[2][rows] + contract(s_h, theirs[2]) + got
+            other_x = early[1][rows] + contract(s_h, theirs[1]) + got
             sent.append(other_x.astype(jnp.bfloat16))
             got_x.append(swap(sent[-1], "rx"))
         _, late_give, late_keep, t_give, t_keep = lax.optimization_barrier(
-            (tuple(sent), early[1], early[3], theirs[1], theirs[3])
+            (tuple(sent), early[2], early[3], theirs[2], theirs[3])
         )
         out = jnp.zeros((width, rw), jnp.float32)
         for h, rows in enumerate(cuts):

time: 488 us -> 535 us (1.096)
  waiting for transfers between devices: 319 us -> 375 us
  blocking collectives: 12.3 us -> 0 us
    ppermute x13 -> x11, waiting for transfers between devices: 252 us -> 321 us  [swap(): return lax.ppermute(x, axis, [(0, 1), (1, 0)])]
    all_gather x3, waiting for transfers between devices: 66.8 us -> 35.2 us  [body(): lax.all_gather(lax.dynamic_slice_in_dim(rest, m * rw, rw, axis=1), 'az',...]
    all_to_all x0 -> x1, waiting for transfers between devices: none -> 17.8 us  [body(): lax.all_to_all(scale(w_own, b_rows), ('az', 'ay'), 1, 0, tiled=True)]
    unnamed x1 -> x0, blocking collectives: 12.3 us -> none
    all_to_all x0 -> x1, starting transfers between devices: none -> 7.54 us  [body(): lax.all_to_all(scale(w_own, b_rows), ('az', 'ay'), 1, 0, tiled=True)]
    ppermute x13 -> x11, starting transfers between devices: 14.5 us -> 11.3 us  [swap(): return lax.ppermute(x, axis, [(0, 1), (1, 0)])]
  transfers between devices with their start and end apart: 17 -> 16, of which waited for: 9 -> 12; matrix products, arithmetic and copies ran while one was open for 19% -> 18% of each run, Pallas kernels for 0% -> 0%
where the time goes in v5:
time: 535 us; the launch traced here: 527 us
  waiting for transfers between devices  375 us (70%)
  matrix products  64.9 us (12%)
  other arithmetic  36.6 us (7%)
  starting transfers between devices  19 us (4%)
  local copies, waits for them, and re-layouts  17.3 us (3%)
  between operations  15.1 us (3%)
    ppermute x11, waiting for transfers between devices, swap(): return lax.ppermute(x, axis, [(0, 1), (1, 0)])  321 us
    dot_general x16, matrix products, contract(): lax.dot_general(left, right, (((0,), (0,)), ((), ())), preferred_element_...  64.9 us
    all_gather x3, waiting for transfers between devices, body(): lax.all_gather(lax.dynamic_slice_in_dim(rest, m * rw, rw, axis=1), 'az',...  35.2 us
    concatenate x5, other arithmetic, others(): doubled = jnp.concatenate([v, v], axis=0)  19.3 us
    all_to_all x1, waiting for transfers between devices, body(): lax.all_to_all(scale(w_own, b_rows), ('az', 'ay'), 1, 0, tiled=True)  17.8 us
    ppermute x11, starting transfers between devices, swap(): return lax.ppermute(x, axis, [(0, 1), (1, 0)])  11.3 us
  transfers between devices with their start and end apart: 16, of which 12 were waited for; matrix products, arithmetic and copies ran while one was open for 18% of the time, Pallas kernels for 0%

profile of v5, /device:TPU:0, one launch (start us, length us, event | category | flops | bytes accessed | tf_op | source)
XLA Modules:
  0.0 527.5 jit_solution(18039344290167139808)
XLA Ops:
  8.5 1.0 select_reduce_fusion
  10.4 2.6 multiply_convert_fusion
  13.0 2.1 copy.12
  15.1 7.5 %all-to-all-start = ((bf16[192,8,1024]{2,0,1:T(8,128)(2,1)}), bf16[192,8,1024]{2,0,1:T(8,128)(2,1)}, u32[]{:S(2)}, u32[]{:S(2)}) async-start(bf16[192,8,1024]{2,0,1:T(8,128)(2,1)} %bitcast.27), calls=%async_computation | async-start | bytes 6291456 | tf_op jit(solution)/shard_map/all_to_all | solution.py:57
  23.7 2.0 collective-permute-start
  25.7 100.5 %collective-permute-done = bf16[192,8192]{1,0:T(8,128)(2,1)} collective-permute-done((bf16[192,8192]{1,0:T(8,128)(2,1)S(1)}, bf16[192,8192]{1,0:T(8,128)(2,1)}, u32[]{:S(2)}, u32[]{:S(2)}) %collective-permute-start) | collective-permute-done | bytes 3145760 | tf_op jit(solution)/shard_map/ppermute | solution.py:30
  126.2 17.8 %all-to-all-done = bf16[192,8,1024]{2,0,1:T(8,128)(2,1)} async-done(((bf16[192,8,1024]{2,0,1:T(8,128)(2,1)}), bf16[192,8,1024]{2,0,1:T(8,128)(2,1)}, u32[]{:S(2)}, u32[]{:S(2)}) %all-to-all-start) | async-done | bytes 3145760 | tf_op jit(solution)/shard_map/all_to_all | solution.py:57
  145.1 5.0 fusion.8
  150.1 1.4 collective-permute-start.2
  151.5 52.1 %collective-permute-done.2 = bf16[576,2048]{1,0:T(8,128)(2,1)} collective-permute-done((bf16[576,2048]{1,0:T(8,128)(2,1)}, bf16[576,2048]{1,0:T(8,128)(2,1)}, u32[]{:S(2)}, u32[]{:S(2)}) %collective-permute-start.2) | collective-permute-done | bytes 2359328 | tf_op jit(solution)/shard_map/ppermute | solution.py:30
  203.6 4.0 all-gather.7.cloned.1.call-done
  207.7 1.0 constant_dynamic-slice_fusion.1
  208.7 5.0 fusion.9
  213.8 1.5 collective-permute-start.1
  215.3 2.5 constant_dynamic-slice_fusion.5
  217.8 1.5 fusion.10
  219.3 5.9 %fusion.40 = f32[1024,2048]{1,0:T(8,128)} fusion(bf16[768,1024]{1,0:T(8,128)(2,1)S(1)} %bitcast.34, bf16[768,2048]{1,0:T(8,128)(2,1)S(1)} %copy-done.1), kind=kOutput, calls=%fused_computation.74 | convolution fusion | flops 3221225472 | bytes 13107200 | tf_op jit(solution)/shard_map/dot_general | solution.py:24
  225.2 41.9 %collective-permute-done.1 = bf16[576,2048]{1,0:T(8,128)(2,1)} collective-permute-done((bf16[576,2048]{1,0:T(8,128)(2,1)}, bf16[576,2048]{1,0:T(8,128)(2,1)}, u32[]{:S(2)}, u32[]{:S(2)}) %collective-permute-start.1) | collective-permute-done | bytes 2359328 | tf_op jit(solution)/shard_map/ppermute | solution.py:30
  267.1 4.3 all-gather.9.cloned.1.call-done
  271.4 2.2 constant_dynamic-slice_fusion
  273.6 5.0 convolution_add_fusion.2
  278.6 3.8 fusion.3
  282.5 3.7 fusion
  287.0 3.6 fusion.39
  290.6 2.5 convolution_add_fusion.3
  293.0 5.0 fusion.5
  298.1 5.5 %fusion.2 = bf16[512,2048]{1,0:T(8,128)(2,1)} fusion(f32[1024,2048]{1,0:T(8,128)S(1)} %convolution_add_fusion.3, bf16[512,2048]{1,0:T(8,128)(2,1)S(1)} %collective-permute-done.4, bf16[576,2048]{1,0:T(8,128)(2,1)} %collective-permute-done.1, bf16[576,1024]{1,0:T(8,128)(2,1)S(1)} %fusion.10), kind=kOutput, calls=%fused_computation.17 | convolution fusion | flops 1212153856 | bytes 11337728 | tf_op jit(solution)/shard_map/dot_general | solution.py:24
  303.6 4.1 fusion.7
  307.6 1.5 collective-permute-start.5
  309.1 26.8 %all-gather.11.cloned.1.call-done = bf16[768,2048]{1,0:T(8,128)(2,1)} async-done(((bf16[192,2048]{1,0:T(8,128)(2,1)}), bf16[768,2048]{1,0:T(8,128)(2,1)}) %all-gather.11.cloned.1.call-update) | async-done | bytes 3145744 | tf_op jit(solution)/shard_map/all_gather | solution.py:62
  335.9 3.7 fusion.6
  339.7 1.5 collective-permute-start.6
  341.2 3.5 fusion.41
  344.8 2.6 convolution_add_fusion.1
  347.4 6.0 %fusion.42 = f32[1024,2048]{1,0:T(8,128)} fusion(bf16[768,1024]{1,0:T(8,128)(2,1)S(1)} %bitcast.37, bf16[768,2048]{1,0:T(8,128)(2,1)S(1)} %copy-done.5), kind=kOutput, calls=%fused_computation.76 | convolution fusion | flops 3221225472 | bytes 13107200 | tf_op jit(solution)/shard_map/dot_general | solution.py:24
  353.3 5.0 convolution_add_fusion
  358.3 3.7 collective-permute-done.5
  362.0 49.5 %collective-permute-done.6 = bf16[576,2048]{1,0:T(8,128)(2,1)S(1)} collective-permute-done((bf16[576,2048]{1,0:T(8,128)(2,1)S(1)}, bf16[576,2048]{1,0:T(8,128)(2,1)S(1)}, u32[]{:S(2)}, u32[]{:S(2)}) %collective-permute-start.6) | collective-permute-done | bytes 2359328 | tf_op jit(solution)/shard_map/ppermute | solution.py:30
  411.6 3.5 slice_add_fusion.5
  415.2 5.7 %slice_add_fusion.4 = f32[512,2048]{1,0:T(8,128)} fusion(f32[1024,2048]{1,0:T(8,128)S(1)} %convolution_add_fusion.1, bf16[576,2048]{1,0:T(8,128)(2,1)} %collective-permute-done.5, bf16[576,1024]{1,0:T(8,128)(2,1)S(1)} %fusion.10), kind=kOutput, calls=%fused_computation.24 | convolution fusion | flops 1209008128 | bytes 11337728 | tf_op jit(solution)/shard_map/dot_general | solution.py:24
  421.3 1.5 collective-permute-start.8
  423.3 1.9 fusion.25
  425.2 1.8 fusion.17
  427.0 42.8 %collective-permute-done.8 = bf16[512,2048]{1,0:T(8,128)(2,1)} collective-permute-done((bf16[512,2048]{1,0:T(8,128)(2,1)S(1)}, bf16[512,2048]{1,0:T(8,128)(2,1)}, u32[]{:S(2)}, u32[]{:S(2)}) %collective-permute-start.8) | collective-permute-done | bytes 2097184 | tf_op jit(solution)/shard_map/ppermute | solution.py:30
  469.9 6.4 %convert_add_fusion = f32[512,2048]{1,0:T(8,128)} fusion(bf16[512,2048]{1,0:T(8,128)(2,1)} %collective-permute-done.8, f32[512,2048]{1,0:T(8,128)} %collective-permute-done.7, f32[512,2048]{1,0:T(8,128)S(1)} %fusion.25, f32[1024,2048]{1,0:T(8,128)S(1)} %convolution_add_fusion), kind=kLoop, calls=%fused_computation.25 | loop fusion | flops 4194304 | bytes 18874368 | tf_op jit(solution)/shard_map/add | solution.py:93
  476.3 6.8 %dynamic_update_slice.6 = f32[1024,2048]{1,0:T(8,128)} pad(f32[512,2048]{1,0:T(8,128)} %convert_add_fusion, f32[]{:T(128)} %constant.50.clone.1), padding=0_512x0_0 | pad | bytes 12582916 | tf_op jit(solution)/shard_map/dynamic_update_slice | solution.py:93
  483.1 30.9 %collective-permute-done.10 = bf16[512,2048]{1,0:T(8,128)(2,1)} collective-permute-done((bf16[512,2048]{1,0:T(8,128)(2,1)}, bf16[512,2048]{1,0:T(8,128)(2,1)}, u32[]{:S(2)}, u32[]{:S(2)}) %collective-permute-start.10) | collective-permute-done | bytes 2097184 | tf_op jit(solution)/shard_map/ppermute | solution.py:30
  514.0 6.5 %add_dynamic-update-slice_fusion = f32[1024,2048]{1,0:T(8,128)} fusion(f32[1024,2048]{1,0:T(8,128)} %dynamic_update_slice.6, bf16[512,2048]{1,0:T(8,128)(2,1)} %collective-permute-done.10, f32[512,2048]{1,0:T(8,128)} %collective-permute-done.9, f32[512,2048]{1,0:T(8,128)S(1)} %fusion.17, f32[1024,2048]{1,0:T(8,128)S(1)} %convolution_add_fusion), kind=kLoop, calls=%fused_computation.23 | loop fusion | flops 4194304 | bytes 18874368 | tf_op jit(solution)/shard_map/dynamic_update_slice | solution.py:93
  (44 shorter events, 5.6 us)
Async XLA Ops:
  15.1 7.6 %copy-start = (bf16[192,8192]{1,0:T(8,128)(2,1)S(1)}, bf16[192,8192]{1,0:T(8,128)(2,1)}, u32[]{:S(2)}) copy-start(bf16[192,8192]{1,0:T(8,128)(2,1)} %param.6) | copy-start | bytes 9437188
  15.1 128.9 %all-to-all-start = ((bf16[192,8,1024]{2,0,1:T(8,128)(2,1)}), bf16[192,8,1024]{2,0,1:T(8,128)(2,1)}, u32[]{:S(2)}, u32[]{:S(2)}) async-start(bf16[192,8,1024]{2,0,1:T(8,128)(2,1)} %bitcast.27), calls=%async_computation | async-start | bytes 6291456 | tf_op jit(solution)/shard_map/all_to_all | solution.py:57
  22.6 121.5 %all-gather.5.cloned.1.call-start = ((), (), s32[]{:S(2)}) async-start(), calls=%async_computation.1 | async-start | bytes 3932160 | tf_op jit(solution)/shard_map/all_gather | solution.py:54
  23.6 184.0 %all-gather.7.cloned.1.call-start = ((), (), s32[]{:S(2)}) async-start(), calls=%async_computation.2 | async-start | bytes 3932160 | tf_op jit(solution)/shard_map/all_gather | solution.py:62
  23.7 102.5 %collective-permute-start = (bf16[192,8192]{1,0:T(8,128)(2,1)S(1)}, bf16[192,8192]{1,0:T(8,128)(2,1)}, u32[]{:S(2)}, u32[]{:S(2)}) collective-permute-start(bf16[192,8192]{1,0:T(8,128)(2,1)S(1)} %copy-done), channel_id=1, source_target_pairs={{0,1},{1,0},{2,3},{3,2},{4,5},{5,4},{6,7},{7,6},{8,9},{9,8},{10,11... | collective-permute-start | bytes 9437192 | tf_op jit(solution)/shard_map/ppermute | solution.py:30
  145.0 126.4 %all-gather.9.cloned.1.call-start = ((), (), s32[]{:S(2)}) async-start(), calls=%async_computation.3 | async-start | bytes 3932160 | tf_op jit(solution)/shard_map/all_gather | solution.py:62
  150.1 53.5 %collective-permute-start.2 = (bf16[576,2048]{1,0:T(8,128)(2,1)}, bf16[576,2048]{1,0:T(8,128)(2,1)}, u32[]{:S(2)}, u32[]{:S(2)}) collective-permute-start(bf16[576,2048]{1,0:T(8,128)(2,1)} %fusion.8), channel_id=1, source_target_pairs={{0,1},{1,0},{2,3},{3,2},{4,5},{5,4},{6,7},{7,6},{8,9},{9,8},{10,11... | collective-permute-start | bytes 7077896 | tf_op jit(solution)/shard_map/ppermute | solution.py:30
  208.7 127.2 %all-gather.11.cloned.1.call-start = ((), (), s32[]{:S(2)}) async-start(), calls=%async_computation.4 | async-start | bytes 3932160 | tf_op jit(solution)/shard_map/all_gather | solution.py:62
  213.8 53.3 %collective-permute-start.1 = (bf16[576,2048]{1,0:T(8,128)(2,1)}, bf16[576,2048]{1,0:T(8,128)(2,1)}, u32[]{:S(2)}, u32[]{:S(2)}) collective-permute-start(bf16[576,2048]{1,0:T(8,128)(2,1)} %fusion.9), channel_id=1, source_target_pairs={{0,1},{1,0},{2,3},{3,2},{4,5},{5,4},{6,7},{7,6},{8,9},{9,8},{10,11... | collective-permute-start | bytes 7077896 | tf_op jit(solution)/shard_map/ppermute | solution.py:30
  215.2 4.0 copy-start.1
  217.8 7.4 %copy-start.6 = (bf16[4,1,192,1024]{3,2,1,0:T(8,128)(2,1)}, bf16[4,1,192,1024]{3,2,1,0:T(8,128)(2,1)S(1)}, u32[]{:S(2)}) copy-start(bf16[4,1,192,1024]{3,2,1,0:T(8,128)(2,1)S(1)} %get-tuple-element.26) | copy-start | bytes 4718596
  282.4 4.7 copy-start.2
  282.4 4.6 copy-start.7
  282.4 10.7 %collective-permute-start.3 = (bf16[512,2048]{1,0:T(8,128)(2,1)S(1)}, bf16[512,2048]{1,0:T(8,128)(2,1)S(1)}, u32[]{:S(2)}, u32[]{:S(2)}) collective-permute-start(bf16[512,2048]{1,0:T(8,128)(2,1)S(1)} %fusion.3), channel_id=1, source_target_pairs={{0,8},{8,0},{1,9},{9,1},{2,10},{10,2},{3,11},{11,3},{4,12},{12,4},... | collective-permute-start | bytes 6291464 | tf_op jit(solution)/shard_map/ppermute | solution.py:30
  286.2 11.9 %collective-permute-start.4 = (bf16[512,2048]{1,0:T(8,128)(2,1)S(1)}, bf16[512,2048]{1,0:T(8,128)(2,1)S(1)}, u32[]{:S(2)}, u32[]{:S(2)}) collective-permute-start(bf16[512,2048]{1,0:T(8,128)(2,1)S(1)} %fusion), channel_id=1, source_target_pairs={{0,8},{8,0},{1,9},{9,1},{2,10},{10,2},{3,11},{11,3},{4,12},{12,4},... | collective-permute-start | bytes 6291464 | tf_op jit(solution)/shard_map/ppermute | solution.py:30
  298.1 5.5 %copy-start.3 = (bf16[768,2048]{1,0:T(8,128)(2,1)S(1)}, bf16[768,2048]{1,0:T(8,128)(2,1)}, u32[]{:S(2)}) copy-start(bf16[768,2048]{1,0:T(8,128)(2,1)} %all-gather.9.cloned.1.call-done) | copy-start | bytes 9437188
  307.6 54.4 %collective-permute-start.5 = (bf16[576,2048]{1,0:T(8,128)(2,1)}, bf16[576,2048]{1,0:T(8,128)(2,1)}, u32[]{:S(2)}, u32[]{:S(2)}) collective-permute-start(bf16[576,2048]{1,0:T(8,128)(2,1)} %fusion.7), channel_id=1, source_target_pairs={{0,1},{1,0},{2,3},{3,2},{4,5},{5,4},{6,7},{7,6},{8,9},{9,8},{10,11... | collective-permute-start | bytes 7077896 | tf_op jit(solution)/shard_map/ppermute | solution.py:30
  335.9 5.3 %copy-start.4 = (bf16[768,2048]{1,0:T(8,128)(2,1)S(1)}, bf16[768,2048]{1,0:T(8,128)(2,1)}, u32[]{:S(2)}) copy-start(bf16[768,2048]{1,0:T(8,128)(2,1)} %all-gather.9.cloned.1.call-done) | copy-start | bytes 9437188
  335.9 5.3 %copy-start.8 = (bf16[4,1,192,1024]{3,2,1,0:T(8,128)(2,1)S(1)}, bf16[4,1,192,1024]{3,2,1,0:T(8,128)(2,1)}, u32[]{:S(2)}) copy-start(bf16[4,1,192,1024]{3,2,1,0:T(8,128)(2,1)} %copy-done.6) | copy-start | bytes 4718596
  339.7 71.9 %collective-permute-start.6 = (bf16[576,2048]{1,0:T(8,128)(2,1)S(1)}, bf16[576,2048]{1,0:T(8,128)(2,1)S(1)}, u32[]{:S(2)}, u32[]{:S(2)}) collective-permute-start(bf16[576,2048]{1,0:T(8,128)(2,1)S(1)} %fusion.6), channel_id=1, source_target_pairs={{0,1},{1,0},{2,3},{3,2},{4,5},{5,4},{6,7},{7,6},{8,9},{9,8},{10,11... | collective-permute-start | bytes 7077896 | tf_op jit(solution)/shard_map/ppermute | solution.py:30
  344.7 2.6 copy-start.5
  415.1 6.2 %copy-start.9 = (bf16[512,2048]{1,0:T(8,128)(2,1)S(1)}, bf16[512,2048]{1,0:T(8,128)(2,1)}, u32[]{:S(2)}) copy-start(bf16[512,2048]{1,0:T(8,128)(2,1)} %fusion.5) | copy-start | bytes 6291460
  415.1 54.8 %collective-permute-start.7 = (f32[512,2048]{1,0:T(8,128)S(1)}, f32[512,2048]{1,0:T(8,128)}, u32[]{:S(2)}, u32[]{:S(2)}) collective-permute-start(f32[512,2048]{1,0:T(8,128)S(1)} %slice_add_fusion.5), channel_id=1, source_target_pairs={{0,8},{8,0},{1,9},{9,1},{2,10},{10,2},{3,11},{11,3},{4,12},{12,4},... | collective-permute-start | bytes 12582920 | tf_op jit(solution)/shard_map/ppermute | solution.py:30
  420.9 93.1 %collective-permute-start.9 = (f32[512,2048]{1,0:T(8,128)}, f32[512,2048]{1,0:T(8,128)}, u32[]{:S(2)}, u32[]{:S(2)}) collective-permute-start(f32[512,2048]{1,0:T(8,128)} %slice_add_fusion.4), channel_id=1, source_target_pairs={{0,8},{8,0},{1,9},{9,1},{2,10},{10,2},{3,11},{11,3},{4,12},{12,4},... | collective-permute-start | bytes 12582920 | tf_op jit(solution)/shard_map/ppermute | solution.py:30
  421.3 48.6 %collective-permute-start.8 = (bf16[512,2048]{1,0:T(8,128)(2,1)S(1)}, bf16[512,2048]{1,0:T(8,128)(2,1)}, u32[]{:S(2)}, u32[]{:S(2)}) collective-permute-start(bf16[512,2048]{1,0:T(8,128)(2,1)S(1)} %copy-done.9), channel_id=1, source_target_pairs={{0,16},{16,0},{1,17},{17,1},{2,18},{18,2},{3,19},{19,3},{4,20},{20... | collective-permute-start | bytes 6291464 | tf_op jit(solution)/shard_map/ppermute | solution.py:30
  422.8 91.2 %collective-permute-start.10 = (bf16[512,2048]{1,0:T(8,128)(2,1)}, bf16[512,2048]{1,0:T(8,128)(2,1)}, u32[]{:S(2)}, u32[]{:S(2)}) collective-permute-start(bf16[512,2048]{1,0:T(8,128)(2,1)} %fusion.2), channel_id=1, source_target_pairs={{0,16},{16,0},{1,17},{17,1},{2,18},{18,2},{3,19},{19,3},{4,20},{20... | collective-permute-start | bytes 6291464 | tf_op jit(solution)/shard_map/ppermute | solution.py:30
Sparse Core Ops, SparseCore 0:
  25.0 119.0 all-gather.4
  145.6 61.9 all-gather.6
  209.2 62.1 all-gather.8
  273.7 62.1 all-gather.10

commit v6 on v5

--- a/solution.py
+++ b/solution.py
@@ -56,32 +56,42 @@
         w_own = row_weights(pair_index, e_occ, e_vir, occ_batch, freq)
         scaled_rows = lax.all_to_all(scale(w_own, b_rows), ("az", "ay"), 1, 0, tiled=True)
         theirs_own, scaled_rows, rest = lax.optimization_barrier((theirs_own, scaled_rows, b_rows))
+        def x_chain(theirs):
+            by_source = scaled_rows.reshape(n_az, n_ay, nloc, width)
+            s_mine = lax.dynamic_index_in_dim(by_source, y, axis=1, keepdims=False).reshape(n_az * nloc, width)
+            s_other = lax.dynamic_index_in_dim(by_source, 1 - y, axis=1, keepdims=False).reshape(n_az * nloc, width)
+            s_a = lax.dynamic_slice_in_dim(s_other, z * nloc, nloc, axis=0)
+            s_b = others(s_other)
+            early = []
+            for k, m in enumerate(order):
+                cols_a = lax.dynamic_slice_in_dim(theirs_own, m * rw, rw, axis=1)
+                early.append(contract(s_a, cols_a) + contract(s_mine, mine[k]))
+            halves = 2 if width % 16 == 0 else 1
+            hw = width // halves
+            cuts = [slice(h * hw, (h + 1) * hw) for h in range(halves)]
+            sent, got_x = [], []
+            for rows in cuts:
+                s_h = s_b[:, rows]
+                give = early[0][rows] + contract(s_h, theirs[0])
+                got = swap(give.astype(jnp.bfloat16), "rc").astype(jnp.float32)
+                other_x = early[1][rows] + contract(s_h, theirs[1]) + got
+                sent.append(other_x.astype(jnp.bfloat16))
+                got_x.append(swap(sent[-1], "rx"))
+            return s_a, s_b, early, tuple(sent), tuple(got_x), cuts, hw, halves
+
+        x_out = {}
         theirs = [swap(others(mine[0]), "ay")]
         for m in order[1:]:
             _, _, rest = lax.optimization_barrier((mine[-1], theirs[-2] if len(theirs) > 1 else theirs_own, rest))
             piece = lax.all_gather(lax.dynamic_slice_in_dim(rest, m * rw, rw, axis=1), "az", axis=0, tiled=True)
             mine.append(piece)
-            theirs.append(swap(others(piece), "ay"))
-        by_source = scaled_rows.reshape(n_az, n_ay, nloc, width)
-        s_mine = lax.dynamic_index_in_dim(by_source, y, axis=1, keepdims=False).reshape(n_az * nloc, width)
-        s_other = lax.dynamic_index_in_dim(by_source, 1 - y, axis=1, keepdims=False).reshape(n_az * nloc, width)
-        s_a = lax.dynamic_slice_in_dim(s_other, z * nloc, nloc, axis=0)
-        s_b = others(s_other)
-        early = []
-        for k, m in enumerate(order):
-            cols_a = lax.dynamic_slice_in_dim(theirs_own, m * rw, rw, axis=1)
-            early.append(contract(s_a, cols_a) + contract(s_mine, mine[k]))
-        halves = 2 if width % 16 == 0 else 1
-        hw = width // halves
-        cuts = [slice(h * hw, (h + 1) * hw) for h in range(halves)]
-        sent, got_x = [], []
-        for rows in cuts:
-            s_h = s_b[:, rows]
-            give = early[0][rows] + contract(s_h, theirs[0])
-            got = swap(give.astype(jnp.bfloat16), "rc").astype(jnp.float32)
-            other_x = early[1][rows] + contract(s_h, theirs[1]) + got
-            sent.append(other_x.astype(jnp.bfloat16))
-            got_x.append(swap(sent[-1], "rx"))
+            outgoing = others(piece)
+            if len(mine) == len(order):
+                x_out["v"] = x_chain(theirs)
+                outgoing = lax.optimization_barrier((outgoing, x_out["v"][4]))[0]
+            theirs.append(swap(outgoing, "ay"))
+        s_a, s_b, early_part, sent, got_x, cuts, hw, halves = x_out["v"]
+        early = list(early_part)
         _, late_give, late_keep, t_give, t_keep = lax.optimization_barrier(
             (tuple(sent), early[2], early[3], theirs[2], theirs[3])
         )

time: 535 us -> 481 us (0.90)
  waiting for transfers between devices: 375 us -> 323 us
    ppermute x11, waiting for transfers between devices: 321 us -> 265 us  [swap(): return lax.ppermute(x, axis, [(0, 1), (1, 0)])]
  transfers between devices with their start and end apart: 16 -> 16, of which waited for: 12 -> 10; matrix products, arithmetic and copies ran while one was open for 18% -> 20% of each run, Pallas kernels for 0% -> 0%
where the time goes in v6:
time: 481 us; the launch traced here: 477 us
  waiting for transfers between devices  323 us (67%)
  matrix products  62.7 us (13%)
  other arithmetic  36.8 us (8%)
  local copies, waits for them, and re-layouts  20.6 us (4%)
  starting transfers between devices  18.7 us (4%)
  between operations  14.9 us (3%)
    ppermute x11, waiting for transfers between devices, swap(): return lax.ppermute(x, axis, [(0, 1), (1, 0)])  265 us
    dot_general x16, matrix products, contract(): lax.dot_general(left, right, (((0,), (0,)), ((), ())), preferred_element_...  62.7 us
    all_gather x3, waiting for transfers between devices, body(): lax.all_gather(lax.dynamic_slice_in_dim(rest, m * rw, rw, axis=1), 'az',...  40.5 us
    concatenate x5, other arithmetic, others(): doubled = jnp.concatenate([v, v], axis=0)  19.5 us
    all_to_all x1, waiting for transfers between devices, body(): lax.all_to_all(scale(w_own, b_rows), ('az', 'ay'), 1, 0, tiled=True)  17.8 us
    ppermute x11, starting transfers between devices, swap(): return lax.ppermute(x, axis, [(0, 1), (1, 0)])  10.8 us
  transfers between devices with their start and end apart: 16, of which 10 were waited for; matrix products, arithmetic and copies ran while one was open for 20% of the time, Pallas kernels for 0%

profile of v6, /device:TPU:0, one launch (start us, length us, event | category | flops | bytes accessed | tf_op | source)
XLA Modules:
  0.0 476.8 jit_solution(13853728281110434812)
XLA Ops:
  8.5 1.0 select_reduce_fusion
  10.4 2.6 multiply_convert_fusion
  13.0 2.1 copy.12
  15.1 7.5 %all-to-all-start = ((bf16[192,8,1024]{2,0,1:T(8,128)(2,1)}), bf16[192,8,1024]{2,0,1:T(8,128)(2,1)}, u32[]{:S(2)}, u32[]{:S(2)}) async-start(bf16[192,8,1024]{2,0,1:T(8,128)(2,1)} %bitcast.27), calls=%async_computation | async-start | bytes 6291456 | tf_op jit(solution)/shard_map/all_to_all | solution.py:57
  23.7 2.0 collective-permute-start
  25.7 100.5 %collective-permute-done = bf16[192,8192]{1,0:T(8,128)(2,1)} collective-permute-done((bf16[192,8192]{1,0:T(8,128)(2,1)S(1)}, bf16[192,8192]{1,0:T(8,128)(2,1)}, u32[]{:S(2)}, u32[]{:S(2)}) %collective-permute-start) | collective-permute-done | bytes 3145760 | tf_op jit(solution)/shard_map/ppermute | solution.py:30
  126.2 17.8 %all-to-all-done = bf16[192,8,1024]{2,0,1:T(8,128)(2,1)} async-done(((bf16[192,8,1024]{2,0,1:T(8,128)(2,1)}), bf16[192,8,1024]{2,0,1:T(8,128)(2,1)}, u32[]{:S(2)}, u32[]{:S(2)}) %all-to-all-start) | async-done | bytes 3145760 | tf_op jit(solution)/shard_map/all_to_all | solution.py:57
  144.1 1.0 constant_dynamic-slice_fusion.2
  145.1 5.0 %fusion.8 = bf16[576,2048]{1,0:T(8,128)(2,1)} fusion(s32[]{:T(128)S(6)} %select_n.66, bf16[768,2048]{1,0:T(8,128)(2,1)} %all-gather.5.cloned.1.call-done), kind=kLoop, calls=%fused_computation.32 | loop fusion | flops 4718592 | bytes 5505028 | tf_op jit(solution)/shard_map/concatenate | solution.py:50
  150.1 1.4 collective-permute-start.2
  151.5 52.1 %collective-permute-done.2 = bf16[576,2048]{1,0:T(8,128)(2,1)} collective-permute-done((bf16[576,2048]{1,0:T(8,128)(2,1)}, bf16[576,2048]{1,0:T(8,128)(2,1)}, u32[]{:S(2)}, u32[]{:S(2)}) %collective-permute-start.2) | collective-permute-done | bytes 2359328 | tf_op jit(solution)/shard_map/ppermute | solution.py:30
  203.7 4.0 all-gather.7.cloned.1.call-done
  207.7 1.0 constant_dynamic-slice_fusion.1
  208.9 5.0 %fusion.9 = bf16[576,2048]{1,0:T(8,128)(2,1)} fusion(s32[]{:T(128)S(6)} %select_n.66, bf16[768,2048]{1,0:T(8,128)(2,1)} %all-gather.7.cloned.1.call-done), kind=kLoop, calls=%fused_computation.33 | loop fusion | flops 4718592 | bytes 5505028 | tf_op jit(solution)/shard_map/concatenate | solution.py:50
  213.9 1.5 collective-permute-start.1
  215.4 2.6 constant_dynamic-slice_fusion.5
  218.0 1.5 fusion.10
  219.5 3.6 fusion.40
  223.0 2.4 convolution_add_fusion.2
  225.5 3.4 copy-done.1
  228.9 4.9 %fusion.3 = bf16[512,2048]{1,0:T(8,128)(2,1)} fusion(f32[1024,2048]{1,0:T(8,128)S(1)} %convolution_add_fusion.2, bf16[576,2048]{1,0:T(8,128)(2,1)} %collective-permute-done.2, bf16[576,1024]{1,0:T(8,128)(2,1)S(1)} %fusion.10), kind=kOutput, calls=%fused_computation.19 | convolution fusion | flops 1210056704 | bytes 9240576 | tf_op jit(solution)/shard_map/dot_general | solution.py:24
  233.8 33.4 %collective-permute-done.1 = bf16[576,2048]{1,0:T(8,128)(2,1)} collective-permute-done((bf16[576,2048]{1,0:T(8,128)(2,1)}, bf16[576,2048]{1,0:T(8,128)(2,1)}, u32[]{:S(2)}, u32[]{:S(2)}) %collective-permute-start.1) | collective-permute-done | bytes 2359328 | tf_op jit(solution)/shard_map/ppermute | solution.py:30
  267.2 4.2 all-gather.9.cloned.1.call-done
  271.4 2.1 constant_dynamic-slice_fusion
  273.6 4.9 %fusion = bf16[512,2048]{1,0:T(8,128)(2,1)S(1)} fusion(f32[1024,2048]{1,0:T(8,128)} %copy-done.1, bf16[576,2048]{1,0:T(8,128)(2,1)} %collective-permute-done.2, bf16[576,1024]{1,0:T(8,128)(2,1)S(1)} %fusion.10), kind=kOutput, calls=%fused_computation.14 | convolution fusion | flops 1210056704 | bytes 9240576 | tf_op jit(solution)/shard_map/dot_general | solution.py:24
  278.6 4.0 fusion.39
  282.5 2.5 convolution_add_fusion.3
  285.0 5.7 %fusion.5 = bf16[512,2048]{1,0:T(8,128)(2,1)} fusion(f32[1024,2048]{1,0:T(8,128)S(1)} %convolution_add_fusion.3, bf16[512,2048]{1,0:T(8,128)(2,1)} %collective-permute-done.3, bf16[576,2048]{1,0:T(8,128)(2,1)} %collective-permute-done.1, bf16[576,1024]{1,0:T(8,128)(2,1)S(1)} %fusion.10), kind=kOutput, calls=%fused_computation.22 | convolution fusion | flops 1212153856 | bytes 11337728 | tf_op jit(solution)/shard_map/dot_general | solution.py:24
  290.7 1.5 collective-permute-start.6
  292.2 5.1 %fusion.2 = bf16[512,2048]{1,0:T(8,128)(2,1)} fusion(f32[1024,2048]{1,0:T(8,128)S(1)} %convolution_add_fusion.3, bf16[512,2048]{1,0:T(8,128)(2,1)S(1)} %collective-permute-done.4, bf16[576,2048]{1,0:T(8,128)(2,1)} %collective-permute-done.1, bf16[576,1024]{1,0:T(8,128)(2,1)S(1)} %fusion.10), kind=kOutput, calls=%fused_computation.17 | convolution fusion | flops 1212153856 | bytes 11337728 | tf_op jit(solution)/shard_map/dot_general | solution.py:24
  298.1 4.1 fusion.7
  302.2 1.5 collective-permute-start.5
  303.7 32.2 %all-gather.11.cloned.1.call-done = bf16[768,2048]{1,0:T(8,128)(2,1)} async-done(((bf16[192,2048]{1,0:T(8,128)(2,1)}), bf16[768,2048]{1,0:T(8,128)(2,1)}) %all-gather.11.cloned.1.call-update) | async-done | bytes 3145744 | tf_op jit(solution)/shard_map/all_gather | solution.py:86
  335.9 3.9 fusion.6
  339.8 44.2 %collective-permute-done.7 = bf16[512,2048]{1,0:T(8,128)(2,1)} collective-permute-done((bf16[512,2048]{1,0:T(8,128)(2,1)}, bf16[512,2048]{1,0:T(8,128)(2,1)}, u32[]{:S(2)}, u32[]{:S(2)}) %collective-permute-start.7) | collective-permute-done | bytes 2097184 | tf_op jit(solution)/shard_map/ppermute | solution.py:30
  384.0 1.5 collective-permute-start.8
  385.5 3.5 fusion.41
  389.0 2.6 convolution_add_fusion.1
  391.7 5.7 %fusion.42 = f32[1024,2048]{1,0:T(8,128)} fusion(bf16[768,1024]{1,0:T(8,128)(2,1)S(1)} %bitcast.37, bf16[768,2048]{1,0:T(8,128)(2,1)S(1)} %copy-done.6), kind=kOutput, calls=%fused_computation.76 | convolution fusion | flops 3221225472 | bytes 13107200 | tf_op jit(solution)/shard_map/dot_general | solution.py:24
  397.4 4.9 %convolution_add_fusion = f32[1024,2048]{1,0:T(8,128)S(1)} fusion(f32[1024,2048]{1,0:T(8,128)} %fusion.42, bf16[192,8192]{1,0:T(8,128)(2,1)} %collective-permute-done, s32[]{:T(128)S(6)} %select_n.68, bf16[768,1024]{1,0:T(8,128)(2,1)S(1)} %bitcast.32, s32[]{:T(128)S(6)} %select_n.62), kind=kOutput, calls=%fused_computation.9 | convolution fusion | flops 807403520 | bytes 17956872 | tf_op jit(solution)/shard_map/dot_general | solution.py:24
  402.4 34.5 %collective-permute-done.8 = bf16[576,2048]{1,0:T(8,128)(2,1)S(1)} collective-permute-done((bf16[576,2048]{1,0:T(8,128)(2,1)S(1)}, bf16[576,2048]{1,0:T(8,128)(2,1)S(1)}, u32[]{:S(2)}, u32[]{:S(2)}) %collective-permute-start.8) | collective-permute-done | bytes 2359328 | tf_op jit(solution)/shard_map/ppermute | solution.py:30
  436.9 3.5 slice_add_fusion.5
  440.5 5.6 %slice_add_fusion.4 = f32[512,2048]{1,0:T(8,128)} fusion(f32[1024,2048]{1,0:T(8,128)S(1)} %convolution_add_fusion.1, bf16[576,2048]{1,0:T(8,128)(2,1)} %collective-permute-done.5, bf16[576,1024]{1,0:T(8,128)(2,1)S(1)} %fusion.10), kind=kOutput, calls=%fused_computation.24 | convolution fusion | flops 1209008128 | bytes 11337728 | tf_op jit(solution)/shard_map/dot_general | solution.py:24
  446.6 1.9 fusion.25
  448.4 1.8 fusion.17
  450.3 6.4 %convert_add_fusion = f32[512,2048]{1,0:T(8,128)} fusion(bf16[512,2048]{1,0:T(8,128)(2,1)} %collective-permute-done.6, f32[512,2048]{1,0:T(8,128)} %collective-permute-done.9, f32[512,2048]{1,0:T(8,128)S(1)} %fusion.25, f32[1024,2048]{1,0:T(8,128)S(1)} %convolution_add_fusion), kind=kLoop, calls=%fused_computation.25 | loop fusion | flops 4194304 | bytes 18874368 | tf_op jit(solution)/shard_map/add | solution.py:103
  456.7 6.8 %dynamic_update_slice.6 = f32[1024,2048]{1,0:T(8,128)} pad(f32[512,2048]{1,0:T(8,128)} %convert_add_fusion, f32[]{:T(128)} %constant.50.clone.1), padding=0_512x0_0 | pad | bytes 12582916 | tf_op jit(solution)/shard_map/dynamic_update_slice | solution.py:103
  463.6 6.5 %add_dynamic-update-slice_fusion = f32[1024,2048]{1,0:T(8,128)} fusion(f32[1024,2048]{1,0:T(8,128)} %dynamic_update_slice.6, bf16[512,2048]{1,0:T(8,128)(2,1)} %collective-permute-done.7, f32[512,2048]{1,0:T(8,128)} %collective-permute-done.10, f32[512,2048]{1,0:T(8,128)S(1)} %fusion.17, f32[1024,2048]{1,0:T(8,128)S(1)} %convolution_add_fusion), kind=kLoop, calls=%fused_computation.23 | loop fusion | flops 4194304 | bytes 18874368 | tf_op jit(solution)/shard_map/dynamic_update_slice | solution.py:103
  (44 shorter events, 4.5 us)
Async XLA Ops:
  15.1 7.6 %copy-start = (bf16[192,8192]{1,0:T(8,128)(2,1)S(1)}, bf16[192,8192]{1,0:T(8,128)(2,1)}, u32[]{:S(2)}) copy-start(bf16[192,8192]{1,0:T(8,128)(2,1)} %param.6) | copy-start | bytes 9437188
  15.1 128.9 %all-to-all-start = ((bf16[192,8,1024]{2,0,1:T(8,128)(2,1)}), bf16[192,8,1024]{2,0,1:T(8,128)(2,1)}, u32[]{:S(2)}, u32[]{:S(2)}) async-start(bf16[192,8,1024]{2,0,1:T(8,128)(2,1)} %bitcast.27), calls=%async_computation | async-start | bytes 6291456 | tf_op jit(solution)/shard_map/all_to_all | solution.py:57
  22.6 121.5 %all-gather.5.cloned.1.call-start = ((), (), s32[]{:S(2)}) async-start(), calls=%async_computation.1 | async-start | bytes 3932160 | tf_op jit(solution)/shard_map/all_gather | solution.py:54
  23.6 184.0 %all-gather.7.cloned.1.call-start = ((), (), s32[]{:S(2)}) async-start(), calls=%async_computation.2 | async-start | bytes 3932160 | tf_op jit(solution)/shard_map/all_gather | solution.py:86
  23.7 102.5 %collective-permute-start = (bf16[192,8192]{1,0:T(8,128)(2,1)S(1)}, bf16[192,8192]{1,0:T(8,128)(2,1)}, u32[]{:S(2)}, u32[]{:S(2)}) collective-permute-start(bf16[192,8192]{1,0:T(8,128)(2,1)S(1)} %copy-done), channel_id=1, source_target_pairs={{0,1},{1,0},{2,3},{3,2},{4,5},{5,4},{6,7},{7,6},{8,9},{9,8},{10,11... | collective-permute-start | bytes 9437192 | tf_op jit(solution)/shard_map/ppermute | solution.py:30
  145.0 126.4 %all-gather.9.cloned.1.call-start = ((), (), s32[]{:S(2)}) async-start(), calls=%async_computation.3 | async-start | bytes 3932160 | tf_op jit(solution)/shard_map/all_gather | solution.py:86
  150.1 53.5 %collective-permute-start.2 = (bf16[576,2048]{1,0:T(8,128)(2,1)}, bf16[576,2048]{1,0:T(8,128)(2,1)}, u32[]{:S(2)}, u32[]{:S(2)}) collective-permute-start(bf16[576,2048]{1,0:T(8,128)(2,1)} %fusion.8), channel_id=1, source_target_pairs={{0,1},{1,0},{2,3},{3,2},{4,5},{5,4},{6,7},{7,6},{8,9},{9,8},{10,11... | collective-permute-start | bytes 7077896 | tf_op jit(solution)/shard_map/ppermute | solution.py:30
  208.7 127.2 %all-gather.11.cloned.1.call-start = ((), (), s32[]{:S(2)}) async-start(), calls=%async_computation.4 | async-start | bytes 3932160 | tf_op jit(solution)/shard_map/all_gather | solution.py:86
  213.9 53.3 %collective-permute-start.1 = (bf16[576,2048]{1,0:T(8,128)(2,1)}, bf16[576,2048]{1,0:T(8,128)(2,1)}, u32[]{:S(2)}, u32[]{:S(2)}) collective-permute-start(bf16[576,2048]{1,0:T(8,128)(2,1)} %fusion.9), channel_id=1, source_target_pairs={{0,1},{1,0},{2,3},{3,2},{4,5},{5,4},{6,7},{7,6},{8,9},{9,8},{10,11... | collective-permute-start | bytes 7077896 | tf_op jit(solution)/shard_map/ppermute | solution.py:30
  215.4 4.1 copy-start.2
  218.0 1.5 copy-start.7
  225.5 3.4 copy-start.1
  233.8 51.2 %collective-permute-start.3 = (bf16[512,2048]{1,0:T(8,128)(2,1)}, bf16[512,2048]{1,0:T(8,128)(2,1)}, u32[]{:S(2)}, u32[]{:S(2)}) collective-permute-start(bf16[512,2048]{1,0:T(8,128)(2,1)} %fusion.3), channel_id=1, source_target_pairs={{0,8},{8,0},{1,9},{9,1},{2,10},{10,2},{3,11},{11,3},{4,12},{12,4},... | collective-permute-start | bytes 6291464 | tf_op jit(solution)/shard_map/ppermute | solution.py:30
  273.6 5.0 %copy-start.3 = (bf16[768,2048]{1,0:T(8,128)(2,1)S(1)}, bf16[768,2048]{1,0:T(8,128)(2,1)}, u32[]{:S(2)}) copy-start(bf16[768,2048]{1,0:T(8,128)(2,1)} %all-gather.7.cloned.1.call-done) | copy-start | bytes 9437188
  273.6 5.0 %copy-start.8 = (bf16[4,1,192,1024]{3,2,1,0:T(8,128)(2,1)S(1)}, bf16[4,1,192,1024]{3,2,1,0:T(8,128)(2,1)}, u32[]{:S(2)}) copy-start(bf16[4,1,192,1024]{3,2,1,0:T(8,128)(2,1)} %copy-done.7) | copy-start | bytes 4718596
  278.5 13.7 %collective-permute-start.4 = (bf16[512,2048]{1,0:T(8,128)(2,1)S(1)}, bf16[512,2048]{1,0:T(8,128)(2,1)S(1)}, u32[]{:S(2)}, u32[]{:S(2)}) collective-permute-start(bf16[512,2048]{1,0:T(8,128)(2,1)S(1)} %fusion), channel_id=1, source_target_pairs={{0,8},{8,0},{1,9},{9,1},{2,10},{10,2},{3,11},{11,3},{4,12},{12,4},... | collective-permute-start | bytes 6291464 | tf_op jit(solution)/shard_map/ppermute | solution.py:30
  290.7 7.5 %copy-start.4 = (bf16[768,2048]{1,0:T(8,128)(2,1)S(1)}, bf16[768,2048]{1,0:T(8,128)(2,1)}, u32[]{:S(2)}) copy-start(bf16[768,2048]{1,0:T(8,128)(2,1)} %all-gather.9.cloned.1.call-done) | copy-start | bytes 9437188
  290.7 49.1 %collective-permute-start.6 = (bf16[512,2048]{1,0:T(8,128)(2,1)}, bf16[512,2048]{1,0:T(8,128)(2,1)}, u32[]{:S(2)}, u32[]{:S(2)}) collective-permute-start(bf16[512,2048]{1,0:T(8,128)(2,1)} %fusion.5), channel_id=1, source_target_pairs={{0,16},{16,0},{1,17},{17,1},{2,18},{18,2},{3,19},{19,3},{4,20},{20... | collective-permute-start | bytes 6291464 | tf_op jit(solution)/shard_map/ppermute | solution.py:30
  297.3 86.7 %collective-permute-start.7 = (bf16[512,2048]{1,0:T(8,128)(2,1)}, bf16[512,2048]{1,0:T(8,128)(2,1)}, u32[]{:S(2)}, u32[]{:S(2)}) collective-permute-start(bf16[512,2048]{1,0:T(8,128)(2,1)} %fusion.2), channel_id=1, source_target_pairs={{0,16},{16,0},{1,17},{17,1},{2,18},{18,2},{3,19},{19,3},{4,20},{20... | collective-permute-start | bytes 6291464 | tf_op jit(solution)/shard_map/ppermute | solution.py:30
  302.2 100.1 %collective-permute-start.5 = (bf16[576,2048]{1,0:T(8,128)(2,1)}, bf16[576,2048]{1,0:T(8,128)(2,1)}, u32[]{:S(2)}, u32[]{:S(2)}) collective-permute-start(bf16[576,2048]{1,0:T(8,128)(2,1)} %fusion.7), channel_id=1, source_target_pairs={{0,1},{1,0},{2,3},{3,2},{4,5},{5,4},{6,7},{7,6},{8,9},{9,8},{10,11... | collective-permute-start | bytes 7077896 | tf_op jit(solution)/shard_map/ppermute | solution.py:30
  335.9 49.6 %copy-start.5 = (bf16[768,2048]{1,0:T(8,128)(2,1)S(1)}, bf16[768,2048]{1,0:T(8,128)(2,1)}, u32[]{:S(2)}) copy-start(bf16[768,2048]{1,0:T(8,128)(2,1)} %all-gather.9.cloned.1.call-done) | copy-start | bytes 9437188
  335.9 49.6 %copy-start.9 = (bf16[4,1,192,1024]{3,2,1,0:T(8,128)(2,1)S(1)}, bf16[4,1,192,1024]{3,2,1,0:T(8,128)(2,1)}, u32[]{:S(2)}) copy-start(bf16[4,1,192,1024]{3,2,1,0:T(8,128)(2,1)} %copy-done.7) | copy-start | bytes 4718596
  384.0 52.9 %collective-permute-start.8 = (bf16[576,2048]{1,0:T(8,128)(2,1)S(1)}, bf16[576,2048]{1,0:T(8,128)(2,1)S(1)}, u32[]{:S(2)}, u32[]{:S(2)}) collective-permute-start(bf16[576,2048]{1,0:T(8,128)(2,1)S(1)} %fusion.6), channel_id=1, source_target_pairs={{0,1},{1,0},{2,3},{3,2},{4,5},{5,4},{6,7},{7,6},{8,9},{9,8},{10,11... | collective-permute-start | bytes 7077896 | tf_op jit(solution)/shard_map/ppermute | solution.py:30
  389.0 2.6 copy-start.6
  440.4 9.9 %collective-permute-start.9 = (f32[512,2048]{1,0:T(8,128)S(1)}, f32[512,2048]{1,0:T(8,128)}, u32[]{:S(2)}, u32[]{:S(2)}) collective-permute-start(f32[512,2048]{1,0:T(8,128)S(1)} %slice_add_fusion.5), channel_id=1, source_target_pairs={{0,8},{8,0},{1,9},{9,1},{2,10},{10,2},{3,11},{11,3},{4,12},{12,4},... | collective-permute-start | bytes 12582920 | tf_op jit(solution)/shard_map/ppermute | solution.py:30
  446.1 17.5 %collective-permute-start.10 = (f32[512,2048]{1,0:T(8,128)}, f32[512,2048]{1,0:T(8,128)}, u32[]{:S(2)}, u32[]{:S(2)}) collective-permute-start(f32[512,2048]{1,0:T(8,128)} %slice_add_fusion.4), channel_id=1, source_target_pairs={{0,8},{8,0},{1,9},{9,1},{2,10},{10,2},{3,11},{11,3},{4,12},{12,4},... | collective-permute-start | bytes 12582920 | tf_op jit(solution)/shard_map/ppermute | solution.py:30
Sparse Core Ops, SparseCore 0:
  25.0 119.0 all-gather.4
  145.6 62.0 all-gather.6
  209.2 62.1 all-gather.8
  273.7 62.1 all-gather.10

commit v7 on v6

--- a/solution.py
+++ b/solution.py
@@ -88,7 +88,7 @@
             outgoing = others(piece)
             if len(mine) == len(order):
                 x_out["v"] = x_chain(theirs)
-                outgoing = lax.optimization_barrier((outgoing, x_out["v"][4]))[0]
+                outgoing = lax.optimization_barrier((outgoing, x_out["v"][4][0]))[0]
             theirs.append(swap(outgoing, "ay"))
         s_a, s_b, early_part, sent, got_x, cuts, hw, halves = x_out["v"]
         early = list(early_part)

time: 481 us -> 485 us (level)
    ppermute x11, waiting for transfers between devices: 265 us -> 274 us  [swap(): return lax.ppermute(x, axis, [(0, 1), (1, 0)])]
  transfers between devices with their start and end apart: 16 -> 16, of which waited for: 10 -> 11; matrix products, arithmetic and copies ran while one was open for 20% -> 20% of each run, Pallas kernels for 0% -> 0%
where the time goes in v7:
time: 485 us; the launch traced here: 481 us
  waiting for transfers between devices  327 us (67%)
  matrix products  65.7 us (14%)
  other arithmetic  36.8 us (8%)
  starting transfers between devices  19.6 us (4%)
  local copies, waits for them, and re-layouts  17.2 us (4%)
  between operations  14.9 us (3%)
    ppermute x11, waiting for transfers between devices, swap(): return lax.ppermute(x, axis, [(0, 1), (1, 0)])  274 us
    dot_general x16, matrix products, contract(): lax.dot_general(left, right, (((0,), (0,)), ((), ())), preferred_element_...  65.7 us
    all_gather x3, waiting for transfers between devices, body(): lax.all_gather(lax.dynamic_slice_in_dim(rest, m * rw, rw, axis=1), 'az',...  35.7 us
    concatenate x5, other arithmetic, others(): doubled = jnp.concatenate([v, v], axis=0)  19.5 us
    all_to_all x1, waiting for transfers between devices, body(): lax.all_to_all(scale(w_own, b_rows), ('az', 'ay'), 1, 0, tiled=True)  17.8 us
    ppermute x11, starting transfers between devices, swap(): return lax.ppermute(x, axis, [(0, 1), (1, 0)])  11.8 us
  transfers between devices with their start and end apart: 16, of which 11 were waited for; matrix products, arithmetic and copies ran while one was open for 20% of the time, Pallas kernels for 0%

profile of v7, /device:TPU:0, one launch (start us, length us, event | category | flops | bytes accessed | tf_op | source)
XLA Modules:
  0.0 481.4 jit_solution(3197266683464338990)
XLA Ops:
  8.5 1.0 select_reduce_fusion
  10.4 2.6 multiply_convert_fusion
  13.0 2.1 copy.12
  15.1 7.5 %all-to-all-start = ((bf16[192,8,1024]{2,0,1:T(8,128)(2,1)}), bf16[192,8,1024]{2,0,1:T(8,128)(2,1)}, u32[]{:S(2)}, u32[]{:S(2)}) async-start(bf16[192,8,1024]{2,0,1:T(8,128)(2,1)} %bitcast.27), calls=%async_computation | async-start | bytes 6291456 | tf_op jit(solution)/shard_map/all_to_all | solution.py:57
  23.7 2.0 collective-permute-start
  25.7 100.5 %collective-permute-done = bf16[192,8192]{1,0:T(8,128)(2,1)} collective-permute-done((bf16[192,8192]{1,0:T(8,128)(2,1)S(1)}, bf16[192,8192]{1,0:T(8,128)(2,1)}, u32[]{:S(2)}, u32[]{:S(2)}) %collective-permute-start) | collective-permute-done | bytes 3145760 | tf_op jit(solution)/shard_map/ppermute | solution.py:30
  126.2 17.8 %all-to-all-done = bf16[192,8,1024]{2,0,1:T(8,128)(2,1)} async-done(((bf16[192,8,1024]{2,0,1:T(8,128)(2,1)}), bf16[192,8,1024]{2,0,1:T(8,128)(2,1)}, u32[]{:S(2)}, u32[]{:S(2)}) %all-to-all-start) | async-done | bytes 3145760 | tf_op jit(solution)/shard_map/all_to_all | solution.py:57
  145.1 5.0 %fusion.8 = bf16[576,2048]{1,0:T(8,128)(2,1)} fusion(s32[]{:T(128)S(6)} %select_n.66, bf16[768,2048]{1,0:T(8,128)(2,1)} %all-gather.5.cloned.1.call-done), kind=kLoop, calls=%fused_computation.32 | loop fusion | flops 4718592 | bytes 5505028 | tf_op jit(solution)/shard_map/concatenate | solution.py:50
  150.1 1.4 collective-permute-start.2
  151.5 52.1 %collective-permute-done.2 = bf16[576,2048]{1,0:T(8,128)(2,1)} collective-permute-done((bf16[576,2048]{1,0:T(8,128)(2,1)}, bf16[576,2048]{1,0:T(8,128)(2,1)}, u32[]{:S(2)}, u32[]{:S(2)}) %collective-permute-start.2) | collective-permute-done | bytes 2359328 | tf_op jit(solution)/shard_map/ppermute | solution.py:30
  203.6 4.0 all-gather.7.cloned.1.call-done
  207.7 1.0 constant_dynamic-slice_fusion.1
  208.9 5.0 %fusion.9 = bf16[576,2048]{1,0:T(8,128)(2,1)} fusion(s32[]{:T(128)S(6)} %select_n.66, bf16[768,2048]{1,0:T(8,128)(2,1)} %all-gather.7.cloned.1.call-done), kind=kLoop, calls=%fused_computation.33 | loop fusion | flops 4718592 | bytes 5505028 | tf_op jit(solution)/shard_map/concatenate | solution.py:50
  213.9 1.5 collective-permute-start.1
  215.4 2.6 constant_dynamic-slice_fusion.5
  218.0 1.5 fusion.10
  219.5 3.6 fusion.40
  223.0 5.9 %convolution_add_fusion.2 = f32[1024,2048]{1,0:T(8,128)} fusion(f32[1024,2048]{1,0:T(8,128)S(1)} %fusion.40, bf16[192,8192]{1,0:T(8,128)(2,1)} %collective-permute-done, s32[]{:T(128)S(6)} %select_n.65, bf16[768,1024]{1,0:T(8,128)(2,1)S(1)} %bitcast.29, s32[]{:T(128)S(6)} %select_n.62), kind=kOutput, calls=%fused_computation.11 | convolution fusion | flops 807403520 | bytes 17956872 | tf_op jit(solution)/shard_map/dot_general | solution.py:24
  228.9 38.3 %collective-permute-done.1 = bf16[576,2048]{1,0:T(8,128)(2,1)} collective-permute-done((bf16[576,2048]{1,0:T(8,128)(2,1)}, bf16[576,2048]{1,0:T(8,128)(2,1)}, u32[]{:S(2)}, u32[]{:S(2)}) %collective-permute-start.1) | collective-permute-done | bytes 2359328 | tf_op jit(solution)/shard_map/ppermute | solution.py:30
  267.2 4.2 all-gather.9.cloned.1.call-done
  271.4 2.1 constant_dynamic-slice_fusion
  273.6 4.7 fusion.3
  278.4 5.3 %fusion = bf16[512,2048]{1,0:T(8,128)(2,1)S(1)} fusion(f32[1024,2048]{1,0:T(8,128)} %convolution_add_fusion.2, bf16[576,2048]{1,0:T(8,128)(2,1)} %collective-permute-done.2, bf16[576,1024]{1,0:T(8,128)(2,1)S(1)} %fusion.10), kind=kOutput, calls=%fused_computation.14 | convolution fusion | flops 1210056704 | bytes 9240576 | tf_op jit(solution)/shard_map/dot_general | solution.py:24
  283.7 1.1 collective-permute-start.4
  284.9 4.0 fusion.39
  288.8 2.5 convolution_add_fusion.3
  291.3 5.1 %fusion.5 = bf16[512,2048]{1,0:T(8,128)(2,1)} fusion(f32[1024,2048]{1,0:T(8,128)S(1)} %convolution_add_fusion.3, bf16[512,2048]{1,0:T(8,128)(2,1)S(1)} %collective-permute-done.3, bf16[576,2048]{1,0:T(8,128)(2,1)} %collective-permute-done.1, bf16[576,1024]{1,0:T(8,128)(2,1)S(1)} %fusion.10), kind=kOutput, calls=%fused_computation.22 | convolution fusion | flops 1212153856 | bytes 11337728 | tf_op jit(solution)/shard_map/dot_general | solution.py:24
  296.4 1.4 collective-permute-start.6
  297.8 5.1 %fusion.2 = bf16[512,2048]{1,0:T(8,128)(2,1)} fusion(f32[1024,2048]{1,0:T(8,128)S(1)} %convolution_add_fusion.3, bf16[512,2048]{1,0:T(8,128)(2,1)S(1)} %collective-permute-done.4, bf16[576,2048]{1,0:T(8,128)(2,1)} %collective-permute-done.1, bf16[576,1024]{1,0:T(8,128)(2,1)S(1)} %fusion.10), kind=kOutput, calls=%fused_computation.17 | convolution fusion | flops 1212153856 | bytes 11337728 | tf_op jit(solution)/shard_map/dot_general | solution.py:24
  302.9 4.0 fusion.7
  306.9 1.5 collective-permute-start.5
  308.4 27.4 %all-gather.11.cloned.1.call-done = bf16[768,2048]{1,0:T(8,128)(2,1)} async-done(((bf16[192,2048]{1,0:T(8,128)(2,1)}), bf16[768,2048]{1,0:T(8,128)(2,1)}) %all-gather.11.cloned.1.call-update) | async-done | bytes 3145744 | tf_op jit(solution)/shard_map/all_gather | solution.py:86
  335.9 3.9 fusion.6
  339.8 4.5 collective-permute-done.6
  344.3 1.4 collective-permute-start.7
  345.7 3.5 fusion.41
  349.2 2.6 convolution_add_fusion.1
  351.9 5.7 %fusion.42 = f32[1024,2048]{1,0:T(8,128)} fusion(bf16[768,1024]{1,0:T(8,128)(2,1)S(1)} %bitcast.37, bf16[768,2048]{1,0:T(8,128)(2,1)S(1)} %copy-done.5), kind=kOutput, calls=%fused_computation.76 | convolution fusion | flops 3221225472 | bytes 13107200 | tf_op jit(solution)/shard_map/dot_general | solution.py:24
  357.6 4.9 %convolution_add_fusion = f32[1024,2048]{1,0:T(8,128)S(1)} fusion(f32[1024,2048]{1,0:T(8,128)} %fusion.42, bf16[192,8192]{1,0:T(8,128)(2,1)} %collective-permute-done, s32[]{:T(128)S(6)} %select_n.68, bf16[768,1024]{1,0:T(8,128)(2,1)S(1)} %bitcast.32, s32[]{:T(128)S(6)} %select_n.62), kind=kOutput, calls=%fused_computation.9 | convolution fusion | flops 807403520 | bytes 17956872 | tf_op jit(solution)/shard_map/dot_general | solution.py:24
  362.6 48.0 %collective-permute-done.7 = bf16[576,2048]{1,0:T(8,128)(2,1)S(1)} collective-permute-done((bf16[576,2048]{1,0:T(8,128)(2,1)S(1)}, bf16[576,2048]{1,0:T(8,128)(2,1)S(1)}, u32[]{:S(2)}, u32[]{:S(2)}) %collective-permute-start.7) | collective-permute-done | bytes 2359328 | tf_op jit(solution)/shard_map/ppermute | solution.py:30
  410.6 3.5 slice_add_fusion.5
  414.2 5.6 %slice_add_fusion.4 = f32[512,2048]{1,0:T(8,128)} fusion(f32[1024,2048]{1,0:T(8,128)S(1)} %convolution_add_fusion.1, bf16[576,2048]{1,0:T(8,128)(2,1)} %collective-permute-done.5, bf16[576,1024]{1,0:T(8,128)(2,1)S(1)} %fusion.10), kind=kOutput, calls=%fused_computation.24 | convolution fusion | flops 1209008128 | bytes 11337728 | tf_op jit(solution)/shard_map/dot_general | solution.py:24
  421.1 1.9 fusion.25
  423.0 1.8 fusion.17
  424.8 6.4 %convert_add_fusion = f32[512,2048]{1,0:T(8,128)} fusion(bf16[512,2048]{1,0:T(8,128)(2,1)} %collective-permute-done.6, f32[512,2048]{1,0:T(8,128)} %collective-permute-done.8, f32[512,2048]{1,0:T(8,128)S(1)} %fusion.25, f32[1024,2048]{1,0:T(8,128)S(1)} %convolution_add_fusion), kind=kLoop, calls=%fused_computation.25 | loop fusion | flops 4194304 | bytes 18874368 | tf_op jit(solution)/shard_map/add | solution.py:103
  431.3 6.8 %dynamic_update_slice.6 = f32[1024,2048]{1,0:T(8,128)} pad(f32[512,2048]{1,0:T(8,128)} %convert_add_fusion, f32[]{:T(128)} %constant.50.clone.1), padding=0_512x0_0 | pad | bytes 12582916 | tf_op jit(solution)/shard_map/dynamic_update_slice | solution.py:103
  438.1 30.1 %collective-permute-done.10 = bf16[512,2048]{1,0:T(8,128)(2,1)} collective-permute-done((bf16[512,2048]{1,0:T(8,128)(2,1)}, bf16[512,2048]{1,0:T(8,128)(2,1)}, u32[]{:S(2)}, u32[]{:S(2)}) %collective-permute-start.10) | collective-permute-done | bytes 2097184 | tf_op jit(solution)/shard_map/ppermute | solution.py:30
  468.1 6.5 %add_dynamic-update-slice_fusion = f32[1024,2048]{1,0:T(8,128)} fusion(f32[1024,2048]{1,0:T(8,128)} %dynamic_update_slice.6, bf16[512,2048]{1,0:T(8,128)(2,1)} %collective-permute-done.10, f32[512,2048]{1,0:T(8,128)} %collective-permute-done.9, f32[512,2048]{1,0:T(8,128)S(1)} %fusion.17, f32[1024,2048]{1,0:T(8,128)S(1)} %convolution_add_fusion), kind=kLoop, calls=%fused_computation.23 | loop fusion | flops 4194304 | bytes 18874368 | tf_op jit(solution)/shard_map/dynamic_update_slice | solution.py:103
  (42 shorter events, 5.4 us)
Async XLA Ops:
  15.1 7.6 %copy-start = (bf16[192,8192]{1,0:T(8,128)(2,1)S(1)}, bf16[192,8192]{1,0:T(8,128)(2,1)}, u32[]{:S(2)}) copy-start(bf16[192,8192]{1,0:T(8,128)(2,1)} %param.6) | copy-start | bytes 9437188
  15.1 128.9 %all-to-all-start = ((bf16[192,8,1024]{2,0,1:T(8,128)(2,1)}), bf16[192,8,1024]{2,0,1:T(8,128)(2,1)}, u32[]{:S(2)}, u32[]{:S(2)}) async-start(bf16[192,8,1024]{2,0,1:T(8,128)(2,1)} %bitcast.27), calls=%async_computation | async-start | bytes 6291456 | tf_op jit(solution)/shard_map/all_to_all | solution.py:57
  22.6 121.5 %all-gather.5.cloned.1.call-start = ((), (), s32[]{:S(2)}) async-start(), calls=%async_computation.1 | async-start | bytes 3932160 | tf_op jit(solution)/shard_map/all_gather | solution.py:54
  23.6 184.0 %all-gather.7.cloned.1.call-start = ((), (), s32[]{:S(2)}) async-start(), calls=%async_computation.2 | async-start | bytes 3932160 | tf_op jit(solution)/shard_map/all_gather | solution.py:86
  23.7 102.5 %collective-permute-start = (bf16[192,8192]{1,0:T(8,128)(2,1)S(1)}, bf16[192,8192]{1,0:T(8,128)(2,1)}, u32[]{:S(2)}, u32[]{:S(2)}) collective-permute-start(bf16[192,8192]{1,0:T(8,128)(2,1)S(1)} %copy-done), channel_id=1, source_target_pairs={{0,1},{1,0},{2,3},{3,2},{4,5},{5,4},{6,7},{7,6},{8,9},{9,8},{10,11... | collective-permute-start | bytes 9437192 | tf_op jit(solution)/shard_map/ppermute | solution.py:30
  145.0 126.4 %all-gather.9.cloned.1.call-start = ((), (), s32[]{:S(2)}) async-start(), calls=%async_computation.3 | async-start | bytes 3932160 | tf_op jit(solution)/shard_map/all_gather | solution.py:86
  150.1 53.5 %collective-permute-start.2 = (bf16[576,2048]{1,0:T(8,128)(2,1)}, bf16[576,2048]{1,0:T(8,128)(2,1)}, u32[]{:S(2)}, u32[]{:S(2)}) collective-permute-start(bf16[576,2048]{1,0:T(8,128)(2,1)} %fusion.8), channel_id=1, source_target_pairs={{0,1},{1,0},{2,3},{3,2},{4,5},{5,4},{6,7},{7,6},{8,9},{9,8},{10,11... | collective-permute-start | bytes 7077896 | tf_op jit(solution)/shard_map/ppermute | solution.py:30
  208.6 127.2 %all-gather.11.cloned.1.call-start = ((), (), s32[]{:S(2)}) async-start(), calls=%async_computation.4 | async-start | bytes 3932160 | tf_op jit(solution)/shard_map/all_gather | solution.py:86
  213.9 53.3 %collective-permute-start.1 = (bf16[576,2048]{1,0:T(8,128)(2,1)}, bf16[576,2048]{1,0:T(8,128)(2,1)}, u32[]{:S(2)}, u32[]{:S(2)}) collective-permute-start(bf16[576,2048]{1,0:T(8,128)(2,1)} %fusion.9), channel_id=1, source_target_pairs={{0,1},{1,0},{2,3},{3,2},{4,5},{5,4},{6,7},{7,6},{8,9},{9,8},{10,11... | collective-permute-start | bytes 7077896 | tf_op jit(solution)/shard_map/ppermute | solution.py:30
  215.4 4.1 copy-start.1
  217.9 1.5 copy-start.6
  278.3 6.6 %copy-start.2 = (bf16[768,2048]{1,0:T(8,128)(2,1)S(1)}, bf16[768,2048]{1,0:T(8,128)(2,1)}, u32[]{:S(2)}) copy-start(bf16[768,2048]{1,0:T(8,128)(2,1)} %all-gather.7.cloned.1.call-done) | copy-start | bytes 9437188
  278.3 6.6 %copy-start.7 = (bf16[4,1,192,1024]{3,2,1,0:T(8,128)(2,1)S(1)}, bf16[4,1,192,1024]{3,2,1,0:T(8,128)(2,1)}, u32[]{:S(2)}) copy-start(bf16[4,1,192,1024]{3,2,1,0:T(8,128)(2,1)} %copy-done.6) | copy-start | bytes 4718596
  278.3 13.0 %collective-permute-start.3 = (bf16[512,2048]{1,0:T(8,128)(2,1)S(1)}, bf16[512,2048]{1,0:T(8,128)(2,1)S(1)}, u32[]{:S(2)}, u32[]{:S(2)}) collective-permute-start(bf16[512,2048]{1,0:T(8,128)(2,1)S(1)} %fusion.3), channel_id=1, source_target_pairs={{0,8},{8,0},{1,9},{9,1},{2,10},{10,2},{3,11},{11,3},{4,12},{12,4},... | collective-permute-start | bytes 6291464 | tf_op jit(solution)/shard_map/ppermute | solution.py:30
  283.7 14.1 %collective-permute-start.4 = (bf16[512,2048]{1,0:T(8,128)(2,1)S(1)}, bf16[512,2048]{1,0:T(8,128)(2,1)S(1)}, u32[]{:S(2)}, u32[]{:S(2)}) collective-permute-start(bf16[512,2048]{1,0:T(8,128)(2,1)S(1)} %fusion), channel_id=1, source_target_pairs={{0,8},{8,0},{1,9},{9,1},{2,10},{10,2},{3,11},{11,3},{4,12},{12,4},... | collective-permute-start | bytes 6291464 | tf_op jit(solution)/shard_map/ppermute | solution.py:30
  296.4 6.5 %copy-start.3 = (bf16[768,2048]{1,0:T(8,128)(2,1)S(1)}, bf16[768,2048]{1,0:T(8,128)(2,1)}, u32[]{:S(2)}) copy-start(bf16[768,2048]{1,0:T(8,128)(2,1)} %all-gather.9.cloned.1.call-done) | copy-start | bytes 9437188
  296.4 47.9 %collective-permute-start.6 = (bf16[512,2048]{1,0:T(8,128)(2,1)}, bf16[512,2048]{1,0:T(8,128)(2,1)}, u32[]{:S(2)}, u32[]{:S(2)}) collective-permute-start(bf16[512,2048]{1,0:T(8,128)(2,1)} %fusion.5), channel_id=1, source_target_pairs={{0,16},{16,0},{1,17},{17,1},{2,18},{18,2},{3,19},{19,3},{4,20},{20... | collective-permute-start | bytes 6291464 | tf_op jit(solution)/shard_map/ppermute | solution.py:30
  306.9 55.6 %collective-permute-start.5 = (bf16[576,2048]{1,0:T(8,128)(2,1)}, bf16[576,2048]{1,0:T(8,128)(2,1)}, u32[]{:S(2)}, u32[]{:S(2)}) collective-permute-start(bf16[576,2048]{1,0:T(8,128)(2,1)} %fusion.7), channel_id=1, source_target_pairs={{0,1},{1,0},{2,3},{3,2},{4,5},{5,4},{6,7},{7,6},{8,9},{9,8},{10,11... | collective-permute-start | bytes 7077896 | tf_op jit(solution)/shard_map/ppermute | solution.py:30
  335.9 9.8 %copy-start.4 = (bf16[768,2048]{1,0:T(8,128)(2,1)S(1)}, bf16[768,2048]{1,0:T(8,128)(2,1)}, u32[]{:S(2)}) copy-start(bf16[768,2048]{1,0:T(8,128)(2,1)} %all-gather.9.cloned.1.call-done) | copy-start | bytes 9437188
  335.9 9.8 %copy-start.8 = (bf16[4,1,192,1024]{3,2,1,0:T(8,128)(2,1)S(1)}, bf16[4,1,192,1024]{3,2,1,0:T(8,128)(2,1)}, u32[]{:S(2)}) copy-start(bf16[4,1,192,1024]{3,2,1,0:T(8,128)(2,1)} %copy-done.6) | copy-start | bytes 4718596
  344.3 66.3 %collective-permute-start.7 = (bf16[576,2048]{1,0:T(8,128)(2,1)S(1)}, bf16[576,2048]{1,0:T(8,128)(2,1)S(1)}, u32[]{:S(2)}, u32[]{:S(2)}) collective-permute-start(bf16[576,2048]{1,0:T(8,128)(2,1)S(1)} %fusion.6), channel_id=1, source_target_pairs={{0,1},{1,0},{2,3},{3,2},{4,5},{5,4},{6,7},{7,6},{8,9},{9,8},{10,11... | collective-permute-start | bytes 7077896 | tf_op jit(solution)/shard_map/ppermute | solution.py:30
  349.2 2.6 copy-start.5
  414.1 10.7 %collective-permute-start.8 = (f32[512,2048]{1,0:T(8,128)S(1)}, f32[512,2048]{1,0:T(8,128)}, u32[]{:S(2)}, u32[]{:S(2)}) collective-permute-start(f32[512,2048]{1,0:T(8,128)S(1)} %slice_add_fusion.5), channel_id=1, source_target_pairs={{0,8},{8,0},{1,9},{9,1},{2,10},{10,2},{3,11},{11,3},{4,12},{12,4},... | collective-permute-start | bytes 12582920 | tf_op jit(solution)/shard_map/ppermute | solution.py:30
  419.8 48.4 %collective-permute-start.9 = (f32[512,2048]{1,0:T(8,128)}, f32[512,2048]{1,0:T(8,128)}, u32[]{:S(2)}, u32[]{:S(2)}) collective-permute-start(f32[512,2048]{1,0:T(8,128)} %slice_add_fusion.4), channel_id=1, source_target_pairs={{0,8},{8,0},{1,9},{9,1},{2,10},{10,2},{3,11},{11,3},{4,12},{12,4},... | collective-permute-start | bytes 12582920 | tf_op jit(solution)/shard_map/ppermute | solution.py:30
  420.3 47.9 %collective-permute-start.10 = (bf16[512,2048]{1,0:T(8,128)(2,1)}, bf16[512,2048]{1,0:T(8,128)(2,1)}, u32[]{:S(2)}, u32[]{:S(2)}) collective-permute-start(bf16[512,2048]{1,0:T(8,128)(2,1)} %fusion.2), channel_id=1, source_target_pairs={{0,16},{16,0},{1,17},{17,1},{2,18},{18,2},{3,19},{19,3},{4,20},{20... | collective-permute-start | bytes 6291464 | tf_op jit(solution)/shard_map/ppermute | solution.py:30
Sparse Core Ops, SparseCore 0:
  25.0 119.0 all-gather.4
  145.6 61.9 all-gather.6
  209.2 62.1 all-gather.8
  273.7 62.1 all-gather.10

commit v8 on v6

--- a/solution.py
+++ b/solution.py
@@ -86,6 +86,13 @@
             piece = lax.all_gather(lax.dynamic_slice_in_dim(rest, m * rw, rw, axis=1), "az", axis=0, tiled=True)
             mine.append(piece)
             outgoing = others(piece)
+            if len(mine) == len(order) and outgoing.shape[0] % 16 == 0:
+                x_out["v"] = x_chain(theirs)
+                split_at = outgoing.shape[0] // 2
+                head = swap(outgoing[:split_at], "ay")
+                tail = lax.optimization_barrier((outgoing[split_at:], x_out["v"][4]))[0]
+                theirs.append(jnp.concatenate([head, swap(tail, "ay")], axis=0))
+                continue
             if len(mine) == len(order):
                 x_out["v"] = x_chain(theirs)
                 outgoing = lax.optimization_barrier((outgoing, x_out["v"][4]))[0]

time: 481 us -> 481 us (level)
    ppermute x11 -> x12, waiting for transfers between devices: 265 us -> 275 us  [swap(): return lax.ppermute(x, axis, [(0, 1), (1, 0)])]
    all_gather x3, waiting for transfers between devices: 40.5 us -> 30.8 us  [body(): lax.all_gather(lax.dynamic_slice_in_dim(rest, m * rw, rw, axis=1), 'az',...]
    ppermute x11 -> x12, starting transfers between devices: 10.8 us -> 11.4 us  [swap(): return lax.ppermute(x, axis, [(0, 1), (1, 0)])]
  transfers between devices with their start and end apart: 16 -> 17, of which waited for: 10 -> 11; matrix products, arithmetic and copies ran while one was open for 20% -> 20% of each run, Pallas kernels for 0% -> 0%
where the time goes in v8:
time: 481 us; the launch traced here: 477 us
  waiting for transfers between devices  323 us (67%)
  matrix products  61.7 us (13%)
  other arithmetic  36.6 us (8%)
  local copies, waits for them, and re-layouts  20.8 us (4%)
  starting transfers between devices  19.5 us (4%)
  between operations  15.2 us (3%)
    ppermute x12, waiting for transfers between devices, swap(): return lax.ppermute(x, axis, [(0, 1), (1, 0)])  275 us
    dot_general x16, matrix products, contract(): lax.dot_general(left, right, (((0,), (0,)), ((), ())), preferred_element_...  61.7 us
    all_gather x3, waiting for transfers between devices, body(): lax.all_gather(lax.dynamic_slice_in_dim(rest, m * rw, rw, axis=1), 'az',...  30.8 us
    concatenate x5, other arithmetic, others(): doubled = jnp.concatenate([v, v], axis=0)  19.2 us
    all_to_all x1, waiting for transfers between devices, body(): lax.all_to_all(scale(w_own, b_rows), ('az', 'ay'), 1, 0, tiled=True)  17.8 us
    ppermute x12, starting transfers between devices, swap(): return lax.ppermute(x, axis, [(0, 1), (1, 0)])  11.4 us
  transfers between devices with their start and end apart: 17, of which 11 were waited for; matrix products, arithmetic and copies ran while one was open for 20% of the time, Pallas kernels for 0%

profile of v8, /device:TPU:0, one launch (start us, length us, event | category | flops | bytes accessed | tf_op | source)
XLA Modules:
  0.0 477.3 jit_solution(1736537453004574036)
XLA Ops:
  8.5 1.0 select_reduce_fusion
  10.4 2.6 multiply_convert_fusion
  13.0 2.1 copy.12
  15.1 7.5 %all-to-all-start = ((bf16[192,8,1024]{2,0,1:T(8,128)(2,1)}), bf16[192,8,1024]{2,0,1:T(8,128)(2,1)}, u32[]{:S(2)}, u32[]{:S(2)}) async-start(bf16[192,8,1024]{2,0,1:T(8,128)(2,1)} %bitcast.27), calls=%async_computation | async-start | bytes 6291456 | tf_op jit(solution)/shard_map/all_to_all | solution.py:57
  23.7 2.0 collective-permute-start
  25.7 100.5 %collective-permute-done = bf16[192,8192]{1,0:T(8,128)(2,1)} collective-permute-done((bf16[192,8192]{1,0:T(8,128)(2,1)S(1)}, bf16[192,8192]{1,0:T(8,128)(2,1)}, u32[]{:S(2)}, u32[]{:S(2)}) %collective-permute-start) | collective-permute-done | bytes 3145760 | tf_op jit(solution)/shard_map/ppermute | solution.py:30
  126.2 17.8 %all-to-all-done = bf16[192,8,1024]{2,0,1:T(8,128)(2,1)} async-done(((bf16[192,8,1024]{2,0,1:T(8,128)(2,1)}), bf16[192,8,1024]{2,0,1:T(8,128)(2,1)}, u32[]{:S(2)}, u32[]{:S(2)}) %all-to-all-start) | async-done | bytes 3145760 | tf_op jit(solution)/shard_map/all_to_all | solution.py:57
  145.1 5.0 %fusion.8 = bf16[576,2048]{1,0:T(8,128)(2,1)} fusion(s32[]{:T(128)S(6)} %select_n.66, bf16[768,2048]{1,0:T(8,128)(2,1)} %all-gather.5.cloned.1.call-done), kind=kLoop, calls=%fused_computation.32 | loop fusion | flops 4718592 | bytes 5505028 | tf_op jit(solution)/shard_map/concatenate | solution.py:50
  150.1 1.4 collective-permute-start.2
  151.5 52.1 %collective-permute-done.2 = bf16[576,2048]{1,0:T(8,128)(2,1)} collective-permute-done((bf16[576,2048]{1,0:T(8,128)(2,1)}, bf16[576,2048]{1,0:T(8,128)(2,1)}, u32[]{:S(2)}, u32[]{:S(2)}) %collective-permute-start.2) | collective-permute-done | bytes 2359328 | tf_op jit(solution)/shard_map/ppermute | solution.py:30
  203.6 4.0 all-gather.7.cloned.1.call-done
  207.7 0.9 constant_dynamic-slice_fusion.1
  209.2 5.0 %fusion.9 = bf16[576,2048]{1,0:T(8,128)(2,1)} fusion(s32[]{:T(128)S(6)} %select_n.66, bf16[768,2048]{1,0:T(8,128)(2,1)} %all-gather.7.cloned.1.call-done), kind=kLoop, calls=%fused_computation.33 | loop fusion | flops 4718592 | bytes 5505028 | tf_op jit(solution)/shard_map/concatenate | solution.py:50
  214.2 1.5 collective-permute-start.1
  215.7 2.6 constant_dynamic-slice_fusion.5
  218.3 1.5 fusion.10
  219.8 3.6 fusion.41
  223.3 2.5 convolution_add_fusion.2
  225.8 3.4 copy-done.1
  229.2 4.9 %fusion.3 = bf16[512,2048]{1,0:T(8,128)(2,1)} fusion(f32[1024,2048]{1,0:T(8,128)S(1)} %convolution_add_fusion.2, bf16[576,2048]{1,0:T(8,128)(2,1)} %collective-permute-done.2, bf16[576,1024]{1,0:T(8,128)(2,1)S(1)} %fusion.10), kind=kOutput, calls=%fused_computation.19 | convolution fusion | flops 1210056704 | bytes 9240576 | tf_op jit(solution)/shard_map/dot_general | solution.py:24
  234.1 33.3 %collective-permute-done.1 = bf16[576,2048]{1,0:T(8,128)(2,1)} collective-permute-done((bf16[576,2048]{1,0:T(8,128)(2,1)}, bf16[576,2048]{1,0:T(8,128)(2,1)}, u32[]{:S(2)}, u32[]{:S(2)}) %collective-permute-start.1) | collective-permute-done | bytes 2359328 | tf_op jit(solution)/shard_map/ppermute | solution.py:30
  267.5 4.0 all-gather.9.cloned.1.call-done
  271.4 2.1 constant_dynamic-slice_fusion
  273.6 4.9 %fusion = bf16[512,2048]{1,0:T(8,128)(2,1)S(1)} fusion(f32[1024,2048]{1,0:T(8,128)} %copy-done.1, bf16[576,2048]{1,0:T(8,128)(2,1)} %collective-permute-done.2, bf16[576,1024]{1,0:T(8,128)(2,1)S(1)} %fusion.10), kind=kOutput, calls=%fused_computation.14 | convolution fusion | flops 1210056704 | bytes 9240576 | tf_op jit(solution)/shard_map/dot_general | solution.py:24
  278.6 3.7 fusion.40
  282.3 2.4 convolution_add_fusion.3
  284.8 5.7 %fusion.5 = bf16[512,2048]{1,0:T(8,128)(2,1)} fusion(f32[1024,2048]{1,0:T(8,128)S(1)} %convolution_add_fusion.3, bf16[512,2048]{1,0:T(8,128)(2,1)} %collective-permute-done.3, bf16[576,2048]{1,0:T(8,128)(2,1)} %collective-permute-done.1, bf16[576,1024]{1,0:T(8,128)(2,1)S(1)} %fusion.10), kind=kOutput, calls=%fused_computation.22 | convolution fusion | flops 1212153856 | bytes 11337728 | tf_op jit(solution)/shard_map/dot_general | solution.py:24
  290.5 1.5 collective-permute-start.7
  291.9 5.1 %fusion.2 = bf16[512,2048]{1,0:T(8,128)(2,1)} fusion(f32[1024,2048]{1,0:T(8,128)S(1)} %convolution_add_fusion.3, bf16[512,2048]{1,0:T(8,128)(2,1)S(1)} %collective-permute-done.4, bf16[576,2048]{1,0:T(8,128)(2,1)} %collective-permute-done.1, bf16[576,1024]{1,0:T(8,128)(2,1)S(1)} %fusion.10), kind=kOutput, calls=%fused_computation.17 | convolution fusion | flops 1212153856 | bytes 11337728 | tf_op jit(solution)/shard_map/dot_general | solution.py:24
  297.9 4.0 fusion.7
  301.9 1.5 collective-permute-start.5
  303.4 3.7 fusion.42
  307.2 5.9 %convolution_add_fusion.1 = f32[1024,2048]{1,0:T(8,128)} fusion(f32[1024,2048]{1,0:T(8,128)S(1)} %fusion.42, bf16[192,8192]{1,0:T(8,128)(2,1)} %collective-permute-done, s32[]{:T(128)S(6)} %select_n.67, bf16[768,1024]{1,0:T(8,128)(2,1)S(1)} %bitcast.33, s32[]{:T(128)S(6)} %select_n.62), kind=kOutput, calls=%fused_computation.10 | convolution fusion | flops 807403520 | bytes 17956872 | tf_op jit(solution)/shard_map/dot_general | solution.py:24
  313.0 22.8 %all-gather.11.cloned.1.call-done = bf16[768,2048]{1,0:T(8,128)(2,1)} async-done(((bf16[192,2048]{1,0:T(8,128)(2,1)}), bf16[768,2048]{1,0:T(8,128)(2,1)}) %all-gather.11.cloned.1.call-update) | async-done | bytes 3145744 | tf_op jit(solution)/shard_map/all_gather | solution.py:86
  335.9 3.6 fusion.6
  339.7 44.1 %collective-permute-done.8 = bf16[512,2048]{1,0:T(8,128)(2,1)} collective-permute-done((bf16[512,2048]{1,0:T(8,128)(2,1)}, bf16[512,2048]{1,0:T(8,128)(2,1)}, u32[]{:S(2)}, u32[]{:S(2)}) %collective-permute-start.8) | collective-permute-done | bytes 2097184 | tf_op jit(solution)/shard_map/ppermute | solution.py:30
  383.8 1.5 collective-permute-start.9
  385.8 3.6 fusion.43
  389.4 2.6 convolution_add_fusion
  392.0 20.6 %collective-permute-done.9 = bf16[288,2048]{1,0:T(8,128)(2,1)S(1)} collective-permute-done((bf16[288,2048]{1,0:T(8,128)(2,1)S(1)}, bf16[288,2048]{1,0:T(8,128)(2,1)S(1)}, u32[]{:S(2)}, u32[]{:S(2)}) %collective-permute-start.9) | collective-permute-done | bytes 1179680 | tf_op jit(solution)/shard_map/ppermute | solution.py:30
  412.6 24.0 %collective-permute-done.6 = bf16[288,2048]{1,0:T(8,128)(2,1)S(1)} collective-permute-done((bf16[288,2048]{1,0:T(8,128)(2,1)S(1)}, bf16[288,2048]{1,0:T(8,128)(2,1)S(1)}, u32[]{:S(2)}, u32[]{:S(2)}) %collective-permute-start.6) | collective-permute-done | bytes 1179680 | tf_op jit(solution)/shard_map/ppermute | solution.py:30
  436.9 3.6 slice_add_fusion.5
  440.5 5.9 %slice_add_fusion.4 = f32[512,2048]{1,0:T(8,128)} fusion(f32[1024,2048]{1,0:T(8,128)S(1)} %bitcast.29, bf16[576,2048]{1,0:T(8,128)(2,1)} %collective-permute-done.5, bf16[576,1024]{1,0:T(8,128)(2,1)S(1)} %fusion.10), kind=kOutput, calls=%fused_computation.24 | convolution fusion | flops 1209008128 | bytes 11337728 | tf_op jit(solution)/shard_map/dot_general | solution.py:24
  446.9 1.8 fusion.25
  448.7 1.8 fusion.17
  450.6 6.4 %convert_add_fusion = f32[512,2048]{1,0:T(8,128)} fusion(bf16[512,2048]{1,0:T(8,128)(2,1)} %collective-permute-done.7, f32[512,2048]{1,0:T(8,128)} %collective-permute-done.10, f32[512,2048]{1,0:T(8,128)S(1)} %fusion.25, f32[1024,2048]{1,0:T(8,128)S(1)} %convolution_add_fusion), kind=kLoop, calls=%fused_computation.25 | loop fusion | flops 4194304 | bytes 18874368 | tf_op jit(solution)/shard_map/add | solution.py:110
  457.0 6.8 %dynamic_update_slice.6 = f32[1024,2048]{1,0:T(8,128)} pad(f32[512,2048]{1,0:T(8,128)} %convert_add_fusion, f32[]{:T(128)} %constant.50.clone.1), padding=0_512x0_0 | pad | bytes 12582916 | tf_op jit(solution)/shard_map/dynamic_update_slice | solution.py:110
  463.8 6.5 %add_dynamic-update-slice_fusion = f32[1024,2048]{1,0:T(8,128)} fusion(f32[1024,2048]{1,0:T(8,128)} %dynamic_update_slice.6, bf16[512,2048]{1,0:T(8,128)(2,1)} %collective-permute-done.8, f32[512,2048]{1,0:T(8,128)} %collective-permute-done.11, f32[512,2048]{1,0:T(8,128)S(1)} %fusion.17, f32[1024,2048]{1,0:T(8,128)S(1)} %convolution_add_fusion), kind=kLoop, calls=%fused_computation.23 | loop fusion | flops 4194304 | bytes 18874368 | tf_op jit(solution)/shard_map/dynamic_update_slice | solution.py:110
  (51 shorter events, 6.6 us)
Async XLA Ops:
  15.1 7.6 %copy-start = (bf16[192,8192]{1,0:T(8,128)(2,1)S(1)}, bf16[192,8192]{1,0:T(8,128)(2,1)}, u32[]{:S(2)}) copy-start(bf16[192,8192]{1,0:T(8,128)(2,1)} %param.6) | copy-start | bytes 9437188
  15.1 128.9 %all-to-all-start = ((bf16[192,8,1024]{2,0,1:T(8,128)(2,1)}), bf16[192,8,1024]{2,0,1:T(8,128)(2,1)}, u32[]{:S(2)}, u32[]{:S(2)}) async-start(bf16[192,8,1024]{2,0,1:T(8,128)(2,1)} %bitcast.27), calls=%async_computation | async-start | bytes 6291456 | tf_op jit(solution)/shard_map/all_to_all | solution.py:57
  22.6 121.5 %all-gather.5.cloned.1.call-start = ((), (), s32[]{:S(2)}) async-start(), calls=%async_computation.1 | async-start | bytes 3932160 | tf_op jit(solution)/shard_map/all_gather | solution.py:54
  23.6 184.0 %all-gather.7.cloned.1.call-start = ((), (), s32[]{:S(2)}) async-start(), calls=%async_computation.2 | async-start | bytes 3932160 | tf_op jit(solution)/shard_map/all_gather | solution.py:86
  23.7 102.5 %collective-permute-start = (bf16[192,8192]{1,0:T(8,128)(2,1)S(1)}, bf16[192,8192]{1,0:T(8,128)(2,1)}, u32[]{:S(2)}, u32[]{:S(2)}) collective-permute-start(bf16[192,8192]{1,0:T(8,128)(2,1)S(1)} %copy-done), channel_id=1, source_target_pairs={{0,1},{1,0},{2,3},{3,2},{4,5},{5,4},{6,7},{7,6},{8,9},{9,8},{10,11... | collective-permute-start | bytes 9437192 | tf_op jit(solution)/shard_map/ppermute | solution.py:30
  145.0 126.4 %all-gather.9.cloned.1.call-start = ((), (), s32[]{:S(2)}) async-start(), calls=%async_computation.3 | async-start | bytes 3932160 | tf_op jit(solution)/shard_map/all_gather | solution.py:86
  150.1 53.5 %collective-permute-start.2 = (bf16[576,2048]{1,0:T(8,128)(2,1)}, bf16[576,2048]{1,0:T(8,128)(2,1)}, u32[]{:S(2)}, u32[]{:S(2)}) collective-permute-start(bf16[576,2048]{1,0:T(8,128)(2,1)} %fusion.8), channel_id=1, source_target_pairs={{0,1},{1,0},{2,3},{3,2},{4,5},{5,4},{6,7},{7,6},{8,9},{9,8},{10,11... | collective-permute-start | bytes 7077896 | tf_op jit(solution)/shard_map/ppermute | solution.py:30
  208.6 127.2 %all-gather.11.cloned.1.call-start = ((), (), s32[]{:S(2)}) async-start(), calls=%async_computation.4 | async-start | bytes 3932160 | tf_op jit(solution)/shard_map/all_gather | solution.py:86
  214.2 53.3 %collective-permute-start.1 = (bf16[576,2048]{1,0:T(8,128)(2,1)}, bf16[576,2048]{1,0:T(8,128)(2,1)}, u32[]{:S(2)}, u32[]{:S(2)}) collective-permute-start(bf16[576,2048]{1,0:T(8,128)(2,1)} %fusion.9), channel_id=1, source_target_pairs={{0,1},{1,0},{2,3},{3,2},{4,5},{5,4},{6,7},{7,6},{8,9},{9,8},{10,11... | collective-permute-start | bytes 7077896 | tf_op jit(solution)/shard_map/ppermute | solution.py:30
  215.7 4.1 copy-start.2
  218.3 1.5 copy-start.6
  225.8 3.4 copy-start.1
  234.1 50.6 %collective-permute-start.3 = (bf16[512,2048]{1,0:T(8,128)(2,1)}, bf16[512,2048]{1,0:T(8,128)(2,1)}, u32[]{:S(2)}, u32[]{:S(2)}) collective-permute-start(bf16[512,2048]{1,0:T(8,128)(2,1)} %fusion.3), channel_id=1, source_target_pairs={{0,8},{8,0},{1,9},{9,1},{2,10},{10,2},{3,11},{11,3},{4,12},{12,4},... | collective-permute-start | bytes 6291464 | tf_op jit(solution)/shard_map/ppermute | solution.py:30
  273.6 5.0 %copy-start.3 = (bf16[768,2048]{1,0:T(8,128)(2,1)S(1)}, bf16[768,2048]{1,0:T(8,128)(2,1)}, u32[]{:S(2)}) copy-start(bf16[768,2048]{1,0:T(8,128)(2,1)} %all-gather.7.cloned.1.call-done) | copy-start | bytes 9437188
  273.6 5.0 %copy-start.7 = (bf16[4,1,192,1024]{3,2,1,0:T(8,128)(2,1)S(1)}, bf16[4,1,192,1024]{3,2,1,0:T(8,128)(2,1)}, u32[]{:S(2)}) copy-start(bf16[4,1,192,1024]{3,2,1,0:T(8,128)(2,1)} %copy-done.6) | copy-start | bytes 4718596
  278.5 13.5 %collective-permute-start.4 = (bf16[512,2048]{1,0:T(8,128)(2,1)S(1)}, bf16[512,2048]{1,0:T(8,128)(2,1)S(1)}, u32[]{:S(2)}, u32[]{:S(2)}) collective-permute-start(bf16[512,2048]{1,0:T(8,128)(2,1)S(1)} %fusion), channel_id=1, source_target_pairs={{0,8},{8,0},{1,9},{9,1},{2,10},{10,2},{3,11},{11,3},{4,12},{12,4},... | collective-permute-start | bytes 6291464 | tf_op jit(solution)/shard_map/ppermute | solution.py:30
  290.5 7.5 %copy-start.4 = (bf16[768,2048]{1,0:T(8,128)(2,1)S(1)}, bf16[768,2048]{1,0:T(8,128)(2,1)}, u32[]{:S(2)}) copy-start(bf16[768,2048]{1,0:T(8,128)(2,1)} %all-gather.9.cloned.1.call-done) | copy-start | bytes 9437188
  290.5 49.2 %collective-permute-start.7 = (bf16[512,2048]{1,0:T(8,128)(2,1)}, bf16[512,2048]{1,0:T(8,128)(2,1)}, u32[]{:S(2)}, u32[]{:S(2)}) collective-permute-start(bf16[512,2048]{1,0:T(8,128)(2,1)} %fusion.5), channel_id=1, source_target_pairs={{0,16},{16,0},{1,17},{17,1},{2,18},{18,2},{3,19},{19,3},{4,20},{20... | collective-permute-start | bytes 6291464 | tf_op jit(solution)/shard_map/ppermute | solution.py:30
  297.1 86.7 %collective-permute-start.8 = (bf16[512,2048]{1,0:T(8,128)(2,1)}, bf16[512,2048]{1,0:T(8,128)(2,1)}, u32[]{:S(2)}, u32[]{:S(2)}) collective-permute-start(bf16[512,2048]{1,0:T(8,128)(2,1)} %fusion.2), channel_id=1, source_target_pairs={{0,16},{16,0},{1,17},{17,1},{2,18},{18,2},{3,19},{19,3},{4,20},{20... | collective-permute-start | bytes 6291464 | tf_op jit(solution)/shard_map/ppermute | solution.py:30
  301.9 134.9 %collective-permute-start.5 = (bf16[576,2048]{1,0:T(8,128)(2,1)}, bf16[576,2048]{1,0:T(8,128)(2,1)}, u32[]{:S(2)}, u32[]{:S(2)}) collective-permute-start(bf16[576,2048]{1,0:T(8,128)(2,1)} %fusion.7), channel_id=1, source_target_pairs={{0,1},{1,0},{2,3},{3,2},{4,5},{5,4},{6,7},{7,6},{8,9},{9,8},{10,11... | collective-permute-start | bytes 7077896 | tf_op jit(solution)/shard_map/ppermute | solution.py:30
  339.5 46.3 %copy-start.5 = (bf16[768,2048]{1,0:T(8,128)(2,1)S(1)}, bf16[768,2048]{1,0:T(8,128)(2,1)}, u32[]{:S(2)}) copy-start(bf16[768,2048]{1,0:T(8,128)(2,1)} %all-gather.11.cloned.1.call-done) | copy-start | bytes 9437188
  339.5 46.3 %copy-start.8 = (bf16[4,1,192,1024]{3,2,1,0:T(8,128)(2,1)S(1)}, bf16[4,1,192,1024]{3,2,1,0:T(8,128)(2,1)}, u32[]{:S(2)}) copy-start(bf16[4,1,192,1024]{3,2,1,0:T(8,128)(2,1)} %copy-done.6) | copy-start | bytes 4718596
  383.8 28.9 %collective-permute-start.9 = (bf16[288,2048]{1,0:T(8,128)(2,1)S(1)}, bf16[288,2048]{1,0:T(8,128)(2,1)S(1)}, u32[]{:S(2)}, u32[]{:S(2)}) collective-permute-start(bf16[288,2048]{1,0:T(8,128)(2,1)S(1)} %get-tuple-element.22), channel_id=1, source_target_pairs={{0,1},{1,0},{2,3},{3,2},{4,5},{5,4},{6,7},{7,6},{8,9},{9,8},{10,11... | collective-permute-start | bytes 3538952 | tf_op jit(solution)/shard_map/ppermute | solution.py:30
  385.2 51.4 %collective-permute-start.6 = (bf16[288,2048]{1,0:T(8,128)(2,1)S(1)}, bf16[288,2048]{1,0:T(8,128)(2,1)S(1)}, u32[]{:S(2)}, u32[]{:S(2)}) collective-permute-start(bf16[288,2048]{1,0:T(8,128)(2,1)S(1)} %get-tuple-element.29), channel_id=1, source_target_pairs={{0,1},{1,0},{2,3},{3,2},{4,5},{5,4},{6,7},{7,6},{8,9},{9,8},{10,11... | collective-permute-start | bytes 3538952 | tf_op jit(solution)/shard_map/ppermute | solution.py:30
  385.8 51.0 %slice-start = ((s8[8388608]{0:T(1024)(128)(4,1)}), s8[4194304]{0:T(1024)(128)(4,1)S(1)}, s32[]{:S(2)}) async-start(s8[8388608]{0:T(1024)(128)(4,1)} %bitcast.28), calls=%async_computation.5 | async-start | bytes 8388608
  389.4 47.5 %slice-start.1 = ((s8[8388608]{0:T(1024)(128)(4,1)}), s8[4194304]{0:T(1024)(128)(4,1)S(1)}, s32[]{:S(2)}) async-start(s8[8388608]{0:T(1024)(128)(4,1)} %bitcast.28), calls=%async_computation.6 | async-start | bytes 8388608
  440.4 10.1 %collective-permute-start.10 = (f32[512,2048]{1,0:T(8,128)S(1)}, f32[512,2048]{1,0:T(8,128)}, u32[]{:S(2)}, u32[]{:S(2)}) collective-permute-start(f32[512,2048]{1,0:T(8,128)S(1)} %slice_add_fusion.5), channel_id=1, source_target_pairs={{0,8},{8,0},{1,9},{9,1},{2,10},{10,2},{3,11},{11,3},{4,12},{12,4},... | collective-permute-start | bytes 12582920 | tf_op jit(solution)/shard_map/ppermute | solution.py:30
  446.4 17.4 %collective-permute-start.11 = (f32[512,2048]{1,0:T(8,128)}, f32[512,2048]{1,0:T(8,128)}, u32[]{:S(2)}, u32[]{:S(2)}) collective-permute-start(f32[512,2048]{1,0:T(8,128)} %slice_add_fusion.4), channel_id=1, source_target_pairs={{0,8},{8,0},{1,9},{9,1},{2,10},{10,2},{3,11},{11,3},{4,12},{12,4},... | collective-permute-start | bytes 12582920 | tf_op jit(solution)/shard_map/ppermute | solution.py:30
Sparse Core Ops, SparseCore 0:
  25.0 119.0 all-gather.4
  145.6 61.9 all-gather.6
  209.2 62.1 all-gather.8
  273.7 62.1 all-gather.10

commit v9 on v6

--- a/solution.py
+++ b/solution.py
@@ -66,7 +66,7 @@
             for k, m in enumerate(order):
                 cols_a = lax.dynamic_slice_in_dim(theirs_own, m * rw, rw, axis=1)
                 early.append(contract(s_a, cols_a) + contract(s_mine, mine[k]))
-            halves = 2 if width % 16 == 0 else 1
+            halves = 1
             hw = width // halves
             cuts = [slice(h * hw, (h + 1) * hw) for h in range(halves)]
             sent, got_x = [], []

time: 481 us -> 503 us (1.046)
  other arithmetic: 36.8 us -> 57.2 us
  matrix products: 62.7 us -> 74.9 us
  local copies, waits for them, and re-layouts: 20.6 us -> 12.9 us
    convert_element_type x0 -> x1, other arithmetic: none -> 14.3 us  [x_chain(): sent.append(other_x.astype(jnp.bfloat16))]
    dot_general x16 -> x12, matrix products: 62.7 us -> 74.9 us  [contract(): lax.dot_general(left, right, (((0,), (0,)), ((), ())), preferred_element_...]
    add x0 -> x1, other arithmetic: none -> 11.9 us  [body(): give = late_give[rows] + contract(s_h, t_give)]
    ppermute x11 -> x8, waiting for transfers between devices: 265 us -> 256 us  [swap(): return lax.ppermute(x, axis, [(0, 1), (1, 0)])]
    dynamic_update_slice x1 -> x0, local copies, waits for them, and re-layouts: 6.82 us -> none  [body(): lax.dynamic_update_slice_in_dim(out, own_x + got_x[h].astype(jnp.float32)...]
    dynamic_update_slice x1 -> x0, other arithmetic: 6.5 us -> none  [body(): lax.dynamic_update_slice_in_dim(out, own_x + got_x[h].astype(jnp.float32)...]
    ppermute x11 -> x8, starting transfers between devices: 10.8 us -> 8.84 us  [swap(): return lax.ppermute(x, axis, [(0, 1), (1, 0)])]
  transfers between devices with their start and end apart: 16 -> 13, of which waited for: 10 -> 10; matrix products, arithmetic and copies ran while one was open for 20% -> 21% of each run, Pallas kernels for 0% -> 0%
where the time goes in v9:
time: 503 us; the launch traced here: 496 us
  waiting for transfers between devices  319 us (63%)
  matrix products  74.9 us (15%)
  other arithmetic  57.2 us (11%)
  starting transfers between devices  16.7 us (3%)
  between operations  15 us (3%)
  local copies, waits for them, and re-layouts  12.9 us (3%)
    ppermute x8, waiting for transfers between devices, swap(): return lax.ppermute(x, axis, [(0, 1), (1, 0)])  256 us
    dot_general x12, matrix products, contract(): lax.dot_general(left, right, (((0,), (0,)), ((), ())), preferred_element_...  74.9 us
    all_gather x3, waiting for transfers between devices, body(): lax.all_gather(lax.dynamic_slice_in_dim(rest, m * rw, rw, axis=1), 'az',...  44.7 us
    concatenate x5, other arithmetic, others(): doubled = jnp.concatenate([v, v], axis=0)  18.3 us
    all_to_all x1, waiting for transfers between devices, body(): lax.all_to_all(scale(w_own, b_rows), ('az', 'ay'), 1, 0, tiled=True)  17.8 us
    convert_element_type x1, other arithmetic, x_chain(): sent.append(other_x.astype(jnp.bfloat16))  14.3 us
    add x1, other arithmetic, body(): give = late_give[rows] + contract(s_h, t_give)  11.9 us
  transfers between devices with their start and end apart: 13, of which 10 were waited for; matrix products, arithmetic and copies ran while one was open for 21% of the time, Pallas kernels for 0%

profile of v9, /device:TPU:0, one launch (start us, length us, event | category | flops | bytes accessed | tf_op | source)
XLA Modules:
  0.0 495.7 jit_solution(1757995189847650583)
XLA Ops:
  6.5 0.7 and_select_fusion
  8.5 1.0 select_reduce_fusion
  9.5 0.8 dynamic_slice.52
  10.4 2.6 multiply_convert_fusion
  13.0 2.1 copy.12
  15.1 7.5 %all-to-all-start = ((bf16[192,8,1024]{2,0,1:T(8,128)(2,1)}), bf16[192,8,1024]{2,0,1:T(8,128)(2,1)}, u32[]{:S(2)}, u32[]{:S(2)}) async-start(bf16[192,8,1024]{2,0,1:T(8,128)(2,1)} %bitcast.27), calls=%async_computation | async-start | bytes 6291456 | tf_op jit(solution)/shard_map/all_to_all | solution.py:57
  22.7 0.9 constant_dynamic-slice_fusion.3
  23.7 2.0 collective-permute-start
  25.7 100.5 %collective-permute-done = bf16[192,8192]{1,0:T(8,128)(2,1)} collective-permute-done((bf16[192,8192]{1,0:T(8,128)(2,1)S(1)}, bf16[192,8192]{1,0:T(8,128)(2,1)}, u32[]{:S(2)}, u32[]{:S(2)}) %collective-permute-start) | collective-permute-done | bytes 3145760 | tf_op jit(solution)/shard_map/ppermute | solution.py:30
  126.2 17.8 %all-to-all-done = bf16[192,8,1024]{2,0,1:T(8,128)(2,1)} async-done(((bf16[192,8,1024]{2,0,1:T(8,128)(2,1)}), bf16[192,8,1024]{2,0,1:T(8,128)(2,1)}, u32[]{:S(2)}, u32[]{:S(2)}) %all-to-all-start) | async-done | bytes 3145760 | tf_op jit(solution)/shard_map/all_to_all | solution.py:57
  144.1 1.0 constant_dynamic-slice_fusion.2
  145.1 5.1 %fusion.2 = bf16[576,2048]{1,0:T(8,128)(2,1)} fusion(s32[]{:T(128)S(6)} %select_n.66, bf16[768,2048]{1,0:T(8,128)(2,1)} %all-gather.5.cloned.1.call-done), kind=kLoop, calls=%fused_computation.19 | loop fusion | flops 4718592 | bytes 5505028 | tf_op jit(solution)/shard_map/concatenate | solution.py:50
  150.2 1.4 collective-permute-start.2
  151.5 2.4 constant_dynamic-slice_fusion.4
  153.9 1.5 fusion.4
  155.4 6.0 %fusion.7 = f32[1024,2048]{1,0:T(8,128)} fusion(bf16[192,8192]{1,0:T(8,128)(2,1)} %collective-permute-done, s32[]{:T(128)S(6)} %select_n.65, bf16[768,1024]{1,0:T(8,128)(2,1)S(1)} %bitcast.29, s32[]{:T(128)S(6)} %select_n.62), kind=kOutput, calls=%fused_computation.26 | convolution fusion | flops 805306368 | bytes 9568264 | tf_op jit(solution)/shard_map/dot_general | solution.py:24
  161.4 5.8 %fusion.21 = f32[1024,2048]{1,0:T(8,128)} fusion(bf16[768,1024]{1,0:T(8,128)(2,1)S(1)} %bitcast.34, bf16[768,2048]{1,0:T(8,128)(2,1)S(1)} %copy-done.4), kind=kOutput, calls=%fused_computation.52 | convolution fusion | flops 3221225472 | bytes 13107200 | tf_op jit(solution)/shard_map/dot_general | solution.py:24
  167.2 36.5 %collective-permute-done.2 = bf16[576,2048]{1,0:T(8,128)(2,1)} collective-permute-done((bf16[576,2048]{1,0:T(8,128)(2,1)}, bf16[576,2048]{1,0:T(8,128)(2,1)}, u32[]{:S(2)}, u32[]{:S(2)}) %collective-permute-start.2) | collective-permute-done | bytes 2359328 | tf_op jit(solution)/shard_map/ppermute | solution.py:30
  203.7 4.0 all-gather.7.cloned.1.call-done
  207.7 2.1 constant_dynamic-slice_fusion.1
  209.8 0.2 all-gather.11.cloned.1.call-start
  210.1 10.3 %add_convert_fusion.1 = bf16[1024,2048]{1,0:T(8,128)(2,1)} fusion(f32[1024,2048]{1,0:T(8,128)} %fusion.7, f32[1024,2048]{1,0:T(8,128)} %fusion.21, bf16[576,1024]{1,0:T(8,128)(2,1)S(1)} %fusion.4, bf16[576,2048]{1,0:T(8,128)(2,1)} %collective-permute-done.2), kind=kOutput, calls=%fused_computation.2 | convolution fusion | flops 2422210560 | bytes 24510464 | tf_op jit(solution)/shard_map/dot_general | solution.py:24
  220.4 4.0 fusion.3
  224.4 1.3 collective-permute-start.1
  225.7 5.9 %fusion.9 = f32[1024,2048]{1,0:T(8,128)} fusion(bf16[192,8192]{1,0:T(8,128)(2,1)} %collective-permute-done, s32[]{:T(128)S(6)} %select_n.63, bf16[768,1024]{1,0:T(8,128)(2,1)S(1)} %bitcast.30, s32[]{:T(128)S(6)} %select_n.62), kind=kOutput, calls=%fused_computation.28 | convolution fusion | flops 805306368 | bytes 9568264 | tf_op jit(solution)/shard_map/dot_general | solution.py:24
  231.6 5.8 %fusion.19 = f32[1024,2048]{1,0:T(8,128)} fusion(bf16[768,1024]{1,0:T(8,128)(2,1)S(1)} %bitcast.35, bf16[768,2048]{1,0:T(8,128)(2,1)S(1)} %copy-done.3), kind=kOutput, calls=%fused_computation.50 | convolution fusion | flops 3221225472 | bytes 13107200 | tf_op jit(solution)/shard_map/dot_general | solution.py:24
  237.4 41.0 %collective-permute-done.1 = bf16[576,2048]{1,0:T(8,128)(2,1)} collective-permute-done((bf16[576,2048]{1,0:T(8,128)(2,1)}, bf16[576,2048]{1,0:T(8,128)(2,1)}, u32[]{:S(2)}, u32[]{:S(2)}) %collective-permute-start.1) | collective-permute-done | bytes 2359328 | tf_op jit(solution)/shard_map/ppermute | solution.py:30
  278.4 7.4 %fusion.20 = f32[1024,2048]{1,0:T(8,128)} fusion(bf16[576,1024]{1,0:T(8,128)(2,1)S(1)} %fusion.4, bf16[576,2048]{1,0:T(8,128)(2,1)} %collective-permute-done.1), kind=kOutput, calls=%fused_computation.51 | convolution fusion | flops 2415919104 | bytes 11927552 | tf_op jit(solution)/shard_map/dot_general | solution.py:24
  285.7 2.1 constant_dynamic-slice_fusion
  287.9 14.3 %add_convert_fusion = bf16[1024,2048]{1,0:T(8,128)(2,1)} fusion(bf16[1024,2048]{1,0:T(8,128)(2,1)} %collective-permute-done.3, f32[1024,2048]{1,0:T(8,128)} %fusion.20, f32[1024,2048]{1,0:T(8,128)} %fusion.9, f32[1024,2048]{1,0:T(8,128)} %fusion.19), kind=kLoop, calls=%fused_computation.1 | loop fusion | flops 10485760 | bytes 33554432 | tf_op jit(solution)/shard_map/convert_element_type | solution.py:78
  302.2 1.2 collective-permute-start.5
  303.5 4.0 fusion.1
  307.5 1.5 collective-permute-start.4
  309.0 40.7 %all-gather.11.cloned.1.call-done = bf16[768,2048]{1,0:T(8,128)(2,1)} async-done(((bf16[192,2048]{1,0:T(8,128)(2,1)}), bf16[768,2048]{1,0:T(8,128)(2,1)}) %all-gather.11.cloned.1.call-update) | async-done | bytes 3145744 | tf_op jit(solution)/shard_map/all_gather | solution.py:86
  349.6 3.7 fusion
  353.4 41.2 %collective-permute-done.5 = bf16[1024,2048]{1,0:T(8,128)(2,1)} collective-permute-done((bf16[1024,2048]{1,0:T(8,128)(2,1)}, bf16[1024,2048]{1,0:T(8,128)(2,1)}, u32[]{:S(2)}, u32[]{:S(2)}) %collective-permute-start.5) | collective-permute-done | bytes 4194336 | tf_op jit(solution)/shard_map/ppermute | solution.py:30
  394.6 1.4 collective-permute-start.6
  396.0 3.5 fusion.22
  399.5 6.0 %convolution_add_fusion.1 = f32[1024,2048]{1,0:T(8,128)} fusion(f32[1024,2048]{1,0:T(8,128)S(1)} %fusion.22, bf16[192,8192]{1,0:T(8,128)(2,1)} %collective-permute-done, s32[]{:T(128)S(6)} %select_n.67, bf16[768,1024]{1,0:T(8,128)(2,1)S(1)} %bitcast.31, s32[]{:T(128)S(6)} %select_n.62), kind=kOutput, calls=%fused_computation.13 | convolution fusion | flops 807403520 | bytes 17956872 | tf_op jit(solution)/shard_map/dot_general | solution.py:24
  405.5 3.8 fusion.23
  409.3 5.7 %convolution_add_fusion = f32[1024,2048]{1,0:T(8,128)} fusion(f32[1024,2048]{1,0:T(8,128)S(1)} %fusion.23, bf16[192,8192]{1,0:T(8,128)(2,1)} %collective-permute-done, s32[]{:T(128)S(6)} %select_n.68, bf16[768,1024]{1,0:T(8,128)(2,1)S(1)} %bitcast.32, s32[]{:T(128)S(6)} %select_n.62), kind=kOutput, calls=%fused_computation.12 | convolution fusion | flops 807403520 | bytes 17956872 | tf_op jit(solution)/shard_map/dot_general | solution.py:24
  415.0 31.3 %collective-permute-done.6 = bf16[576,2048]{1,0:T(8,128)(2,1)S(1)} collective-permute-done((bf16[576,2048]{1,0:T(8,128)(2,1)S(1)}, bf16[576,2048]{1,0:T(8,128)(2,1)S(1)}, u32[]{:S(2)}, u32[]{:S(2)}) %collective-permute-start.6) | collective-permute-done | bytes 2359328 | tf_op jit(solution)/shard_map/ppermute | solution.py:30
  446.4 1.5 copy-done.11
  447.9 7.3 %fusion.25 = f32[1024,2048]{1,0:T(8,128)} fusion(bf16[576,1024]{1,0:T(8,128)(2,1)S(1)} %fusion.4, bf16[576,2048]{1,0:T(8,128)(2,1)} %collective-permute-done.4), kind=kOutput, calls=%fused_computation.56 | convolution fusion | flops 2415919104 | bytes 11927552 | tf_op jit(solution)/shard_map/dot_general | solution.py:24
  455.2 11.9 %add.131 = f32[1024,2048]{1,0:T(8,128)} add(f32[1024,2048]{1,0:T(8,128)} %convolution_add_fusion.1, f32[1024,2048]{1,0:T(8,128)} %fusion.25) | non-fusion elementwise | flops 2097152 | bytes 25165824 | tf_op jit(solution)/shard_map/add | solution.py:101
  467.0 7.5 %fusion.24 = f32[1024,2048]{1,0:T(8,128)} fusion(bf16[576,1024]{1,0:T(8,128)(2,1)S(1)} %fusion.4, bf16[576,2048]{1,0:T(8,128)(2,1)} %copy-done.11), kind=kOutput, calls=%fused_computation.55 | convolution fusion | flops 2415919104 | bytes 11927552 | tf_op jit(solution)/shard_map/dot_general | solution.py:24
  474.5 5.9 %collective-permute-done.7 = f32[1024,2048]{1,0:T(8,128)S(1)} collective-permute-done((f32[1024,2048]{1,0:T(8,128)}, f32[1024,2048]{1,0:T(8,128)S(1)}, u32[]{:S(2)}, u32[]{:S(2)}) %collective-permute-start.7) | collective-permute-done | bytes 8388640 | tf_op jit(solution)/shard_map/ppermute | solution.py:30
  480.4 8.4 %convert_add_fusion = f32[1024,2048]{1,0:T(8,128)} fusion(bf16[1024,2048]{1,0:T(8,128)(2,1)} %collective-permute-done.5, f32[1024,2048]{1,0:T(8,128)S(1)} %collective-permute-done.7, f32[1024,2048]{1,0:T(8,128)S(1)} %copy-done, f32[1024,2048]{1,0:T(8,128)} %fusion.24), kind=kLoop, calls=%fused_computation | loop fusion | flops 8388608 | bytes 37748736 | tf_op jit(solution)/shard_map/add | solution.py:103
  (38 shorter events, 0.4 us)
Async XLA Ops:
  15.1 7.6 %copy-start.1 = (bf16[192,8192]{1,0:T(8,128)(2,1)S(1)}, bf16[192,8192]{1,0:T(8,128)(2,1)}, u32[]{:S(2)}) copy-start(bf16[192,8192]{1,0:T(8,128)(2,1)} %param.6) | copy-start | bytes 9437188
  15.1 128.9 %all-to-all-start = ((bf16[192,8,1024]{2,0,1:T(8,128)(2,1)}), bf16[192,8,1024]{2,0,1:T(8,128)(2,1)}, u32[]{:S(2)}, u32[]{:S(2)}) async-start(bf16[192,8,1024]{2,0,1:T(8,128)(2,1)} %bitcast.27), calls=%async_computation | async-start | bytes 6291456 | tf_op jit(solution)/shard_map/all_to_all | solution.py:57
  22.6 121.5 %all-gather.5.cloned.1.call-start = ((), (), s32[]{:S(2)}) async-start(), calls=%async_computation.1 | async-start | bytes 3932160 | tf_op jit(solution)/shard_map/all_gather | solution.py:54
  23.6 184.0 %all-gather.7.cloned.1.call-start = ((), (), s32[]{:S(2)}) async-start(), calls=%async_computation.2 | async-start | bytes 3932160 | tf_op jit(solution)/shard_map/all_gather | solution.py:86
  23.7 102.5 %collective-permute-start = (bf16[192,8192]{1,0:T(8,128)(2,1)S(1)}, bf16[192,8192]{1,0:T(8,128)(2,1)}, u32[]{:S(2)}, u32[]{:S(2)}) collective-permute-start(bf16[192,8192]{1,0:T(8,128)(2,1)S(1)} %copy-done.1), channel_id=1, source_target_pairs={{0,1},{1,0},{2,3},{3,2},{4,5},{5,4},{6,7},{7,6},{8,9},{9,8},{10,11... | collective-permute-start | bytes 9437192 | tf_op jit(solution)/shard_map/ppermute | solution.py:30
  145.0 140.7 %all-gather.9.cloned.1.call-start = ((), (), s32[]{:S(2)}) async-start(), calls=%async_computation.3 | async-start | bytes 3932160 | tf_op jit(solution)/shard_map/all_gather | solution.py:86
  150.2 53.5 %collective-permute-start.2 = (bf16[576,2048]{1,0:T(8,128)(2,1)}, bf16[576,2048]{1,0:T(8,128)(2,1)}, u32[]{:S(2)}, u32[]{:S(2)}) collective-permute-start(bf16[576,2048]{1,0:T(8,128)(2,1)} %fusion.2), channel_id=1, source_target_pairs={{0,1},{1,0},{2,3},{3,2},{4,5},{5,4},{6,7},{7,6},{8,9},{9,8},{10,11... | collective-permute-start | bytes 7077896 | tf_op jit(solution)/shard_map/ppermute | solution.py:30
  153.9 7.5 %copy-start.8 = (bf16[4,1,192,1024]{3,2,1,0:T(8,128)(2,1)}, bf16[4,1,192,1024]{3,2,1,0:T(8,128)(2,1)S(1)}, u32[]{:S(2)}) copy-start(bf16[4,1,192,1024]{3,2,1,0:T(8,128)(2,1)S(1)} %get-tuple-element.27) | copy-start | bytes 4718596
  155.4 6.0 %copy-start.4 = (bf16[768,2048]{1,0:T(8,128)(2,1)S(1)}, bf16[768,2048]{1,0:T(8,128)(2,1)}, u32[]{:S(2)}) copy-start(bf16[768,2048]{1,0:T(8,128)(2,1)} %all-gather.5.cloned.1.call-done) | copy-start | bytes 9437188
  209.8 139.8 %all-gather.11.cloned.1.call-start = ((), (), s32[]{:S(2)}) async-start(), calls=%async_computation.4 | async-start | bytes 3932160 | tf_op jit(solution)/shard_map/all_gather | solution.py:86
  210.0 10.4 %copy-start.2 = (bf16[768,2048]{1,0:T(8,128)(2,1)S(1)}, bf16[768,2048]{1,0:T(8,128)(2,1)}, u32[]{:S(2)}) copy-start(bf16[768,2048]{1,0:T(8,128)(2,1)} %all-gather.7.cloned.1.call-done) | copy-start | bytes 9437188
  220.4 67.5 %collective-permute-start.3 = (bf16[1024,2048]{1,0:T(8,128)(2,1)}, bf16[1024,2048]{1,0:T(8,128)(2,1)}, u32[]{:S(2)}, u32[]{:S(2)}) collective-permute-start(bf16[1024,2048]{1,0:T(8,128)(2,1)} %add_convert_fusion.1), channel_id=1, source_target_pairs={{0,8},{8,0},{1,9},{9,1},{2,10},{10,2},{3,11},{11,3},{4,12},{12,4},... | collective-permute-start | bytes 12582920 | tf_op jit(solution)/shard_map/ppermute | solution.py:30
  224.4 54.0 %collective-permute-start.1 = (bf16[576,2048]{1,0:T(8,128)(2,1)}, bf16[576,2048]{1,0:T(8,128)(2,1)}, u32[]{:S(2)}, u32[]{:S(2)}) collective-permute-start(bf16[576,2048]{1,0:T(8,128)(2,1)} %fusion.3), channel_id=1, source_target_pairs={{0,1},{1,0},{2,3},{3,2},{4,5},{5,4},{6,7},{7,6},{8,9},{9,8},{10,11... | collective-permute-start | bytes 7077896 | tf_op jit(solution)/shard_map/ppermute | solution.py:30
  225.7 5.9 %copy-start.3 = (bf16[768,2048]{1,0:T(8,128)(2,1)S(1)}, bf16[768,2048]{1,0:T(8,128)(2,1)}, u32[]{:S(2)}) copy-start(bf16[768,2048]{1,0:T(8,128)(2,1)} %all-gather.7.cloned.1.call-done) | copy-start | bytes 9437188
  225.7 5.9 %copy-start.9 = (bf16[4,1,192,1024]{3,2,1,0:T(8,128)(2,1)S(1)}, bf16[4,1,192,1024]{3,2,1,0:T(8,128)(2,1)}, u32[]{:S(2)}) copy-start(bf16[4,1,192,1024]{3,2,1,0:T(8,128)(2,1)} %copy-done.8) | copy-start | bytes 4718596
  287.8 15.6 %copy-start.5 = (bf16[768,2048]{1,0:T(8,128)(2,1)S(1)}, bf16[768,2048]{1,0:T(8,128)(2,1)}, u32[]{:S(2)}) copy-start(bf16[768,2048]{1,0:T(8,128)(2,1)} %all-gather.9.cloned.1.call-done) | copy-start | bytes 9437188
  302.2 92.4 %collective-permute-start.5 = (bf16[1024,2048]{1,0:T(8,128)(2,1)}, bf16[1024,2048]{1,0:T(8,128)(2,1)}, u32[]{:S(2)}, u32[]{:S(2)}) collective-permute-start(bf16[1024,2048]{1,0:T(8,128)(2,1)} %add_convert_fusion), channel_id=1, source_target_pairs={{0,16},{16,0},{1,17},{17,1},{2,18},{18,2},{3,19},{19,3},{4,20},{20... | collective-permute-start | bytes 12582920 | tf_op jit(solution)/shard_map/ppermute | solution.py:30
  307.5 107.6 %collective-permute-start.4 = (bf16[576,2048]{1,0:T(8,128)(2,1)}, bf16[576,2048]{1,0:T(8,128)(2,1)}, u32[]{:S(2)}, u32[]{:S(2)}) collective-permute-start(bf16[576,2048]{1,0:T(8,128)(2,1)} %fusion.1), channel_id=1, source_target_pairs={{0,1},{1,0},{2,3},{3,2},{4,5},{5,4},{6,7},{7,6},{8,9},{9,8},{10,11... | collective-permute-start | bytes 7077896 | tf_op jit(solution)/shard_map/ppermute | solution.py:30
  349.6 46.3 %copy-start.6 = (bf16[768,2048]{1,0:T(8,128)(2,1)S(1)}, bf16[768,2048]{1,0:T(8,128)(2,1)}, u32[]{:S(2)}) copy-start(bf16[768,2048]{1,0:T(8,128)(2,1)} %all-gather.9.cloned.1.call-done) | copy-start | bytes 9437188
  349.6 46.3 %copy-start.10 = (bf16[4,1,192,1024]{3,2,1,0:T(8,128)(2,1)S(1)}, bf16[4,1,192,1024]{3,2,1,0:T(8,128)(2,1)}, u32[]{:S(2)}) copy-start(bf16[4,1,192,1024]{3,2,1,0:T(8,128)(2,1)} %copy-done.8) | copy-start | bytes 4718596
  394.6 51.8 %collective-permute-start.6 = (bf16[576,2048]{1,0:T(8,128)(2,1)S(1)}, bf16[576,2048]{1,0:T(8,128)(2,1)S(1)}, u32[]{:S(2)}, u32[]{:S(2)}) collective-permute-start(bf16[576,2048]{1,0:T(8,128)(2,1)S(1)} %fusion), channel_id=1, source_target_pairs={{0,1},{1,0},{2,3},{3,2},{4,5},{5,4},{6,7},{7,6},{8,9},{9,8},{10,11... | collective-permute-start | bytes 7077896 | tf_op jit(solution)/shard_map/ppermute | solution.py:30
  399.5 6.0 %copy-start.7 = (bf16[768,2048]{1,0:T(8,128)(2,1)S(1)}, bf16[768,2048]{1,0:T(8,128)(2,1)}, u32[]{:S(2)}) copy-start(bf16[768,2048]{1,0:T(8,128)(2,1)} %all-gather.11.cloned.1.call-done) | copy-start | bytes 9437188
  446.4 1.5 copy-start.11
  467.0 13.4 %collective-permute-start.7 = (f32[1024,2048]{1,0:T(8,128)}, f32[1024,2048]{1,0:T(8,128)S(1)}, u32[]{:S(2)}, u32[]{:S(2)}) collective-permute-start(f32[1024,2048]{1,0:T(8,128)} %add.131), channel_id=1, source_target_pairs={{0,8},{8,0},{1,9},{9,1},{2,10},{10,2},{3,11},{11,3},{4,12},{12,4},... | collective-permute-start | bytes 25165832 | tf_op jit(solution)/shard_map/ppermute | solution.py:30
  467.0 13.4 %copy-start = (f32[1024,2048]{1,0:T(8,128)S(1)}, f32[1024,2048]{1,0:T(8,128)}, u32[]{:S(2)}) copy-start(f32[1024,2048]{1,0:T(8,128)} %convolution_add_fusion) | copy-start | bytes 25165828
Sparse Core Ops, SparseCore 0:
  25.0 119.0 all-gather.4
  145.6 62.0 all-gather.6
  209.9 62.1 all-gather.8
  288.0 61.6 all-gather.10

commit v10 on v6

--- a/solution.py
+++ b/solution.py
@@ -55,7 +55,7 @@
         theirs_own = swap(b_rows, "ay")
         w_own = row_weights(pair_index, e_occ, e_vir, occ_batch, freq)
         scaled_rows = lax.all_to_all(scale(w_own, b_rows), ("az", "ay"), 1, 0, tiled=True)
-        theirs_own, scaled_rows, rest = lax.optimization_barrier((theirs_own, scaled_rows, b_rows))
+        theirs_own, rest = lax.optimization_barrier((theirs_own, b_rows))
         def x_chain(theirs):
             by_source = scaled_rows.reshape(n_az, n_ay, nloc, width)
             s_mine = lax.dynamic_index_in_dim(by_source, y, axis=1, keepdims=False).reshape(n_az * nloc, width)

time: 481 us -> 478 us (level)
    all_gather x3, waiting for transfers between devices: 40.5 us -> 65.3 us  [body(): lax.all_gather(lax.dynamic_slice_in_dim(rest, m * rw, rw, axis=1), 'az',...]
    all_to_all x1, waiting for transfers between devices: 17.8 us -> 0.01 us  [body(): lax.all_to_all(scale(w_own, b_rows), ('az', 'ay'), 1, 0, tiled=True)]
    ppermute x11, waiting for transfers between devices: 265 us -> 256 us  [swap(): return lax.ppermute(x, axis, [(0, 1), (1, 0)])]
  transfers between devices with their start and end apart: 16 -> 16, of which waited for: 10 -> 8; matrix products, arithmetic and copies ran while one was open for 20% -> 22% of each run, Pallas kernels for 0% -> 0%
where the time goes in v10:
time: 478 us; the launch traced here: 474 us
  waiting for transfers between devices  321 us (67%)
  matrix products  62.6 us (13%)
  other arithmetic  35 us (7%)
  local copies, waits for them, and re-layouts  23.1 us (5%)
  starting transfers between devices  17.3 us (4%)
  between operations  14.9 us (3%)
    ppermute x11, waiting for transfers between devices, swap(): return lax.ppermute(x, axis, [(0, 1), (1, 0)])  256 us
    all_gather x3, waiting for transfers between devices, body(): lax.all_gather(lax.dynamic_slice_in_dim(rest, m * rw, rw, axis=1), 'az',...  65.3 us
    dot_general x16, matrix products, contract(): lax.dot_general(left, right, (((0,), (0,)), ((), ())), preferred_element_...  62.6 us
    concatenate x5, other arithmetic, others(): doubled = jnp.concatenate([v, v], axis=0)  19.6 us
    ppermute x11, starting transfers between devices, swap(): return lax.ppermute(x, axis, [(0, 1), (1, 0)])  11 us
  transfers between devices with their start and end apart: 16, of which 8 were waited for; matrix products, arithmetic and copies ran while one was open for 22% of the time, Pallas kernels for 0%

profile of v10, /device:TPU:0, one launch (start us, length us, event | category | flops | bytes accessed | tf_op | source)
XLA Modules:
  0.0 473.8 jit_solution(644788389753364393)
XLA Ops:
  6.5 2.2 constant_dynamic-slice_fusion.3
  8.9 3.0 collective-permute-start
  13.2 0.8 dynamic_slice.52
  14.7 1.0 select_reduce_fusion
  15.7 64.6 %collective-permute-done = bf16[192,8192]{1,0:T(8,128)(2,1)} collective-permute-done((bf16[192,8192]{1,0:T(8,128)(2,1)}, bf16[192,8192]{1,0:T(8,128)(2,1)}, u32[]{:S(2)}, u32[]{:S(2)}) %collective-permute-start) | collective-permute-done | bytes 3145760 | tf_op jit(solution)/shard_map/ppermute | solution.py:30
  80.3 2.1 constant_dynamic-slice_fusion.2
  83.2 2.1 copy.12
  85.3 6.1 %all-to-all-start = ((bf16[192,8,1024]{2,0,1:T(8,128)(2,1)}), bf16[192,8,1024]{2,0,1:T(8,128)(2,1)}, u32[]{:S(2)}, u32[]{:S(2)}) async-start(bf16[192,8,1024]{2,0,1:T(8,128)(2,1)} %bitcast.26), calls=%async_computation | async-start | bytes 6291456 | tf_op jit(solution)/shard_map/all_to_all | solution.py:57
  91.4 5.2 %fusion.8 = bf16[576,2048]{1,0:T(8,128)(2,1)} fusion(s32[]{:T(128)S(6)} %select_n.66, bf16[768,2048]{1,0:T(8,128)(2,1)} %all-gather.5.cloned.1.call-done), kind=kLoop, calls=%fused_computation.32 | loop fusion | flops 4718592 | bytes 5505028 | tf_op jit(solution)/shard_map/concatenate | solution.py:50
  96.5 1.9 collective-permute-start.2
  98.5 77.1 %collective-permute-done.2 = bf16[576,2048]{1,0:T(8,128)(2,1)} collective-permute-done((bf16[576,2048]{1,0:T(8,128)(2,1)}, bf16[576,2048]{1,0:T(8,128)(2,1)}, u32[]{:S(2)}, u32[]{:S(2)}) %collective-permute-start.2) | collective-permute-done | bytes 2359328 | tf_op jit(solution)/shard_map/ppermute | solution.py:30
  175.6 30.5 %all-gather.7.cloned.1.call-done = bf16[768,2048]{1,0:T(8,128)(2,1)} async-done(((bf16[192,2048]{1,0:T(8,128)(2,1)}), bf16[768,2048]{1,0:T(8,128)(2,1)}) %all-gather.7.cloned.1.call-update) | async-done | bytes 3145744 | tf_op jit(solution)/shard_map/all_gather | solution.py:86
  206.0 1.0 constant_dynamic-slice_fusion.1
  207.2 5.0 %fusion.9 = bf16[576,2048]{1,0:T(8,128)(2,1)} fusion(s32[]{:T(128)S(6)} %select_n.66, bf16[768,2048]{1,0:T(8,128)(2,1)} %all-gather.7.cloned.1.call-done), kind=kLoop, calls=%fused_computation.33 | loop fusion | flops 4718592 | bytes 5505028 | tf_op jit(solution)/shard_map/concatenate | solution.py:50
  212.4 2.6 constant_dynamic-slice_fusion.5
  214.9 1.5 fusion.10
  216.4 3.6 fusion.40
  220.0 2.4 convolution_add_fusion.2
  222.5 3.4 copy-done.1
  225.9 4.9 %fusion.3 = bf16[512,2048]{1,0:T(8,128)(2,1)} fusion(f32[1024,2048]{1,0:T(8,128)S(1)} %convolution_add_fusion.2, bf16[576,2048]{1,0:T(8,128)(2,1)} %collective-permute-done.2, bf16[576,1024]{1,0:T(8,128)(2,1)S(1)} %fusion.10), kind=kOutput, calls=%fused_computation.19 | convolution fusion | flops 1210056704 | bytes 9240576 | tf_op jit(solution)/shard_map/dot_general | solution.py:24
  230.8 35.0 %collective-permute-done.1 = bf16[576,2048]{1,0:T(8,128)(2,1)} collective-permute-done((bf16[576,2048]{1,0:T(8,128)(2,1)}, bf16[576,2048]{1,0:T(8,128)(2,1)}, u32[]{:S(2)}, u32[]{:S(2)}) %collective-permute-start.1) | collective-permute-done | bytes 2359328 | tf_op jit(solution)/shard_map/ppermute | solution.py:30
  265.8 2.6 all-gather.9.cloned.1.call-done
  268.4 2.1 constant_dynamic-slice_fusion
  270.5 4.9 %fusion = bf16[512,2048]{1,0:T(8,128)(2,1)S(1)} fusion(f32[1024,2048]{1,0:T(8,128)} %copy-done.1, bf16[576,2048]{1,0:T(8,128)(2,1)} %collective-permute-done.2, bf16[576,1024]{1,0:T(8,128)(2,1)S(1)} %fusion.10), kind=kOutput, calls=%fused_computation.14 | convolution fusion | flops 1210056704 | bytes 9240576 | tf_op jit(solution)/shard_map/dot_general | solution.py:24
  275.5 4.0 fusion.39
  279.5 2.4 convolution_add_fusion.3
  281.9 5.7 %fusion.5 = bf16[512,2048]{1,0:T(8,128)(2,1)} fusion(f32[1024,2048]{1,0:T(8,128)S(1)} %convolution_add_fusion.3, bf16[512,2048]{1,0:T(8,128)(2,1)} %collective-permute-done.3, bf16[576,2048]{1,0:T(8,128)(2,1)} %collective-permute-done.1, bf16[576,1024]{1,0:T(8,128)(2,1)S(1)} %fusion.10), kind=kOutput, calls=%fused_computation.22 | convolution fusion | flops 1212153856 | bytes 11337728 | tf_op jit(solution)/shard_map/dot_general | solution.py:24
  287.6 1.5 collective-permute-start.6
  289.1 5.1 %fusion.2 = bf16[512,2048]{1,0:T(8,128)(2,1)} fusion(f32[1024,2048]{1,0:T(8,128)S(1)} %convolution_add_fusion.3, bf16[512,2048]{1,0:T(8,128)(2,1)S(1)} %collective-permute-done.4, bf16[576,2048]{1,0:T(8,128)(2,1)} %collective-permute-done.1, bf16[576,1024]{1,0:T(8,128)(2,1)S(1)} %fusion.10), kind=kOutput, calls=%fused_computation.17 | convolution fusion | flops 1212153856 | bytes 11337728 | tf_op jit(solution)/shard_map/dot_general | solution.py:24
  294.2 0.9 collective-permute-start.7
  295.0 4.1 fusion.7
  299.1 1.5 collective-permute-start.5
  300.6 32.2 %all-gather.11.cloned.1.call-done = bf16[768,2048]{1,0:T(8,128)(2,1)} async-done(((bf16[192,2048]{1,0:T(8,128)(2,1)}), bf16[768,2048]{1,0:T(8,128)(2,1)}) %all-gather.11.cloned.1.call-update) | async-done | bytes 3145744 | tf_op jit(solution)/shard_map/all_gather | solution.py:86
  332.8 3.9 fusion.6
  336.7 44.2 %collective-permute-done.7 = bf16[512,2048]{1,0:T(8,128)(2,1)} collective-permute-done((bf16[512,2048]{1,0:T(8,128)(2,1)}, bf16[512,2048]{1,0:T(8,128)(2,1)}, u32[]{:S(2)}, u32[]{:S(2)}) %collective-permute-start.7) | collective-permute-done | bytes 2097184 | tf_op jit(solution)/shard_map/ppermute | solution.py:30
  380.9 1.5 collective-permute-start.8
  382.4 3.5 fusion.41
  386.0 2.6 convolution_add_fusion.1
  388.6 5.7 %fusion.42 = f32[1024,2048]{1,0:T(8,128)} fusion(bf16[768,1024]{1,0:T(8,128)(2,1)S(1)} %bitcast.36, bf16[768,2048]{1,0:T(8,128)(2,1)S(1)} %copy-done.6), kind=kOutput, calls=%fused_computation.76 | convolution fusion | flops 3221225472 | bytes 13107200 | tf_op jit(solution)/shard_map/dot_general | solution.py:24
  394.3 4.9 %convolution_add_fusion = f32[1024,2048]{1,0:T(8,128)S(1)} fusion(f32[1024,2048]{1,0:T(8,128)} %fusion.42, bf16[192,8192]{1,0:T(8,128)(2,1)} %collective-permute-done, s32[]{:T(128)S(6)} %select_n.68, bf16[768,1024]{1,0:T(8,128)(2,1)S(1)} %bitcast.31, s32[]{:T(128)S(6)} %select_n.62), kind=kOutput, calls=%fused_computation.9 | convolution fusion | flops 807403520 | bytes 17956872 | tf_op jit(solution)/shard_map/dot_general | solution.py:24
  399.3 34.6 %collective-permute-done.8 = bf16[576,2048]{1,0:T(8,128)(2,1)S(1)} collective-permute-done((bf16[576,2048]{1,0:T(8,128)(2,1)S(1)}, bf16[576,2048]{1,0:T(8,128)(2,1)S(1)}, u32[]{:S(2)}, u32[]{:S(2)}) %collective-permute-start.8) | collective-permute-done | bytes 2359328 | tf_op jit(solution)/shard_map/ppermute | solution.py:30
  433.9 3.5 slice_add_fusion.5
  437.5 5.6 %slice_add_fusion.4 = f32[512,2048]{1,0:T(8,128)} fusion(f32[1024,2048]{1,0:T(8,128)S(1)} %convolution_add_fusion.1, bf16[576,2048]{1,0:T(8,128)(2,1)} %collective-permute-done.5, bf16[576,1024]{1,0:T(8,128)(2,1)S(1)} %fusion.10), kind=kOutput, calls=%fused_computation.24 | convolution fusion | flops 1209008128 | bytes 11337728 | tf_op jit(solution)/shard_map/dot_general | solution.py:24
  443.5 1.9 fusion.25
  445.4 1.8 fusion.17
  447.3 6.4 %convert_add_fusion = f32[512,2048]{1,0:T(8,128)} fusion(bf16[512,2048]{1,0:T(8,128)(2,1)} %collective-permute-done.6, f32[512,2048]{1,0:T(8,128)} %collective-permute-done.9, f32[512,2048]{1,0:T(8,128)S(1)} %fusion.25, f32[1024,2048]{1,0:T(8,128)S(1)} %convolution_add_fusion), kind=kLoop, calls=%fused_computation.25 | loop fusion | flops 4194304 | bytes 18874368 | tf_op jit(solution)/shard_map/add | solution.py:103
  453.7 6.8 %dynamic_update_slice.6 = f32[1024,2048]{1,0:T(8,128)} pad(f32[512,2048]{1,0:T(8,128)} %convert_add_fusion, f32[]{:T(128)} %constant.50.clone.1), padding=0_512x0_0 | pad | bytes 12582916 | tf_op jit(solution)/shard_map/dynamic_update_slice | solution.py:103
  460.6 6.5 %add_dynamic-update-slice_fusion = f32[1024,2048]{1,0:T(8,128)} fusion(f32[1024,2048]{1,0:T(8,128)} %dynamic_update_slice.6, bf16[512,2048]{1,0:T(8,128)(2,1)} %collective-permute-done.7, f32[512,2048]{1,0:T(8,128)} %collective-permute-done.10, f32[512,2048]{1,0:T(8,128)S(1)} %fusion.17, f32[1024,2048]{1,0:T(8,128)S(1)} %convolution_add_fusion), kind=kLoop, calls=%fused_computation.23 | loop fusion | flops 4194304 | bytes 18874368 | tf_op jit(solution)/shard_map/dynamic_update_slice | solution.py:103
  (44 shorter events, 2.6 us)
Async XLA Ops:
  6.5 75.9 %copy-start = (bf16[192,8192]{1,0:T(8,128)(2,1)S(1)}, bf16[192,8192]{1,0:T(8,128)(2,1)}, u32[]{:S(2)}) copy-start(bf16[192,8192]{1,0:T(8,128)(2,1)} %param.6) | copy-start | bytes 9437188
  6.5 73.8 %all-gather.5.cloned.1.call-start = ((), (), s32[]{:S(2)}) async-start(), calls=%async_computation.1 | async-start | bytes 3932160 | tf_op jit(solution)/shard_map/all_gather | solution.py:54
  8.8 197.2 %all-gather.7.cloned.1.call-start = ((), (), s32[]{:S(2)}) async-start(), calls=%async_computation.2 | async-start | bytes 3932160 | tf_op jit(solution)/shard_map/all_gather | solution.py:86
  8.9 71.5 %collective-permute-start = (bf16[192,8192]{1,0:T(8,128)(2,1)}, bf16[192,8192]{1,0:T(8,128)(2,1)}, u32[]{:S(2)}, u32[]{:S(2)}) collective-permute-start(bf16[192,8192]{1,0:T(8,128)(2,1)} %param.6), channel_id=1, source_target_pairs={{0,1},{1,0},{2,3},{3,2},{4,5},{5,4},{6,7},{7,6},{8,9},{9,8},{10,11... | collective-permute-start | bytes 9437192 | tf_op jit(solution)/shard_map/ppermute | solution.py:30
  85.3 127.1 %all-to-all-start = ((bf16[192,8,1024]{2,0,1:T(8,128)(2,1)}), bf16[192,8,1024]{2,0,1:T(8,128)(2,1)}, u32[]{:S(2)}, u32[]{:S(2)}) async-start(bf16[192,8,1024]{2,0,1:T(8,128)(2,1)} %bitcast.26), calls=%async_computation | async-start | bytes 6291456 | tf_op jit(solution)/shard_map/all_to_all | solution.py:57
  91.3 177.1 %all-gather.9.cloned.1.call-start = ((), (), s32[]{:S(2)}) async-start(), calls=%async_computation.3 | async-start | bytes 3932160 | tf_op jit(solution)/shard_map/all_gather | solution.py:86
  96.5 79.0 %collective-permute-start.2 = (bf16[576,2048]{1,0:T(8,128)(2,1)}, bf16[576,2048]{1,0:T(8,128)(2,1)}, u32[]{:S(2)}, u32[]{:S(2)}) collective-permute-start(bf16[576,2048]{1,0:T(8,128)(2,1)} %fusion.8), channel_id=1, source_target_pairs={{0,1},{1,0},{2,3},{3,2},{4,5},{5,4},{6,7},{7,6},{8,9},{9,8},{10,11... | collective-permute-start | bytes 7077896 | tf_op jit(solution)/shard_map/ppermute | solution.py:30
  207.0 125.8 %all-gather.11.cloned.1.call-start = ((), (), s32[]{:S(2)}) async-start(), calls=%async_computation.4 | async-start | bytes 3932160 | tf_op jit(solution)/shard_map/all_gather | solution.py:86
  212.3 53.5 %collective-permute-start.1 = (bf16[576,2048]{1,0:T(8,128)(2,1)}, bf16[576,2048]{1,0:T(8,128)(2,1)}, u32[]{:S(2)}, u32[]{:S(2)}) collective-permute-start(bf16[576,2048]{1,0:T(8,128)(2,1)} %fusion.9), channel_id=1, source_target_pairs={{0,1},{1,0},{2,3},{3,2},{4,5},{5,4},{6,7},{7,6},{8,9},{9,8},{10,11... | collective-permute-start | bytes 7077896 | tf_op jit(solution)/shard_map/ppermute | solution.py:30
  212.4 4.1 copy-start.2
  214.9 1.5 copy-start.7
  222.5 3.4 copy-start.1
  230.8 51.1 %collective-permute-start.3 = (bf16[512,2048]{1,0:T(8,128)(2,1)}, bf16[512,2048]{1,0:T(8,128)(2,1)}, u32[]{:S(2)}, u32[]{:S(2)}) collective-permute-start(bf16[512,2048]{1,0:T(8,128)(2,1)} %fusion.3), channel_id=1, source_target_pairs={{0,8},{8,0},{1,9},{9,1},{2,10},{10,2},{3,11},{11,3},{4,12},{12,4},... | collective-permute-start | bytes 6291464 | tf_op jit(solution)/shard_map/ppermute | solution.py:30
  270.5 5.0 %copy-start.3 = (bf16[768,2048]{1,0:T(8,128)(2,1)S(1)}, bf16[768,2048]{1,0:T(8,128)(2,1)}, u32[]{:S(2)}) copy-start(bf16[768,2048]{1,0:T(8,128)(2,1)} %all-gather.7.cloned.1.call-done) | copy-start | bytes 9437188
  270.5 5.0 %copy-start.8 = (bf16[4,1,192,1024]{3,2,1,0:T(8,128)(2,1)S(1)}, bf16[4,1,192,1024]{3,2,1,0:T(8,128)(2,1)}, u32[]{:S(2)}) copy-start(bf16[4,1,192,1024]{3,2,1,0:T(8,128)(2,1)} %copy-done.7) | copy-start | bytes 4718596
  275.4 13.7 %collective-permute-start.4 = (bf16[512,2048]{1,0:T(8,128)(2,1)S(1)}, bf16[512,2048]{1,0:T(8,128)(2,1)S(1)}, u32[]{:S(2)}, u32[]{:S(2)}) collective-permute-start(bf16[512,2048]{1,0:T(8,128)(2,1)S(1)} %fusion), channel_id=1, source_target_pairs={{0,8},{8,0},{1,9},{9,1},{2,10},{10,2},{3,11},{11,3},{4,12},{12,4},... | collective-permute-start | bytes 6291464 | tf_op jit(solution)/shard_map/ppermute | solution.py:30
  287.6 7.4 %copy-start.4 = (bf16[768,2048]{1,0:T(8,128)(2,1)S(1)}, bf16[768,2048]{1,0:T(8,128)(2,1)}, u32[]{:S(2)}) copy-start(bf16[768,2048]{1,0:T(8,128)(2,1)} %all-gather.9.cloned.1.call-done) | copy-start | bytes 9437188
  287.6 49.1 %collective-permute-start.6 = (bf16[512,2048]{1,0:T(8,128)(2,1)}, bf16[512,2048]{1,0:T(8,128)(2,1)}, u32[]{:S(2)}, u32[]{:S(2)}) collective-permute-start(bf16[512,2048]{1,0:T(8,128)(2,1)} %fusion.5), channel_id=1, source_target_pairs={{0,16},{16,0},{1,17},{17,1},{2,18},{18,2},{3,19},{19,3},{4,20},{20... | collective-permute-start | bytes 6291464 | tf_op jit(solution)/shard_map/ppermute | solution.py:30
  294.2 86.8 %collective-permute-start.7 = (bf16[512,2048]{1,0:T(8,128)(2,1)}, bf16[512,2048]{1,0:T(8,128)(2,1)}, u32[]{:S(2)}, u32[]{:S(2)}) collective-permute-start(bf16[512,2048]{1,0:T(8,128)(2,1)} %fusion.2), channel_id=1, source_target_pairs={{0,16},{16,0},{1,17},{17,1},{2,18},{18,2},{3,19},{19,3},{4,20},{20... | collective-permute-start | bytes 6291464 | tf_op jit(solution)/shard_map/ppermute | solution.py:30
  299.1 100.2 %collective-permute-start.5 = (bf16[576,2048]{1,0:T(8,128)(2,1)}, bf16[576,2048]{1,0:T(8,128)(2,1)}, u32[]{:S(2)}, u32[]{:S(2)}) collective-permute-start(bf16[576,2048]{1,0:T(8,128)(2,1)} %fusion.7), channel_id=1, source_target_pairs={{0,1},{1,0},{2,3},{3,2},{4,5},{5,4},{6,7},{7,6},{8,9},{9,8},{10,11... | collective-permute-start | bytes 7077896 | tf_op jit(solution)/shard_map/ppermute | solution.py:30
  332.8 49.6 %copy-start.5 = (bf16[768,2048]{1,0:T(8,128)(2,1)S(1)}, bf16[768,2048]{1,0:T(8,128)(2,1)}, u32[]{:S(2)}) copy-start(bf16[768,2048]{1,0:T(8,128)(2,1)} %all-gather.9.cloned.1.call-done) | copy-start | bytes 9437188
  332.8 49.6 %copy-start.9 = (bf16[4,1,192,1024]{3,2,1,0:T(8,128)(2,1)S(1)}, bf16[4,1,192,1024]{3,2,1,0:T(8,128)(2,1)}, u32[]{:S(2)}) copy-start(bf16[4,1,192,1024]{3,2,1,0:T(8,128)(2,1)} %copy-done.7) | copy-start | bytes 4718596
  380.9 52.9 %collective-permute-start.8 = (bf16[576,2048]{1,0:T(8,128)(2,1)S(1)}, bf16[576,2048]{1,0:T(8,128)(2,1)S(1)}, u32[]{:S(2)}, u32[]{:S(2)}) collective-permute-start(bf16[576,2048]{1,0:T(8,128)(2,1)S(1)} %fusion.6), channel_id=1, source_target_pairs={{0,1},{1,0},{2,3},{3,2},{4,5},{5,4},{6,7},{7,6},{8,9},{9,8},{10,11... | collective-permute-start | bytes 7077896 | tf_op jit(solution)/shard_map/ppermute | solution.py:30
  385.9 2.6 copy-start.6
  437.4 9.9 %collective-permute-start.9 = (f32[512,2048]{1,0:T(8,128)S(1)}, f32[512,2048]{1,0:T(8,128)}, u32[]{:S(2)}, u32[]{:S(2)}) collective-permute-start(f32[512,2048]{1,0:T(8,128)S(1)} %slice_add_fusion.5), channel_id=1, source_target_pairs={{0,8},{8,0},{1,9},{9,1},{2,10},{10,2},{3,11},{11,3},{4,12},{12,4},... | collective-permute-start | bytes 12582920 | tf_op jit(solution)/shard_map/ppermute | solution.py:30
  443.0 17.5 %collective-permute-start.10 = (f32[512,2048]{1,0:T(8,128)}, f32[512,2048]{1,0:T(8,128)}, u32[]{:S(2)}, u32[]{:S(2)}) collective-permute-start(f32[512,2048]{1,0:T(8,128)} %slice_add_fusion.4), channel_id=1, source_target_pairs={{0,8},{8,0},{1,9},{9,1},{2,10},{10,2},{3,11},{11,3},{4,12},{12,4},... | collective-permute-start | bytes 12582920 | tf_op jit(solution)/shard_map/ppermute | solution.py:30
Sparse Core Ops, SparseCore 0:
  8.9 66.1 all-gather.4
  82.6 123.4 all-gather.6
  207.6 60.7 all-gather.8
  270.6 62.1 all-gather.10

commit v11 on v10

--- a/solution.py
+++ b/solution.py
@@ -66,7 +66,7 @@
             for k, m in enumerate(order):
                 cols_a = lax.dynamic_slice_in_dim(theirs_own, m * rw, rw, axis=1)
                 early.append(contract(s_a, cols_a) + contract(s_mine, mine[k]))
-            halves = 2 if width % 16 == 0 else 1
+            halves = 4 if width % 32 == 0 else 1
             hw = width // halves
             cuts = [slice(h * hw, (h + 1) * hw) for h in range(halves)]
             sent, got_x = [], []

time: 478 us -> 476 us (level)
  waiting for transfers between devices: 321 us -> 330 us
  matrix products: 62.6 us -> 54 us
    ppermute x11 -> x17, waiting for transfers between devices: 256 us -> 270 us  [swap(): return lax.ppermute(x, axis, [(0, 1), (1, 0)])]
    dot_general x16 -> x24, matrix products: 62.6 us -> 54 us  [contract(): lax.dot_general(left, right, (((0,), (0,)), ((), ())), preferred_element_...]
    dynamic_update_slice x1, local copies, waits for them, and re-layouts: 6.82 us -> 1.03 us  [body(): lax.dynamic_update_slice_in_dim(out, own_x + got_x[h].astype(jnp.float32)...]
    all_gather x3, waiting for transfers between devices: 65.3 us -> 59.5 us  [body(): lax.all_gather(lax.dynamic_slice_in_dim(rest, m * rw, rw, axis=1), 'az',...]
    ppermute x11 -> x17, starting transfers between devices: 11 us -> 14.1 us  [swap(): return lax.ppermute(x, axis, [(0, 1), (1, 0)])]
  transfers between devices with their start and end apart: 16 -> 22, of which waited for: 8 -> 11; matrix products, arithmetic and copies ran while one was open for 22% -> 19% of each run, Pallas kernels for 0% -> 0%
where the time goes in v11:
time: 476 us; the launch traced here: 471 us
  waiting for transfers between devices  330 us (69%)
  matrix products  54 us (11%)
  other arithmetic  31.7 us (7%)
  starting transfers between devices  20.7 us (4%)
  local copies, waits for them, and re-layouts  19.6 us (4%)
  between operations  15 us (3%)
    ppermute x17, waiting for transfers between devices, swap(): return lax.ppermute(x, axis, [(0, 1), (1, 0)])  270 us
    all_gather x3, waiting for transfers between devices, body(): lax.all_gather(lax.dynamic_slice_in_dim(rest, m * rw, rw, axis=1), 'az',...  59.5 us
    dot_general x24, matrix products, contract(): lax.dot_general(left, right, (((0,), (0,)), ((), ())), preferred_element_...  54 us
    concatenate x5, other arithmetic, others(): doubled = jnp.concatenate([v, v], axis=0)  20 us
    ppermute x17, starting transfers between devices, swap(): return lax.ppermute(x, axis, [(0, 1), (1, 0)])  14.1 us
  transfers between devices with their start and end apart: 22, of which 11 were waited for; matrix products, arithmetic and copies ran while one was open for 19% of the time, Pallas kernels for 0%

profile of v11, /device:TPU:0, one launch (start us, length us, event | category | flops | bytes accessed | tf_op | source)
XLA Modules:
  0.0 471.1 jit_solution(12496241205369001959)
XLA Ops:
  6.5 2.2 constant_dynamic-slice_fusion.3
  8.9 3.0 collective-permute-start
  14.3 66.0 %collective-permute-done = bf16[192,8192]{1,0:T(8,128)(2,1)} collective-permute-done((bf16[192,8192]{1,0:T(8,128)(2,1)}, bf16[192,8192]{1,0:T(8,128)(2,1)}, u32[]{:S(2)}, u32[]{:S(2)}) %collective-permute-start) | collective-permute-done | bytes 3145760 | tf_op jit(solution)/shard_map/ppermute | solution.py:30
  80.3 2.1 constant_dynamic-slice_fusion.2
  83.2 2.1 copy.12
  85.3 6.3 %all-to-all-start = ((bf16[192,8,1024]{2,0,1:T(8,128)(2,1)}), bf16[192,8,1024]{2,0,1:T(8,128)(2,1)}, u32[]{:S(2)}, u32[]{:S(2)}) async-start(bf16[192,8,1024]{2,0,1:T(8,128)(2,1)} %bitcast.34), calls=%async_computation | async-start | bytes 6291456 | tf_op jit(solution)/shard_map/all_to_all | solution.py:57
  91.7 3.9 fusion.14
  95.6 2.0 collective-permute-start.2
  97.5 78.3 %collective-permute-done.2 = bf16[576,2048]{1,0:T(8,128)(2,1)S(1)} collective-permute-done((bf16[576,2048]{1,0:T(8,128)(2,1)}, bf16[576,2048]{1,0:T(8,128)(2,1)S(1)}, u32[]{:S(2)}, u32[]{:S(2)}) %collective-permute-start.2) | collective-permute-done | bytes 2359328 | tf_op jit(solution)/shard_map/ppermute | solution.py:30
  175.8 30.2 %all-gather.7.cloned.1.call-done = bf16[768,2048]{1,0:T(8,128)(2,1)} async-done(((bf16[192,2048]{1,0:T(8,128)(2,1)}), bf16[768,2048]{1,0:T(8,128)(2,1)}) %all-gather.7.cloned.1.call-update) | async-done | bytes 3145744 | tf_op jit(solution)/shard_map/all_gather | solution.py:86
  206.1 2.1 constant_dynamic-slice_fusion.1
  208.5 5.1 %fusion.15 = bf16[576,2048]{1,0:T(8,128)(2,1)} fusion(s32[]{:T(128)S(6)} %select_n.66, bf16[768,2048]{1,0:T(8,128)(2,1)} %all-gather.7.cloned.1.call-done), kind=kLoop, calls=%fused_computation.39 | loop fusion | flops 4718592 | bytes 5505028 | tf_op jit(solution)/shard_map/concatenate | solution.py:50
  213.8 2.6 constant_dynamic-slice_fusion.5
  216.4 1.5 fusion.16
  218.0 3.6 fusion.62
  221.5 2.6 convolution_add_fusion.2
  224.2 2.5 fusion.11
  227.9 39.1 %collective-permute-done.1 = bf16[576,2048]{1,0:T(8,128)(2,1)S(1)} collective-permute-done((bf16[576,2048]{1,0:T(8,128)(2,1)}, bf16[576,2048]{1,0:T(8,128)(2,1)S(1)}, u32[]{:S(2)}, u32[]{:S(2)}) %collective-permute-start.1) | collective-permute-done | bytes 2359328 | tf_op jit(solution)/shard_map/ppermute | solution.py:30
  266.9 2.2 all-gather.9.cloned.1.call-done
  269.1 2.1 constant_dynamic-slice_fusion
  271.3 3.5 fusion.9
  274.8 2.6 fusion.7
  278.0 3.2 fusion.5
  281.4 3.8 fusion.61
  285.2 2.6 convolution_add_fusion.3
  287.8 3.3 fusion.10
  291.0 1.4 collective-permute-start.11
  292.5 2.0 fusion.8
  295.1 2.0 fusion.6
  298.5 2.0 fusion.4
  301.1 4.0 fusion.13
  305.1 1.4 collective-permute-start.7
  306.5 27.0 %all-gather.11.cloned.1.call-done = bf16[768,2048]{1,0:T(8,128)(2,1)} async-done(((bf16[192,2048]{1,0:T(8,128)(2,1)}), bf16[768,2048]{1,0:T(8,128)(2,1)}) %all-gather.11.cloned.1.call-update) | async-done | bytes 3145744 | tf_op jit(solution)/shard_map/all_gather | solution.py:86
  333.6 5.5 %fusion.12 = bf16[576,2048]{1,0:T(8,128)(2,1)} fusion(s32[]{:T(128)S(6)} %select_n.66, bf16[768,2048]{1,0:T(8,128)(2,1)} %all-gather.11.cloned.1.call-done), kind=kLoop, calls=%fused_computation.36 | loop fusion | flops 4718592 | bytes 5505028 | tf_op jit(solution)/shard_map/concatenate | solution.py:50
  339.8 22.5 %collective-permute-done.9 = bf16[256,2048]{1,0:T(8,128)(2,1)} collective-permute-done((bf16[256,2048]{1,0:T(8,128)(2,1)}, bf16[256,2048]{1,0:T(8,128)(2,1)}, u32[]{:S(2)}, u32[]{:S(2)}) %collective-permute-start.9) | collective-permute-done | bytes 1048608 | tf_op jit(solution)/shard_map/ppermute | solution.py:30
  362.3 22.0 %collective-permute-done.8 = bf16[256,2048]{1,0:T(8,128)(2,1)} collective-permute-done((bf16[256,2048]{1,0:T(8,128)(2,1)}, bf16[256,2048]{1,0:T(8,128)(2,1)}, u32[]{:S(2)}, u32[]{:S(2)}) %collective-permute-start.8) | collective-permute-done | bytes 1048608 | tf_op jit(solution)/shard_map/ppermute | solution.py:30
  384.3 1.4 collective-permute-start.12
  385.7 3.5 fusion.63
  389.3 2.6 convolution_add_fusion.1
  391.9 3.5 fusion.64
  395.4 2.5 convolution_add_fusion
  397.9 39.5 %collective-permute-done.12 = bf16[576,2048]{1,0:T(8,128)(2,1)S(1)} collective-permute-done((bf16[576,2048]{1,0:T(8,128)(2,1)}, bf16[576,2048]{1,0:T(8,128)(2,1)S(1)}, u32[]{:S(2)}, u32[]{:S(2)}) %collective-permute-start.12) | collective-permute-done | bytes 2359328 | tf_op jit(solution)/shard_map/ppermute | solution.py:30
  446.9 2.4 collective-permute-done.13
  449.2 2.0 convert_add_fusion
  452.3 2.7 add_dynamic-update-slice_fusion.2
  455.0 2.7 add_dynamic-update-slice_fusion.1
  457.7 3.4 copy-done.7
  461.0 3.3 add_dynamic-update-slice_fusion
  (84 shorter events, 18.3 us)
Async XLA Ops:
  6.5 7.4 %copy-start.18 = (s32[192]{0:T(256)S(1)}, s32[192]{0:T(256)}, u32[]{:S(2)}) copy-start(s32[192]{0:T(256)} %param.7) | copy-start | bytes 2308
  6.5 7.5 %copy-start.17 = (f32[1536]{0:T(1024)S(1)}, f32[1536]{0:T(1024)}, u32[]{:S(2)}) copy-start(f32[1536]{0:T(1024)} %param.9) | copy-start | bytes 18436
  6.5 73.8 %all-gather.5.cloned.1.call-start = ((), (), s32[]{:S(2)}) async-start(), calls=%async_computation.1 | async-start | bytes 3932160 | tf_op jit(solution)/shard_map/all_gather | solution.py:54
  6.5 75.9 %copy-start.6 = (bf16[192,8192]{1,0:T(8,128)(2,1)S(1)}, bf16[192,8192]{1,0:T(8,128)(2,1)}, u32[]{:S(2)}) copy-start(bf16[192,8192]{1,0:T(8,128)(2,1)} %param.6) | copy-start | bytes 9437188
  8.8 197.3 %all-gather.7.cloned.1.call-start = ((), (), s32[]{:S(2)}) async-start(), calls=%async_computation.2 | async-start | bytes 3932160 | tf_op jit(solution)/shard_map/all_gather | solution.py:86
  8.9 71.5 %collective-permute-start = (bf16[192,8192]{1,0:T(8,128)(2,1)}, bf16[192,8192]{1,0:T(8,128)(2,1)}, u32[]{:S(2)}, u32[]{:S(2)}) collective-permute-start(bf16[192,8192]{1,0:T(8,128)(2,1)} %param.6), channel_id=1, source_target_pairs={{0,1},{1,0},{2,3},{3,2},{4,5},{5,4},{6,7},{7,6},{8,9},{9,8},{10,11... | collective-permute-start | bytes 9437192 | tf_op jit(solution)/shard_map/ppermute | solution.py:30
  85.3 6.4 %copy-start.8 = (bf16[768,2048]{1,0:T(8,128)(2,1)S(1)}, bf16[768,2048]{1,0:T(8,128)(2,1)}, u32[]{:S(2)}) copy-start(bf16[768,2048]{1,0:T(8,128)(2,1)} %all-gather.5.cloned.1.call-done) | copy-start | bytes 9437188
  85.3 128.5 %all-to-all-start = ((bf16[192,8,1024]{2,0,1:T(8,128)(2,1)}), bf16[192,8,1024]{2,0,1:T(8,128)(2,1)}, u32[]{:S(2)}, u32[]{:S(2)}) async-start(bf16[192,8,1024]{2,0,1:T(8,128)(2,1)} %bitcast.34), calls=%async_computation | async-start | bytes 6291456 | tf_op jit(solution)/shard_map/all_to_all | solution.py:57
  91.6 177.5 %all-gather.9.cloned.1.call-start = ((), (), s32[]{:S(2)}) async-start(), calls=%async_computation.3 | async-start | bytes 3932160 | tf_op jit(solution)/shard_map/all_gather | solution.py:86
  95.6 80.3 %collective-permute-start.2 = (bf16[576,2048]{1,0:T(8,128)(2,1)}, bf16[576,2048]{1,0:T(8,128)(2,1)S(1)}, u32[]{:S(2)}, u32[]{:S(2)}) collective-permute-start(bf16[576,2048]{1,0:T(8,128)(2,1)} %fusion.14), channel_id=1, source_target_pairs={{0,1},{1,0},{2,3},{3,2},{4,5},{5,4},{6,7},{7,6},{8,9},{9,8},{10,11... | collective-permute-start | bytes 7077896 | tf_op jit(solution)/shard_map/ppermute | solution.py:30
  175.8 32.6 %copy-start = (bf16[576,2048]{1,0:T(8,128)(2,1)}, bf16[576,2048]{1,0:T(8,128)(2,1)S(1)}, u32[]{:S(2)}) copy-start(bf16[576,2048]{1,0:T(8,128)(2,1)S(1)} %collective-permute-done.2) | copy-start | bytes 7077892
  208.2 125.3 %all-gather.11.cloned.1.call-start = ((), (), s32[]{:S(2)}) async-start(), calls=%async_computation.4 | async-start | bytes 3932160 | tf_op jit(solution)/shard_map/all_gather | solution.py:86
  213.5 53.4 %collective-permute-start.1 = (bf16[576,2048]{1,0:T(8,128)(2,1)}, bf16[576,2048]{1,0:T(8,128)(2,1)S(1)}, u32[]{:S(2)}, u32[]{:S(2)}) collective-permute-start(bf16[576,2048]{1,0:T(8,128)(2,1)} %fusion.15), channel_id=1, source_target_pairs={{0,1},{1,0},{2,3},{3,2},{4,5},{5,4},{6,7},{7,6},{8,9},{9,8},{10,11... | collective-permute-start | bytes 7077896 | tf_op jit(solution)/shard_map/ppermute | solution.py:30
  213.8 4.1 copy-start.9
  216.4 1.5 copy-start.14
  216.4 5.1 %copy-start.4 = (bf16[4,1,192,1024]{3,2,1,0:T(8,128)(2,1)}, bf16[4,1,192,1024]{3,2,1,0:T(8,128)(2,1)S(1)}, u32[]{:S(2)}) copy-start(bf16[4,1,192,1024]{3,2,1,0:T(8,128)(2,1)S(1)} %get-tuple-element.25) | copy-start | bytes 4718596
  221.5 2.6 copy-start.1
  224.2 3.7 copy-start.3
  227.9 59.9 %collective-permute-start.6 = (bf16[256,2048]{1,0:T(8,128)(2,1)}, bf16[256,2048]{1,0:T(8,128)(2,1)}, u32[]{:S(2)}, u32[]{:S(2)}) collective-permute-start(bf16[256,2048]{1,0:T(8,128)(2,1)} %fusion.11), channel_id=1, source_target_pairs={{0,8},{8,0},{1,9},{9,1},{2,10},{10,2},{3,11},{11,3},{4,12},{12,4},... | collective-permute-start | bytes 3145736 | tf_op jit(solution)/shard_map/ppermute | solution.py:30
  271.2 3.6 copy-start.2
  274.7 17.8 %collective-permute-start.5 = (bf16[256,2048]{1,0:T(8,128)(2,1)S(1)}, bf16[256,2048]{1,0:T(8,128)(2,1)S(1)}, u32[]{:S(2)}, u32[]{:S(2)}) collective-permute-start(bf16[256,2048]{1,0:T(8,128)(2,1)S(1)} %fusion.9), channel_id=1, source_target_pairs={{0,8},{8,0},{1,9},{9,1},{2,10},{10,2},{3,11},{11,3},{4,12},{12,4},... | collective-permute-start | bytes 3145736 | tf_op jit(solution)/shard_map/ppermute | solution.py:30
  277.4 3.9 copy-start.12
  277.4 3.9 copy-start.15
  277.4 17.6 %collective-permute-start.4 = (bf16[256,2048]{1,0:T(8,128)(2,1)S(1)}, bf16[256,2048]{1,0:T(8,128)(2,1)S(1)}, u32[]{:S(2)}, u32[]{:S(2)}) collective-permute-start(bf16[256,2048]{1,0:T(8,128)(2,1)S(1)} %fusion.7), channel_id=1, source_target_pairs={{0,8},{8,0},{1,9},{9,1},{2,10},{10,2},{3,11},{11,3},{4,12},{12,4},... | collective-permute-start | bytes 3145736 | tf_op jit(solution)/shard_map/ppermute | solution.py:30
  281.3 17.2 %collective-permute-start.3 = (bf16[256,2048]{1,0:T(8,128)(2,1)S(1)}, bf16[256,2048]{1,0:T(8,128)(2,1)S(1)}, u32[]{:S(2)}, u32[]{:S(2)}) collective-permute-start(bf16[256,2048]{1,0:T(8,128)(2,1)S(1)} %fusion.5), channel_id=1, source_target_pairs={{0,8},{8,0},{1,9},{9,1},{2,10},{10,2},{3,11},{11,3},{4,12},{12,4},... | collective-permute-start | bytes 3145736 | tf_op jit(solution)/shard_map/ppermute | solution.py:30
  291.0 48.1 %collective-permute-start.11 = (bf16[256,2048]{1,0:T(8,128)(2,1)}, bf16[256,2048]{1,0:T(8,128)(2,1)}, u32[]{:S(2)}, u32[]{:S(2)}) collective-permute-start(bf16[256,2048]{1,0:T(8,128)(2,1)} %fusion.10), channel_id=1, source_target_pairs={{0,16},{16,0},{1,17},{17,1},{2,18},{18,2},{3,19},{19,3},{4,20},{20... | collective-permute-start | bytes 3145736 | tf_op jit(solution)/shard_map/ppermute | solution.py:30
  294.5 45.3 %collective-permute-start.10 = (bf16[256,2048]{1,0:T(8,128)(2,1)}, bf16[256,2048]{1,0:T(8,128)(2,1)}, u32[]{:S(2)}, u32[]{:S(2)}) collective-permute-start(bf16[256,2048]{1,0:T(8,128)(2,1)} %fusion.8), channel_id=1, source_target_pairs={{0,16},{16,0},{1,17},{17,1},{2,18},{18,2},{3,19},{19,3},{4,20},{20... | collective-permute-start | bytes 3145736 | tf_op jit(solution)/shard_map/ppermute | solution.py:30
  297.1 4.0 copy-start.10
  297.1 65.2 %collective-permute-start.9 = (bf16[256,2048]{1,0:T(8,128)(2,1)}, bf16[256,2048]{1,0:T(8,128)(2,1)}, u32[]{:S(2)}, u32[]{:S(2)}) collective-permute-start(bf16[256,2048]{1,0:T(8,128)(2,1)} %fusion.6), channel_id=1, source_target_pairs={{0,16},{16,0},{1,17},{17,1},{2,18},{18,2},{3,19},{19,3},{4,20},{20... | collective-permute-start | bytes 3145736 | tf_op jit(solution)/shard_map/ppermute | solution.py:30
  300.5 83.8 %collective-permute-start.8 = (bf16[256,2048]{1,0:T(8,128)(2,1)}, bf16[256,2048]{1,0:T(8,128)(2,1)}, u32[]{:S(2)}, u32[]{:S(2)}) collective-permute-start(bf16[256,2048]{1,0:T(8,128)(2,1)} %fusion.4), channel_id=1, source_target_pairs={{0,16},{16,0},{1,17},{17,1},{2,18},{18,2},{3,19},{19,3},{4,20},{20... | collective-permute-start | bytes 3145736 | tf_op jit(solution)/shard_map/ppermute | solution.py:30
  305.1 92.7 %collective-permute-start.7 = (bf16[576,2048]{1,0:T(8,128)(2,1)}, bf16[576,2048]{1,0:T(8,128)(2,1)S(1)}, u32[]{:S(2)}, u32[]{:S(2)}) collective-permute-start(bf16[576,2048]{1,0:T(8,128)(2,1)} %fusion.13), channel_id=1, source_target_pairs={{0,1},{1,0},{2,3},{3,2},{4,5},{5,4},{6,7},{7,6},{8,9},{9,8},{10,11... | collective-permute-start | bytes 7077896 | tf_op jit(solution)/shard_map/ppermute | solution.py:30
  333.6 52.2 %copy-start.11 = (bf16[768,2048]{1,0:T(8,128)(2,1)S(1)}, bf16[768,2048]{1,0:T(8,128)(2,1)}, u32[]{:S(2)}) copy-start(bf16[768,2048]{1,0:T(8,128)(2,1)} %all-gather.9.cloned.1.call-done) | copy-start | bytes 9437188
  333.6 52.2 %copy-start.16 = (bf16[4,1,192,1024]{3,2,1,0:T(8,128)(2,1)S(1)}, bf16[4,1,192,1024]{3,2,1,0:T(8,128)(2,1)}, u32[]{:S(2)}) copy-start(bf16[4,1,192,1024]{3,2,1,0:T(8,128)(2,1)} %copy-done.14) | copy-start | bytes 4718596
  339.1 50.1 %copy-start.5 = (bf16[4,1,192,1024]{3,2,1,0:T(8,128)(2,1)S(1)}, bf16[4,1,192,1024]{3,2,1,0:T(8,128)(2,1)}, u32[]{:S(2)}) copy-start(bf16[4,1,192,1024]{3,2,1,0:T(8,128)(2,1)} %copy-done.4) | copy-start | bytes 4718596
  384.3 53.0 %collective-permute-start.12 = (bf16[576,2048]{1,0:T(8,128)(2,1)}, bf16[576,2048]{1,0:T(8,128)(2,1)S(1)}, u32[]{:S(2)}, u32[]{:S(2)}) collective-permute-start(bf16[576,2048]{1,0:T(8,128)(2,1)} %fusion.12), channel_id=1, source_target_pairs={{0,1},{1,0},{2,3},{3,2},{4,5},{5,4},{6,7},{7,6},{8,9},{9,8},{10,11... | collective-permute-start | bytes 7077896 | tf_op jit(solution)/shard_map/ppermute | solution.py:30
  389.2 2.6 copy-start.13
  439.4 15.6 %collective-permute-start.15 = (f32[256,2048]{1,0:T(8,128)S(1)}, f32[256,2048]{1,0:T(8,128)}, u32[]{:S(2)}, u32[]{:S(2)}) collective-permute-start(f32[256,2048]{1,0:T(8,128)S(1)} %slice_add_fusion.1), channel_id=1, source_target_pairs={{0,8},{8,0},{1,9},{9,1},{2,10},{10,2},{3,11},{11,3},{4,12},{12,4},... | collective-permute-start | bytes 6291464 | tf_op jit(solution)/shard_map/ppermute | solution.py:30
  439.5 9.8 %collective-permute-start.13 = (f32[256,2048]{1,0:T(8,128)S(1)}, f32[256,2048]{1,0:T(8,128)S(1)}, u32[]{:S(2)}, u32[]{:S(2)}) collective-permute-start(f32[256,2048]{1,0:T(8,128)S(1)} %slice_add_fusion.3), channel_id=1, source_target_pairs={{0,8},{8,0},{1,9},{9,1},{2,10},{10,2},{3,11},{11,3},{4,12},{12,4},... | collective-permute-start | bytes 6291464 | tf_op jit(solution)/shard_map/ppermute | solution.py:30
  441.0 11.3 %collective-permute-start.14 = (f32[256,2048]{1,0:T(8,128)S(1)}, f32[256,2048]{1,0:T(8,128)}, u32[]{:S(2)}, u32[]{:S(2)}) collective-permute-start(f32[256,2048]{1,0:T(8,128)S(1)} %slice_add_fusion.2), channel_id=1, source_target_pairs={{0,8},{8,0},{1,9},{9,1},{2,10},{10,2},{3,11},{11,3},{4,12},{12,4},... | collective-permute-start | bytes 6291464 | tf_op jit(solution)/shard_map/ppermute | solution.py:30
  444.3 13.3 %collective-permute-start.16 = (f32[256,2048]{1,0:T(8,128)S(1)}, f32[256,2048]{1,0:T(8,128)S(1)}, u32[]{:S(2)}, u32[]{:S(2)}) collective-permute-start(f32[256,2048]{1,0:T(8,128)S(1)} %slice_add_fusion), channel_id=1, source_target_pairs={{0,8},{8,0},{1,9},{9,1},{2,10},{10,2},{3,11},{11,3},{4,12},{12,4},... | collective-permute-start | bytes 6291464 | tf_op jit(solution)/shard_map/ppermute | solution.py:30
  457.6 3.4 copy-start.7
Sparse Core Ops, SparseCore 0:
  8.9 66.1 all-gather.4
  82.6 123.4 all-gather.6
  208.3 60.7 all-gather.8
  271.4 62.1 all-gather.10

commit v12 on v11

--- a/solution.py
+++ b/solution.py
@@ -66,7 +66,7 @@
             for k, m in enumerate(order):
                 cols_a = lax.dynamic_slice_in_dim(theirs_own, m * rw, rw, axis=1)
                 early.append(contract(s_a, cols_a) + contract(s_mine, mine[k]))
-            halves = 4 if width % 32 == 0 else 1
+            halves = 8 if width % 64 == 0 else 1
             hw = width // halves
             cuts = [slice(h * hw, (h + 1) * hw) for h in range(halves)]
             sent, got_x = [], []

time: 476 us -> 479 us (level)
  waiting for transfers between devices: 330 us -> 307 us
  matrix products: 54 us -> 72.9 us
  starting transfers between devices: 20.7 us -> 28.1 us
    all_gather x3, waiting for transfers between devices: 59.5 us -> 5.34 us  [body(): lax.all_gather(lax.dynamic_slice_in_dim(rest, m * rw, rw, axis=1), 'az',...]
    all_gather x1, waiting for transfers between devices: 0.01 us -> 33.6 us  [body(): mine = [lax.all_gather(first, 'az', axis=0, tiled=True)]]
    dot_general x24 -> x40, matrix products: 54 us -> 72.9 us  [contract(): lax.dot_general(left, right, (((0,), (0,)), ((), ())), preferred_element_...]
    ppermute x17 -> x29, starting transfers between devices: 14.1 us -> 22.6 us  [swap(): return lax.ppermute(x, axis, [(0, 1), (1, 0)])]
    ppermute x17 -> x29, waiting for transfers between devices: 270 us -> 268 us  [swap(): return lax.ppermute(x, axis, [(0, 1), (1, 0)])]
    dynamic_update_slice x3 -> x7, other arithmetic: 8.67 us -> 9.74 us  [body(): lax.dynamic_update_slice_in_dim(out, own_x + got_x[h].astype(jnp.float32)...]
  transfers between devices with their start and end apart: 22 -> 34, of which waited for: 11 -> 14; matrix products, arithmetic and copies ran while one was open for 19% -> 23% of each run, Pallas kernels for 0% -> 0%
where the time goes in v12:
time: 479 us; the launch traced here: 475 us
  waiting for transfers between devices  307 us (64%)
  matrix products  72.9 us (15%)
  other arithmetic  32.5 us (7%)
  starting transfers between devices  28.1 us (6%)
  local copies, waits for them, and re-layouts  18.7 us (4%)
  between operations  15.4 us (3%)
    ppermute x29, waiting for transfers between devices, swap(): return lax.ppermute(x, axis, [(0, 1), (1, 0)])  268 us
    dot_general x40, matrix products, contract(): lax.dot_general(left, right, (((0,), (0,)), ((), ())), preferred_element_...  72.9 us
    all_gather x1, waiting for transfers between devices, body(): mine = [lax.all_gather(first, 'az', axis=0, tiled=True)]  33.6 us
    ppermute x29, starting transfers between devices, swap(): return lax.ppermute(x, axis, [(0, 1), (1, 0)])  22.6 us
    concatenate x5, other arithmetic, others(): doubled = jnp.concatenate([v, v], axis=0)  18.5 us
    dynamic_update_slice x7, other arithmetic, body(): lax.dynamic_update_slice_in_dim(out, own_x + got_x[h].astype(jnp.float32)...  9.74 us
  transfers between devices with their start and end apart: 34, of which 14 were waited for; matrix products, arithmetic and copies ran while one was open for 23% of the time, Pallas kernels for 0%

profile of v12, /device:TPU:0, one launch (start us, length us, event | category | flops | bytes accessed | tf_op | source)
XLA Modules:
  0.0 475.1 jit_solution(11166606232220037280)
XLA Ops:
  6.5 2.1 constant_dynamic-slice_fusion.3
  8.7 3.0 collective-permute-start
  14.2 2.6 multiply_convert_fusion
  16.8 2.1 copy.12
  18.9 4.9 %all-to-all-start = ((bf16[192,8,1024]{2,0,1:T(8,128)(2,1)}), bf16[192,8,1024]{2,0,1:T(8,128)(2,1)}, u32[]{:S(2)}, u32[]{:S(2)}) async-start(bf16[192,8,1024]{2,0,1:T(8,128)(2,1)} %bitcast.50), calls=%async_computation | async-start | bytes 6291456 | tf_op jit(solution)/shard_map/all_to_all | solution.py:57
  23.8 75.0 %collective-permute-done = bf16[192,8192]{1,0:T(8,128)(2,1)S(1)} collective-permute-done((bf16[192,8192]{1,0:T(8,128)(2,1)}, bf16[192,8192]{1,0:T(8,128)(2,1)S(1)}, u32[]{:S(2)}, u32[]{:S(2)}) %collective-permute-start) | collective-permute-done | bytes 3145760 | tf_op jit(solution)/shard_map/ppermute | solution.py:30
  98.8 33.6 %all-gather.5.cloned.1.call-done = bf16[768,2048]{1,0:T(8,128)(2,1)} async-done(((bf16[192,2048]{1,0:T(8,128)(2,1)}), bf16[768,2048]{1,0:T(8,128)(2,1)}) %all-gather.5.cloned.1.call-update) | async-done | bytes 3145744 | tf_op jit(solution)/shard_map/all_gather | solution.py:54
  132.4 2.1 constant_dynamic-slice_fusion.2
  134.6 5.0 %fusion.26 = bf16[576,2048]{1,0:T(8,128)(2,1)} fusion(s32[]{:T(128)S(6)} %select_n.66, bf16[768,2048]{1,0:T(8,128)(2,1)} %all-gather.5.cloned.1.call-done), kind=kLoop, calls=%fused_computation.58 | loop fusion | flops 4718592 | bytes 5505028 | tf_op jit(solution)/shard_map/concatenate | solution.py:50
  139.7 1.6 collective-permute-start.2
  141.3 51.1 %collective-permute-done.2 = bf16[576,2048]{1,0:T(8,128)(2,1)S(1)} collective-permute-done((bf16[576,2048]{1,0:T(8,128)(2,1)}, bf16[576,2048]{1,0:T(8,128)(2,1)S(1)}, u32[]{:S(2)}, u32[]{:S(2)}) %collective-permute-start.2) | collective-permute-done | bytes 2359328 | tf_op jit(solution)/shard_map/ppermute | solution.py:30
  192.4 4.1 all-gather.7.cloned.1.call-done
  196.5 2.1 constant_dynamic-slice_fusion.1
  199.2 2.4 constant_dynamic-slice_fusion.5
  202.0 3.6 fusion.106
  205.6 2.7 convolution_add_fusion.2
  208.3 2.6 fusion.27
  222.0 1.7 fusion.13
  225.1 38.8 %collective-permute-done.1 = bf16[576,2048]{1,0:T(8,128)(2,1)} collective-permute-done((bf16[576,2048]{1,0:T(8,128)(2,1)S(1)}, bf16[576,2048]{1,0:T(8,128)(2,1)}, u32[]{:S(2)}, u32[]{:S(2)}) %collective-permute-start.1) | collective-permute-done | bytes 2359328 | tf_op jit(solution)/shard_map/ppermute | solution.py:30
  264.0 2.1 constant_dynamic-slice_fusion
  266.1 2.0 fusion.9
  268.3 5.1 %fusion.105 = f32[1024,2048]{1,0:T(8,128)S(1)} fusion(bf16[768,1024]{1,0:T(8,128)(2,1)} %bitcast.58, bf16[768,2048]{1,0:T(8,128)(2,1)S(1)} %copy-done.10), kind=kOutput, calls=%fused_computation.151 | convolution fusion | flops 3221225472 | bytes 13107200 | tf_op jit(solution)/shard_map/dot_general | solution.py:24
  273.4 2.6 convolution_add_fusion.3
  276.6 2.4 fusion.22
  279.1 2.4 fusion.20
  282.0 2.4 fusion.18
  285.9 3.2 fusion.16
  289.7 3.2 fusion.14
  294.3 3.1 fusion.12
  298.0 3.1 fusion.10
  302.5 3.1 fusion.8
  306.5 4.1 collective-permute-done.18
  312.0 9.8 %collective-permute-done.17 = bf16[128,2048]{1,0:T(8,128)(2,1)} collective-permute-done((bf16[128,2048]{1,0:T(8,128)(2,1)S(1)}, bf16[128,2048]{1,0:T(8,128)(2,1)}, u32[]{:S(2)}, u32[]{:S(2)}) %collective-permute-start.17) | collective-permute-done | bytes 524320 | tf_op jit(solution)/shard_map/ppermute | solution.py:30
  323.3 4.2 fusion.25
  328.7 5.2 %fusion.24 = bf16[576,2048]{1,0:T(8,128)(2,1)} fusion(s32[]{:T(128)S(6)} %select_n.66, bf16[768,2048]{1,0:T(8,128)(2,1)} %all-gather.11.cloned.1.call-done), kind=kLoop, calls=%fused_computation.56 | loop fusion | flops 4718592 | bytes 5505028 | tf_op jit(solution)/shard_map/concatenate | solution.py:50
  335.4 8.9 %collective-permute-done.15 = bf16[128,2048]{1,0:T(8,128)(2,1)} collective-permute-done((bf16[128,2048]{1,0:T(8,128)(2,1)}, bf16[128,2048]{1,0:T(8,128)(2,1)}, u32[]{:S(2)}, u32[]{:S(2)}) %collective-permute-start.15) | collective-permute-done | bytes 524320 | tf_op jit(solution)/shard_map/ppermute | solution.py:30
  344.3 11.2 %collective-permute-done.14 = bf16[128,2048]{1,0:T(8,128)(2,1)} collective-permute-done((bf16[128,2048]{1,0:T(8,128)(2,1)}, bf16[128,2048]{1,0:T(8,128)(2,1)}, u32[]{:S(2)}, u32[]{:S(2)}) %collective-permute-start.14) | collective-permute-done | bytes 524320 | tf_op jit(solution)/shard_map/ppermute | solution.py:30
  355.5 11.2 %collective-permute-done.13 = bf16[128,2048]{1,0:T(8,128)(2,1)} collective-permute-done((bf16[128,2048]{1,0:T(8,128)(2,1)}, bf16[128,2048]{1,0:T(8,128)(2,1)}, u32[]{:S(2)}, u32[]{:S(2)}) %collective-permute-start.13) | collective-permute-done | bytes 524320 | tf_op jit(solution)/shard_map/ppermute | solution.py:30
  366.8 10.4 %collective-permute-done.12 = bf16[128,2048]{1,0:T(8,128)(2,1)} collective-permute-done((bf16[128,2048]{1,0:T(8,128)(2,1)}, bf16[128,2048]{1,0:T(8,128)(2,1)}, u32[]{:S(2)}, u32[]{:S(2)}) %collective-permute-start.12) | collective-permute-done | bytes 524320 | tf_op jit(solution)/shard_map/ppermute | solution.py:30
  378.6 3.5 fusion.107
  383.5 5.9 %fusion.108 = f32[1024,2048]{1,0:T(8,128)S(1)} fusion(bf16[768,1024]{1,0:T(8,128)(2,1)} %bitcast.59, bf16[768,2048]{1,0:T(8,128)(2,1)} %all-gather.11.cloned.1.call-done), kind=kOutput, calls=%fused_computation.154 | convolution fusion | flops 3221225472 | bytes 13107200 | tf_op jit(solution)/shard_map/dot_general | solution.py:24
  389.4 1.6 convolution_add_fusion
  391.0 46.7 %collective-permute-done.20 = bf16[576,2048]{1,0:T(8,128)(2,1)S(1)} collective-permute-done((bf16[576,2048]{1,0:T(8,128)(2,1)}, bf16[576,2048]{1,0:T(8,128)(2,1)S(1)}, u32[]{:S(2)}, u32[]{:S(2)}) %collective-permute-start.20) | collective-permute-done | bytes 2359328 | tf_op jit(solution)/shard_map/ppermute | solution.py:30
  440.1 1.6 slice_add_fusion.6
  449.2 1.6 slice_add_fusion.5
  453.7 1.7 add_dynamic-update-slice_fusion.6
  462.5 3.4 copy-done.3
  465.9 2.3 add_dynamic-update-slice_fusion
  (128 shorter events, 50.9 us)
Async XLA Ops:
  6.5 7.2 %copy-start.18 = (s32[192]{0:T(256)S(1)}, s32[192]{0:T(256)}, u32[]{:S(2)}) copy-start(s32[192]{0:T(256)} %param.7) | copy-start | bytes 2308
  6.5 7.4 %copy-start.17 = (f32[1536]{0:T(1024)S(1)}, f32[1536]{0:T(1024)}, u32[]{:S(2)}) copy-start(f32[1536]{0:T(1024)} %param.9) | copy-start | bytes 18436
  6.5 125.9 %all-gather.5.cloned.1.call-start = ((), (), s32[]{:S(2)}) async-start(), calls=%async_computation.1 | async-start | bytes 3932160 | tf_op jit(solution)/shard_map/all_gather | solution.py:54
  8.7 90.1 %collective-permute-start = (bf16[192,8192]{1,0:T(8,128)(2,1)}, bf16[192,8192]{1,0:T(8,128)(2,1)S(1)}, u32[]{:S(2)}, u32[]{:S(2)}) collective-permute-start(bf16[192,8192]{1,0:T(8,128)(2,1)} %param.6), channel_id=1, source_target_pairs={{0,1},{1,0},{2,3},{3,2},{4,5},{5,4},{6,7},{7,6},{8,9},{9,8},{10,11... | collective-permute-start | bytes 9437192 | tf_op jit(solution)/shard_map/ppermute | solution.py:30
  18.9 180.3 %all-to-all-start = ((bf16[192,8,1024]{2,0,1:T(8,128)(2,1)}), bf16[192,8,1024]{2,0,1:T(8,128)(2,1)}, u32[]{:S(2)}, u32[]{:S(2)}) async-start(bf16[192,8,1024]{2,0,1:T(8,128)(2,1)} %bitcast.50), calls=%async_computation | async-start | bytes 6291456 | tf_op jit(solution)/shard_map/all_to_all | solution.py:57
  23.8 172.8 %all-gather.7.cloned.1.call-start = ((), (), s32[]{:S(2)}) async-start(), calls=%async_computation.2 | async-start | bytes 3932160 | tf_op jit(solution)/shard_map/all_gather | solution.py:86
  98.8 35.8 %copy-start.4 = (bf16[192,8192]{1,0:T(8,128)(2,1)}, bf16[192,8192]{1,0:T(8,128)(2,1)S(1)}, u32[]{:S(2)}) copy-start(bf16[192,8192]{1,0:T(8,128)(2,1)S(1)} %collective-permute-done) | copy-start | bytes 9437188
  134.6 129.4 %all-gather.9.cloned.1.call-start = ((), (), s32[]{:S(2)}) async-start(), calls=%async_computation.3 | async-start | bytes 3932160 | tf_op jit(solution)/shard_map/all_gather | solution.py:86
  139.7 52.7 %collective-permute-start.2 = (bf16[576,2048]{1,0:T(8,128)(2,1)}, bf16[576,2048]{1,0:T(8,128)(2,1)S(1)}, u32[]{:S(2)}, u32[]{:S(2)}) collective-permute-start(bf16[576,2048]{1,0:T(8,128)(2,1)} %fusion.26), channel_id=1, source_target_pairs={{0,1},{1,0},{2,3},{3,2},{4,5},{5,4},{6,7},{7,6},{8,9},{9,8},{10,11... | collective-permute-start | bytes 7077896 | tf_op jit(solution)/shard_map/ppermute | solution.py:30
  198.6 130.1 %all-gather.11.cloned.1.call-start = ((), (), s32[]{:S(2)}) async-start(), calls=%async_computation.4 | async-start | bytes 3932160 | tf_op jit(solution)/shard_map/all_gather | solution.py:86
  201.5 4.0 copy-start.11
  201.5 10.8 %copy-start.1 = (bf16[4,1,192,1024]{3,2,1,0:T(8,128)(2,1)}, bf16[4,1,192,1024]{3,2,1,0:T(8,128)(2,1)S(1)}, u32[]{:S(2)}) copy-start(bf16[4,1,192,1024]{3,2,1,0:T(8,128)(2,1)S(1)} %get-tuple-element.25) | copy-start | bytes 4718596
  208.3 15.3 %copy-start = (f32[1024,2048]{1,0:T(8,128)}, f32[1024,2048]{1,0:T(8,128)S(1)}, u32[]{:S(2)}) copy-start(f32[1024,2048]{1,0:T(8,128)S(1)} %convolution_add_fusion.2) | copy-start | bytes 25165828
  210.9 53.1 %collective-permute-start.1 = (bf16[576,2048]{1,0:T(8,128)(2,1)S(1)}, bf16[576,2048]{1,0:T(8,128)(2,1)}, u32[]{:S(2)}, u32[]{:S(2)}) collective-permute-start(bf16[576,2048]{1,0:T(8,128)(2,1)S(1)} %fusion.27), channel_id=1, source_target_pairs={{0,1},{1,0},{2,3},{3,2},{4,5},{5,4},{6,7},{7,6},{8,9},{9,8},{10,11... | collective-permute-start | bytes 7077896 | tf_op jit(solution)/shard_map/ppermute | solution.py:30
  215.3 60.7 %collective-permute-start.10 = (bf16[128,2048]{1,0:T(8,128)(2,1)}, bf16[128,2048]{1,0:T(8,128)(2,1)}, u32[]{:S(2)}, u32[]{:S(2)}) collective-permute-start(bf16[128,2048]{1,0:T(8,128)(2,1)} %fusion.23), channel_id=1, source_target_pairs={{0,8},{8,0},{1,9},{9,1},{2,10},{10,2},{3,11},{11,3},{4,12},{12,4},... | collective-permute-start | bytes 1572872 | tf_op jit(solution)/shard_map/ppermute | solution.py:30
  216.7 62.3 %collective-permute-start.9 = (bf16[128,2048]{1,0:T(8,128)(2,1)}, bf16[128,2048]{1,0:T(8,128)(2,1)}, u32[]{:S(2)}, u32[]{:S(2)}) collective-permute-start(bf16[128,2048]{1,0:T(8,128)(2,1)} %fusion.21), channel_id=1, source_target_pairs={{0,8},{8,0},{1,9},{9,1},{2,10},{10,2},{3,11},{11,3},{4,12},{12,4},... | collective-permute-start | bytes 1572872 | tf_op jit(solution)/shard_map/ppermute | solution.py:30
  218.6 62.9 %collective-permute-start.8 = (bf16[128,2048]{1,0:T(8,128)(2,1)}, bf16[128,2048]{1,0:T(8,128)(2,1)}, u32[]{:S(2)}, u32[]{:S(2)}) collective-permute-start(bf16[128,2048]{1,0:T(8,128)(2,1)} %fusion.19), channel_id=1, source_target_pairs={{0,8},{8,0},{1,9},{9,1},{2,10},{10,2},{3,11},{11,3},{4,12},{12,4},... | collective-permute-start | bytes 1572872 | tf_op jit(solution)/shard_map/ppermute | solution.py:30
  220.0 64.4 %collective-permute-start.7 = (bf16[128,2048]{1,0:T(8,128)(2,1)}, bf16[128,2048]{1,0:T(8,128)(2,1)}, u32[]{:S(2)}, u32[]{:S(2)}) collective-permute-start(bf16[128,2048]{1,0:T(8,128)(2,1)} %fusion.17), channel_id=1, source_target_pairs={{0,8},{8,0},{1,9},{9,1},{2,10},{10,2},{3,11},{11,3},{4,12},{12,4},... | collective-permute-start | bytes 1572872 | tf_op jit(solution)/shard_map/ppermute | solution.py:30
  264.0 25.2 %collective-permute-start.6 = (bf16[128,2048]{1,0:T(8,128)(2,1)}, bf16[128,2048]{1,0:T(8,128)(2,1)}, u32[]{:S(2)}, u32[]{:S(2)}) collective-permute-start(bf16[128,2048]{1,0:T(8,128)(2,1)} %fusion.15), channel_id=1, source_target_pairs={{0,8},{8,0},{1,9},{9,1},{2,10},{10,2},{3,11},{11,3},{4,12},{12,4},... | collective-permute-start | bytes 1572872 | tf_op jit(solution)/shard_map/ppermute | solution.py:30
  268.3 5.1 %copy-start.2 = (bf16[4,1,192,1024]{3,2,1,0:T(8,128)(2,1)S(1)}, bf16[4,1,192,1024]{3,2,1,0:T(8,128)(2,1)}, u32[]{:S(2)}) copy-start(bf16[4,1,192,1024]{3,2,1,0:T(8,128)(2,1)} %copy-done.1) | copy-start | bytes 4718596
  276.0 3.0 copy-start.15
  276.0 16.9 %collective-permute-start.5 = (bf16[128,2048]{1,0:T(8,128)(2,1)S(1)}, bf16[128,2048]{1,0:T(8,128)(2,1)S(1)}, u32[]{:S(2)}, u32[]{:S(2)}) collective-permute-start(bf16[128,2048]{1,0:T(8,128)(2,1)S(1)} %copy-done.16), channel_id=1, source_target_pairs={{0,8},{8,0},{1,9},{9,1},{2,10},{10,2},{3,11},{11,3},{4,12},{12,4},... | collective-permute-start | bytes 1572872 | tf_op jit(solution)/shard_map/ppermute | solution.py:30
  279.0 18.4 %collective-permute-start.4 = (bf16[128,2048]{1,0:T(8,128)(2,1)S(1)}, bf16[128,2048]{1,0:T(8,128)(2,1)S(1)}, u32[]{:S(2)}, u32[]{:S(2)}) collective-permute-start(bf16[128,2048]{1,0:T(8,128)(2,1)S(1)} %copy-done.15), channel_id=1, source_target_pairs={{0,8},{8,0},{1,9},{9,1},{2,10},{10,2},{3,11},{11,3},{4,12},{12,4},... | collective-permute-start | bytes 1572872 | tf_op jit(solution)/shard_map/ppermute | solution.py:30
  281.5 19.5 %collective-permute-start.3 = (bf16[128,2048]{1,0:T(8,128)(2,1)S(1)}, bf16[128,2048]{1,0:T(8,128)(2,1)S(1)}, u32[]{:S(2)}, u32[]{:S(2)}) collective-permute-start(bf16[128,2048]{1,0:T(8,128)(2,1)S(1)} %fusion.9), channel_id=1, source_target_pairs={{0,8},{8,0},{1,9},{9,1},{2,10},{10,2},{3,11},{11,3},{4,12},{12,4},... | collective-permute-start | bytes 1572872 | tf_op jit(solution)/shard_map/ppermute | solution.py:30
  284.4 21.2 %collective-permute-start.19 = (bf16[128,2048]{1,0:T(8,128)(2,1)S(1)}, bf16[128,2048]{1,0:T(8,128)(2,1)}, u32[]{:S(2)}, u32[]{:S(2)}) collective-permute-start(bf16[128,2048]{1,0:T(8,128)(2,1)S(1)} %fusion.22), channel_id=1, source_target_pairs={{0,16},{16,0},{1,17},{17,1},{2,18},{18,2},{3,19},{19,3},{4,20},{20... | collective-permute-start | bytes 1572872 | tf_op jit(solution)/shard_map/ppermute | solution.py:30
  289.1 21.5 %collective-permute-start.18 = (bf16[128,2048]{1,0:T(8,128)(2,1)S(1)}, bf16[128,2048]{1,0:T(8,128)(2,1)}, u32[]{:S(2)}, u32[]{:S(2)}) collective-permute-start(bf16[128,2048]{1,0:T(8,128)(2,1)S(1)} %fusion.20), channel_id=1, source_target_pairs={{0,16},{16,0},{1,17},{17,1},{2,18},{18,2},{3,19},{19,3},{4,20},{20... | collective-permute-start | bytes 1572872 | tf_op jit(solution)/shard_map/ppermute | solution.py:30
  292.9 29.0 %collective-permute-start.17 = (bf16[128,2048]{1,0:T(8,128)(2,1)S(1)}, bf16[128,2048]{1,0:T(8,128)(2,1)}, u32[]{:S(2)}, u32[]{:S(2)}) collective-permute-start(bf16[128,2048]{1,0:T(8,128)(2,1)S(1)} %fusion.18), channel_id=1, source_target_pairs={{0,16},{16,0},{1,17},{17,1},{2,18},{18,2},{3,19},{19,3},{4,20},{20... | collective-permute-start | bytes 1572872 | tf_op jit(solution)/shard_map/ppermute | solution.py:30
  297.4 36.5 %collective-permute-start.16 = (bf16[128,2048]{1,0:T(8,128)(2,1)}, bf16[128,2048]{1,0:T(8,128)(2,1)S(1)}, u32[]{:S(2)}, u32[]{:S(2)}) collective-permute-start(bf16[128,2048]{1,0:T(8,128)(2,1)} %fusion.16), channel_id=1, source_target_pairs={{0,16},{16,0},{1,17},{17,1},{2,18},{18,2},{3,19},{19,3},{4,20},{20... | collective-permute-start | bytes 1572872 | tf_op jit(solution)/shard_map/ppermute | solution.py:30
  301.0 22.2 %copy-start.6 = (bf16[768,2048]{1,0:T(8,128)(2,1)S(1)}, bf16[768,2048]{1,0:T(8,128)(2,1)}, u32[]{:S(2)}) copy-start(bf16[768,2048]{1,0:T(8,128)(2,1)} %all-gather.9.cloned.1.call-done) | copy-start | bytes 9437188
  301.1 43.3 %collective-permute-start.15 = (bf16[128,2048]{1,0:T(8,128)(2,1)}, bf16[128,2048]{1,0:T(8,128)(2,1)}, u32[]{:S(2)}, u32[]{:S(2)}) collective-permute-start(bf16[128,2048]{1,0:T(8,128)(2,1)} %fusion.14), channel_id=1, source_target_pairs={{0,16},{16,0},{1,17},{17,1},{2,18},{18,2},{3,19},{19,3},{4,20},{20... | collective-permute-start | bytes 1572872 | tf_op jit(solution)/shard_map/ppermute | solution.py:30
  305.6 50.0 %collective-permute-start.14 = (bf16[128,2048]{1,0:T(8,128)(2,1)}, bf16[128,2048]{1,0:T(8,128)(2,1)}, u32[]{:S(2)}, u32[]{:S(2)}) collective-permute-start(bf16[128,2048]{1,0:T(8,128)(2,1)} %fusion.12), channel_id=1, source_target_pairs={{0,16},{16,0},{1,17},{17,1},{2,18},{18,2},{3,19},{19,3},{4,20},{20... | collective-permute-start | bytes 1572872 | tf_op jit(solution)/shard_map/ppermute | solution.py:30
  310.6 56.2 %collective-permute-start.13 = (bf16[128,2048]{1,0:T(8,128)(2,1)}, bf16[128,2048]{1,0:T(8,128)(2,1)}, u32[]{:S(2)}, u32[]{:S(2)}) collective-permute-start(bf16[128,2048]{1,0:T(8,128)(2,1)} %fusion.10), channel_id=1, source_target_pairs={{0,16},{16,0},{1,17},{17,1},{2,18},{18,2},{3,19},{19,3},{4,20},{20... | collective-permute-start | bytes 1572872 | tf_op jit(solution)/shard_map/ppermute | solution.py:30
  321.8 55.3 %collective-permute-start.12 = (bf16[128,2048]{1,0:T(8,128)(2,1)}, bf16[128,2048]{1,0:T(8,128)(2,1)}, u32[]{:S(2)}, u32[]{:S(2)}) collective-permute-start(bf16[128,2048]{1,0:T(8,128)(2,1)} %fusion.8), channel_id=1, source_target_pairs={{0,16},{16,0},{1,17},{17,1},{2,18},{18,2},{3,19},{19,3},{4,20},{20... | collective-permute-start | bytes 1572872 | tf_op jit(solution)/shard_map/ppermute | solution.py:30
  328.7 49.9 %copy-start.7 = (bf16[768,2048]{1,0:T(8,128)(2,1)S(1)}, bf16[768,2048]{1,0:T(8,128)(2,1)}, u32[]{:S(2)}) copy-start(bf16[768,2048]{1,0:T(8,128)(2,1)} %all-gather.9.cloned.1.call-done) | copy-start | bytes 9437188
  328.7 49.9 %copy-start.12 = (bf16[4,1,192,1024]{3,2,1,0:T(8,128)(2,1)S(1)}, bf16[4,1,192,1024]{3,2,1,0:T(8,128)(2,1)}, u32[]{:S(2)}) copy-start(bf16[4,1,192,1024]{3,2,1,0:T(8,128)(2,1)} %copy-done.11) | copy-start | bytes 4718596
  333.9 48.3 %copy-start.5 = (bf16[192,8192]{1,0:T(8,128)(2,1)S(1)}, bf16[192,8192]{1,0:T(8,128)(2,1)}, u32[]{:S(2)}) copy-start(bf16[192,8192]{1,0:T(8,128)(2,1)} %copy-done.4) | copy-start | bytes 9437188
  333.9 48.2 %copy-start.13 = (bf16[128,2048]{1,0:T(8,128)(2,1)}, bf16[128,2048]{1,0:T(8,128)(2,1)S(1)}, u32[]{:S(2)}) copy-start(bf16[128,2048]{1,0:T(8,128)(2,1)S(1)} %collective-permute-done.16) | copy-start | bytes 1572868
  333.9 57.1 %collective-permute-start.11 = (bf16[576,2048]{1,0:T(8,128)(2,1)}, bf16[576,2048]{1,0:T(8,128)(2,1)S(1)}, u32[]{:S(2)}, u32[]{:S(2)}) collective-permute-start(bf16[576,2048]{1,0:T(8,128)(2,1)} %fusion.25), channel_id=1, source_target_pairs={{0,1},{1,0},{2,3},{3,2},{4,5},{5,4},{6,7},{7,6},{8,9},{9,8},{10,11... | collective-permute-start | bytes 7077896 | tf_op jit(solution)/shard_map/ppermute | solution.py:30
  377.2 60.5 %collective-permute-start.20 = (bf16[576,2048]{1,0:T(8,128)(2,1)}, bf16[576,2048]{1,0:T(8,128)(2,1)S(1)}, u32[]{:S(2)}, u32[]{:S(2)}) collective-permute-start(bf16[576,2048]{1,0:T(8,128)(2,1)} %fusion.24), channel_id=1, source_target_pairs={{0,1},{1,0},{2,3},{3,2},{4,5},{5,4},{6,7},{7,6},{8,9},{9,8},{10,11... | collective-permute-start | bytes 7077896 | tf_op jit(solution)/shard_map/ppermute | solution.py:30
  446.0 4.7 collective-permute-start.21
  446.7 6.9 %collective-permute-start.22 = (f32[128,2048]{1,0:T(8,128)}, f32[128,2048]{1,0:T(8,128)}, u32[]{:S(2)}, u32[]{:S(2)}) collective-permute-start(f32[128,2048]{1,0:T(8,128)} %slice_add_fusion.6), channel_id=1, source_target_pairs={{0,8},{8,0},{1,9},{9,1},{2,10},{10,2},{3,11},{11,3},{4,12},{12,4},... | collective-permute-start | bytes 3145736 | tf_op jit(solution)/shard_map/ppermute | solution.py:30
  448.5 13.9 %collective-permute-start.28 = (f32[128,2048]{1,0:T(8,128)S(1)}, f32[128,2048]{1,0:T(8,128)S(1)}, u32[]{:S(2)}, u32[]{:S(2)}) collective-permute-start(f32[128,2048]{1,0:T(8,128)S(1)} %slice_add_fusion), channel_id=1, source_target_pairs={{0,8},{8,0},{1,9},{9,1},{2,10},{10,2},{3,11},{11,3},{4,12},{12,4},... | collective-permute-start | bytes 3145736 | tf_op jit(solution)/shard_map/ppermute | solution.py:30
  448.6 12.5 %collective-permute-start.27 = (f32[128,2048]{1,0:T(8,128)S(1)}, f32[128,2048]{1,0:T(8,128)S(1)}, u32[]{:S(2)}, u32[]{:S(2)}) collective-permute-start(f32[128,2048]{1,0:T(8,128)S(1)} %slice_add_fusion.1), channel_id=1, source_target_pairs={{0,8},{8,0},{1,9},{9,1},{2,10},{10,2},{3,11},{11,3},{4,12},{12,4},... | collective-permute-start | bytes 3145736 | tf_op jit(solution)/shard_map/ppermute | solution.py:30
  449.1 10.6 %collective-permute-start.26 = (f32[128,2048]{1,0:T(8,128)S(1)}, f32[128,2048]{1,0:T(8,128)S(1)}, u32[]{:S(2)}, u32[]{:S(2)}) collective-permute-start(f32[128,2048]{1,0:T(8,128)S(1)} %slice_add_fusion.2), channel_id=1, source_target_pairs={{0,8},{8,0},{1,9},{9,1},{2,10},{10,2},{3,11},{11,3},{4,12},{12,4},... | collective-permute-start | bytes 3145736 | tf_op jit(solution)/shard_map/ppermute | solution.py:30
  450.8 5.7 %collective-permute-start.23 = (f32[128,2048]{1,0:T(8,128)}, f32[128,2048]{1,0:T(8,128)S(1)}, u32[]{:S(2)}, u32[]{:S(2)}) collective-permute-start(f32[128,2048]{1,0:T(8,128)} %slice_add_fusion.5), channel_id=1, source_target_pairs={{0,8},{8,0},{1,9},{9,1},{2,10},{10,2},{3,11},{11,3},{4,12},{12,4},... | collective-permute-start | bytes 3145736 | tf_op jit(solution)/shard_map/ppermute | solution.py:30
  453.6 4.4 collective-permute-start.24
  456.5 2.9 collective-permute-start.25
  462.5 3.4 copy-start.3
  (5 other events, 11.8 us)
Sparse Core Ops, SparseCore 0:
  8.9 123.4 all-gather.4
  134.7 61.7 all-gather.6
  198.7 62.1 all-gather.8
  266.2 62.4 all-gather.10

commit v13 on v11

--- a/solution.py
+++ b/solution.py
@@ -92,9 +92,8 @@
             theirs.append(swap(outgoing, "ay"))
         s_a, s_b, early_part, sent, got_x, cuts, hw, halves = x_out["v"]
         early = list(early_part)
-        _, late_give, late_keep, t_give, t_keep = lax.optimization_barrier(
-            (tuple(sent), early[2], early[3], theirs[2], theirs[3])
-        )
+        _, late_give, t_give = lax.optimization_barrier((tuple(sent), early[2], theirs[2]))
+        late_keep, t_keep = early[3], theirs[3]
         out = jnp.zeros((width, rw), jnp.float32)
         for h, rows in enumerate(cuts):
             s_h = s_b[:, rows]

time: 476 us -> 454 us (0.954)
  waiting for transfers between devices: 330 us -> 304 us
  matrix products: 54 us -> 72.9 us
  other arithmetic: 31.7 us -> 15.4 us
    all_gather x3, waiting for transfers between devices: 59.5 us -> 30.3 us  [body(): lax.all_gather(lax.dynamic_slice_in_dim(rest, m * rw, rw, axis=1), 'az',...]
    dot_general x24, matrix products: 54 us -> 72.9 us  [contract(): lax.dot_general(left, right, (((0,), (0,)), ((), ())), preferred_element_...]
    dynamic_update_slice x3 -> x0, other arithmetic: 8.67 us -> none  [body(): lax.dynamic_update_slice_in_dim(out, own_x + got_x[h].astype(jnp.float32)...]
    concatenate x5, other arithmetic: 20 us -> 14.3 us  [others(): doubled = jnp.concatenate([v, v], axis=0)]
  transfers between devices with their start and end apart: 22 -> 22, of which waited for: 11 -> 9; matrix products, arithmetic and copies ran while one was open for 19% -> 21% of each run, Pallas kernels for 0% -> 0%
where the time goes in v13:
time: 454 us; the launch traced here: 449 us
  waiting for transfers between devices  304 us (67%)
  matrix products  72.9 us (16%)
  starting transfers between devices  22.4 us (5%)
  local copies, waits for them, and re-layouts  19.4 us (4%)
  other arithmetic  15.4 us (3%)
  between operations  14.9 us (3%)
    ppermute x17, waiting for transfers between devices, swap(): return lax.ppermute(x, axis, [(0, 1), (1, 0)])  270 us
    dot_general x24, matrix products, contract(): lax.dot_general(left, right, (((0,), (0,)), ((), ())), preferred_element_...  72.9 us
    all_gather x3, waiting for transfers between devices, body(): lax.all_gather(lax.dynamic_slice_in_dim(rest, m * rw, rw, axis=1), 'az',...  30.3 us
    ppermute x17, starting transfers between devices, swap(): return lax.ppermute(x, axis, [(0, 1), (1, 0)])  15.8 us
    concatenate x5, other arithmetic, others(): doubled = jnp.concatenate([v, v], axis=0)  14.3 us
  transfers between devices with their start and end apart: 22, of which 9 were waited for; matrix products, arithmetic and copies ran while one was open for 21% of the time, Pallas kernels for 0%

profile of v13, /device:TPU:0, one launch (start us, length us, event | category | flops | bytes accessed | tf_op | source)
XLA Modules:
  0.0 449.2 jit_solution(8196437851497654670)
XLA Ops:
  6.5 2.2 constant_dynamic-slice_fusion.3
  8.9 3.0 collective-permute-start
  14.3 66.0 %collective-permute-done = bf16[192,8192]{1,0:T(8,128)(2,1)} collective-permute-done((bf16[192,8192]{1,0:T(8,128)(2,1)}, bf16[192,8192]{1,0:T(8,128)(2,1)}, u32[]{:S(2)}, u32[]{:S(2)}) %collective-permute-start) | collective-permute-done | bytes 3145760 | tf_op jit(solution)/shard_map/ppermute | solution.py:30
  80.3 2.1 constant_dynamic-slice_fusion.2
  83.2 2.1 copy.12
  85.3 6.3 %all-to-all-start = ((bf16[192,8,1024]{2,0,1:T(8,128)(2,1)}), bf16[192,8,1024]{2,0,1:T(8,128)(2,1)}, u32[]{:S(2)}, u32[]{:S(2)}) async-start(bf16[192,8,1024]{2,0,1:T(8,128)(2,1)} %bitcast.34), calls=%async_computation | async-start | bytes 6291456 | tf_op jit(solution)/shard_map/all_to_all | solution.py:57
  91.7 3.9 fusion.26
  95.5 2.0 collective-permute-start.1
  97.5 78.3 %collective-permute-done.1 = bf16[576,2048]{1,0:T(8,128)(2,1)S(1)} collective-permute-done((bf16[576,2048]{1,0:T(8,128)(2,1)}, bf16[576,2048]{1,0:T(8,128)(2,1)S(1)}, u32[]{:S(2)}, u32[]{:S(2)}) %collective-permute-start.1) | collective-permute-done | bytes 2359328 | tf_op jit(solution)/shard_map/ppermute | solution.py:30
  175.8 30.3 %all-gather.7.cloned.1.call-done = bf16[768,2048]{1,0:T(8,128)(2,1)} async-done(((bf16[192,2048]{1,0:T(8,128)(2,1)}), bf16[768,2048]{1,0:T(8,128)(2,1)}) %all-gather.7.cloned.1.call-update) | async-done | bytes 3145744 | tf_op jit(solution)/shard_map/all_gather | solution.py:86
  206.1 2.1 constant_dynamic-slice_fusion.1
  208.5 3.6 all-to-all-done
  212.1 2.7 constant_dynamic-slice_fusion.5
  215.4 2.6 fusion.25
  219.5 3.5 fusion.70
  224.5 2.5 convolution_add_fusion.1
  227.0 2.1 fusion.22
  229.0 2.0 fusion.20
  231.5 2.0 fusion.18
  233.5 2.2 fusion.16
  236.2 33.7 %collective-permute-done.2 = bf16[576,2048]{1,0:T(8,128)(2,1)} collective-permute-done((bf16[576,2048]{1,0:T(8,128)(2,1)S(1)}, bf16[576,2048]{1,0:T(8,128)(2,1)}, u32[]{:S(2)}, u32[]{:S(2)}) %collective-permute-start.2) | collective-permute-done | bytes 2359328 | tf_op jit(solution)/shard_map/ppermute | solution.py:30
  270.0 2.1 constant_dynamic-slice_fusion
  272.1 5.6 %fusion.69 = f32[1024,2048]{1,0:T(8,128)S(1)} fusion(bf16[768,1024]{1,0:T(8,128)(2,1)S(1)} %bitcast.42, bf16[768,2048]{1,0:T(8,128)(2,1)} %all-gather.7.cloned.1.call-done), kind=kOutput, calls=%fused_computation.107 | convolution fusion | flops 3221225472 | bytes 13107200 | tf_op jit(solution)/shard_map/dot_general | solution.py:24
  277.7 2.5 convolution_add_fusion.2
  280.2 4.3 fusion.21
  286.0 2.6 fusion.23
  288.5 1.9 collective-permute-start.12
  290.4 4.0 fusion.19
  294.9 4.0 fusion.17
  300.4 4.0 fusion.15
  304.9 3.9 fusion.71
  308.9 2.4 convolution_add_fusion
  311.3 29.2 %collective-permute-done.12 = bf16[576,2048]{1,0:T(8,128)(2,1)S(1)} collective-permute-done((bf16[576,2048]{1,0:T(8,128)(2,1)S(1)}, bf16[576,2048]{1,0:T(8,128)(2,1)S(1)}, u32[]{:S(2)}, u32[]{:S(2)}) %collective-permute-start.12) | collective-permute-done | bytes 2359328 | tf_op jit(solution)/shard_map/ppermute | solution.py:30
  340.5 2.4 slice_add_fusion
  342.9 3.7 fusion.24
  346.7 9.2 %collective-permute-done.6 = bf16[256,2048]{1,0:T(8,128)(2,1)} collective-permute-done((bf16[256,2048]{1,0:T(8,128)(2,1)}, bf16[256,2048]{1,0:T(8,128)(2,1)}, u32[]{:S(2)}, u32[]{:S(2)}) %collective-permute-start.6) | collective-permute-done | bytes 1048608 | tf_op jit(solution)/shard_map/ppermute | solution.py:30
  355.9 20.4 %collective-permute-done.4 = bf16[256,2048]{1,0:T(8,128)(2,1)} collective-permute-done((bf16[256,2048]{1,0:T(8,128)(2,1)}, bf16[256,2048]{1,0:T(8,128)(2,1)}, u32[]{:S(2)}, u32[]{:S(2)}) %collective-permute-start.4) | collective-permute-done | bytes 1048608 | tf_op jit(solution)/shard_map/ppermute | solution.py:30
  377.8 4.0 slice_add_fusion.3
  382.3 2.3 slice_add_fusion.2
  384.6 2.3 slice_add_fusion.1
  387.7 3.6 fusion.68
  391.3 2.8 convolution_add_fusion.3
  394.1 33.4 %collective-permute-done.11 = bf16[576,2048]{1,0:T(8,128)(2,1)S(1)} collective-permute-done((bf16[576,2048]{1,0:T(8,128)(2,1)S(1)}, bf16[576,2048]{1,0:T(8,128)(2,1)S(1)}, u32[]{:S(2)}, u32[]{:S(2)}) %collective-permute-start.11) | collective-permute-done | bytes 2359328 | tf_op jit(solution)/shard_map/ppermute | solution.py:30
  427.5 2.3 fusion.8
  430.8 2.3 fusion.10
  433.2 2.3 fusion.12
  435.5 3.4 copy-done.5
  438.9 3.6 fusion.14
  (76 shorter events, 14.7 us)
Async XLA Ops:
  6.5 7.4 %copy-start.16 = (s32[192]{0:T(256)S(1)}, s32[192]{0:T(256)}, u32[]{:S(2)}) copy-start(s32[192]{0:T(256)} %param.7) | copy-start | bytes 2308
  6.5 7.5 %copy-start.15 = (f32[1536]{0:T(1024)S(1)}, f32[1536]{0:T(1024)}, u32[]{:S(2)}) copy-start(f32[1536]{0:T(1024)} %param.9) | copy-start | bytes 18436
  6.5 73.8 %all-gather.5.cloned.1.call-start = ((), (), s32[]{:S(2)}) async-start(), calls=%async_computation.1 | async-start | bytes 3932160 | tf_op jit(solution)/shard_map/all_gather | solution.py:54
  6.5 75.9 %copy-start.4 = (bf16[192,8192]{1,0:T(8,128)(2,1)S(1)}, bf16[192,8192]{1,0:T(8,128)(2,1)}, u32[]{:S(2)}) copy-start(bf16[192,8192]{1,0:T(8,128)(2,1)} %param.6) | copy-start | bytes 9437188
  8.8 197.3 %all-gather.7.cloned.1.call-start = ((), (), s32[]{:S(2)}) async-start(), calls=%async_computation.2 | async-start | bytes 3932160 | tf_op jit(solution)/shard_map/all_gather | solution.py:86
  8.9 71.5 %collective-permute-start = (bf16[192,8192]{1,0:T(8,128)(2,1)}, bf16[192,8192]{1,0:T(8,128)(2,1)}, u32[]{:S(2)}, u32[]{:S(2)}) collective-permute-start(bf16[192,8192]{1,0:T(8,128)(2,1)} %param.6), channel_id=1, source_target_pairs={{0,1},{1,0},{2,3},{3,2},{4,5},{5,4},{6,7},{7,6},{8,9},{9,8},{10,11... | collective-permute-start | bytes 9437192 | tf_op jit(solution)/shard_map/ppermute | solution.py:30
  85.3 6.4 %copy-start.6 = (bf16[768,2048]{1,0:T(8,128)(2,1)S(1)}, bf16[768,2048]{1,0:T(8,128)(2,1)}, u32[]{:S(2)}) copy-start(bf16[768,2048]{1,0:T(8,128)(2,1)} %all-gather.5.cloned.1.call-done) | copy-start | bytes 9437188
  85.3 126.8 %all-to-all-start = ((bf16[192,8,1024]{2,0,1:T(8,128)(2,1)}), bf16[192,8,1024]{2,0,1:T(8,128)(2,1)}, u32[]{:S(2)}, u32[]{:S(2)}) async-start(bf16[192,8,1024]{2,0,1:T(8,128)(2,1)} %bitcast.34), calls=%async_computation | async-start | bytes 6291456 | tf_op jit(solution)/shard_map/all_to_all | solution.py:57
  91.6 178.4 %all-gather.9.cloned.1.call-start = ((), (), s32[]{:S(2)}) async-start(), calls=%async_computation.3 | async-start | bytes 3932160 | tf_op jit(solution)/shard_map/all_gather | solution.py:86
  95.5 80.3 %collective-permute-start.1 = (bf16[576,2048]{1,0:T(8,128)(2,1)}, bf16[576,2048]{1,0:T(8,128)(2,1)S(1)}, u32[]{:S(2)}, u32[]{:S(2)}) collective-permute-start(bf16[576,2048]{1,0:T(8,128)(2,1)} %fusion.26), channel_id=1, source_target_pairs={{0,1},{1,0},{2,3},{3,2},{4,5},{5,4},{6,7},{7,6},{8,9},{9,8},{10,11... | collective-permute-start | bytes 7077896 | tf_op jit(solution)/shard_map/ppermute | solution.py:30
  208.2 134.7 %all-gather.11.cloned.1.call-start = ((), (), s32[]{:S(2)}) async-start(), calls=%async_computation.4 | async-start | bytes 3932160 | tf_op jit(solution)/shard_map/all_gather | solution.py:86
  212.1 3.3 copy-start.8
  215.4 4.0 copy-start.11
  215.4 9.1 %copy-start.2 = (bf16[4,1,192,1024]{3,2,1,0:T(8,128)(2,1)}, bf16[4,1,192,1024]{3,2,1,0:T(8,128)(2,1)S(1)}, u32[]{:S(2)}) copy-start(bf16[4,1,192,1024]{3,2,1,0:T(8,128)(2,1)S(1)} %get-tuple-element.21) | copy-start | bytes 4718596
  215.4 4.0 copy-start.7
  218.0 52.0 %collective-permute-start.2 = (bf16[576,2048]{1,0:T(8,128)(2,1)S(1)}, bf16[576,2048]{1,0:T(8,128)(2,1)}, u32[]{:S(2)}, u32[]{:S(2)}) collective-permute-start(bf16[576,2048]{1,0:T(8,128)(2,1)S(1)} %fusion.25), channel_id=1, source_target_pairs={{0,1},{1,0},{2,3},{3,2},{4,5},{5,4},{6,7},{7,6},{8,9},{9,8},{10,11... | collective-permute-start | bytes 7077896 | tf_op jit(solution)/shard_map/ppermute | solution.py:30
  229.0 51.2 %collective-permute-start.9 = (bf16[256,2048]{1,0:T(8,128)(2,1)}, bf16[256,2048]{1,0:T(8,128)(2,1)}, u32[]{:S(2)}, u32[]{:S(2)}) collective-permute-start(bf16[256,2048]{1,0:T(8,128)(2,1)} %fusion.22), channel_id=1, source_target_pairs={{0,8},{8,0},{1,9},{9,1},{2,10},{10,2},{3,11},{11,3},{4,12},{12,4},... | collective-permute-start | bytes 3145736 | tf_op jit(solution)/shard_map/ppermute | solution.py:30
  231.0 59.4 %collective-permute-start.7 = (bf16[256,2048]{1,0:T(8,128)(2,1)}, bf16[256,2048]{1,0:T(8,128)(2,1)}, u32[]{:S(2)}, u32[]{:S(2)}) collective-permute-start(bf16[256,2048]{1,0:T(8,128)(2,1)} %fusion.20), channel_id=1, source_target_pairs={{0,8},{8,0},{1,9},{9,1},{2,10},{10,2},{3,11},{11,3},{4,12},{12,4},... | collective-permute-start | bytes 3145736 | tf_op jit(solution)/shard_map/ppermute | solution.py:30
  233.5 61.4 %collective-permute-start.5 = (bf16[256,2048]{1,0:T(8,128)(2,1)}, bf16[256,2048]{1,0:T(8,128)(2,1)}, u32[]{:S(2)}, u32[]{:S(2)}) collective-permute-start(bf16[256,2048]{1,0:T(8,128)(2,1)} %fusion.18), channel_id=1, source_target_pairs={{0,8},{8,0},{1,9},{9,1},{2,10},{10,2},{3,11},{11,3},{4,12},{12,4},... | collective-permute-start | bytes 3145736 | tf_op jit(solution)/shard_map/ppermute | solution.py:30
  235.7 36.4 %copy-start.12 = (bf16[4,1,192,1024]{3,2,1,0:T(8,128)(2,1)S(1)}, bf16[4,1,192,1024]{3,2,1,0:T(8,128)(2,1)}, u32[]{:S(2)}) copy-start(bf16[4,1,192,1024]{3,2,1,0:T(8,128)(2,1)} %copy-done.11) | copy-start | bytes 4718596
  235.7 64.7 %collective-permute-start.3 = (bf16[256,2048]{1,0:T(8,128)(2,1)}, bf16[256,2048]{1,0:T(8,128)(2,1)}, u32[]{:S(2)}, u32[]{:S(2)}) collective-permute-start(bf16[256,2048]{1,0:T(8,128)(2,1)} %fusion.16), channel_id=1, source_target_pairs={{0,8},{8,0},{1,9},{9,1},{2,10},{10,2},{3,11},{11,3},{4,12},{12,4},... | collective-permute-start | bytes 3145736 | tf_op jit(solution)/shard_map/ppermute | solution.py:30
  272.1 5.6 %copy-start.3 = (bf16[4,1,192,1024]{3,2,1,0:T(8,128)(2,1)S(1)}, bf16[4,1,192,1024]{3,2,1,0:T(8,128)(2,1)}, u32[]{:S(2)}) copy-start(bf16[4,1,192,1024]{3,2,1,0:T(8,128)(2,1)} %copy-done.2) | copy-start | bytes 4718596
  280.2 5.8 %copy-start.9 = (bf16[768,2048]{1,0:T(8,128)(2,1)S(1)}, bf16[768,2048]{1,0:T(8,128)(2,1)}, u32[]{:S(2)}) copy-start(bf16[768,2048]{1,0:T(8,128)(2,1)} %all-gather.9.cloned.1.call-done) | copy-start | bytes 9437188
  284.6 62.1 %collective-permute-start.10 = (bf16[256,2048]{1,0:T(8,128)(2,1)}, bf16[256,2048]{1,0:T(8,128)(2,1)}, u32[]{:S(2)}, u32[]{:S(2)}) collective-permute-start(bf16[256,2048]{1,0:T(8,128)(2,1)} %fusion.21), channel_id=1, source_target_pairs={{0,16},{16,0},{1,17},{17,1},{2,18},{18,2},{3,19},{19,3},{4,20},{20... | collective-permute-start | bytes 3145736 | tf_op jit(solution)/shard_map/ppermute | solution.py:30
  288.5 52.0 %collective-permute-start.12 = (bf16[576,2048]{1,0:T(8,128)(2,1)S(1)}, bf16[576,2048]{1,0:T(8,128)(2,1)S(1)}, u32[]{:S(2)}, u32[]{:S(2)}) collective-permute-start(bf16[576,2048]{1,0:T(8,128)(2,1)S(1)} %fusion.23), channel_id=1, source_target_pairs={{0,1},{1,0},{2,3},{3,2},{4,5},{5,4},{6,7},{7,6},{8,9},{9,8},{10,11... | collective-permute-start | bytes 7077896 | tf_op jit(solution)/shard_map/ppermute | solution.py:30
  294.4 52.3 %collective-permute-start.8 = (bf16[256,2048]{1,0:T(8,128)(2,1)}, bf16[256,2048]{1,0:T(8,128)(2,1)}, u32[]{:S(2)}, u32[]{:S(2)}) collective-permute-start(bf16[256,2048]{1,0:T(8,128)(2,1)} %fusion.19), channel_id=1, source_target_pairs={{0,16},{16,0},{1,17},{17,1},{2,18},{18,2},{3,19},{19,3},{4,20},{20... | collective-permute-start | bytes 3145736 | tf_op jit(solution)/shard_map/ppermute | solution.py:30
  298.9 6.0 %copy-start.13 = (bf16[4,1,192,1024]{3,2,1,0:T(8,128)(2,1)S(1)}, bf16[4,1,192,1024]{3,2,1,0:T(8,128)(2,1)}, u32[]{:S(2)}) copy-start(bf16[4,1,192,1024]{3,2,1,0:T(8,128)(2,1)} %copy-done.11) | copy-start | bytes 4718596
  298.9 57.0 %collective-permute-start.6 = (bf16[256,2048]{1,0:T(8,128)(2,1)}, bf16[256,2048]{1,0:T(8,128)(2,1)}, u32[]{:S(2)}, u32[]{:S(2)}) collective-permute-start(bf16[256,2048]{1,0:T(8,128)(2,1)} %fusion.17), channel_id=1, source_target_pairs={{0,16},{16,0},{1,17},{17,1},{2,18},{18,2},{3,19},{19,3},{4,20},{20... | collective-permute-start | bytes 3145736 | tf_op jit(solution)/shard_map/ppermute | solution.py:30
  304.4 71.9 %collective-permute-start.4 = (bf16[256,2048]{1,0:T(8,128)(2,1)}, bf16[256,2048]{1,0:T(8,128)(2,1)}, u32[]{:S(2)}, u32[]{:S(2)}) collective-permute-start(bf16[256,2048]{1,0:T(8,128)(2,1)} %fusion.15), channel_id=1, source_target_pairs={{0,16},{16,0},{1,17},{17,1},{2,18},{18,2},{3,19},{19,3},{4,20},{20... | collective-permute-start | bytes 3145736 | tf_op jit(solution)/shard_map/ppermute | solution.py:30
  311.3 29.2 %copy-start = (f32[1024,2048]{1,0:T(8,128)}, f32[1024,2048]{1,0:T(8,128)S(1)}, u32[]{:S(2)}) copy-start(f32[1024,2048]{1,0:T(8,128)S(1)} %convolution_add_fusion) | copy-start | bytes 25165828
  342.9 39.4 %copy-start.1 = (f32[1024,2048]{1,0:T(8,128)S(1)}, f32[1024,2048]{1,0:T(8,128)}, u32[]{:S(2)}) copy-start(f32[1024,2048]{1,0:T(8,128)} %copy-done) | copy-start | bytes 25165828
  376.3 51.2 %collective-permute-start.11 = (bf16[576,2048]{1,0:T(8,128)(2,1)S(1)}, bf16[576,2048]{1,0:T(8,128)(2,1)S(1)}, u32[]{:S(2)}, u32[]{:S(2)}) collective-permute-start(bf16[576,2048]{1,0:T(8,128)(2,1)S(1)} %fusion.24), channel_id=1, source_target_pairs={{0,1},{1,0},{2,3},{3,2},{4,5},{5,4},{6,7},{7,6},{8,9},{9,8},{10,11... | collective-permute-start | bytes 7077896 | tf_op jit(solution)/shard_map/ppermute | solution.py:30
  381.8 53.7 %collective-permute-start.16 = (f32[256,2048]{1,0:T(8,128)}, f32[256,2048]{1,0:T(8,128)S(1)}, u32[]{:S(2)}, u32[]{:S(2)}) collective-permute-start(f32[256,2048]{1,0:T(8,128)} %slice_add_fusion), channel_id=1, source_target_pairs={{0,8},{8,0},{1,9},{9,1},{2,10},{10,2},{3,11},{11,3},{4,12},{12,4},... | collective-permute-start | bytes 6291464 | tf_op jit(solution)/shard_map/ppermute | solution.py:30
  381.8 12.3 %collective-permute-start.13 = (f32[256,2048]{1,0:T(8,128)}, f32[256,2048]{1,0:T(8,128)S(1)}, u32[]{:S(2)}, u32[]{:S(2)}) collective-permute-start(f32[256,2048]{1,0:T(8,128)} %slice_add_fusion.3), channel_id=1, source_target_pairs={{0,8},{8,0},{1,9},{9,1},{2,10},{10,2},{3,11},{11,3},{4,12},{12,4},... | collective-permute-start | bytes 6291464 | tf_op jit(solution)/shard_map/ppermute | solution.py:30
  384.6 2.9 copy-start.10
  384.6 3.1 copy-start.14
  384.6 46.2 %collective-permute-start.14 = (f32[256,2048]{1,0:T(8,128)}, f32[256,2048]{1,0:T(8,128)S(1)}, u32[]{:S(2)}, u32[]{:S(2)}) collective-permute-start(f32[256,2048]{1,0:T(8,128)} %slice_add_fusion.2), channel_id=1, source_target_pairs={{0,8},{8,0},{1,9},{9,1},{2,10},{10,2},{3,11},{11,3},{4,12},{12,4},... | collective-permute-start | bytes 6291464 | tf_op jit(solution)/shard_map/ppermute | solution.py:30
  387.0 46.2 %collective-permute-start.15 = (f32[256,2048]{1,0:T(8,128)}, f32[256,2048]{1,0:T(8,128)S(1)}, u32[]{:S(2)}, u32[]{:S(2)}) collective-permute-start(f32[256,2048]{1,0:T(8,128)} %slice_add_fusion.1), channel_id=1, source_target_pairs={{0,8},{8,0},{1,9},{9,1},{2,10},{10,2},{3,11},{11,3},{4,12},{12,4},... | collective-permute-start | bytes 6291464 | tf_op jit(solution)/shard_map/ppermute | solution.py:30
  435.5 3.4 copy-start.5
Sparse Core Ops, SparseCore 0:
  8.9 66.1 all-gather.4
  82.6 123.4 all-gather.6
  208.4 60.7 all-gather.8
  272.2 63.5 all-gather.10

commit v14 on v13

--- a/solution.py
+++ b/solution.py
@@ -88,11 +88,11 @@
             outgoing = others(piece)
             if len(mine) == len(order):
                 x_out["v"] = x_chain(theirs)
-                outgoing = lax.optimization_barrier((outgoing, x_out["v"][4]))[0]
+                outgoing = lax.optimization_barrier((outgoing, x_out["v"][4][:-1] or x_out["v"][4]))[0]
             theirs.append(swap(outgoing, "ay"))
         s_a, s_b, early_part, sent, got_x, cuts, hw, halves = x_out["v"]
         early = list(early_part)
-        _, late_give, t_give = lax.optimization_barrier((tuple(sent), early[2], theirs[2]))
+        _, _, late_give, t_give = lax.optimization_barrier((tuple(sent), got_x[-1], early[2], theirs[2]))
         late_keep, t_keep = early[3], theirs[3]
         out = jnp.zeros((width, rw), jnp.float32)
         for h, rows in enumerate(cuts):

time: 454 us -> 451 us (level)
  no operation moved by 1% of the time
where the time goes in v14:
time: 451 us; the launch traced here: 447 us
  waiting for transfers between devices  304 us (67%)
  matrix products  70.6 us (16%)
  starting transfers between devices  22.5 us (5%)
  local copies, waits for them, and re-layouts  19.5 us (4%)
  other arithmetic  15.4 us (3%)
  between operations  15 us (3%)
    ppermute x17, waiting for transfers between devices, swap(): return lax.ppermute(x, axis, [(0, 1), (1, 0)])  270 us
    dot_general x24, matrix products, contract(): lax.dot_general(left, right, (((0,), (0,)), ((), ())), preferred_element_...  70.6 us
    all_gather x3, waiting for transfers between devices, body(): lax.all_gather(lax.dynamic_slice_in_dim(rest, m * rw, rw, axis=1), 'az',...  30.3 us
    ppermute x17, starting transfers between devices, swap(): return lax.ppermute(x, axis, [(0, 1), (1, 0)])  15.9 us
    concatenate x5, other arithmetic, others(): doubled = jnp.concatenate([v, v], axis=0)  14.3 us
  transfers between devices with their start and end apart: 22, of which 9 were waited for; matrix products, arithmetic and copies ran while one was open for 21% of the time, Pallas kernels for 0%

profile of v14, /device:TPU:0, one launch (start us, length us, event | category | flops | bytes accessed | tf_op | source)
XLA Modules:
  0.0 446.9 jit_solution(7156772327923904962)
XLA Ops:
  6.5 2.2 constant_dynamic-slice_fusion.3
  8.9 3.0 collective-permute-start
  14.3 66.0 %collective-permute-done = bf16[192,8192]{1,0:T(8,128)(2,1)} collective-permute-done((bf16[192,8192]{1,0:T(8,128)(2,1)}, bf16[192,8192]{1,0:T(8,128)(2,1)}, u32[]{:S(2)}, u32[]{:S(2)}) %collective-permute-start) | collective-permute-done | bytes 3145760 | tf_op jit(solution)/shard_map/ppermute | solution.py:30
  80.3 2.1 constant_dynamic-slice_fusion.2
  83.2 2.1 copy.12
  85.3 6.3 %all-to-all-start = ((bf16[192,8,1024]{2,0,1:T(8,128)(2,1)}), bf16[192,8,1024]{2,0,1:T(8,128)(2,1)}, u32[]{:S(2)}, u32[]{:S(2)}) async-start(bf16[192,8,1024]{2,0,1:T(8,128)(2,1)} %bitcast.34), calls=%async_computation | async-start | bytes 6291456 | tf_op jit(solution)/shard_map/all_to_all | solution.py:57
  91.7 3.9 fusion.26
  95.6 2.0 collective-permute-start.1
  97.5 78.3 %collective-permute-done.1 = bf16[576,2048]{1,0:T(8,128)(2,1)S(1)} collective-permute-done((bf16[576,2048]{1,0:T(8,128)(2,1)}, bf16[576,2048]{1,0:T(8,128)(2,1)S(1)}, u32[]{:S(2)}, u32[]{:S(2)}) %collective-permute-start.1) | collective-permute-done | bytes 2359328 | tf_op jit(solution)/shard_map/ppermute | solution.py:30
  175.8 30.3 %all-gather.7.cloned.1.call-done = bf16[768,2048]{1,0:T(8,128)(2,1)} async-done(((bf16[192,2048]{1,0:T(8,128)(2,1)}), bf16[768,2048]{1,0:T(8,128)(2,1)}) %all-gather.7.cloned.1.call-update) | async-done | bytes 3145744 | tf_op jit(solution)/shard_map/all_gather | solution.py:86
  206.1 2.1 constant_dynamic-slice_fusion.1
  208.5 3.6 all-to-all-done
  212.1 2.6 constant_dynamic-slice_fusion.5
  215.4 2.6 fusion.25
  219.5 3.5 fusion.70
  224.5 2.5 convolution_add_fusion.1
  227.0 2.0 fusion.22
  229.0 2.0 fusion.20
  231.5 2.0 fusion.18
  233.5 2.2 fusion.16
  236.2 33.8 %collective-permute-done.2 = bf16[576,2048]{1,0:T(8,128)(2,1)} collective-permute-done((bf16[576,2048]{1,0:T(8,128)(2,1)S(1)}, bf16[576,2048]{1,0:T(8,128)(2,1)}, u32[]{:S(2)}, u32[]{:S(2)}) %collective-permute-start.2) | collective-permute-done | bytes 2359328 | tf_op jit(solution)/shard_map/ppermute | solution.py:30
  270.0 2.1 constant_dynamic-slice_fusion
  272.1 5.6 %fusion.69 = f32[1024,2048]{1,0:T(8,128)S(1)} fusion(bf16[768,1024]{1,0:T(8,128)(2,1)S(1)} %bitcast.42, bf16[768,2048]{1,0:T(8,128)(2,1)} %all-gather.7.cloned.1.call-done), kind=kOutput, calls=%fused_computation.107 | convolution fusion | flops 3221225472 | bytes 13107200 | tf_op jit(solution)/shard_map/dot_general | solution.py:24
  277.7 2.5 convolution_add_fusion.2
  280.2 3.4 fusion.21
  285.1 2.6 fusion.23
  287.6 1.9 collective-permute-start.12
  289.5 4.0 fusion.19
  294.0 4.0 fusion.17
  299.5 4.0 fusion.15
  304.0 3.9 fusion.71
  307.9 2.5 convolution_add_fusion
  310.4 29.2 %collective-permute-done.12 = bf16[576,2048]{1,0:T(8,128)(2,1)S(1)} collective-permute-done((bf16[576,2048]{1,0:T(8,128)(2,1)S(1)}, bf16[576,2048]{1,0:T(8,128)(2,1)S(1)}, u32[]{:S(2)}, u32[]{:S(2)}) %collective-permute-start.12) | collective-permute-done | bytes 2359328 | tf_op jit(solution)/shard_map/ppermute | solution.py:30
  339.6 2.4 slice_add_fusion
  342.0 3.7 fusion.24
  345.7 9.1 %collective-permute-done.6 = bf16[256,2048]{1,0:T(8,128)(2,1)} collective-permute-done((bf16[256,2048]{1,0:T(8,128)(2,1)}, bf16[256,2048]{1,0:T(8,128)(2,1)}, u32[]{:S(2)}, u32[]{:S(2)}) %collective-permute-start.6) | collective-permute-done | bytes 1048608 | tf_op jit(solution)/shard_map/ppermute | solution.py:30
  354.8 20.4 %collective-permute-done.4 = bf16[256,2048]{1,0:T(8,128)(2,1)} collective-permute-done((bf16[256,2048]{1,0:T(8,128)(2,1)}, bf16[256,2048]{1,0:T(8,128)(2,1)}, u32[]{:S(2)}, u32[]{:S(2)}) %collective-permute-start.4) | collective-permute-done | bytes 1048608 | tf_op jit(solution)/shard_map/ppermute | solution.py:30
  376.7 4.0 slice_add_fusion.3
  381.2 2.3 slice_add_fusion.2
  383.5 2.3 slice_add_fusion.1
  386.6 3.6 fusion.68
  390.2 2.7 convolution_add_fusion.3
  392.9 33.4 %collective-permute-done.9 = bf16[576,2048]{1,0:T(8,128)(2,1)S(1)} collective-permute-done((bf16[576,2048]{1,0:T(8,128)(2,1)S(1)}, bf16[576,2048]{1,0:T(8,128)(2,1)S(1)}, u32[]{:S(2)}, u32[]{:S(2)}) %collective-permute-start.9) | collective-permute-done | bytes 2359328 | tf_op jit(solution)/shard_map/ppermute | solution.py:30
  426.3 2.3 fusion.8
  429.7 2.3 fusion.10
  432.0 2.4 fusion.12
  434.4 3.4 copy-done.5
  437.8 2.3 fusion.14
  (80 shorter events, 14.7 us)
Async XLA Ops:
  6.5 7.4 %copy-start.18 = (s32[192]{0:T(256)S(1)}, s32[192]{0:T(256)}, u32[]{:S(2)}) copy-start(s32[192]{0:T(256)} %param.7) | copy-start | bytes 2308
  6.5 7.5 %copy-start.17 = (f32[1536]{0:T(1024)S(1)}, f32[1536]{0:T(1024)}, u32[]{:S(2)}) copy-start(f32[1536]{0:T(1024)} %param.9) | copy-start | bytes 18436
  6.5 73.8 %all-gather.5.cloned.1.call-start = ((), (), s32[]{:S(2)}) async-start(), calls=%async_computation.1 | async-start | bytes 3932160 | tf_op jit(solution)/shard_map/all_gather | solution.py:54
  6.5 75.9 %copy-start.4 = (bf16[192,8192]{1,0:T(8,128)(2,1)S(1)}, bf16[192,8192]{1,0:T(8,128)(2,1)}, u32[]{:S(2)}) copy-start(bf16[192,8192]{1,0:T(8,128)(2,1)} %param.6) | copy-start | bytes 9437188
  8.8 197.3 %all-gather.7.cloned.1.call-start = ((), (), s32[]{:S(2)}) async-start(), calls=%async_computation.2 | async-start | bytes 3932160 | tf_op jit(solution)/shard_map/all_gather | solution.py:86
  8.9 71.5 %collective-permute-start = (bf16[192,8192]{1,0:T(8,128)(2,1)}, bf16[192,8192]{1,0:T(8,128)(2,1)}, u32[]{:S(2)}, u32[]{:S(2)}) collective-permute-start(bf16[192,8192]{1,0:T(8,128)(2,1)} %param.6), channel_id=1, source_target_pairs={{0,1},{1,0},{2,3},{3,2},{4,5},{5,4},{6,7},{7,6},{8,9},{9,8},{10,11... | collective-permute-start | bytes 9437192 | tf_op jit(solution)/shard_map/ppermute | solution.py:30
  85.3 6.4 %copy-start.6 = (bf16[768,2048]{1,0:T(8,128)(2,1)S(1)}, bf16[768,2048]{1,0:T(8,128)(2,1)}, u32[]{:S(2)}) copy-start(bf16[768,2048]{1,0:T(8,128)(2,1)} %all-gather.5.cloned.1.call-done) | copy-start | bytes 9437188
  85.3 126.8 %all-to-all-start = ((bf16[192,8,1024]{2,0,1:T(8,128)(2,1)}), bf16[192,8,1024]{2,0,1:T(8,128)(2,1)}, u32[]{:S(2)}, u32[]{:S(2)}) async-start(bf16[192,8,1024]{2,0,1:T(8,128)(2,1)} %bitcast.34), calls=%async_computation | async-start | bytes 6291456 | tf_op jit(solution)/shard_map/all_to_all | solution.py:57
  91.6 178.4 %all-gather.9.cloned.1.call-start = ((), (), s32[]{:S(2)}) async-start(), calls=%async_computation.3 | async-start | bytes 3932160 | tf_op jit(solution)/shard_map/all_gather | solution.py:86
  95.6 80.3 %collective-permute-start.1 = (bf16[576,2048]{1,0:T(8,128)(2,1)}, bf16[576,2048]{1,0:T(8,128)(2,1)S(1)}, u32[]{:S(2)}, u32[]{:S(2)}) collective-permute-start(bf16[576,2048]{1,0:T(8,128)(2,1)} %fusion.26), channel_id=1, source_target_pairs={{0,1},{1,0},{2,3},{3,2},{4,5},{5,4},{6,7},{7,6},{8,9},{9,8},{10,11... | collective-permute-start | bytes 7077896 | tf_op jit(solution)/shard_map/ppermute | solution.py:30
  208.2 133.8 %all-gather.11.cloned.1.call-start = ((), (), s32[]{:S(2)}) async-start(), calls=%async_computation.4 | async-start | bytes 3932160 | tf_op jit(solution)/shard_map/all_gather | solution.py:86
  212.1 3.3 copy-start.8
  215.4 4.0 copy-start.11
  215.4 9.1 %copy-start.2 = (bf16[4,1,192,1024]{3,2,1,0:T(8,128)(2,1)}, bf16[4,1,192,1024]{3,2,1,0:T(8,128)(2,1)S(1)}, u32[]{:S(2)}) copy-start(bf16[4,1,192,1024]{3,2,1,0:T(8,128)(2,1)S(1)} %get-tuple-element.21) | copy-start | bytes 4718596
  215.4 4.0 copy-start.7
  218.0 52.0 %collective-permute-start.2 = (bf16[576,2048]{1,0:T(8,128)(2,1)S(1)}, bf16[576,2048]{1,0:T(8,128)(2,1)}, u32[]{:S(2)}, u32[]{:S(2)}) collective-permute-start(bf16[576,2048]{1,0:T(8,128)(2,1)S(1)} %fusion.25), channel_id=1, source_target_pairs={{0,1},{1,0},{2,3},{3,2},{4,5},{5,4},{6,7},{7,6},{8,9},{9,8},{10,11... | collective-permute-start | bytes 7077896 | tf_op jit(solution)/shard_map/ppermute | solution.py:30
  229.0 51.2 %collective-permute-start.10 = (bf16[256,2048]{1,0:T(8,128)(2,1)}, bf16[256,2048]{1,0:T(8,128)(2,1)}, u32[]{:S(2)}, u32[]{:S(2)}) collective-permute-start(bf16[256,2048]{1,0:T(8,128)(2,1)} %fusion.22), channel_id=1, source_target_pairs={{0,8},{8,0},{1,9},{9,1},{2,10},{10,2},{3,11},{11,3},{4,12},{12,4},... | collective-permute-start | bytes 3145736 | tf_op jit(solution)/shard_map/ppermute | solution.py:30
  231.0 58.5 %collective-permute-start.7 = (bf16[256,2048]{1,0:T(8,128)(2,1)}, bf16[256,2048]{1,0:T(8,128)(2,1)}, u32[]{:S(2)}, u32[]{:S(2)}) collective-permute-start(bf16[256,2048]{1,0:T(8,128)(2,1)} %fusion.20), channel_id=1, source_target_pairs={{0,8},{8,0},{1,9},{9,1},{2,10},{10,2},{3,11},{11,3},{4,12},{12,4},... | collective-permute-start | bytes 3145736 | tf_op jit(solution)/shard_map/ppermute | solution.py:30
  233.5 60.5 %collective-permute-start.5 = (bf16[256,2048]{1,0:T(8,128)(2,1)}, bf16[256,2048]{1,0:T(8,128)(2,1)}, u32[]{:S(2)}, u32[]{:S(2)}) collective-permute-start(bf16[256,2048]{1,0:T(8,128)(2,1)} %fusion.18), channel_id=1, source_target_pairs={{0,8},{8,0},{1,9},{9,1},{2,10},{10,2},{3,11},{11,3},{4,12},{12,4},... | collective-permute-start | bytes 3145736 | tf_op jit(solution)/shard_map/ppermute | solution.py:30
  235.7 36.4 %copy-start.12 = (bf16[4,1,192,1024]{3,2,1,0:T(8,128)(2,1)S(1)}, bf16[4,1,192,1024]{3,2,1,0:T(8,128)(2,1)}, u32[]{:S(2)}) copy-start(bf16[4,1,192,1024]{3,2,1,0:T(8,128)(2,1)} %copy-done.11) | copy-start | bytes 4718596
  235.7 63.8 %collective-permute-start.3 = (bf16[256,2048]{1,0:T(8,128)(2,1)}, bf16[256,2048]{1,0:T(8,128)(2,1)}, u32[]{:S(2)}, u32[]{:S(2)}) collective-permute-start(bf16[256,2048]{1,0:T(8,128)(2,1)} %fusion.16), channel_id=1, source_target_pairs={{0,8},{8,0},{1,9},{9,1},{2,10},{10,2},{3,11},{11,3},{4,12},{12,4},... | collective-permute-start | bytes 3145736 | tf_op jit(solution)/shard_map/ppermute | solution.py:30
  272.1 5.6 %copy-start.3 = (bf16[4,1,192,1024]{3,2,1,0:T(8,128)(2,1)S(1)}, bf16[4,1,192,1024]{3,2,1,0:T(8,128)(2,1)}, u32[]{:S(2)}) copy-start(bf16[4,1,192,1024]{3,2,1,0:T(8,128)(2,1)} %copy-done.2) | copy-start | bytes 4718596
  280.2 4.9 %copy-start.9 = (bf16[768,2048]{1,0:T(8,128)(2,1)S(1)}, bf16[768,2048]{1,0:T(8,128)(2,1)}, u32[]{:S(2)}) copy-start(bf16[768,2048]{1,0:T(8,128)(2,1)} %all-gather.9.cloned.1.call-done) | copy-start | bytes 9437188
  283.6 26.8 %collective-permute-start.11 = (bf16[256,2048]{1,0:T(8,128)(2,1)S(1)}, bf16[256,2048]{1,0:T(8,128)(2,1)S(1)}, u32[]{:S(2)}, u32[]{:S(2)}) collective-permute-start(bf16[256,2048]{1,0:T(8,128)(2,1)S(1)} %fusion.21), channel_id=1, source_target_pairs={{0,16},{16,0},{1,17},{17,1},{2,18},{18,2},{3,19},{19,3},{4,20},{20... | collective-permute-start | bytes 3145736 | tf_op jit(solution)/shard_map/ppermute | solution.py:30
  287.6 52.0 %collective-permute-start.12 = (bf16[576,2048]{1,0:T(8,128)(2,1)S(1)}, bf16[576,2048]{1,0:T(8,128)(2,1)S(1)}, u32[]{:S(2)}, u32[]{:S(2)}) collective-permute-start(bf16[576,2048]{1,0:T(8,128)(2,1)S(1)} %fusion.23), channel_id=1, source_target_pairs={{0,1},{1,0},{2,3},{3,2},{4,5},{5,4},{6,7},{7,6},{8,9},{9,8},{10,11... | collective-permute-start | bytes 7077896 | tf_op jit(solution)/shard_map/ppermute | solution.py:30
  293.5 52.3 %collective-permute-start.8 = (bf16[256,2048]{1,0:T(8,128)(2,1)}, bf16[256,2048]{1,0:T(8,128)(2,1)}, u32[]{:S(2)}, u32[]{:S(2)}) collective-permute-start(bf16[256,2048]{1,0:T(8,128)(2,1)} %fusion.19), channel_id=1, source_target_pairs={{0,16},{16,0},{1,17},{17,1},{2,18},{18,2},{3,19},{19,3},{4,20},{20... | collective-permute-start | bytes 3145736 | tf_op jit(solution)/shard_map/ppermute | solution.py:30
  297.9 6.0 %copy-start.13 = (bf16[4,1,192,1024]{3,2,1,0:T(8,128)(2,1)S(1)}, bf16[4,1,192,1024]{3,2,1,0:T(8,128)(2,1)}, u32[]{:S(2)}) copy-start(bf16[4,1,192,1024]{3,2,1,0:T(8,128)(2,1)} %copy-done.11) | copy-start | bytes 4718596
  298.0 56.9 %collective-permute-start.6 = (bf16[256,2048]{1,0:T(8,128)(2,1)}, bf16[256,2048]{1,0:T(8,128)(2,1)}, u32[]{:S(2)}, u32[]{:S(2)}) collective-permute-start(bf16[256,2048]{1,0:T(8,128)(2,1)} %fusion.17), channel_id=1, source_target_pairs={{0,16},{16,0},{1,17},{17,1},{2,18},{18,2},{3,19},{19,3},{4,20},{20... | collective-permute-start | bytes 3145736 | tf_op jit(solution)/shard_map/ppermute | solution.py:30
  303.4 71.7 %collective-permute-start.4 = (bf16[256,2048]{1,0:T(8,128)(2,1)}, bf16[256,2048]{1,0:T(8,128)(2,1)}, u32[]{:S(2)}, u32[]{:S(2)}) collective-permute-start(bf16[256,2048]{1,0:T(8,128)(2,1)} %fusion.15), channel_id=1, source_target_pairs={{0,16},{16,0},{1,17},{17,1},{2,18},{18,2},{3,19},{19,3},{4,20},{20... | collective-permute-start | bytes 3145736 | tf_op jit(solution)/shard_map/ppermute | solution.py:30
  310.4 29.2 %copy-start = (f32[1024,2048]{1,0:T(8,128)}, f32[1024,2048]{1,0:T(8,128)S(1)}, u32[]{:S(2)}) copy-start(f32[1024,2048]{1,0:T(8,128)S(1)} %convolution_add_fusion) | copy-start | bytes 25165828
  310.4 29.2 %copy-start.15 = (bf16[256,2048]{1,0:T(8,128)(2,1)}, bf16[256,2048]{1,0:T(8,128)(2,1)S(1)}, u32[]{:S(2)}) copy-start(bf16[256,2048]{1,0:T(8,128)(2,1)S(1)} %collective-permute-done.11) | copy-start | bytes 3145732
  342.0 39.2 %copy-start.1 = (f32[1024,2048]{1,0:T(8,128)S(1)}, f32[1024,2048]{1,0:T(8,128)}, u32[]{:S(2)}) copy-start(f32[1024,2048]{1,0:T(8,128)} %copy-done) | copy-start | bytes 25165828
  375.2 51.2 %collective-permute-start.9 = (bf16[576,2048]{1,0:T(8,128)(2,1)S(1)}, bf16[576,2048]{1,0:T(8,128)(2,1)S(1)}, u32[]{:S(2)}, u32[]{:S(2)}) collective-permute-start(bf16[576,2048]{1,0:T(8,128)(2,1)S(1)} %fusion.24), channel_id=1, source_target_pairs={{0,1},{1,0},{2,3},{3,2},{4,5},{5,4},{6,7},{7,6},{8,9},{9,8},{10,11... | collective-permute-start | bytes 7077896 | tf_op jit(solution)/shard_map/ppermute | solution.py:30
  380.7 53.7 %collective-permute-start.16 = (f32[256,2048]{1,0:T(8,128)}, f32[256,2048]{1,0:T(8,128)S(1)}, u32[]{:S(2)}, u32[]{:S(2)}) collective-permute-start(f32[256,2048]{1,0:T(8,128)} %slice_add_fusion), channel_id=1, source_target_pairs={{0,8},{8,0},{1,9},{9,1},{2,10},{10,2},{3,11},{11,3},{4,12},{12,4},... | collective-permute-start | bytes 6291464 | tf_op jit(solution)/shard_map/ppermute | solution.py:30
  380.7 12.3 %collective-permute-start.13 = (f32[256,2048]{1,0:T(8,128)}, f32[256,2048]{1,0:T(8,128)S(1)}, u32[]{:S(2)}, u32[]{:S(2)}) collective-permute-start(f32[256,2048]{1,0:T(8,128)} %slice_add_fusion.3), channel_id=1, source_target_pairs={{0,8},{8,0},{1,9},{9,1},{2,10},{10,2},{3,11},{11,3},{4,12},{12,4},... | collective-permute-start | bytes 6291464 | tf_op jit(solution)/shard_map/ppermute | solution.py:30
  383.5 2.8 copy-start.10
  383.5 3.1 copy-start.14
  383.5 46.2 %collective-permute-start.14 = (f32[256,2048]{1,0:T(8,128)}, f32[256,2048]{1,0:T(8,128)S(1)}, u32[]{:S(2)}, u32[]{:S(2)}) collective-permute-start(f32[256,2048]{1,0:T(8,128)} %slice_add_fusion.2), channel_id=1, source_target_pairs={{0,8},{8,0},{1,9},{9,1},{2,10},{10,2},{3,11},{11,3},{4,12},{12,4},... | collective-permute-start | bytes 6291464 | tf_op jit(solution)/shard_map/ppermute | solution.py:30
  385.8 46.2 %collective-permute-start.15 = (f32[256,2048]{1,0:T(8,128)}, f32[256,2048]{1,0:T(8,128)S(1)}, u32[]{:S(2)}, u32[]{:S(2)}) collective-permute-start(f32[256,2048]{1,0:T(8,128)} %slice_add_fusion.1), channel_id=1, source_target_pairs={{0,8},{8,0},{1,9},{9,1},{2,10},{10,2},{3,11},{11,3},{4,12},{12,4},... | collective-permute-start | bytes 6291464 | tf_op jit(solution)/shard_map/ppermute | solution.py:30
  432.0 5.8 %copy-start.16 = (bf16[256,2048]{1,0:T(8,128)(2,1)S(1)}, bf16[256,2048]{1,0:T(8,128)(2,1)}, u32[]{:S(2)}) copy-start(bf16[256,2048]{1,0:T(8,128)(2,1)} %copy-done.15) | copy-start | bytes 3145732
  434.4 3.4 copy-start.5
Sparse Core Ops, SparseCore 0:
  8.9 66.1 all-gather.4
  82.6 123.4 all-gather.6
  208.4 60.7 all-gather.8
  272.2 63.5 all-gather.10

commit v15 on v14

--- a/solution.py
+++ b/solution.py
@@ -88,11 +88,11 @@
             outgoing = others(piece)
             if len(mine) == len(order):
                 x_out["v"] = x_chain(theirs)
-                outgoing = lax.optimization_barrier((outgoing, x_out["v"][4][:-1] or x_out["v"][4]))[0]
+                outgoing = lax.optimization_barrier((outgoing, x_out["v"][4][:2]))[0]
             theirs.append(swap(outgoing, "ay"))
         s_a, s_b, early_part, sent, got_x, cuts, hw, halves = x_out["v"]
         early = list(early_part)
-        _, _, late_give, t_give = lax.optimization_barrier((tuple(sent), got_x[-1], early[2], theirs[2]))
+        _, _, late_give, t_give = lax.optimization_barrier((tuple(sent), got_x[2:], early[2], theirs[2]))
         late_keep, t_keep = early[3], theirs[3]
         out = jnp.zeros((width, rw), jnp.float32)
         for h, rows in enumerate(cuts):

time: 451 us -> 450 us (level)
  transfers between devices with their start and end apart: 22 -> 22, of which waited for: 9 -> 11; matrix products, arithmetic and copies ran while one was open for 21% -> 21% of each run, Pallas kernels for 0% -> 0%
where the time goes in v15:
time: 450 us; the launch traced here: 446 us
  waiting for transfers between devices  305 us (68%)
  matrix products  68.4 us (15%)
  starting transfers between devices  22.5 us (5%)
  local copies, waits for them, and re-layouts  19.5 us (4%)
  other arithmetic  15.4 us (3%)
  between operations  15 us (3%)
    ppermute x17, waiting for transfers between devices, swap(): return lax.ppermute(x, axis, [(0, 1), (1, 0)])  271 us
    dot_general x24, matrix products, contract(): lax.dot_general(left, right, (((0,), (0,)), ((), ())), preferred_element_...  68.4 us
    all_gather x3, waiting for transfers between devices, body(): lax.all_gather(lax.dynamic_slice_in_dim(rest, m * rw, rw, axis=1), 'az',...  30.3 us
    ppermute x17, starting transfers between devices, swap(): return lax.ppermute(x, axis, [(0, 1), (1, 0)])  15.9 us
    concatenate x5, other arithmetic, others(): doubled = jnp.concatenate([v, v], axis=0)  14.3 us
  transfers between devices with their start and end apart: 22, of which 11 were waited for; matrix products, arithmetic and copies ran while one was open for 21% of the time, Pallas kernels for 0%

profile of v15, /device:TPU:0, one launch (start us, length us, event | category | flops | bytes accessed | tf_op | source)
XLA Modules:
  0.0 445.6 jit_solution(14394021531830130852)
XLA Ops:
  6.5 2.2 constant_dynamic-slice_fusion.3
  8.9 3.0 collective-permute-start
  14.3 66.0 %collective-permute-done = bf16[192,8192]{1,0:T(8,128)(2,1)} collective-permute-done((bf16[192,8192]{1,0:T(8,128)(2,1)}, bf16[192,8192]{1,0:T(8,128)(2,1)}, u32[]{:S(2)}, u32[]{:S(2)}) %collective-permute-start) | collective-permute-done | bytes 3145760 | tf_op jit(solution)/shard_map/ppermute | solution.py:30
  80.3 2.1 constant_dynamic-slice_fusion.2
  83.2 2.1 copy.12
  85.3 6.3 %all-to-all-start = ((bf16[192,8,1024]{2,0,1:T(8,128)(2,1)}), bf16[192,8,1024]{2,0,1:T(8,128)(2,1)}, u32[]{:S(2)}, u32[]{:S(2)}) async-start(bf16[192,8,1024]{2,0,1:T(8,128)(2,1)} %bitcast.34), calls=%async_computation | async-start | bytes 6291456 | tf_op jit(solution)/shard_map/all_to_all | solution.py:57
  91.7 3.9 fusion.26
  95.6 2.0 collective-permute-start.1
  97.5 78.3 %collective-permute-done.1 = bf16[576,2048]{1,0:T(8,128)(2,1)S(1)} collective-permute-done((bf16[576,2048]{1,0:T(8,128)(2,1)}, bf16[576,2048]{1,0:T(8,128)(2,1)S(1)}, u32[]{:S(2)}, u32[]{:S(2)}) %collective-permute-start.1) | collective-permute-done | bytes 2359328 | tf_op jit(solution)/shard_map/ppermute | solution.py:30
  175.8 30.3 %all-gather.7.cloned.1.call-done = bf16[768,2048]{1,0:T(8,128)(2,1)} async-done(((bf16[192,2048]{1,0:T(8,128)(2,1)}), bf16[768,2048]{1,0:T(8,128)(2,1)}) %all-gather.7.cloned.1.call-update) | async-done | bytes 3145744 | tf_op jit(solution)/shard_map/all_gather | solution.py:86
  206.1 2.1 constant_dynamic-slice_fusion.1
  208.5 3.6 all-to-all-done
  212.1 2.7 constant_dynamic-slice_fusion.5
  215.4 2.6 fusion.25
  219.5 3.5 fusion.70
  224.5 2.5 convolution_add_fusion.1
  227.0 2.0 fusion.22
  229.0 2.0 fusion.20
  231.5 2.0 fusion.18
  233.5 2.2 fusion.16
  236.2 33.8 %collective-permute-done.2 = bf16[576,2048]{1,0:T(8,128)(2,1)} collective-permute-done((bf16[576,2048]{1,0:T(8,128)(2,1)S(1)}, bf16[576,2048]{1,0:T(8,128)(2,1)}, u32[]{:S(2)}, u32[]{:S(2)}) %collective-permute-start.2) | collective-permute-done | bytes 2359328 | tf_op jit(solution)/shard_map/ppermute | solution.py:30
  270.0 2.1 constant_dynamic-slice_fusion
  272.1 5.6 %fusion.69 = f32[1024,2048]{1,0:T(8,128)S(1)} fusion(bf16[768,1024]{1,0:T(8,128)(2,1)S(1)} %bitcast.42, bf16[768,2048]{1,0:T(8,128)(2,1)} %all-gather.7.cloned.1.call-done), kind=kOutput, calls=%fused_computation.107 | convolution fusion | flops 3221225472 | bytes 13107200 | tf_op jit(solution)/shard_map/dot_general | solution.py:24
  277.7 2.5 convolution_add_fusion.2
  280.2 3.4 fusion.21
  285.1 2.6 fusion.23
  287.6 1.9 collective-permute-start.12
  289.5 3.0 fusion.19
  293.1 4.0 fusion.17
  298.6 4.0 fusion.15
  303.1 3.9 fusion.71
  307.0 2.5 convolution_add_fusion
  309.8 22.5 %collective-permute-done.10 = bf16[256,2048]{1,0:T(8,128)(2,1)S(1)} collective-permute-done((bf16[256,2048]{1,0:T(8,128)(2,1)S(1)}, bf16[256,2048]{1,0:T(8,128)(2,1)S(1)}, u32[]{:S(2)}, u32[]{:S(2)}) %collective-permute-start.10) | collective-permute-done | bytes 1048608 | tf_op jit(solution)/shard_map/ppermute | solution.py:30
  332.2 7.4 %collective-permute-done.12 = bf16[576,2048]{1,0:T(8,128)(2,1)S(1)} collective-permute-done((bf16[576,2048]{1,0:T(8,128)(2,1)S(1)}, bf16[576,2048]{1,0:T(8,128)(2,1)S(1)}, u32[]{:S(2)}, u32[]{:S(2)}) %collective-permute-start.12) | collective-permute-done | bytes 2359328 | tf_op jit(solution)/shard_map/ppermute | solution.py:30
  339.6 2.4 slice_add_fusion
  342.0 3.7 fusion.24
  345.8 9.0 %collective-permute-done.6 = bf16[256,2048]{1,0:T(8,128)(2,1)} collective-permute-done((bf16[256,2048]{1,0:T(8,128)(2,1)}, bf16[256,2048]{1,0:T(8,128)(2,1)}, u32[]{:S(2)}, u32[]{:S(2)}) %collective-permute-start.6) | collective-permute-done | bytes 1048608 | tf_op jit(solution)/shard_map/ppermute | solution.py:30
  354.8 20.4 %collective-permute-done.4 = bf16[256,2048]{1,0:T(8,128)(2,1)} collective-permute-done((bf16[256,2048]{1,0:T(8,128)(2,1)}, bf16[256,2048]{1,0:T(8,128)(2,1)}, u32[]{:S(2)}, u32[]{:S(2)}) %collective-permute-start.4) | collective-permute-done | bytes 1048608 | tf_op jit(solution)/shard_map/ppermute | solution.py:30
  376.7 4.0 slice_add_fusion.3
  381.2 2.3 slice_add_fusion.2
  383.6 2.3 slice_add_fusion.1
  386.7 3.6 fusion.68
  390.2 2.8 convolution_add_fusion.3
  393.0 33.3 %collective-permute-done.7 = bf16[576,2048]{1,0:T(8,128)(2,1)S(1)} collective-permute-done((bf16[576,2048]{1,0:T(8,128)(2,1)S(1)}, bf16[576,2048]{1,0:T(8,128)(2,1)S(1)}, u32[]{:S(2)}, u32[]{:S(2)}) %collective-permute-start.7) | collective-permute-done | bytes 2359328 | tf_op jit(solution)/shard_map/ppermute | solution.py:30
  426.4 2.3 fusion.8
  429.7 2.4 fusion.10
  433.2 3.4 copy-done.5
  436.6 2.3 fusion.14
  (84 shorter events, 16.1 us)
Async XLA Ops:
  6.5 7.4 %copy-start.20 = (s32[192]{0:T(256)S(1)}, s32[192]{0:T(256)}, u32[]{:S(2)}) copy-start(s32[192]{0:T(256)} %param.7) | copy-start | bytes 2308
  6.5 7.5 %copy-start.19 = (f32[1536]{0:T(1024)S(1)}, f32[1536]{0:T(1024)}, u32[]{:S(2)}) copy-start(f32[1536]{0:T(1024)} %param.9) | copy-start | bytes 18436
  6.5 73.8 %all-gather.5.cloned.1.call-start = ((), (), s32[]{:S(2)}) async-start(), calls=%async_computation.1 | async-start | bytes 3932160 | tf_op jit(solution)/shard_map/all_gather | solution.py:54
  6.5 75.9 %copy-start.4 = (bf16[192,8192]{1,0:T(8,128)(2,1)S(1)}, bf16[192,8192]{1,0:T(8,128)(2,1)}, u32[]{:S(2)}) copy-start(bf16[192,8192]{1,0:T(8,128)(2,1)} %param.6) | copy-start | bytes 9437188
  8.8 197.3 %all-gather.7.cloned.1.call-start = ((), (), s32[]{:S(2)}) async-start(), calls=%async_computation.2 | async-start | bytes 3932160 | tf_op jit(solution)/shard_map/all_gather | solution.py:86
  8.9 71.5 %collective-permute-start = (bf16[192,8192]{1,0:T(8,128)(2,1)}, bf16[192,8192]{1,0:T(8,128)(2,1)}, u32[]{:S(2)}, u32[]{:S(2)}) collective-permute-start(bf16[192,8192]{1,0:T(8,128)(2,1)} %param.6), channel_id=1, source_target_pairs={{0,1},{1,0},{2,3},{3,2},{4,5},{5,4},{6,7},{7,6},{8,9},{9,8},{10,11... | collective-permute-start | bytes 9437192 | tf_op jit(solution)/shard_map/ppermute | solution.py:30
  85.3 6.4 %copy-start.6 = (bf16[768,2048]{1,0:T(8,128)(2,1)S(1)}, bf16[768,2048]{1,0:T(8,128)(2,1)}, u32[]{:S(2)}) copy-start(bf16[768,2048]{1,0:T(8,128)(2,1)} %all-gather.5.cloned.1.call-done) | copy-start | bytes 9437188
  85.3 126.8 %all-to-all-start = ((bf16[192,8,1024]{2,0,1:T(8,128)(2,1)}), bf16[192,8,1024]{2,0,1:T(8,128)(2,1)}, u32[]{:S(2)}, u32[]{:S(2)}) async-start(bf16[192,8,1024]{2,0,1:T(8,128)(2,1)} %bitcast.34), calls=%async_computation | async-start | bytes 6291456 | tf_op jit(solution)/shard_map/all_to_all | solution.py:57
  91.6 178.4 %all-gather.9.cloned.1.call-start = ((), (), s32[]{:S(2)}) async-start(), calls=%async_computation.3 | async-start | bytes 3932160 | tf_op jit(solution)/shard_map/all_gather | solution.py:86
  95.6 80.3 %collective-permute-start.1 = (bf16[576,2048]{1,0:T(8,128)(2,1)}, bf16[576,2048]{1,0:T(8,128)(2,1)S(1)}, u32[]{:S(2)}, u32[]{:S(2)}) collective-permute-start(bf16[576,2048]{1,0:T(8,128)(2,1)} %fusion.26), channel_id=1, source_target_pairs={{0,1},{1,0},{2,3},{3,2},{4,5},{5,4},{6,7},{7,6},{8,9},{9,8},{10,11... | collective-permute-start | bytes 7077896 | tf_op jit(solution)/shard_map/ppermute | solution.py:30
  208.3 133.8 %all-gather.11.cloned.1.call-start = ((), (), s32[]{:S(2)}) async-start(), calls=%async_computation.4 | async-start | bytes 3932160 | tf_op jit(solution)/shard_map/all_gather | solution.py:86
  212.1 3.3 copy-start.8
  215.4 4.0 copy-start.11
  215.4 9.1 %copy-start.2 = (bf16[4,1,192,1024]{3,2,1,0:T(8,128)(2,1)}, bf16[4,1,192,1024]{3,2,1,0:T(8,128)(2,1)S(1)}, u32[]{:S(2)}) copy-start(bf16[4,1,192,1024]{3,2,1,0:T(8,128)(2,1)S(1)} %get-tuple-element.21) | copy-start | bytes 4718596
  215.4 4.0 copy-start.7
  218.0 52.0 %collective-permute-start.2 = (bf16[576,2048]{1,0:T(8,128)(2,1)S(1)}, bf16[576,2048]{1,0:T(8,128)(2,1)}, u32[]{:S(2)}, u32[]{:S(2)}) collective-permute-start(bf16[576,2048]{1,0:T(8,128)(2,1)S(1)} %fusion.25), channel_id=1, source_target_pairs={{0,1},{1,0},{2,3},{3,2},{4,5},{5,4},{6,7},{7,6},{8,9},{9,8},{10,11... | collective-permute-start | bytes 7077896 | tf_op jit(solution)/shard_map/ppermute | solution.py:30
  229.0 51.2 %collective-permute-start.9 = (bf16[256,2048]{1,0:T(8,128)(2,1)}, bf16[256,2048]{1,0:T(8,128)(2,1)}, u32[]{:S(2)}, u32[]{:S(2)}) collective-permute-start(bf16[256,2048]{1,0:T(8,128)(2,1)} %fusion.22), channel_id=1, source_target_pairs={{0,8},{8,0},{1,9},{9,1},{2,10},{10,2},{3,11},{11,3},{4,12},{12,4},... | collective-permute-start | bytes 3145736 | tf_op jit(solution)/shard_map/ppermute | solution.py:30
  231.0 58.5 %collective-permute-start.8 = (bf16[256,2048]{1,0:T(8,128)(2,1)}, bf16[256,2048]{1,0:T(8,128)(2,1)}, u32[]{:S(2)}, u32[]{:S(2)}) collective-permute-start(bf16[256,2048]{1,0:T(8,128)(2,1)} %fusion.20), channel_id=1, source_target_pairs={{0,8},{8,0},{1,9},{9,1},{2,10},{10,2},{3,11},{11,3},{4,12},{12,4},... | collective-permute-start | bytes 3145736 | tf_op jit(solution)/shard_map/ppermute | solution.py:30
  233.5 59.6 %collective-permute-start.5 = (bf16[256,2048]{1,0:T(8,128)(2,1)}, bf16[256,2048]{1,0:T(8,128)(2,1)}, u32[]{:S(2)}, u32[]{:S(2)}) collective-permute-start(bf16[256,2048]{1,0:T(8,128)(2,1)} %fusion.18), channel_id=1, source_target_pairs={{0,8},{8,0},{1,9},{9,1},{2,10},{10,2},{3,11},{11,3},{4,12},{12,4},... | collective-permute-start | bytes 3145736 | tf_op jit(solution)/shard_map/ppermute | solution.py:30
  235.7 36.4 %copy-start.12 = (bf16[4,1,192,1024]{3,2,1,0:T(8,128)(2,1)S(1)}, bf16[4,1,192,1024]{3,2,1,0:T(8,128)(2,1)}, u32[]{:S(2)}) copy-start(bf16[4,1,192,1024]{3,2,1,0:T(8,128)(2,1)} %copy-done.11) | copy-start | bytes 4718596
  235.7 62.9 %collective-permute-start.3 = (bf16[256,2048]{1,0:T(8,128)(2,1)}, bf16[256,2048]{1,0:T(8,128)(2,1)}, u32[]{:S(2)}, u32[]{:S(2)}) collective-permute-start(bf16[256,2048]{1,0:T(8,128)(2,1)} %fusion.16), channel_id=1, source_target_pairs={{0,8},{8,0},{1,9},{9,1},{2,10},{10,2},{3,11},{11,3},{4,12},{12,4},... | collective-permute-start | bytes 3145736 | tf_op jit(solution)/shard_map/ppermute | solution.py:30
  272.1 5.6 %copy-start.3 = (bf16[4,1,192,1024]{3,2,1,0:T(8,128)(2,1)S(1)}, bf16[4,1,192,1024]{3,2,1,0:T(8,128)(2,1)}, u32[]{:S(2)}) copy-start(bf16[4,1,192,1024]{3,2,1,0:T(8,128)(2,1)} %copy-done.2) | copy-start | bytes 4718596
  280.2 4.9 %copy-start.9 = (bf16[768,2048]{1,0:T(8,128)(2,1)S(1)}, bf16[768,2048]{1,0:T(8,128)(2,1)}, u32[]{:S(2)}) copy-start(bf16[768,2048]{1,0:T(8,128)(2,1)} %all-gather.9.cloned.1.call-done) | copy-start | bytes 9437188
  283.6 26.2 %collective-permute-start.11 = (bf16[256,2048]{1,0:T(8,128)(2,1)S(1)}, bf16[256,2048]{1,0:T(8,128)(2,1)S(1)}, u32[]{:S(2)}, u32[]{:S(2)}) collective-permute-start(bf16[256,2048]{1,0:T(8,128)(2,1)S(1)} %fusion.21), channel_id=1, source_target_pairs={{0,16},{16,0},{1,17},{17,1},{2,18},{18,2},{3,19},{19,3},{4,20},{20... | collective-permute-start | bytes 3145736 | tf_op jit(solution)/shard_map/ppermute | solution.py:30
  287.6 52.0 %collective-permute-start.12 = (bf16[576,2048]{1,0:T(8,128)(2,1)S(1)}, bf16[576,2048]{1,0:T(8,128)(2,1)S(1)}, u32[]{:S(2)}, u32[]{:S(2)}) collective-permute-start(bf16[576,2048]{1,0:T(8,128)(2,1)S(1)} %fusion.23), channel_id=1, source_target_pairs={{0,1},{1,0},{2,3},{3,2},{4,5},{5,4},{6,7},{7,6},{8,9},{9,8},{10,11... | collective-permute-start | bytes 7077896 | tf_op jit(solution)/shard_map/ppermute | solution.py:30
  292.5 39.7 %collective-permute-start.10 = (bf16[256,2048]{1,0:T(8,128)(2,1)S(1)}, bf16[256,2048]{1,0:T(8,128)(2,1)S(1)}, u32[]{:S(2)}, u32[]{:S(2)}) collective-permute-start(bf16[256,2048]{1,0:T(8,128)(2,1)S(1)} %fusion.19), channel_id=1, source_target_pairs={{0,16},{16,0},{1,17},{17,1},{2,18},{18,2},{3,19},{19,3},{4,20},{20... | collective-permute-start | bytes 3145736 | tf_op jit(solution)/shard_map/ppermute | solution.py:30
  297.1 6.0 %copy-start.13 = (bf16[4,1,192,1024]{3,2,1,0:T(8,128)(2,1)S(1)}, bf16[4,1,192,1024]{3,2,1,0:T(8,128)(2,1)}, u32[]{:S(2)}) copy-start(bf16[4,1,192,1024]{3,2,1,0:T(8,128)(2,1)} %copy-done.11) | copy-start | bytes 4718596
  297.1 57.8 %collective-permute-start.6 = (bf16[256,2048]{1,0:T(8,128)(2,1)}, bf16[256,2048]{1,0:T(8,128)(2,1)}, u32[]{:S(2)}, u32[]{:S(2)}) collective-permute-start(bf16[256,2048]{1,0:T(8,128)(2,1)} %fusion.17), channel_id=1, source_target_pairs={{0,16},{16,0},{1,17},{17,1},{2,18},{18,2},{3,19},{19,3},{4,20},{20... | collective-permute-start | bytes 3145736 | tf_op jit(solution)/shard_map/ppermute | solution.py:30
  302.6 72.6 %collective-permute-start.4 = (bf16[256,2048]{1,0:T(8,128)(2,1)}, bf16[256,2048]{1,0:T(8,128)(2,1)}, u32[]{:S(2)}, u32[]{:S(2)}) collective-permute-start(bf16[256,2048]{1,0:T(8,128)(2,1)} %fusion.15), channel_id=1, source_target_pairs={{0,16},{16,0},{1,17},{17,1},{2,18},{18,2},{3,19},{19,3},{4,20},{20... | collective-permute-start | bytes 3145736 | tf_op jit(solution)/shard_map/ppermute | solution.py:30
  309.5 30.1 %copy-start = (f32[1024,2048]{1,0:T(8,128)}, f32[1024,2048]{1,0:T(8,128)S(1)}, u32[]{:S(2)}) copy-start(f32[1024,2048]{1,0:T(8,128)S(1)} %convolution_add_fusion) | copy-start | bytes 25165828
  309.8 29.8 %copy-start.15 = (bf16[256,2048]{1,0:T(8,128)(2,1)}, bf16[256,2048]{1,0:T(8,128)(2,1)S(1)}, u32[]{:S(2)}) copy-start(bf16[256,2048]{1,0:T(8,128)(2,1)S(1)} %collective-permute-done.11) | copy-start | bytes 3145732
  332.2 7.4 %copy-start.17 = (bf16[256,2048]{1,0:T(8,128)(2,1)}, bf16[256,2048]{1,0:T(8,128)(2,1)S(1)}, u32[]{:S(2)}) copy-start(bf16[256,2048]{1,0:T(8,128)(2,1)S(1)} %collective-permute-done.10) | copy-start | bytes 3145732
  342.0 39.2 %copy-start.1 = (f32[1024,2048]{1,0:T(8,128)S(1)}, f32[1024,2048]{1,0:T(8,128)}, u32[]{:S(2)}) copy-start(f32[1024,2048]{1,0:T(8,128)} %copy-done) | copy-start | bytes 25165828
  375.2 51.2 %collective-permute-start.7 = (bf16[576,2048]{1,0:T(8,128)(2,1)S(1)}, bf16[576,2048]{1,0:T(8,128)(2,1)S(1)}, u32[]{:S(2)}, u32[]{:S(2)}) collective-permute-start(bf16[576,2048]{1,0:T(8,128)(2,1)S(1)} %fusion.24), channel_id=1, source_target_pairs={{0,1},{1,0},{2,3},{3,2},{4,5},{5,4},{6,7},{7,6},{8,9},{9,8},{10,11... | collective-permute-start | bytes 7077896 | tf_op jit(solution)/shard_map/ppermute | solution.py:30
  380.7 52.5 %collective-permute-start.16 = (f32[256,2048]{1,0:T(8,128)}, f32[256,2048]{1,0:T(8,128)S(1)}, u32[]{:S(2)}, u32[]{:S(2)}) collective-permute-start(f32[256,2048]{1,0:T(8,128)} %slice_add_fusion), channel_id=1, source_target_pairs={{0,8},{8,0},{1,9},{9,1},{2,10},{10,2},{3,11},{11,3},{4,12},{12,4},... | collective-permute-start | bytes 6291464 | tf_op jit(solution)/shard_map/ppermute | solution.py:30
  380.7 12.3 %collective-permute-start.13 = (f32[256,2048]{1,0:T(8,128)}, f32[256,2048]{1,0:T(8,128)S(1)}, u32[]{:S(2)}, u32[]{:S(2)}) collective-permute-start(f32[256,2048]{1,0:T(8,128)} %slice_add_fusion.3), channel_id=1, source_target_pairs={{0,8},{8,0},{1,9},{9,1},{2,10},{10,2},{3,11},{11,3},{4,12},{12,4},... | collective-permute-start | bytes 6291464 | tf_op jit(solution)/shard_map/ppermute | solution.py:30
  383.5 2.8 copy-start.10
  383.5 3.1 copy-start.14
  383.5 46.2 %collective-permute-start.14 = (f32[256,2048]{1,0:T(8,128)}, f32[256,2048]{1,0:T(8,128)S(1)}, u32[]{:S(2)}, u32[]{:S(2)}) collective-permute-start(f32[256,2048]{1,0:T(8,128)} %slice_add_fusion.2), channel_id=1, source_target_pairs={{0,8},{8,0},{1,9},{9,1},{2,10},{10,2},{3,11},{11,3},{4,12},{12,4},... | collective-permute-start | bytes 6291464 | tf_op jit(solution)/shard_map/ppermute | solution.py:30
  385.9 46.3 %collective-permute-start.15 = (f32[256,2048]{1,0:T(8,128)}, f32[256,2048]{1,0:T(8,128)S(1)}, u32[]{:S(2)}, u32[]{:S(2)}) collective-permute-start(f32[256,2048]{1,0:T(8,128)} %slice_add_fusion.1), channel_id=1, source_target_pairs={{0,8},{8,0},{1,9},{9,1},{2,10},{10,2},{3,11},{11,3},{4,12},{12,4},... | collective-permute-start | bytes 6291464 | tf_op jit(solution)/shard_map/ppermute | solution.py:30
  429.7 2.4 copy-start.18
  432.1 4.5 copy-start.16
  433.2 3.4 copy-start.5
Sparse Core Ops, SparseCore 0:
  8.9 66.1 all-gather.4
  82.6 123.4 all-gather.6
  208.4 60.7 all-gather.8
  272.2 63.5 all-gather.10

commit v16 on v15

--- a/solution.py
+++ b/solution.py
@@ -88,11 +88,11 @@
             outgoing = others(piece)
             if len(mine) == len(order):
                 x_out["v"] = x_chain(theirs)
-                outgoing = lax.optimization_barrier((outgoing, x_out["v"][4][:2]))[0]
+                outgoing = lax.optimization_barrier((outgoing, x_out["v"][3]))[0]
             theirs.append(swap(outgoing, "ay"))
         s_a, s_b, early_part, sent, got_x, cuts, hw, halves = x_out["v"]
         early = list(early_part)
-        _, _, late_give, t_give = lax.optimization_barrier((tuple(sent), got_x[2:], early[2], theirs[2]))
+        _, _, late_give, t_give = lax.optimization_barrier((tuple(sent), got_x, early[2], theirs[2]))
         late_keep, t_keep = early[3], theirs[3]
         out = jnp.zeros((width, rw), jnp.float32)
         for h, rows in enumerate(cuts):

time: 450 us -> 455 us (1.011)
  waiting for transfers between devices: 305 us -> 313 us
  matrix products: 68.4 us -> 63.8 us
    ppermute x17, waiting for transfers between devices: 271 us -> 279 us  [swap(): return lax.ppermute(x, axis, [(0, 1), (1, 0)])]
    dot_general x24, matrix products: 68.4 us -> 63.8 us  [contract(): lax.dot_general(left, right, (((0,), (0,)), ((), ())), preferred_element_...]
  transfers between devices with their start and end apart: 22 -> 22, of which waited for: 11 -> 10; matrix products, arithmetic and copies ran while one was open for 21% -> 19% of each run, Pallas kernels for 0% -> 0%
where the time goes in v16:
time: 455 us; the launch traced here: 450 us
  waiting for transfers between devices  313 us (69%)
  matrix products  63.8 us (14%)
  starting transfers between devices  22.7 us (5%)
  local copies, waits for them, and re-layouts  20.6 us (5%)
  other arithmetic  15.4 us (3%)
  between operations  15 us (3%)
    ppermute x17, waiting for transfers between devices, swap(): return lax.ppermute(x, axis, [(0, 1), (1, 0)])  279 us
    dot_general x24, matrix products, contract(): lax.dot_general(left, right, (((0,), (0,)), ((), ())), preferred_element_...  63.8 us
    all_gather x3, waiting for transfers between devices, body(): lax.all_gather(lax.dynamic_slice_in_dim(rest, m * rw, rw, axis=1), 'az',...  30.3 us
    ppermute x17, starting transfers between devices, swap(): return lax.ppermute(x, axis, [(0, 1), (1, 0)])  16.1 us
    concatenate x5, other arithmetic, others(): doubled = jnp.concatenate([v, v], axis=0)  14.4 us
  transfers between devices with their start and end apart: 22, of which 10 were waited for; matrix products, arithmetic and copies ran while one was open for 19% of the time, Pallas kernels for 0%

profile of v16, /device:TPU:0, one launch (start us, length us, event | category | flops | bytes accessed | tf_op | source)
XLA Modules:
  0.0 450.1 jit_solution(16433631382235604546)
XLA Ops:
  6.5 2.2 constant_dynamic-slice_fusion.3
  8.9 3.0 collective-permute-start
  14.3 66.0 %collective-permute-done = bf16[192,8192]{1,0:T(8,128)(2,1)} collective-permute-done((bf16[192,8192]{1,0:T(8,128)(2,1)}, bf16[192,8192]{1,0:T(8,128)(2,1)}, u32[]{:S(2)}, u32[]{:S(2)}) %collective-permute-start) | collective-permute-done | bytes 3145760 | tf_op jit(solution)/shard_map/ppermute | solution.py:30
  80.3 2.1 constant_dynamic-slice_fusion.2
  83.1 2.1 copy.12
  85.2 6.3 %all-to-all-start = ((bf16[192,8,1024]{2,0,1:T(8,128)(2,1)}), bf16[192,8,1024]{2,0,1:T(8,128)(2,1)}, u32[]{:S(2)}, u32[]{:S(2)}) async-start(bf16[192,8,1024]{2,0,1:T(8,128)(2,1)} %bitcast.34), calls=%async_computation | async-start | bytes 6291456 | tf_op jit(solution)/shard_map/all_to_all | solution.py:57
  91.6 4.0 fusion.26
  95.6 2.0 collective-permute-start.1
  97.6 78.2 %collective-permute-done.1 = bf16[576,2048]{1,0:T(8,128)(2,1)S(1)} collective-permute-done((bf16[576,2048]{1,0:T(8,128)(2,1)}, bf16[576,2048]{1,0:T(8,128)(2,1)S(1)}, u32[]{:S(2)}, u32[]{:S(2)}) %collective-permute-start.1) | collective-permute-done | bytes 2359328 | tf_op jit(solution)/shard_map/ppermute | solution.py:30
  175.8 30.3 %all-gather.7.cloned.1.call-done = bf16[768,2048]{1,0:T(8,128)(2,1)} async-done(((bf16[192,2048]{1,0:T(8,128)(2,1)}), bf16[768,2048]{1,0:T(8,128)(2,1)}) %all-gather.7.cloned.1.call-update) | async-done | bytes 3145744 | tf_op jit(solution)/shard_map/all_gather | solution.py:86
  206.1 2.1 constant_dynamic-slice_fusion.1
  208.4 3.7 all-to-all-done
  212.1 2.6 constant_dynamic-slice_fusion.5
  215.4 2.6 fusion.25
  219.4 3.5 fusion.70
  224.5 2.5 convolution_add_fusion.1
  227.0 2.0 fusion.22
  229.0 2.0 fusion.20
  231.5 2.0 fusion.18
  233.5 2.2 fusion.16
  236.2 33.8 %collective-permute-done.2 = bf16[576,2048]{1,0:T(8,128)(2,1)} collective-permute-done((bf16[576,2048]{1,0:T(8,128)(2,1)S(1)}, bf16[576,2048]{1,0:T(8,128)(2,1)}, u32[]{:S(2)}, u32[]{:S(2)}) %collective-permute-start.2) | collective-permute-done | bytes 2359328 | tf_op jit(solution)/shard_map/ppermute | solution.py:30
  269.9 2.1 constant_dynamic-slice_fusion
  272.1 5.6 %fusion.69 = f32[1024,2048]{1,0:T(8,128)S(1)} fusion(bf16[768,1024]{1,0:T(8,128)(2,1)S(1)} %bitcast.42, bf16[768,2048]{1,0:T(8,128)(2,1)} %all-gather.7.cloned.1.call-done), kind=kOutput, calls=%fused_computation.107 | convolution fusion | flops 3221225472 | bytes 13107200 | tf_op jit(solution)/shard_map/dot_general | solution.py:24
  277.6 2.5 convolution_add_fusion.2
  280.2 3.4 fusion.21
  285.0 2.6 fusion.23
  287.6 1.9 collective-permute-start.12
  289.5 3.0 fusion.19
  293.0 3.0 fusion.17
  296.0 1.6 collective-permute-start.9
  297.6 3.0 fusion.15
  301.2 3.9 fusion.71
  305.1 2.5 convolution_add_fusion
  307.6 2.1 collective-permute-done.11
  309.7 22.5 %collective-permute-done.10 = bf16[256,2048]{1,0:T(8,128)(2,1)S(1)} collective-permute-done((bf16[256,2048]{1,0:T(8,128)(2,1)S(1)}, bf16[256,2048]{1,0:T(8,128)(2,1)S(1)}, u32[]{:S(2)}, u32[]{:S(2)}) %collective-permute-start.10) | collective-permute-done | bytes 1048608 | tf_op jit(solution)/shard_map/ppermute | solution.py:30
  332.2 22.5 %collective-permute-done.9 = bf16[256,2048]{1,0:T(8,128)(2,1)S(1)} collective-permute-done((bf16[256,2048]{1,0:T(8,128)(2,1)S(1)}, bf16[256,2048]{1,0:T(8,128)(2,1)S(1)}, u32[]{:S(2)}, u32[]{:S(2)}) %collective-permute-start.9) | collective-permute-done | bytes 1048608 | tf_op jit(solution)/shard_map/ppermute | solution.py:30
  354.6 20.3 %collective-permute-done.8 = bf16[256,2048]{1,0:T(8,128)(2,1)S(1)} collective-permute-done((bf16[256,2048]{1,0:T(8,128)(2,1)S(1)}, bf16[256,2048]{1,0:T(8,128)(2,1)S(1)}, u32[]{:S(2)}, u32[]{:S(2)}) %collective-permute-start.8) | collective-permute-done | bytes 1048608 | tf_op jit(solution)/shard_map/ppermute | solution.py:30
  376.0 2.4 slice_add_fusion
  378.3 3.7 fusion.24
  382.1 1.6 collective-permute-start.7
  383.6 4.0 slice_add_fusion.3
  388.1 2.3 slice_add_fusion.2
  390.5 2.3 slice_add_fusion.1
  393.6 3.6 fusion.68
  397.2 2.8 convolution_add_fusion.3
  400.0 33.3 %collective-permute-done.7 = bf16[576,2048]{1,0:T(8,128)(2,1)S(1)} collective-permute-done((bf16[576,2048]{1,0:T(8,128)(2,1)S(1)}, bf16[576,2048]{1,0:T(8,128)(2,1)S(1)}, u32[]{:S(2)}, u32[]{:S(2)}) %collective-permute-start.7) | collective-permute-done | bytes 2359328 | tf_op jit(solution)/shard_map/ppermute | solution.py:30
  437.7 3.4 copy-done.5
  441.1 2.3 fusion.14
  (92 shorter events, 16.0 us)
Async XLA Ops:
  6.5 7.4 %copy-start.24 = (s32[192]{0:T(256)S(1)}, s32[192]{0:T(256)}, u32[]{:S(2)}) copy-start(s32[192]{0:T(256)} %param.7) | copy-start | bytes 2308
  6.5 7.5 %copy-start.23 = (f32[1536]{0:T(1024)S(1)}, f32[1536]{0:T(1024)}, u32[]{:S(2)}) copy-start(f32[1536]{0:T(1024)} %param.9) | copy-start | bytes 18436
  6.5 73.8 %all-gather.5.cloned.1.call-start = ((), (), s32[]{:S(2)}) async-start(), calls=%async_computation.1 | async-start | bytes 3932160 | tf_op jit(solution)/shard_map/all_gather | solution.py:54
  6.5 75.9 %copy-start.4 = (bf16[192,8192]{1,0:T(8,128)(2,1)S(1)}, bf16[192,8192]{1,0:T(8,128)(2,1)}, u32[]{:S(2)}) copy-start(bf16[192,8192]{1,0:T(8,128)(2,1)} %param.6) | copy-start | bytes 9437188
  8.8 197.3 %all-gather.7.cloned.1.call-start = ((), (), s32[]{:S(2)}) async-start(), calls=%async_computation.2 | async-start | bytes 3932160 | tf_op jit(solution)/shard_map/all_gather | solution.py:86
  8.9 71.5 %collective-permute-start = (bf16[192,8192]{1,0:T(8,128)(2,1)}, bf16[192,8192]{1,0:T(8,128)(2,1)}, u32[]{:S(2)}, u32[]{:S(2)}) collective-permute-start(bf16[192,8192]{1,0:T(8,128)(2,1)} %param.6), channel_id=1, source_target_pairs={{0,1},{1,0},{2,3},{3,2},{4,5},{5,4},{6,7},{7,6},{8,9},{9,8},{10,11... | collective-permute-start | bytes 9437192 | tf_op jit(solution)/shard_map/ppermute | solution.py:30
  85.2 6.4 %copy-start.6 = (bf16[768,2048]{1,0:T(8,128)(2,1)S(1)}, bf16[768,2048]{1,0:T(8,128)(2,1)}, u32[]{:S(2)}) copy-start(bf16[768,2048]{1,0:T(8,128)(2,1)} %all-gather.5.cloned.1.call-done) | copy-start | bytes 9437188
  85.2 126.8 %all-to-all-start = ((bf16[192,8,1024]{2,0,1:T(8,128)(2,1)}), bf16[192,8,1024]{2,0,1:T(8,128)(2,1)}, u32[]{:S(2)}, u32[]{:S(2)}) async-start(bf16[192,8,1024]{2,0,1:T(8,128)(2,1)} %bitcast.34), calls=%async_computation | async-start | bytes 6291456 | tf_op jit(solution)/shard_map/all_to_all | solution.py:57
  91.6 178.4 %all-gather.9.cloned.1.call-start = ((), (), s32[]{:S(2)}) async-start(), calls=%async_computation.3 | async-start | bytes 3932160 | tf_op jit(solution)/shard_map/all_gather | solution.py:86
  95.6 80.2 %collective-permute-start.1 = (bf16[576,2048]{1,0:T(8,128)(2,1)}, bf16[576,2048]{1,0:T(8,128)(2,1)S(1)}, u32[]{:S(2)}, u32[]{:S(2)}) collective-permute-start(bf16[576,2048]{1,0:T(8,128)(2,1)} %fusion.26), channel_id=1, source_target_pairs={{0,1},{1,0},{2,3},{3,2},{4,5},{5,4},{6,7},{7,6},{8,9},{9,8},{10,11... | collective-permute-start | bytes 7077896 | tf_op jit(solution)/shard_map/ppermute | solution.py:30
  208.2 170.2 %all-gather.11.cloned.1.call-start = ((), (), s32[]{:S(2)}) async-start(), calls=%async_computation.4 | async-start | bytes 3932160 | tf_op jit(solution)/shard_map/all_gather | solution.py:86
  212.1 3.3 copy-start.8
  215.4 4.1 copy-start.11
  215.4 9.1 %copy-start.2 = (bf16[4,1,192,1024]{3,2,1,0:T(8,128)(2,1)}, bf16[4,1,192,1024]{3,2,1,0:T(8,128)(2,1)S(1)}, u32[]{:S(2)}) copy-start(bf16[4,1,192,1024]{3,2,1,0:T(8,128)(2,1)S(1)} %get-tuple-element.21) | copy-start | bytes 4718596
  215.4 4.0 copy-start.7
  218.0 52.0 %collective-permute-start.2 = (bf16[576,2048]{1,0:T(8,128)(2,1)S(1)}, bf16[576,2048]{1,0:T(8,128)(2,1)}, u32[]{:S(2)}, u32[]{:S(2)}) collective-permute-start(bf16[576,2048]{1,0:T(8,128)(2,1)S(1)} %fusion.25), channel_id=1, source_target_pairs={{0,1},{1,0},{2,3},{3,2},{4,5},{5,4},{6,7},{7,6},{8,9},{9,8},{10,11... | collective-permute-start | bytes 7077896 | tf_op jit(solution)/shard_map/ppermute | solution.py:30
  229.0 51.2 %collective-permute-start.6 = (bf16[256,2048]{1,0:T(8,128)(2,1)}, bf16[256,2048]{1,0:T(8,128)(2,1)}, u32[]{:S(2)}, u32[]{:S(2)}) collective-permute-start(bf16[256,2048]{1,0:T(8,128)(2,1)} %fusion.22), channel_id=1, source_target_pairs={{0,8},{8,0},{1,9},{9,1},{2,10},{10,2},{3,11},{11,3},{4,12},{12,4},... | collective-permute-start | bytes 3145736 | tf_op jit(solution)/shard_map/ppermute | solution.py:30
  231.0 58.5 %collective-permute-start.5 = (bf16[256,2048]{1,0:T(8,128)(2,1)}, bf16[256,2048]{1,0:T(8,128)(2,1)}, u32[]{:S(2)}, u32[]{:S(2)}) collective-permute-start(bf16[256,2048]{1,0:T(8,128)(2,1)} %fusion.20), channel_id=1, source_target_pairs={{0,8},{8,0},{1,9},{9,1},{2,10},{10,2},{3,11},{11,3},{4,12},{12,4},... | collective-permute-start | bytes 3145736 | tf_op jit(solution)/shard_map/ppermute | solution.py:30
  233.5 59.6 %collective-permute-start.4 = (bf16[256,2048]{1,0:T(8,128)(2,1)}, bf16[256,2048]{1,0:T(8,128)(2,1)}, u32[]{:S(2)}, u32[]{:S(2)}) collective-permute-start(bf16[256,2048]{1,0:T(8,128)(2,1)} %fusion.18), channel_id=1, source_target_pairs={{0,8},{8,0},{1,9},{9,1},{2,10},{10,2},{3,11},{11,3},{4,12},{12,4},... | collective-permute-start | bytes 3145736 | tf_op jit(solution)/shard_map/ppermute | solution.py:30
  235.7 36.4 %copy-start.12 = (bf16[4,1,192,1024]{3,2,1,0:T(8,128)(2,1)S(1)}, bf16[4,1,192,1024]{3,2,1,0:T(8,128)(2,1)}, u32[]{:S(2)}) copy-start(bf16[4,1,192,1024]{3,2,1,0:T(8,128)(2,1)} %copy-done.11) | copy-start | bytes 4718596
  235.7 62.0 %collective-permute-start.3 = (bf16[256,2048]{1,0:T(8,128)(2,1)}, bf16[256,2048]{1,0:T(8,128)(2,1)}, u32[]{:S(2)}, u32[]{:S(2)}) collective-permute-start(bf16[256,2048]{1,0:T(8,128)(2,1)} %fusion.16), channel_id=1, source_target_pairs={{0,8},{8,0},{1,9},{9,1},{2,10},{10,2},{3,11},{11,3},{4,12},{12,4},... | collective-permute-start | bytes 3145736 | tf_op jit(solution)/shard_map/ppermute | solution.py:30
  272.0 5.6 %copy-start.3 = (bf16[4,1,192,1024]{3,2,1,0:T(8,128)(2,1)S(1)}, bf16[4,1,192,1024]{3,2,1,0:T(8,128)(2,1)}, u32[]{:S(2)}) copy-start(bf16[4,1,192,1024]{3,2,1,0:T(8,128)(2,1)} %copy-done.2) | copy-start | bytes 4718596
  280.1 4.9 %copy-start.9 = (bf16[768,2048]{1,0:T(8,128)(2,1)S(1)}, bf16[768,2048]{1,0:T(8,128)(2,1)}, u32[]{:S(2)}) copy-start(bf16[768,2048]{1,0:T(8,128)(2,1)} %all-gather.9.cloned.1.call-done) | copy-start | bytes 9437188
  283.5 26.2 %collective-permute-start.11 = (bf16[256,2048]{1,0:T(8,128)(2,1)S(1)}, bf16[256,2048]{1,0:T(8,128)(2,1)S(1)}, u32[]{:S(2)}, u32[]{:S(2)}) collective-permute-start(bf16[256,2048]{1,0:T(8,128)(2,1)S(1)} %fusion.21), channel_id=1, source_target_pairs={{0,16},{16,0},{1,17},{17,1},{2,18},{18,2},{3,19},{19,3},{4,20},{20... | collective-permute-start | bytes 3145736 | tf_op jit(solution)/shard_map/ppermute | solution.py:30
  287.6 87.4 %collective-permute-start.12 = (bf16[576,2048]{1,0:T(8,128)(2,1)S(1)}, bf16[576,2048]{1,0:T(8,128)(2,1)S(1)}, u32[]{:S(2)}, u32[]{:S(2)}) collective-permute-start(bf16[576,2048]{1,0:T(8,128)(2,1)S(1)} %fusion.23), channel_id=1, source_target_pairs={{0,1},{1,0},{2,3},{3,2},{4,5},{5,4},{6,7},{7,6},{8,9},{9,8},{10,11... | collective-permute-start | bytes 7077896 | tf_op jit(solution)/shard_map/ppermute | solution.py:30
  292.5 39.7 %collective-permute-start.10 = (bf16[256,2048]{1,0:T(8,128)(2,1)S(1)}, bf16[256,2048]{1,0:T(8,128)(2,1)S(1)}, u32[]{:S(2)}, u32[]{:S(2)}) collective-permute-start(bf16[256,2048]{1,0:T(8,128)(2,1)S(1)} %fusion.19), channel_id=1, source_target_pairs={{0,16},{16,0},{1,17},{17,1},{2,18},{18,2},{3,19},{19,3},{4,20},{20... | collective-permute-start | bytes 3145736 | tf_op jit(solution)/shard_map/ppermute | solution.py:30
  296.0 5.1 %copy-start.13 = (bf16[4,1,192,1024]{3,2,1,0:T(8,128)(2,1)S(1)}, bf16[4,1,192,1024]{3,2,1,0:T(8,128)(2,1)}, u32[]{:S(2)}) copy-start(bf16[4,1,192,1024]{3,2,1,0:T(8,128)(2,1)} %copy-done.11) | copy-start | bytes 4718596
  296.0 58.6 %collective-permute-start.9 = (bf16[256,2048]{1,0:T(8,128)(2,1)S(1)}, bf16[256,2048]{1,0:T(8,128)(2,1)S(1)}, u32[]{:S(2)}, u32[]{:S(2)}) collective-permute-start(bf16[256,2048]{1,0:T(8,128)(2,1)S(1)} %fusion.17), channel_id=1, source_target_pairs={{0,16},{16,0},{1,17},{17,1},{2,18},{18,2},{3,19},{19,3},{4,20},{20... | collective-permute-start | bytes 3145736 | tf_op jit(solution)/shard_map/ppermute | solution.py:30
  300.6 74.4 %collective-permute-start.8 = (bf16[256,2048]{1,0:T(8,128)(2,1)S(1)}, bf16[256,2048]{1,0:T(8,128)(2,1)S(1)}, u32[]{:S(2)}, u32[]{:S(2)}) collective-permute-start(bf16[256,2048]{1,0:T(8,128)(2,1)S(1)} %fusion.15), channel_id=1, source_target_pairs={{0,16},{16,0},{1,17},{17,1},{2,18},{18,2},{3,19},{19,3},{4,20},{20... | collective-permute-start | bytes 3145736 | tf_op jit(solution)/shard_map/ppermute | solution.py:30
  307.6 67.4 %copy-start = (f32[1024,2048]{1,0:T(8,128)}, f32[1024,2048]{1,0:T(8,128)S(1)}, u32[]{:S(2)}) copy-start(f32[1024,2048]{1,0:T(8,128)S(1)} %convolution_add_fusion) | copy-start | bytes 25165828
  309.7 65.3 %copy-start.15 = (bf16[256,2048]{1,0:T(8,128)(2,1)}, bf16[256,2048]{1,0:T(8,128)(2,1)S(1)}, u32[]{:S(2)}) copy-start(bf16[256,2048]{1,0:T(8,128)(2,1)S(1)} %collective-permute-done.11) | copy-start | bytes 3145732
  332.2 42.8 %copy-start.17 = (bf16[256,2048]{1,0:T(8,128)(2,1)}, bf16[256,2048]{1,0:T(8,128)(2,1)S(1)}, u32[]{:S(2)}) copy-start(bf16[256,2048]{1,0:T(8,128)(2,1)S(1)} %collective-permute-done.10) | copy-start | bytes 3145732
  354.6 20.4 %copy-start.19 = (bf16[256,2048]{1,0:T(8,128)(2,1)}, bf16[256,2048]{1,0:T(8,128)(2,1)S(1)}, u32[]{:S(2)}) copy-start(bf16[256,2048]{1,0:T(8,128)(2,1)S(1)} %collective-permute-done.9) | copy-start | bytes 3145732
  375.0 1.0 copy-start.21
  378.3 9.8 %copy-start.1 = (f32[1024,2048]{1,0:T(8,128)S(1)}, f32[1024,2048]{1,0:T(8,128)}, u32[]{:S(2)}) copy-start(f32[1024,2048]{1,0:T(8,128)} %copy-done) | copy-start | bytes 25165828
  382.1 51.2 %collective-permute-start.7 = (bf16[576,2048]{1,0:T(8,128)(2,1)S(1)}, bf16[576,2048]{1,0:T(8,128)(2,1)S(1)}, u32[]{:S(2)}, u32[]{:S(2)}) collective-permute-start(bf16[576,2048]{1,0:T(8,128)(2,1)S(1)} %fusion.24), channel_id=1, source_target_pairs={{0,1},{1,0},{2,3},{3,2},{4,5},{5,4},{6,7},{7,6},{8,9},{9,8},{10,11... | collective-permute-start | bytes 7077896 | tf_op jit(solution)/shard_map/ppermute | solution.py:30
  387.6 50.0 %collective-permute-start.16 = (f32[256,2048]{1,0:T(8,128)}, f32[256,2048]{1,0:T(8,128)S(1)}, u32[]{:S(2)}, u32[]{:S(2)}) collective-permute-start(f32[256,2048]{1,0:T(8,128)} %slice_add_fusion), channel_id=1, source_target_pairs={{0,8},{8,0},{1,9},{9,1},{2,10},{10,2},{3,11},{11,3},{4,12},{12,4},... | collective-permute-start | bytes 6291464 | tf_op jit(solution)/shard_map/ppermute | solution.py:30
  387.6 12.4 %collective-permute-start.13 = (f32[256,2048]{1,0:T(8,128)}, f32[256,2048]{1,0:T(8,128)S(1)}, u32[]{:S(2)}, u32[]{:S(2)}) collective-permute-start(f32[256,2048]{1,0:T(8,128)} %slice_add_fusion.3), channel_id=1, source_target_pairs={{0,8},{8,0},{1,9},{9,1},{2,10},{10,2},{3,11},{11,3},{4,12},{12,4},... | collective-permute-start | bytes 6291464 | tf_op jit(solution)/shard_map/ppermute | solution.py:30
  390.5 2.8 copy-start.10
  390.5 3.1 copy-start.14
  390.5 44.9 %collective-permute-start.14 = (f32[256,2048]{1,0:T(8,128)}, f32[256,2048]{1,0:T(8,128)S(1)}, u32[]{:S(2)}, u32[]{:S(2)}) collective-permute-start(f32[256,2048]{1,0:T(8,128)} %slice_add_fusion.2), channel_id=1, source_target_pairs={{0,8},{8,0},{1,9},{9,1},{2,10},{10,2},{3,11},{11,3},{4,12},{12,4},... | collective-permute-start | bytes 6291464 | tf_op jit(solution)/shard_map/ppermute | solution.py:30
  392.8 43.8 %collective-permute-start.15 = (f32[256,2048]{1,0:T(8,128)}, f32[256,2048]{1,0:T(8,128)S(1)}, u32[]{:S(2)}, u32[]{:S(2)}) collective-permute-start(f32[256,2048]{1,0:T(8,128)} %slice_add_fusion.1), channel_id=1, source_target_pairs={{0,8},{8,0},{1,9},{9,1},{2,10},{10,2},{3,11},{11,3},{4,12},{12,4},... | collective-permute-start | bytes 6291464 | tf_op jit(solution)/shard_map/ppermute | solution.py:30
  397.2 36.1 %copy-start.22 = (bf16[256,2048]{1,0:T(8,128)(2,1)S(1)}, bf16[256,2048]{1,0:T(8,128)(2,1)}, u32[]{:S(2)}) copy-start(bf16[256,2048]{1,0:T(8,128)(2,1)} %copy-done.21) | copy-start | bytes 3145732
  434.3 1.2 copy-start.20
  435.4 1.3 copy-start.18
  436.6 4.5 copy-start.16
  437.7 3.4 copy-start.5
Sparse Core Ops, SparseCore 0:
  8.9 66.1 all-gather.4
  82.5 123.4 all-gather.6
  208.3 60.7 all-gather.8
  272.2 63.5 all-gather.10

commit v17 on v16

--- a/solution.py
+++ b/solution.py
@@ -88,11 +88,11 @@
             outgoing = others(piece)
             if len(mine) == len(order):
                 x_out["v"] = x_chain(theirs)
-                outgoing = lax.optimization_barrier((outgoing, x_out["v"][3]))[0]
+                outgoing = lax.optimization_barrier((outgoing, x_out["v"][4][:1]))[0]
             theirs.append(swap(outgoing, "ay"))
         s_a, s_b, early_part, sent, got_x, cuts, hw, halves = x_out["v"]
         early = list(early_part)
-        _, _, late_give, t_give = lax.optimization_barrier((tuple(sent), got_x, early[2], theirs[2]))
+        _, _, late_give, t_give = lax.optimization_barrier((tuple(sent), got_x[1:], early[2], theirs[2]))
         late_keep, t_keep = early[3], theirs[3]
         out = jnp.zeros((width, rw), jnp.float32)
         for h, rows in enumerate(cuts):

time: 455 us -> 449 us (0.987)
  waiting for transfers between devices: 313 us -> 305 us
    ppermute x17, waiting for transfers between devices: 279 us -> 271 us  [swap(): return lax.ppermute(x, axis, [(0, 1), (1, 0)])]
  transfers between devices with their start and end apart: 22 -> 22, of which waited for: 10 -> 10; matrix products, arithmetic and copies ran while one was open for 19% -> 20% of each run, Pallas kernels for 0% -> 0%
where the time goes in v17:
time: 449 us; the launch traced here: 444 us
  waiting for transfers between devices  305 us (68%)
  matrix products  65.9 us (15%)
  starting transfers between devices  22.6 us (5%)
  local copies, waits for them, and re-layouts  20.6 us (5%)
  other arithmetic  15.4 us (3%)
  between operations  15 us (3%)
    ppermute x17, waiting for transfers between devices, swap(): return lax.ppermute(x, axis, [(0, 1), (1, 0)])  271 us
    dot_general x24, matrix products, contract(): lax.dot_general(left, right, (((0,), (0,)), ((), ())), preferred_element_...  65.9 us
    all_gather x3, waiting for transfers between devices, body(): lax.all_gather(lax.dynamic_slice_in_dim(rest, m * rw, rw, axis=1), 'az',...  30.3 us
    ppermute x17, starting transfers between devices, swap(): return lax.ppermute(x, axis, [(0, 1), (1, 0)])  15.9 us
    concatenate x5, other arithmetic, others(): doubled = jnp.concatenate([v, v], axis=0)  14.3 us
  transfers between devices with their start and end apart: 22, of which 10 were waited for; matrix products, arithmetic and copies ran while one was open for 20% of the time, Pallas kernels for 0%

profile of v17, /device:TPU:0, one launch (start us, length us, event | category | flops | bytes accessed | tf_op | source)
XLA Modules:
  0.0 444.4 jit_solution(8953968191564967715)
XLA Ops:
  6.5 2.2 constant_dynamic-slice_fusion.3
  8.9 3.0 collective-permute-start
  14.3 66.0 %collective-permute-done = bf16[192,8192]{1,0:T(8,128)(2,1)} collective-permute-done((bf16[192,8192]{1,0:T(8,128)(2,1)}, bf16[192,8192]{1,0:T(8,128)(2,1)}, u32[]{:S(2)}, u32[]{:S(2)}) %collective-permute-start) | collective-permute-done | bytes 3145760 | tf_op jit(solution)/shard_map/ppermute | solution.py:30
  80.3 2.1 constant_dynamic-slice_fusion.2
  83.2 2.1 copy.12
  85.3 6.3 %all-to-all-start = ((bf16[192,8,1024]{2,0,1:T(8,128)(2,1)}), bf16[192,8,1024]{2,0,1:T(8,128)(2,1)}, u32[]{:S(2)}, u32[]{:S(2)}) async-start(bf16[192,8,1024]{2,0,1:T(8,128)(2,1)} %bitcast.34), calls=%async_computation | async-start | bytes 6291456 | tf_op jit(solution)/shard_map/all_to_all | solution.py:57
  91.7 3.9 fusion.26
  95.6 2.0 collective-permute-start.1
  97.5 78.3 %collective-permute-done.1 = bf16[576,2048]{1,0:T(8,128)(2,1)S(1)} collective-permute-done((bf16[576,2048]{1,0:T(8,128)(2,1)}, bf16[576,2048]{1,0:T(8,128)(2,1)S(1)}, u32[]{:S(2)}, u32[]{:S(2)}) %collective-permute-start.1) | collective-permute-done | bytes 2359328 | tf_op jit(solution)/shard_map/ppermute | solution.py:30
  175.9 30.3 %all-gather.7.cloned.1.call-done = bf16[768,2048]{1,0:T(8,128)(2,1)} async-done(((bf16[192,2048]{1,0:T(8,128)(2,1)}), bf16[768,2048]{1,0:T(8,128)(2,1)}) %all-gather.7.cloned.1.call-update) | async-done | bytes 3145744 | tf_op jit(solution)/shard_map/all_gather | solution.py:86
  206.1 2.1 constant_dynamic-slice_fusion.1
  208.5 3.6 all-to-all-done
  212.1 2.6 constant_dynamic-slice_fusion.5
  215.4 2.6 fusion.25
  219.5 3.5 fusion.70
  223.0 1.5 fusion.27
  224.5 2.5 convolution_add_fusion.1
  227.0 2.0 fusion.22
  229.0 2.0 fusion.20
  231.5 2.0 fusion.18
  233.5 2.2 fusion.16
  236.2 33.8 %collective-permute-done.2 = bf16[576,2048]{1,0:T(8,128)(2,1)} collective-permute-done((bf16[576,2048]{1,0:T(8,128)(2,1)S(1)}, bf16[576,2048]{1,0:T(8,128)(2,1)}, u32[]{:S(2)}, u32[]{:S(2)}) %collective-permute-start.2) | collective-permute-done | bytes 2359328 | tf_op jit(solution)/shard_map/ppermute | solution.py:30
  270.0 2.1 constant_dynamic-slice_fusion
  272.1 5.6 %fusion.69 = f32[1024,2048]{1,0:T(8,128)S(1)} fusion(bf16[768,1024]{1,0:T(8,128)(2,1)S(1)} %bitcast.42, bf16[768,2048]{1,0:T(8,128)(2,1)} %all-gather.7.cloned.1.call-done), kind=kOutput, calls=%fused_computation.107 | convolution fusion | flops 3221225472 | bytes 13107200 | tf_op jit(solution)/shard_map/dot_general | solution.py:24
  277.7 2.5 convolution_add_fusion.2
  280.2 3.4 fusion.21
  285.1 2.6 fusion.23
  287.6 1.9 collective-permute-start.12
  289.5 3.0 fusion.19
  293.1 3.0 fusion.17
  296.1 1.6 collective-permute-start.9
  297.7 4.0 fusion.15
  302.1 3.9 fusion.71
  306.1 2.4 convolution_add_fusion
  309.8 22.5 %collective-permute-done.10 = bf16[256,2048]{1,0:T(8,128)(2,1)S(1)} collective-permute-done((bf16[256,2048]{1,0:T(8,128)(2,1)S(1)}, bf16[256,2048]{1,0:T(8,128)(2,1)S(1)}, u32[]{:S(2)}, u32[]{:S(2)}) %collective-permute-start.10) | collective-permute-done | bytes 1048608 | tf_op jit(solution)/shard_map/ppermute | solution.py:30
  332.2 22.5 %collective-permute-done.9 = bf16[256,2048]{1,0:T(8,128)(2,1)S(1)} collective-permute-done((bf16[256,2048]{1,0:T(8,128)(2,1)S(1)}, bf16[256,2048]{1,0:T(8,128)(2,1)S(1)}, u32[]{:S(2)}, u32[]{:S(2)}) %collective-permute-start.9) | collective-permute-done | bytes 1048608 | tf_op jit(solution)/shard_map/ppermute | solution.py:30
  355.7 2.4 slice_add_fusion
  358.0 3.7 fusion.24
  361.8 13.4 %collective-permute-done.4 = bf16[256,2048]{1,0:T(8,128)(2,1)} collective-permute-done((bf16[256,2048]{1,0:T(8,128)(2,1)}, bf16[256,2048]{1,0:T(8,128)(2,1)}, u32[]{:S(2)}, u32[]{:S(2)}) %collective-permute-start.4) | collective-permute-done | bytes 1048608 | tf_op jit(solution)/shard_map/ppermute | solution.py:30
  376.7 4.0 slice_add_fusion.3
  381.2 2.3 slice_add_fusion.2
  383.5 2.3 slice_add_fusion.1
  386.6 3.6 fusion.68
  390.2 2.8 convolution_add_fusion.3
  393.0 33.3 %collective-permute-done.5 = bf16[576,2048]{1,0:T(8,128)(2,1)S(1)} collective-permute-done((bf16[576,2048]{1,0:T(8,128)(2,1)S(1)}, bf16[576,2048]{1,0:T(8,128)(2,1)S(1)}, u32[]{:S(2)}, u32[]{:S(2)}) %collective-permute-start.5) | collective-permute-done | bytes 2359328 | tf_op jit(solution)/shard_map/ppermute | solution.py:30
  426.3 2.3 fusion.8
  432.0 3.4 copy-done.5
  435.4 2.3 fusion.14
  (88 shorter events, 16.1 us)
Async XLA Ops:
  6.5 7.4 %copy-start.22 = (s32[192]{0:T(256)S(1)}, s32[192]{0:T(256)}, u32[]{:S(2)}) copy-start(s32[192]{0:T(256)} %param.7) | copy-start | bytes 2308
  6.5 7.5 %copy-start.21 = (f32[1536]{0:T(1024)S(1)}, f32[1536]{0:T(1024)}, u32[]{:S(2)}) copy-start(f32[1536]{0:T(1024)} %param.9) | copy-start | bytes 18436
  6.5 73.8 %all-gather.5.cloned.1.call-start = ((), (), s32[]{:S(2)}) async-start(), calls=%async_computation.1 | async-start | bytes 3932160 | tf_op jit(solution)/shard_map/all_gather | solution.py:54
  6.5 75.9 %copy-start.4 = (bf16[192,8192]{1,0:T(8,128)(2,1)S(1)}, bf16[192,8192]{1,0:T(8,128)(2,1)}, u32[]{:S(2)}) copy-start(bf16[192,8192]{1,0:T(8,128)(2,1)} %param.6) | copy-start | bytes 9437188
  8.8 197.3 %all-gather.7.cloned.1.call-start = ((), (), s32[]{:S(2)}) async-start(), calls=%async_computation.2 | async-start | bytes 3932160 | tf_op jit(solution)/shard_map/all_gather | solution.py:86
  8.9 71.5 %collective-permute-start = (bf16[192,8192]{1,0:T(8,128)(2,1)}, bf16[192,8192]{1,0:T(8,128)(2,1)}, u32[]{:S(2)}, u32[]{:S(2)}) collective-permute-start(bf16[192,8192]{1,0:T(8,128)(2,1)} %param.6), channel_id=1, source_target_pairs={{0,1},{1,0},{2,3},{3,2},{4,5},{5,4},{6,7},{7,6},{8,9},{9,8},{10,11... | collective-permute-start | bytes 9437192 | tf_op jit(solution)/shard_map/ppermute | solution.py:30
  85.3 6.4 %copy-start.6 = (bf16[768,2048]{1,0:T(8,128)(2,1)S(1)}, bf16[768,2048]{1,0:T(8,128)(2,1)}, u32[]{:S(2)}) copy-start(bf16[768,2048]{1,0:T(8,128)(2,1)} %all-gather.5.cloned.1.call-done) | copy-start | bytes 9437188
  85.3 126.8 %all-to-all-start = ((bf16[192,8,1024]{2,0,1:T(8,128)(2,1)}), bf16[192,8,1024]{2,0,1:T(8,128)(2,1)}, u32[]{:S(2)}, u32[]{:S(2)}) async-start(bf16[192,8,1024]{2,0,1:T(8,128)(2,1)} %bitcast.34), calls=%async_computation | async-start | bytes 6291456 | tf_op jit(solution)/shard_map/all_to_all | solution.py:57
  91.6 178.4 %all-gather.9.cloned.1.call-start = ((), (), s32[]{:S(2)}) async-start(), calls=%async_computation.3 | async-start | bytes 3932160 | tf_op jit(solution)/shard_map/all_gather | solution.py:86
  95.6 80.3 %collective-permute-start.1 = (bf16[576,2048]{1,0:T(8,128)(2,1)}, bf16[576,2048]{1,0:T(8,128)(2,1)S(1)}, u32[]{:S(2)}, u32[]{:S(2)}) collective-permute-start(bf16[576,2048]{1,0:T(8,128)(2,1)} %fusion.26), channel_id=1, source_target_pairs={{0,1},{1,0},{2,3},{3,2},{4,5},{5,4},{6,7},{7,6},{8,9},{9,8},{10,11... | collective-permute-start | bytes 7077896 | tf_op jit(solution)/shard_map/ppermute | solution.py:30
  208.2 149.8 %all-gather.11.cloned.1.call-start = ((), (), s32[]{:S(2)}) async-start(), calls=%async_computation.4 | async-start | bytes 3932160 | tf_op jit(solution)/shard_map/all_gather | solution.py:86
  212.1 3.3 copy-start.8
  215.4 4.0 copy-start.11
  215.4 9.1 %copy-start.2 = (bf16[4,1,192,1024]{3,2,1,0:T(8,128)(2,1)}, bf16[4,1,192,1024]{3,2,1,0:T(8,128)(2,1)S(1)}, u32[]{:S(2)}) copy-start(bf16[4,1,192,1024]{3,2,1,0:T(8,128)(2,1)S(1)} %get-tuple-element.21) | copy-start | bytes 4718596
  215.4 4.0 copy-start.7
  218.0 52.0 %collective-permute-start.2 = (bf16[576,2048]{1,0:T(8,128)(2,1)S(1)}, bf16[576,2048]{1,0:T(8,128)(2,1)}, u32[]{:S(2)}, u32[]{:S(2)}) collective-permute-start(bf16[576,2048]{1,0:T(8,128)(2,1)S(1)} %fusion.25), channel_id=1, source_target_pairs={{0,1},{1,0},{2,3},{3,2},{4,5},{5,4},{6,7},{7,6},{8,9},{9,8},{10,11... | collective-permute-start | bytes 7077896 | tf_op jit(solution)/shard_map/ppermute | solution.py:30
  229.0 51.2 %collective-permute-start.8 = (bf16[256,2048]{1,0:T(8,128)(2,1)}, bf16[256,2048]{1,0:T(8,128)(2,1)}, u32[]{:S(2)}, u32[]{:S(2)}) collective-permute-start(bf16[256,2048]{1,0:T(8,128)(2,1)} %fusion.22), channel_id=1, source_target_pairs={{0,8},{8,0},{1,9},{9,1},{2,10},{10,2},{3,11},{11,3},{4,12},{12,4},... | collective-permute-start | bytes 3145736 | tf_op jit(solution)/shard_map/ppermute | solution.py:30
  231.0 58.5 %collective-permute-start.7 = (bf16[256,2048]{1,0:T(8,128)(2,1)}, bf16[256,2048]{1,0:T(8,128)(2,1)}, u32[]{:S(2)}, u32[]{:S(2)}) collective-permute-start(bf16[256,2048]{1,0:T(8,128)(2,1)} %fusion.20), channel_id=1, source_target_pairs={{0,8},{8,0},{1,9},{9,1},{2,10},{10,2},{3,11},{11,3},{4,12},{12,4},... | collective-permute-start | bytes 3145736 | tf_op jit(solution)/shard_map/ppermute | solution.py:30
  233.5 59.6 %collective-permute-start.6 = (bf16[256,2048]{1,0:T(8,128)(2,1)}, bf16[256,2048]{1,0:T(8,128)(2,1)}, u32[]{:S(2)}, u32[]{:S(2)}) collective-permute-start(bf16[256,2048]{1,0:T(8,128)(2,1)} %fusion.18), channel_id=1, source_target_pairs={{0,8},{8,0},{1,9},{9,1},{2,10},{10,2},{3,11},{11,3},{4,12},{12,4},... | collective-permute-start | bytes 3145736 | tf_op jit(solution)/shard_map/ppermute | solution.py:30
  235.7 36.4 %copy-start.12 = (bf16[4,1,192,1024]{3,2,1,0:T(8,128)(2,1)S(1)}, bf16[4,1,192,1024]{3,2,1,0:T(8,128)(2,1)}, u32[]{:S(2)}) copy-start(bf16[4,1,192,1024]{3,2,1,0:T(8,128)(2,1)} %copy-done.11) | copy-start | bytes 4718596
  235.7 62.0 %collective-permute-start.3 = (bf16[256,2048]{1,0:T(8,128)(2,1)}, bf16[256,2048]{1,0:T(8,128)(2,1)}, u32[]{:S(2)}, u32[]{:S(2)}) collective-permute-start(bf16[256,2048]{1,0:T(8,128)(2,1)} %fusion.16), channel_id=1, source_target_pairs={{0,8},{8,0},{1,9},{9,1},{2,10},{10,2},{3,11},{11,3},{4,12},{12,4},... | collective-permute-start | bytes 3145736 | tf_op jit(solution)/shard_map/ppermute | solution.py:30
  272.1 5.6 %copy-start.3 = (bf16[4,1,192,1024]{3,2,1,0:T(8,128)(2,1)S(1)}, bf16[4,1,192,1024]{3,2,1,0:T(8,128)(2,1)}, u32[]{:S(2)}) copy-start(bf16[4,1,192,1024]{3,2,1,0:T(8,128)(2,1)} %copy-done.2) | copy-start | bytes 4718596
  280.2 4.9 %copy-start.9 = (bf16[768,2048]{1,0:T(8,128)(2,1)S(1)}, bf16[768,2048]{1,0:T(8,128)(2,1)}, u32[]{:S(2)}) copy-start(bf16[768,2048]{1,0:T(8,128)(2,1)} %all-gather.9.cloned.1.call-done) | copy-start | bytes 9437188
  283.6 26.2 %collective-permute-start.11 = (bf16[256,2048]{1,0:T(8,128)(2,1)S(1)}, bf16[256,2048]{1,0:T(8,128)(2,1)S(1)}, u32[]{:S(2)}, u32[]{:S(2)}) collective-permute-start(bf16[256,2048]{1,0:T(8,128)(2,1)S(1)} %fusion.21), channel_id=1, source_target_pairs={{0,16},{16,0},{1,17},{17,1},{2,18},{18,2},{3,19},{19,3},{4,20},{20... | collective-permute-start | bytes 3145736 | tf_op jit(solution)/shard_map/ppermute | solution.py:30
  287.6 67.1 %collective-permute-start.12 = (bf16[576,2048]{1,0:T(8,128)(2,1)S(1)}, bf16[576,2048]{1,0:T(8,128)(2,1)S(1)}, u32[]{:S(2)}, u32[]{:S(2)}) collective-permute-start(bf16[576,2048]{1,0:T(8,128)(2,1)S(1)} %fusion.23), channel_id=1, source_target_pairs={{0,1},{1,0},{2,3},{3,2},{4,5},{5,4},{6,7},{7,6},{8,9},{9,8},{10,11... | collective-permute-start | bytes 7077896 | tf_op jit(solution)/shard_map/ppermute | solution.py:30
  292.5 39.7 %collective-permute-start.10 = (bf16[256,2048]{1,0:T(8,128)(2,1)S(1)}, bf16[256,2048]{1,0:T(8,128)(2,1)S(1)}, u32[]{:S(2)}, u32[]{:S(2)}) collective-permute-start(bf16[256,2048]{1,0:T(8,128)(2,1)S(1)} %fusion.19), channel_id=1, source_target_pairs={{0,16},{16,0},{1,17},{17,1},{2,18},{18,2},{3,19},{19,3},{4,20},{20... | collective-permute-start | bytes 3145736 | tf_op jit(solution)/shard_map/ppermute | solution.py:30
  296.1 6.0 %copy-start.13 = (bf16[4,1,192,1024]{3,2,1,0:T(8,128)(2,1)S(1)}, bf16[4,1,192,1024]{3,2,1,0:T(8,128)(2,1)}, u32[]{:S(2)}) copy-start(bf16[4,1,192,1024]{3,2,1,0:T(8,128)(2,1)} %copy-done.11) | copy-start | bytes 4718596
  296.1 58.6 %collective-permute-start.9 = (bf16[256,2048]{1,0:T(8,128)(2,1)S(1)}, bf16[256,2048]{1,0:T(8,128)(2,1)S(1)}, u32[]{:S(2)}, u32[]{:S(2)}) collective-permute-start(bf16[256,2048]{1,0:T(8,128)(2,1)S(1)} %fusion.17), channel_id=1, source_target_pairs={{0,16},{16,0},{1,17},{17,1},{2,18},{18,2},{3,19},{19,3},{4,20},{20... | collective-permute-start | bytes 3145736 | tf_op jit(solution)/shard_map/ppermute | solution.py:30
  301.6 73.5 %collective-permute-start.4 = (bf16[256,2048]{1,0:T(8,128)(2,1)}, bf16[256,2048]{1,0:T(8,128)(2,1)}, u32[]{:S(2)}, u32[]{:S(2)}) collective-permute-start(bf16[256,2048]{1,0:T(8,128)(2,1)} %fusion.15), channel_id=1, source_target_pairs={{0,16},{16,0},{1,17},{17,1},{2,18},{18,2},{3,19},{19,3},{4,20},{20... | collective-permute-start | bytes 3145736 | tf_op jit(solution)/shard_map/ppermute | solution.py:30
  308.5 46.2 %copy-start = (f32[1024,2048]{1,0:T(8,128)}, f32[1024,2048]{1,0:T(8,128)S(1)}, u32[]{:S(2)}) copy-start(f32[1024,2048]{1,0:T(8,128)S(1)} %convolution_add_fusion) | copy-start | bytes 25165828
  309.8 45.0 %copy-start.15 = (bf16[256,2048]{1,0:T(8,128)(2,1)}, bf16[256,2048]{1,0:T(8,128)(2,1)S(1)}, u32[]{:S(2)}) copy-start(bf16[256,2048]{1,0:T(8,128)(2,1)S(1)} %collective-permute-done.11) | copy-start | bytes 3145732
  332.2 22.5 %copy-start.17 = (bf16[256,2048]{1,0:T(8,128)(2,1)}, bf16[256,2048]{1,0:T(8,128)(2,1)S(1)}, u32[]{:S(2)}) copy-start(bf16[256,2048]{1,0:T(8,128)(2,1)S(1)} %collective-permute-done.10) | copy-start | bytes 3145732
  354.7 1.0 copy-start.19
  358.0 23.1 %copy-start.1 = (f32[1024,2048]{1,0:T(8,128)S(1)}, f32[1024,2048]{1,0:T(8,128)}, u32[]{:S(2)}) copy-start(f32[1024,2048]{1,0:T(8,128)} %copy-done) | copy-start | bytes 25165828
  375.2 51.1 %collective-permute-start.5 = (bf16[576,2048]{1,0:T(8,128)(2,1)S(1)}, bf16[576,2048]{1,0:T(8,128)(2,1)S(1)}, u32[]{:S(2)}, u32[]{:S(2)}) collective-permute-start(bf16[576,2048]{1,0:T(8,128)(2,1)S(1)} %fusion.24), channel_id=1, source_target_pairs={{0,1},{1,0},{2,3},{3,2},{4,5},{5,4},{6,7},{7,6},{8,9},{9,8},{10,11... | collective-permute-start | bytes 7077896 | tf_op jit(solution)/shard_map/ppermute | solution.py:30
  380.6 51.3 %collective-permute-start.16 = (f32[256,2048]{1,0:T(8,128)}, f32[256,2048]{1,0:T(8,128)S(1)}, u32[]{:S(2)}, u32[]{:S(2)}) collective-permute-start(f32[256,2048]{1,0:T(8,128)} %slice_add_fusion), channel_id=1, source_target_pairs={{0,8},{8,0},{1,9},{9,1},{2,10},{10,2},{3,11},{11,3},{4,12},{12,4},... | collective-permute-start | bytes 6291464 | tf_op jit(solution)/shard_map/ppermute | solution.py:30
  380.6 12.3 %collective-permute-start.13 = (f32[256,2048]{1,0:T(8,128)}, f32[256,2048]{1,0:T(8,128)S(1)}, u32[]{:S(2)}, u32[]{:S(2)}) collective-permute-start(f32[256,2048]{1,0:T(8,128)} %slice_add_fusion.3), channel_id=1, source_target_pairs={{0,8},{8,0},{1,9},{9,1},{2,10},{10,2},{3,11},{11,3},{4,12},{12,4},... | collective-permute-start | bytes 6291464 | tf_op jit(solution)/shard_map/ppermute | solution.py:30
  383.5 2.8 copy-start.10
  383.5 3.1 copy-start.14
  383.5 46.2 %collective-permute-start.14 = (f32[256,2048]{1,0:T(8,128)}, f32[256,2048]{1,0:T(8,128)S(1)}, u32[]{:S(2)}, u32[]{:S(2)}) collective-permute-start(f32[256,2048]{1,0:T(8,128)} %slice_add_fusion.2), channel_id=1, source_target_pairs={{0,8},{8,0},{1,9},{9,1},{2,10},{10,2},{3,11},{11,3},{4,12},{12,4},... | collective-permute-start | bytes 6291464 | tf_op jit(solution)/shard_map/ppermute | solution.py:30
  385.8 45.1 %collective-permute-start.15 = (f32[256,2048]{1,0:T(8,128)}, f32[256,2048]{1,0:T(8,128)S(1)}, u32[]{:S(2)}, u32[]{:S(2)}) collective-permute-start(f32[256,2048]{1,0:T(8,128)} %slice_add_fusion.1), channel_id=1, source_target_pairs={{0,8},{8,0},{1,9},{9,1},{2,10},{10,2},{3,11},{11,3},{4,12},{12,4},... | collective-permute-start | bytes 6291464 | tf_op jit(solution)/shard_map/ppermute | solution.py:30
  428.6 1.2 copy-start.20
  429.7 1.3 copy-start.18
  430.9 4.5 %copy-start.16 = (bf16[256,2048]{1,0:T(8,128)(2,1)S(1)}, bf16[256,2048]{1,0:T(8,128)(2,1)}, u32[]{:S(2)}) copy-start(bf16[256,2048]{1,0:T(8,128)(2,1)} %copy-done.15) | copy-start | bytes 3145732
  432.0 3.4 copy-start.5
Sparse Core Ops, SparseCore 0:
  8.9 66.1 all-gather.4
  82.6 123.4 all-gather.6
  208.4 60.7 all-gather.8
  272.2 63.5 all-gather.10
